TPU v7x, 32 devices: a whole 2x2x4 slice. The times are simulated.
32 devices in a mesh: depth: 8 (over z, y), rows: 4 (over x, core).
Axes of the slice: x: 2, y: 2, z: 4, core: 2. Of those that a mesh axis runs over, the one named last changes fastest.
Arguments:
- density_raw: bfloat16 [256, 64, 1024], P('depth', 'rows'), may hold values from -6 to 6
- colour_raw: bfloat16 [3, 256, 64, 1024], P(None, 'depth', 'rows'), may hold values from -6 to 6
- target: float32 [3, 64, 1024], P(None, 'rows'), may hold values from 0 to 1
- slab_rank: int32 [8], replicated, may hold values from 0 to 7, each once
Outputs:
- grad_density: float32 [256, 64, 1024], P('depth', 'rows')
- grad_colour: float32 [3, 256, 64, 1024], P(None, 'depth', 'rows')
Inputs may be any that keep to these rules, and one draw needn't show every extreme that they name: slab_rank is a permutation: every slab has its own position along the rays.
All inputs are finite; a program needn't handle non-finite values.
Results may differ from a plain program's by a relative error of at most 0.0003.
Values may be sent and summed in bfloat16 or wider, within the bound.
No kernel may reach another device: no remote copies, remote signals or barrier semaphores. Data moves between devices by JAX's collectives and lax.ppermute only.
A program may use at most 128 MiB of HBM per device.

v0:
```python
import jax
import jax.numpy as jnp
from jax import lax
from jax.sharding import PartitionSpec as P

optical_depth = 2.5
smooth_weight = 0.05


def extended(value, sides, width):
    for axis, dim in sides:
        peers, length = (lax.axis_size(axis), value.shape[dim])
        up = [(i, (i + 1) % peers) for i in range(peers - 1)]
        down = [(j, i) for i, j in up]
        last = lax.slice_in_dim(value, length - width, length, axis=dim)
        initial = lax.slice_in_dim(value, 0, width, axis=dim)
        before = lax.ppermute(last, axis, up)
        after = lax.ppermute(initial, axis, down)
        value = jnp.concatenate([before, value, after], axis=dim)
    return value


def along_rays(matrix, values):
    shape = values.shape
    flat = values.reshape(shape[0], shape[1], -1)
    mixed = jnp.einsum("ij,cjp->cip", matrix, flat, precision=lax.Precision.HIGHEST)
    return mixed.reshape(shape)


def triangles(count):
    index = jnp.arange(count, dtype=jnp.int32)
    before = (index[None, :] < index[:, None]).astype(jnp.float32)
    after = (index[None, :] > index[:, None]).astype(jnp.float32)
    return (before, after)


def slab_terms(density, colour_raw, step_depth):
    dense = density.astype(jnp.float32)
    colour = jax.nn.sigmoid(colour_raw.astype(jnp.float32))
    depth_term = step_depth * jax.nn.softplus(dense)
    opacity = -jnp.expm1(-depth_term)
    kept = jnp.exp(-depth_term)
    before, after = triangles(dense.shape[0])
    front_light = jnp.exp(-along_rays(before, depth_term[None]))[0]
    through = front_light * kept
    passing = jnp.exp(-jnp.sum(depth_term, axis=0))
    weighted = front_light[None] * opacity[None] * colour
    behind_local = along_rays(after, weighted) / through[None]
    after_light = passing[None] / through
    partial_value = jnp.concatenate([jnp.sum(weighted, axis=1), passing[None]], axis=0)
    return (partial_value, (dense, colour, opacity, behind_local, after_light, front_light))


def slab_gradients(saved, scaled_residual, scaled_behind, slices_total):
    dense, colour, opacity, behind_local, after_light, front_light = saved
    lit = front_light * opacity
    grad_colour = slices_total * scaled_residual[:, None] * lit[None] * colour * (1.0 - colour)
    inner = (
        jnp.sum(scaled_residual[:, None] * (colour - behind_local), axis=0)
        - after_light * scaled_behind[None]
    )
    grad_density = optical_depth * front_light * (1.0 - opacity) * jax.nn.sigmoid(dense) * inner
    return (grad_density, grad_colour)


def composite(partials, slab_rank, target_piece):
    count = partials.shape[1]
    one_hot = (slab_rank[:, None] == jnp.arange(count, dtype=jnp.int32)[None]).astype(
        partials.dtype
    )
    ordered = jnp.einsum("sk,csl->ckl", one_hot, partials, precision=lax.Precision.HIGHEST)
    emitted, kept = (ordered[:3], ordered[3:])
    before, after = triangles(count)
    front = jnp.exp(along_rays(before, jnp.log(kept)))
    weighted = front * emitted
    behind = along_rays(after, weighted) / (front * kept)
    residual = jnp.sum(weighted, axis=1) - target_piece
    scaled_residual = front * residual[:, None]
    scaled_behind = front * jnp.sum(residual[:, None] * behind, axis=0, keepdims=True)
    stacked = jnp.concatenate([scaled_residual, scaled_behind], axis=0)
    return jnp.einsum("sk,ckl->csl", one_hot, stacked, precision=lax.Precision.HIGHEST)


def smooth_rims(density_raw, slices_dev, rows_dev):
    padded = extended(density_raw, (("depth", 0), ("rows", 1)), 1).astype(jnp.float32)
    centre = padded[1:-1, 1:-1]
    slice_index = lax.axis_index("depth") * slices_dev + jnp.arange(slices_dev, dtype=jnp.int32)
    row_index = lax.axis_index("rows") * rows_dev + jnp.arange(rows_dev, dtype=jnp.int32)
    last_slice = slices_dev * lax.axis_size("depth") - 1
    last_row = rows_dev * lax.axis_size("rows") - 1
    below = jnp.where((slice_index > 0)[:, None, None], centre - padded[:-2, 1:-1], 0.0)
    above = jnp.where((slice_index < last_slice)[:, None, None], centre - padded[2:, 1:-1], 0.0)
    upper = jnp.where((row_index > 0)[None, :, None], centre - padded[1:-1, :-2], 0.0)
    lower = jnp.where((row_index < last_row)[None, :, None], centre - padded[1:-1, 2:], 0.0)
    return 2.0 * smooth_weight * (below + above + upper + lower)


def local(density_raw, colour_raw, target, slab_rank):
    slices_dev = density_raw.shape[0]
    rows_dev = density_raw.shape[1]
    width = density_raw.shape[2]
    depth_count = lax.axis_size("depth")
    slices_total = slices_dev * depth_count
    partial_value, saved = slab_terms(density_raw, colour_raw, optical_depth / slices_total)
    pixels = rows_dev * width
    stacked = partial_value.reshape(4, 1, pixels)
    target_flat = target.reshape(3, pixels)
    position = lax.axis_index("depth")
    received = lax.all_gather(stacked, "depth", axis=1, tiled=True)
    answers = composite(received, slab_rank, target_flat)
    mine = lax.dynamic_index_in_dim(answers, position, 1, keepdims=False)
    mine = mine.reshape(4, rows_dev, width)
    grad_density, grad_colour = slab_gradients(saved, mine[:3], mine[3], slices_total)
    grad_density = grad_density + smooth_rims(density_raw, slices_dev, rows_dev)
    return (grad_density, grad_colour)


def solution(mesh):
    placed = (P("depth", "rows", None), P(None, "depth", "rows", None), P(None, "rows", None), P())
    return jax.shard_map(
        local,
        mesh=mesh,
        in_specs=placed,
        out_specs=(P("depth", "rows", None), P(None, "depth", "rows", None)),
        check_vma=False,
    )
```

profile of v0, /device:TPU:0, one launch (start us, length us, event | category | flops | bytes accessed | tf_op | source)
XLA Modules:
  0.0 106.4 jit_solution(17140207208497940315)
XLA Ops:
  7.2 0.0 all-gather.2.cloned.1.call-start
  7.2 2.4 %fusion.16 = f32[32,16,1024]{2,1,0:T(8,128)S(1)} fusion(bf16[32,16,1024]{2,1,0:T(8,128)(2,1)} %param.4), kind=kLoop, calls=%fused_computation.28 | loop fusion | flops 4194304 | bytes 3145728 | tf_op jit(solution)/shard_map/mul | solution.py:40
  9.7 1.2 %copy.40 = f32[4,8,16,1024]{3,1,2,0:T(8,128)S(1)} copy(f32[4,8,16,1024]{3,2,1,0:T(8,128)S(1)} %bitcast.83) | data formatting | bytes 4194304
  10.9 1.2 %fusion = f32[16384,32]{0,1:T(8,128)S(1)} fusion(f32[32,16384]{1,0:T(8,128)S(1)} %bitcast.81), kind=kOutput, calls=%fused_computation.2 | convolution fusion | flops 201851904 | bytes 4194304 | tf_op jit(solution)/shard_map/ij,cjp->cip/dot_general | solution.py:26
  12.1 0.0 copy-start.3
  12.1 1.2 %copy.41 = f32[4,8,16,1024]{3,2,1,0:T(8,128)S(1)} copy(f32[4,8,16,1024]{3,1,2,0:T(8,128)S(1)} %bitcast.82) | data formatting | bytes 4194304
  13.3 0.0 copy-start
  13.3 0.0 copy-start.5
  13.4 3.5 %bitcast_multiply_fusion = (f32[32,16,1024]{2,1,0:T(8,128)}, f32[32,16,1024]{2,1,0:T(8,128)S(1)}, f32[16,1024]{1,0:T(8,128)S(1)}) fusion(f32[4,8,16,1024]{3,2,1,0:T(8,128)S(1)} %copy.41, bf16[32,16,1024]{2,1,0:T(8,128)(2,1)S(1)} %copy-done.3), kind=kLoop, calls=%fused_computation.29 | loop fusion | flops 6799360 | bytes 7405568 | tf_op jit(solution)/shard_map/mul | solution.py:45
  16.8 3.6 %fusion.54 = (f32[3,16,1024]{2,1,0:T(8,128)S(1)}, f32[3,32,16,1024]{3,2,1,0:T(8,128)}) fusion(bf16[3,32,16,1024]{3,2,1,0:T(8,128)(2,1)S(1)} %copy-done.5, f32[32,16,1024]{2,1,0:T(8,128)S(1)} %get-tuple-element.13), kind=kLoop, calls=%fused_computation.91 | loop fusion | flops 9388032 | bytes 11730944 | tf_op jit(solution)/shard_map/reduce_sum | solution.py:50
  20.4 0.1 concatenate.15
  20.6 0.1 exp.63
  20.7 0.8 pad_maximum_fusion
  21.5 0.0 all-gather.2.cloned.1.call-update
  21.5 4.9 %collective-permute-start = (bf16[1,16,1024]{2,1,0:T(8,128)(2,1)S(1)}, bf16[1,16,1024]{2,1,0:T(8,128)(2,1)S(1)}, u32[]{:S(2)}, u32[]{:S(2)}) collective-permute-start(bf16[1,16,1024]{2,1,0:T(8,128)(2,1)S(1)} %get-tuple-element.18), channel_id=1, source_target_pairs={{0,4},{4,8},{8,12},{12,16},{16,20},{20,24},{24,28},{1,5},{5,9},{9,... | collective-permute-start | bytes 98312 | tf_op jit(solution)/shard_map/ppermute | solution.py:17
  26.4 1.5 %collective-permute-start.1 = (bf16[1,16,1024]{2,1,0:T(8,128)(2,1)S(1)}, bf16[1,16,1024]{2,1,0:T(8,128)(2,1)S(1)}, u32[]{:S(2)}, u32[]{:S(2)}) collective-permute-start(bf16[1,16,1024]{2,1,0:T(8,128)(2,1)S(1)} %get-tuple-element.17), channel_id=1, source_target_pairs={{4,0},{8,4},{12,8},{16,12},{20,16},{24,20},{28,24},{5,1},{9,5},{13... | collective-permute-start | bytes 98312 | tf_op jit(solution)/shard_map/ppermute | solution.py:18
  27.9 7.2 %reshape.104 = f32[3,32,16384]{2,1,0:T(8,128)} reshape(f32[3,32,16,1024]{3,2,1,0:T(8,128)} %get-tuple-element.9) | data formatting | bytes 12582912 | tf_op jit(solution)/shard_map/reshape | solution.py:25
  35.1 8.7 %fusion.39 = f32[3,16384,32]{1,2,0:T(8,128)} fusion(f32[3,32,16384]{2,1,0:T(8,128)} %reshape.104), kind=kOutput, calls=%fused_computation.72 | convolution fusion | flops 603980800 | bytes 12582912 | tf_op jit(solution)/shard_map/ij,cjp->cip/dot_general | solution.py:26
  43.8 0.9 copy.42
  44.7 10.2 %copy.44 = f32[12,8,16,1024]{3,2,1,0:T(8,128)} copy(f32[12,8,16,1024]{3,1,2,0:T(8,128)} %bitcast.76) | data formatting | bytes 12582912
  54.8 0.0 collective-permute-done
  54.8 0.1 constant_dynamic-update-slice_fusion.1
  54.9 0.0 collective-permute-done.1
  54.9 0.2 fusion.55
  55.2 1.5 %collective-permute-start.2 = (bf16[34,1,1024]{2,0,1:T(8,128)(2,1)S(1)}, bf16[34,1,1024]{2,0,1:T(8,128)(2,1)S(1)}, u32[]{:S(2)}, u32[]{:S(2)}) collective-permute-start(bf16[34,1,1024]{2,0,1:T(8,128)(2,1)S(1)} %copy.34), channel_id=1, source_target_pairs={{0,1},{1,2},{2,3},{4,5},{5,6},{6,7},{8,9},{9,10},{10,11},{12,13},{... | collective-permute-start | bytes 208904 | tf_op jit(solution)/shard_map/ppermute | solution.py:17
  56.7 1.5 %collective-permute-start.3 = (bf16[34,1,1024]{2,0,1:T(8,128)(2,1)S(1)}, bf16[34,1,1024]{2,0,1:T(8,128)(2,1)S(1)}, u32[]{:S(2)}, u32[]{:S(2)}) collective-permute-start(bf16[34,1,1024]{2,0,1:T(8,128)(2,1)S(1)} %copy.35), channel_id=1, source_target_pairs={{1,0},{2,1},{3,2},{5,4},{6,5},{7,6},{9,8},{10,9},{11,10},{13,12},{... | collective-permute-start | bytes 208904 | tf_op jit(solution)/shard_map/ppermute | solution.py:18
  58.2 0.1 copy.36
  58.4 3.1 %collective-permute-done.3 = bf16[34,1,1024]{2,0,1:T(8,128)(2,1)S(1)} collective-permute-done((bf16[34,1,1024]{2,0,1:T(8,128)(2,1)S(1)}, bf16[34,1,1024]{2,0,1:T(8,128)(2,1)S(1)}, u32[]{:S(2)}, u32[]{:S(2)}) %collective-permute-start.3) | collective-permute-done | bytes 69664 | tf_op jit(solution)/shard_map/ppermute | solution.py:18
  61.5 0.1 copy.37
  61.6 0.0 copy-start.11
  61.6 0.7 maximum_convert_fusion
  62.3 11.4 %all-gather.2.cloned.1.call-done = f32[4,8,16384]{2,0,1:T(4,128)} async-done(((f32[4,1,16384]{2,0,1:T(4,128)}), f32[4,8,16384]{2,0,1:T(4,128)}) %all-gather.2.cloned.1.call-update) | async-done | bytes 2097168 | tf_op jit(solution)/shard_map/all_gather | solution.py:109
  73.7 3.9 %convolution_bitcast_fusion = f32[4,8,16384]{2,1,0:T(8,128)S(1)} fusion(f32[4,8,16384]{2,0,1:T(4,128)} %all-gather.2.cloned.1.call-done, s32[8]{0:T(128)S(1)} %copy-done.11), kind=kOutput, calls=%fused_computation | convolution fusion | flops 50331712 | bytes 4194336 | tf_op jit(solution)/shard_map/sk,csl->ckl/dot_general | solution.py:71
  77.5 0.4 convolution_exponential_fusion
  78.0 0.1 fusion.34
  78.0 0.6 fusion.31
  78.7 0.2 copy-done.6
  78.9 0.1 sub.32
  79.0 0.1 broadcast_multiply_fusion.1
  79.1 1.0 fusion.32
  80.2 0.1 bitcast_multiply_fusion.3
  80.2 1.1 %fusion.26 = f32[4,16384,8]{1,2,0:T(8,128)S(1)} fusion(f32[1,8,16384]{2,1,0:T(8,128)S(1)} %bitcast_multiply_fusion.3, f32[3,8,16384]{2,1,0:T(8,128)S(1)} %broadcast_multiply_fusion.1, s32[8]{0:T(128)S(1)} %copy-done.11), kind=kOutput, calls=%fused_computation.45 | convolution fusion | flops 50856000 | bytes 4194336 | tf_op jit(solution)/shard_map/sk,ckl->csl/dot_general | solution.py:81
  81.3 0.6 dynamic-slice_reduce_fusion
  81.9 0.8 broadcast_multiply_fusion.2
  82.7 0.8 dynamic-slice_reduce_fusion.1
  83.6 1.5 %mul.151 = f32[16,1024]{1,0:T(8,128)} reshape(f32[16384]{0:T(1024)} %dynamic-slice_reduce_fusion.1) | data formatting | bytes 131072 | tf_op jit(solution)/shard_map/mul | solution.py:60
  85.0 8.7 %subtract_multiply_fusion = (f32[3,32,16,1024]{3,2,1,0:T(8,128)}, f32[32,16,1024]{2,1,0:T(8,128)S(1)}) fusion(f32[3,16,1024]{2,1,0:T(8,128)S(1)} %get-tuple-element.6, f32[32,16,1024]{2,1,0:T(8,128)} %copy-done.2, bf16[3,32,16,1024]{3,2,1,0:T(8,128)(2,1)} %param.5, f32[32,16,1024]{2,1,0:T(8,128)} %get-tuple-element.12, f32[3,16,1024]{2,1,0:T(8,128)} %get-tuple-element.7, ...), kind=kLoop, calls=%fused_computation.10 | loop fusion | flops 18350080 | bytes 22413312 | tf_op jit(solution)/shard_map/mul | solution.py:57
  93.8 5.7 %fusion.11 = f32[32,16,1024]{2,1,0:T(8,128)} fusion(bf16[32,16,1024]{2,1,0:T(8,128)(2,1)S(1)} %copy-done.4, f32[4,8,16,1024]{3,2,1,0:T(8,128)S(1)} %copy-done.1, f32[34,18,1024]{2,1,0:T(8,128)S(1)} %maximum_convert_fusion, f32[32,16,1024]{2,1,0:T(8,128)S(1)} %get-tuple-element.11, f32[16,1024]{1,0:T(8,128)S(1)} %copy-done.9, f32[16,1024]{1,0:T(8,128)S(1)} %copy-done.8, ...), kind=kLoop, calls=%fused_computation.23 | loop fusion | flops 18350080 | bytes 17956960 | tf_op jit(solution)/shard_map/add | solution.py:114
  (28 shorter events, 0.1 us)
Async XLA Ops:
  7.2 66.5 %all-gather.2.cloned.1.call-start = ((), (), s32[]{:S(2)}) async-start(), calls=%async_computation | async-start | bytes 2359296 | tf_op jit(solution)/shard_map/all_gather | solution.py:109
  12.1 1.2 %copy-start.3 = (bf16[32,16,1024]{2,1,0:T(8,128)(2,1)S(1)}, bf16[32,16,1024]{2,1,0:T(8,128)(2,1)}, u32[]{:S(2)}) copy-start(bf16[32,16,1024]{2,1,0:T(8,128)(2,1)} %param.4) | copy-start | bytes 3145732
  13.3 3.5 %copy-start = (f32[4,8,16,1024]{3,2,1,0:T(8,128)}, f32[4,8,16,1024]{3,2,1,0:T(8,128)S(1)}, u32[]{:S(2)}) copy-start(f32[4,8,16,1024]{3,2,1,0:T(8,128)S(1)} %copy.41) | copy-start | bytes 6291460
  13.3 3.5 %copy-start.5 = (bf16[3,32,16,1024]{3,2,1,0:T(8,128)(2,1)S(1)}, bf16[3,32,16,1024]{3,2,1,0:T(8,128)(2,1)}, u32[]{:S(2)}) copy-start(bf16[3,32,16,1024]{3,2,1,0:T(8,128)(2,1)} %param.5) | copy-start | bytes 9437188
  16.8 3.6 %copy-start.2 = (f32[32,16,1024]{2,1,0:T(8,128)}, f32[32,16,1024]{2,1,0:T(8,128)S(1)}, u32[]{:S(2)}) copy-start(f32[32,16,1024]{2,1,0:T(8,128)S(1)} %get-tuple-element.13) | copy-start | bytes 6291460
  20.6 14.6 %copy-start.7 = (f32[16,1024]{1,0:T(8,128)}, f32[16,1024]{1,0:T(8,128)S(1)}, u32[]{:S(2)}) copy-start(f32[16,1024]{1,0:T(8,128)S(1)} %negate_exponential_fusion) | copy-start | bytes 196612
  21.5 33.3 %collective-permute-start = (bf16[1,16,1024]{2,1,0:T(8,128)(2,1)S(1)}, bf16[1,16,1024]{2,1,0:T(8,128)(2,1)S(1)}, u32[]{:S(2)}, u32[]{:S(2)}) collective-permute-start(bf16[1,16,1024]{2,1,0:T(8,128)(2,1)S(1)} %get-tuple-element.18), channel_id=1, source_target_pairs={{0,4},{4,8},{8,12},{12,16},{16,20},{20,24},{24,28},{1,5},{5,9},{9,... | collective-permute-start | bytes 98312 | tf_op jit(solution)/shard_map/ppermute | solution.py:17
  26.4 28.5 %collective-permute-start.1 = (bf16[1,16,1024]{2,1,0:T(8,128)(2,1)S(1)}, bf16[1,16,1024]{2,1,0:T(8,128)(2,1)S(1)}, u32[]{:S(2)}, u32[]{:S(2)}) collective-permute-start(bf16[1,16,1024]{2,1,0:T(8,128)(2,1)S(1)} %get-tuple-element.17), channel_id=1, source_target_pairs={{4,0},{8,4},{12,8},{16,12},{20,16},{24,20},{28,24},{5,1},{9,5},{13... | collective-permute-start | bytes 98312 | tf_op jit(solution)/shard_map/ppermute | solution.py:18
  35.1 8.7 %copy-start.10 = (f32[3,16,1024]{2,1,0:T(8,128)S(1)}, f32[3,16,1024]{2,1,0:T(8,128)}, u32[]{:S(2)}) copy-start(f32[3,16,1024]{2,1,0:T(8,128)} %param.6) | copy-start | bytes 589828
  55.2 3.0 %collective-permute-start.2 = (bf16[34,1,1024]{2,0,1:T(8,128)(2,1)S(1)}, bf16[34,1,1024]{2,0,1:T(8,128)(2,1)S(1)}, u32[]{:S(2)}, u32[]{:S(2)}) collective-permute-start(bf16[34,1,1024]{2,0,1:T(8,128)(2,1)S(1)} %copy.34), channel_id=1, source_target_pairs={{0,1},{1,2},{2,3},{4,5},{5,6},{6,7},{8,9},{9,10},{10,11},{12,13},{... | collective-permute-start | bytes 208904 | tf_op jit(solution)/shard_map/ppermute | solution.py:17
  56.7 4.8 %collective-permute-start.3 = (bf16[34,1,1024]{2,0,1:T(8,128)(2,1)S(1)}, bf16[34,1,1024]{2,0,1:T(8,128)(2,1)S(1)}, u32[]{:S(2)}, u32[]{:S(2)}) collective-permute-start(bf16[34,1,1024]{2,0,1:T(8,128)(2,1)S(1)} %copy.35), channel_id=1, source_target_pairs={{1,0},{2,1},{3,2},{5,4},{6,5},{7,6},{9,8},{10,9},{11,10},{13,12},{... | collective-permute-start | bytes 208904 | tf_op jit(solution)/shard_map/ppermute | solution.py:18
  61.6 12.1 %copy-start.11 = (s32[8]{0:T(128)S(1)}, s32[8]{0:T(128)}, u32[]{:S(2)}) copy-start(s32[8]{0:T(128)} %param.7) | copy-start | bytes 100
  78.0 1.0 copy-start.6
  85.0 8.8 %copy-start.1 = (f32[4,8,16,1024]{3,2,1,0:T(8,128)S(1)}, f32[4,8,16,1024]{3,2,1,0:T(8,128)}, u32[]{:S(2)}) copy-start(f32[4,8,16,1024]{3,2,1,0:T(8,128)} %copy-done) | copy-start | bytes 6291460
  85.0 8.8 %copy-start.4 = (bf16[32,16,1024]{2,1,0:T(8,128)(2,1)S(1)}, bf16[32,16,1024]{2,1,0:T(8,128)(2,1)}, u32[]{:S(2)}) copy-start(bf16[32,16,1024]{2,1,0:T(8,128)(2,1)} %param.4) | copy-start | bytes 3145732
  85.0 8.8 %copy-start.8 = (f32[16,1024]{1,0:T(8,128)S(1)}, f32[16,1024]{1,0:T(8,128)}, u32[]{:S(2)}) copy-start(f32[16,1024]{1,0:T(8,128)} %copy-done.7) | copy-start | bytes 196612
  85.0 8.8 %copy-start.9 = (f32[16,1024]{1,0:T(8,128)S(1)}, f32[16,1024]{1,0:T(8,128)}, u32[]{:S(2)}) copy-start(f32[16,1024]{1,0:T(8,128)} %mul.151) | copy-start | bytes 196612
Sparse Core Ops, SparseCore 0:
  21.7 51.9 all-gather.1
where the time goes:
time: 107 us; the launch traced here: 106 us
  other arithmetic  27.3 us (26%)
  local copies, waits for them, and re-layouts  24.6 us (23%)
  matrix products  16.3 us (15%)
  waiting for transfers between devices  14.5 us (14%)
  between operations  14.3 us (13%)
  starting transfers between devices  9.35 us (9%)
    unnamed x30, local copies, waits for them, and re-layouts  13.8 us
    all_gather x1, waiting for transfers between devices, local(): received = lax.all_gather(stacked, 'depth', axis=1, tiled=True)  11.4 us
    dot_general x4, matrix products, along_rays(): jnp.einsum('ij,cjp->cip', matrix, flat, precision=lax.Precision.HIGHEST)  11.3 us
    mul x2, other arithmetic, slab_gradients(): slices_total * scaled_residual[:, None] * lit[None] * colour  9.56 us
    reshape x1, local copies, waits for them, and re-layouts, along_rays(): flat = values.reshape(shape[0], shape[1], -1)  7.22 us
    ppermute x2, starting transfers between devices, extended(): before = lax.ppermute(last, axis, up)  6.32 us
    add x1, other arithmetic, local(): grad_density = grad_density + smooth_rims(density_raw, slices_dev, rows_dev)  5.7 us
    dot_general x1, matrix products, composite(): jnp.einsum('sk,csl->ckl', one_hot, partials, precision=lax.Precision.HIGH...  3.86 us
  transfers between devices with their start and end apart: 5, of which 2 were waited for; matrix products, arithmetic and copies ran while one was open for 27% of the time, Pallas kernels for 0%

commit v1 on v0

v1 whole, which is shorter than its diff:
```python
import functools

import jax
import jax.numpy as jnp
from jax import lax
from jax.experimental import pallas as pl
from jax.experimental.pallas import tpu as pltpu
from jax.sharding import PartitionSpec as P

optical_depth = 2.5
smooth_weight = 0.05
lanes = 128


def softplus(x):
    return jnp.maximum(x, 0.0) + jnp.log1p(jnp.exp(-jnp.abs(x)))


def forward_kernel(d_ref, c_ref, out_ref, *, step):
    slices = d_ref.shape[0]
    shape = d_ref.shape[1:]

    def body(z, carry):
        acc, e0, e1, e2 = carry
        dt = step * softplus(d_ref[z].astype(jnp.float32))
        opacity = 1.0 - jnp.exp(-dt)
        lit = jnp.exp(-acc) * opacity
        e0 = e0 + lit * jax.nn.sigmoid(c_ref[0, z].astype(jnp.float32))
        e1 = e1 + lit * jax.nn.sigmoid(c_ref[1, z].astype(jnp.float32))
        e2 = e2 + lit * jax.nn.sigmoid(c_ref[2, z].astype(jnp.float32))
        return (acc + dt, e0, e1, e2)

    zero = jnp.zeros(shape, jnp.float32)
    acc, e0, e1, e2 = lax.fori_loop(0, slices, body, (zero, zero, zero, zero), unroll=4)
    out_ref[0] = e0
    out_ref[1] = e1
    out_ref[2] = e2
    out_ref[3] = jnp.exp(-acc)


def backward_kernel(d_ref, c_ref, part_ref, ans_ref, smooth_ref, gd_ref, gc_ref, *, step, slices_total):
    slices = d_ref.shape[0]
    shape = d_ref.shape[1:]

    def body(z, carry):
        acc, front, w0, w1, w2 = carry
        d = d_ref[z].astype(jnp.float32)
        sp = softplus(d)
        dt = step * sp
        opacity = 1.0 - jnp.exp(-dt)
        acc_next = acc + dt
        through = jnp.exp(-acc_next)
        inv = 1.0 / through
        lit = front * opacity
        col = [jax.nn.sigmoid(c_ref[c, z].astype(jnp.float32)) for c in range(3)]
        w = [w0 + lit * col[0], w1 + lit * col[1], w2 + lit * col[2]]
        inner = -(part_ref[3] * inv) * ans_ref[3]
        for c in range(3):
            sr = ans_ref[c]
            inner = inner + sr * (col[c] - (part_ref[c] - w[c]) * inv)
            gc_ref[c, z] = slices_total * sr * lit * col[c] * (1.0 - col[c])
        gd_ref[z] = optical_depth * through * jnp.exp(d - sp) * inner + smooth_ref[z]
        return (acc_next, through, w[0], w[1], w[2])

    zero = jnp.zeros(shape, jnp.float32)
    one = jnp.ones(shape, jnp.float32)
    lax.fori_loop(0, slices, body, (zero, one, zero, zero, zero), unroll=2)


def forward_partial(density, colour_raw, step):
    slices, rows, width = density.shape
    return pl.pallas_call(
        functools.partial(forward_kernel, step=step),
        grid=(width // lanes,),
        in_specs=[
            pl.BlockSpec((slices, rows, lanes), lambda i: (0, 0, i)),
            pl.BlockSpec((3, slices, rows, lanes), lambda i: (0, 0, 0, i)),
        ],
        out_specs=pl.BlockSpec((4, rows, lanes), lambda i: (0, 0, i)),
        out_shape=jax.ShapeDtypeStruct((4, rows, width), jnp.float32),
    )(density, colour_raw)


def backward_grads(density, colour_raw, partial_value, answers, smooth, step, slices_total):
    slices, rows, width = density.shape
    slab = pl.BlockSpec((slices, rows, lanes), lambda i: (0, 0, i))
    colours = pl.BlockSpec((3, slices, rows, lanes), lambda i: (0, 0, 0, i))
    pixel = pl.BlockSpec((4, rows, lanes), lambda i: (0, 0, i))
    return pl.pallas_call(
        functools.partial(backward_kernel, step=step, slices_total=float(slices_total)),
        grid=(width // lanes,),
        in_specs=[slab, colours, pixel, pixel, slab],
        out_specs=[slab, colours],
        out_shape=[
            jax.ShapeDtypeStruct((slices, rows, width), jnp.float32),
            jax.ShapeDtypeStruct((3, slices, rows, width), jnp.float32),
        ],
        input_output_aliases={4: 0},
    )(density, colour_raw, partial_value, answers, smooth)


def composite(parts, slab_rank, target_piece):
    emitted, passing = (parts[:3], parts[3])
    earlier = (slab_rank[None, :] < slab_rank[:, None]).astype(jnp.float32)
    later = (slab_rank[None, :] > slab_rank[:, None]).astype(jnp.float32)
    front = jnp.exp(jnp.sum(earlier[:, :, None] * jnp.log(passing)[None], axis=1))
    weighted = front[None] * emitted
    behind = jnp.sum(later[None, :, :, None] * weighted[:, None], axis=2) / (front * passing)[None]
    residual = jnp.sum(weighted, axis=1) - target_piece
    scaled_residual = front[None] * residual[:, None]
    scaled_behind = front * jnp.sum(residual[:, None] * behind, axis=0)
    return jnp.concatenate([scaled_residual, scaled_behind[None]], axis=0)


def smooth_rims(density_raw, slices_dev, rows_dev):
    depth_count = lax.axis_size("depth")
    rows_count = lax.axis_size("rows")
    depth_at = lax.axis_index("depth")
    rows_at = lax.axis_index("rows")
    up_d = [(i, i + 1) for i in range(depth_count - 1)]
    up_r = [(i, i + 1) for i in range(rows_count - 1)]
    first_slice = density_raw[:1]
    last_slice = density_raw[-1:]
    first_row = density_raw[:, :1]
    last_row = density_raw[:, -1:]
    prev_slice = lax.ppermute(last_slice, "depth", up_d)
    next_slice = lax.ppermute(first_slice, "depth", [(j, i) for i, j in up_d])
    prev_row = lax.ppermute(last_row, "rows", up_r)
    next_row = lax.ppermute(first_row, "rows", [(j, i) for i, j in up_r])
    prev_slice = jnp.where(depth_at > 0, prev_slice, first_slice)
    next_slice = jnp.where(depth_at < depth_count - 1, next_slice, last_slice)
    prev_row = jnp.where(rows_at > 0, prev_row, first_row)
    next_row = jnp.where(rows_at < rows_count - 1, next_row, last_row)
    dense = density_raw.astype(jnp.float32)
    below = jnp.concatenate([prev_slice, density_raw[:-1]], axis=0).astype(jnp.float32)
    above = jnp.concatenate([density_raw[1:], next_slice], axis=0).astype(jnp.float32)
    upper = jnp.concatenate([prev_row, density_raw[:, :-1]], axis=1).astype(jnp.float32)
    lower = jnp.concatenate([density_raw[:, 1:], next_row], axis=1).astype(jnp.float32)
    return 2.0 * smooth_weight * ((dense - below) + (dense - above) + (dense - upper) + (dense - lower))


def local(density_raw, colour_raw, target, slab_rank):
    slices_dev, rows_dev, width = density_raw.shape
    depth_count = lax.axis_size("depth")
    slices_total = slices_dev * depth_count
    step = optical_depth / slices_total
    pixels = rows_dev * width
    chunk = pixels // depth_count
    partial_value = forward_partial(density_raw, colour_raw, step)
    sent = partial_value.reshape(4, depth_count, chunk)
    received = lax.all_to_all(sent, "depth", 1, 1, tiled=True)
    position = lax.axis_index("depth")
    target_piece = lax.dynamic_slice_in_dim(target.reshape(3, pixels), position * chunk, chunk, axis=1)
    answers = composite(received, slab_rank, target_piece)
    returned = lax.all_to_all(answers, "depth", 1, 1, tiled=True)
    returned = returned.reshape(4, rows_dev, width)
    smooth = smooth_rims(density_raw, slices_dev, rows_dev)
    return backward_grads(density_raw, colour_raw, partial_value, returned, smooth, step, slices_total)


def solution(mesh):
    placed = (P("depth", "rows", None), P(None, "depth", "rows", None), P(None, "rows", None), P())
    return jax.shard_map(
        local,
        mesh=mesh,
        in_specs=placed,
        out_specs=(P("depth", "rows", None), P(None, "depth", "rows", None)),
        check_vma=False,
    )
```

time: 107 us -> 66.1 us (0.62)
  other arithmetic: 27.3 us -> 7.5 us
  Pallas kernels: 0 us -> 19.4 us
  matrix products: 16.3 us -> 0 us
  local copies, waits for them, and re-layouts: 24.6 us -> 9.35 us
  starting transfers between devices: 9.35 us -> 24.1 us
  between operations: 14.3 us -> 0.78 us
  waiting for transfers between devices: 14.5 us -> 3.93 us
    pallas_call x0 -> x2, Pallas kernels: none -> 19.4 us  [the longest x1 12 us: backward_grads(): pl.pallas_call(functools.partial(backward_kernel, step=step, slices_total...]
    dot_general x6 -> x0, matrix products: 16.3 us -> none  [the longest x4 11.3 us: along_rays(): jnp.einsum('ij,cjp->cip', matrix, flat, precision=lax.Precision.HIGHEST)]
    all_to_all x0 -> x2, starting transfers between devices: none -> 12.2 us  [the longest x1 6.22 us: local(): received = lax.all_to_all(sent, 'depth', 1, 1, tiled=True)]
    unnamed x30 -> x5, local copies, waits for them, and re-layouts: 13.8 us -> 1.78 us
    all_gather x1 -> x0, waiting for transfers between devices: 11.4 us -> none  [local(): received = lax.all_gather(stacked, 'depth', axis=1, tiled=True)]
    mul x6 -> x3, other arithmetic: 15.7 us -> 4.36 us  [the longest x1 4.3 us: smooth_rims(): 2.0 * smooth_weight]
    add x1 -> x0, other arithmetic: 5.7 us -> none  [local(): grad_density = grad_density + smooth_rims(density_raw, slices_dev, rows_dev)]
    reshape x1 -> x3, local copies, waits for them, and re-layouts: 7.22 us -> 2.65 us  [the longest x2 1.91 us: local(): sent = partial_value.reshape(4, depth_count, chunk)]
  transfers between devices with their start and end apart: 5 -> 6, of which waited for: 2 -> 1; matrix products, arithmetic and copies ran while one was open for 27% -> 23% of each run, Pallas kernels for 0% -> 11%
where the time goes in v1:
time: 66.1 us; the launch traced here: 65.1 us
  starting transfers between devices  24.1 us (36%)
  Pallas kernels  19.4 us (29%)
  local copies, waits for them, and re-layouts  9.35 us (14%)
  other arithmetic  7.5 us (11%)
  waiting for transfers between devices  3.93 us (6%)
  between operations  0.78 us (1%)
    pallas_call x1, Pallas kernels, backward_grads(): pl.pallas_call(functools.partial(backward_kernel, step=step, slices_total...  12 us
    pallas_call x1, Pallas kernels, forward_partial(): pl.pallas_call(functools.partial(forward_kernel, step=step), grid=(width...  7.39 us
    all_to_all x1, starting transfers between devices, local(): received = lax.all_to_all(sent, 'depth', 1, 1, tiled=True)  6.22 us
    all_to_all x1, starting transfers between devices, local(): returned = lax.all_to_all(answers, 'depth', 1, 1, tiled=True)  5.99 us
    ppermute x1, starting transfers between devices, smooth_rims(): prev_slice = lax.ppermute(last_slice, 'depth', up_d)  5.63 us
    mul x1, other arithmetic, smooth_rims(): 2.0 * smooth_weight  4.3 us
    all_to_all x1, waiting for transfers between devices, local(): returned = lax.all_to_all(answers, 'depth', 1, 1, tiled=True)  3.91 us
    ppermute x1, starting transfers between devices, smooth_rims(): prev_row = lax.ppermute(last_row, 'rows', up_r)  3.69 us
  transfers between devices with their start and end apart: 6, of which 1 were waited for; matrix products, arithmetic and copies ran while one was open for 23% of the time, Pallas kernels for 11%

profile of v1, /device:TPU:0, one launch (start us, length us, event | category | flops | bytes accessed | tf_op | source)
XLA Modules:
  0.0 65.1 jit_solution(5560279652153195630)
XLA Ops:
  0.6 0.8 %fusion.9 = (bf16[1,16,1024]{2,1,0:T(8,128)(2,1)S(1)}, bf16[1,16,1024]{2,1,0:T(8,128)(2,1)S(1)}) fusion(bf16[32,16,1024]{2,1,0:T(8,128)(2,1)} %d_ref.3), kind=kLoop, calls=%fused_computation.29 | loop fusion | bytes 131072 | tf_op jit(solution)/shard_map/slice | solution.py:122
  1.4 1.3 %collective-permute-start.1 = (bf16[1,16,1024]{2,1,0:T(8,128)(2,1)S(1)}, bf16[1,16,1024]{2,1,0:T(8,128)(2,1)S(1)}, u32[]{:S(2)}, u32[]{:S(2)}) collective-permute-start(bf16[1,16,1024]{2,1,0:T(8,128)(2,1)S(1)} %get-tuple-element.14), channel_id=1, source_target_pairs={{4,0},{8,4},{12,8},{16,12},{20,16},{24,20},{28,24},{5,1},{9,5},{13... | collective-permute-start | bytes 98312 | tf_op jit(solution)/shard_map/ppermute | solution.py:127
  2.7 0.0 copy-start
  2.7 5.6 %collective-permute-start = (bf16[1,16,1024]{2,1,0:T(8,128)(2,1)S(1)}, bf16[1,16,1024]{2,1,0:T(8,128)(2,1)S(1)}, u32[]{:S(2)}, u32[]{:S(2)}) collective-permute-start(bf16[1,16,1024]{2,1,0:T(8,128)(2,1)S(1)} %get-tuple-element.15), channel_id=1, source_target_pairs={{0,4},{4,8},{8,12},{12,16},{16,20},{20,24},{24,28},{1,5},{5,9},{9,... | collective-permute-start | bytes 98312 | tf_op jit(solution)/shard_map/ppermute | solution.py:126
  8.4 7.4 %shard_map.59.part_ref = f32[4,16,1024]{2,1,0:T(8,128)} custom-call(bf16[32,16,1024]{2,1,0:T(8,128)(2,1)} %d_ref.3, bf16[3,32,16,1024]{3,2,1,0:T(8,128)(2,1)} %c_ref.3), custom_call_target="tpu_custom_call" | custom-call | tf_op jit(solution)/shard_map/pallas_call | solution.py:72
  15.7 1.0 %reshape.89 = f32[4,8,2048]{2,1,0:T(8,128)S(1)} reshape(f32[4,16,1024]{2,1,0:T(8,128)} %shard_map.59.part_ref) | data formatting | bytes 524288 | tf_op jit(solution)/shard_map/reshape | solution.py:150
  16.8 0.9 %copy.10 = f32[4,8,2048]{2,0,1:T(4,128)} copy(f32[4,8,2048]{2,1,0:T(8,128)S(1)} %reshape.89) | data formatting | bytes 524288 | tf_op jit(solution)/shard_map/reshape | solution.py:150
  17.6 6.2 %all-to-all-start = ((f32[4,8,2048]{2,0,1:T(4,128)}), f32[4,8,2048]{2,0,1:T(4,128)S(1)}, u32[]{:S(2)}, u32[]{:S(2)}) async-start(f32[4,8,2048]{2,0,1:T(4,128)} %copy.10), calls=%async_computation | async-start | bytes 524288 | tf_op jit(solution)/shard_map/all_to_all | solution.py:151
  23.9 0.0 copy-done
  23.9 0.9 %fusion.7 = (bf16[32,1,1024]{2,1,0:T(2,128)(2,1)}, bf16[32,1,1024]{2,1,0:T(2,128)(2,1)}) fusion(bf16[32,16,1024]{2,1,0:T(8,128)(2,1)S(1)} %copy-done), kind=kLoop, calls=%fused_computation.27 | loop fusion | bytes 262144 | tf_op jit(solution)/shard_map/slice | solution.py:124
  24.8 1.3 %collective-permute-start.3 = (bf16[32,1,1024]{2,1,0:T(2,128)(2,1)}, bf16[32,1,1024]{2,1,0:T(2,128)(2,1)}, u32[]{:S(2)}, u32[]{:S(2)}) collective-permute-start(bf16[32,1,1024]{2,1,0:T(2,128)(2,1)} %get-tuple-element.8), channel_id=1, source_target_pairs={{1,0},{2,1},{3,2},{5,4},{6,5},{7,6},{9,8},{10,9},{11,10},{13,12},{... | collective-permute-start | bytes 196616 | tf_op jit(solution)/shard_map/ppermute | solution.py:129
  26.1 3.7 %collective-permute-start.2 = (bf16[32,1,1024]{2,1,0:T(2,128)(2,1)}, bf16[32,1,1024]{2,1,0:T(2,128)(2,1)}, u32[]{:S(2)}, u32[]{:S(2)}) collective-permute-start(bf16[32,1,1024]{2,1,0:T(2,128)(2,1)} %get-tuple-element.9), channel_id=1, source_target_pairs={{0,1},{1,2},{2,3},{4,5},{5,6},{6,7},{8,9},{9,10},{10,11},{12,13},{... | collective-permute-start | bytes 196616 | tf_op jit(solution)/shard_map/ppermute | solution.py:128
  29.8 0.5 fusion.6
  30.3 0.0 copy-start.1
  30.3 1.6 %fusion.8 = (bf16[31,16,1024]{2,1,0:T(8,128)(2,1)}, bf16[31,16,1024]{2,1,0:T(8,128)(2,1)}) fusion(bf16[32,16,1024]{2,1,0:T(8,128)(2,1)S(1)} %copy-done), kind=kLoop, calls=%fused_computation.28 | loop fusion | bytes 4063232 | tf_op jit(solution)/shard_map/slice | solution.py:136
  31.9 0.0 copy-done.1
  31.9 0.1 compare_convert_fusion
  31.9 1.8 %copy.17 = f32[1,3,16,1024]{3,1,2,0:T(4,128)} copy(f32[1,3,16,1024]{3,2,1,0:T(8,128)} %bitcast.16) | data formatting | bytes 393216
  33.7 0.0 collective-permute-done.1
  33.7 0.0 collective-permute-done
  33.7 0.0 all-to-all-done
  33.7 0.1 slice.40
  33.9 0.2 multiply_reduce_fusion.1
  34.1 0.2 fusion.5
  34.3 0.5 multiply_reduce_fusion
  34.9 0.8 %dynamic-slice_subtract_fusion = f32[3,2048]{1,0:T(4,128)S(1)} fusion(f32[3,2048]{1,0:T(4,128)S(1)} %get-tuple-element.2, f32[3,16384]{1,0:T(4,128)} %bitcast.15, s32[]{:T(128)S(6)} %select_n.31), kind=kLoop, calls=%fused_computation.20 | loop fusion | flops 6144 | bytes 73732 | tf_op jit(solution)/shard_map/sub | solution.py:109
  35.7 0.9 %copy.13 = f32[4,8,2048]{2,0,1:T(4,128)} copy(f32[4,8,2048]{2,1,0:T(8,128)S(1)} %pad_maximum_fusion) | data formatting | bytes 524288 | tf_op jit(solution)/shard_map/concatenate | solution.py:112
  36.6 6.0 %all-to-all-start.1 = ((f32[4,8,2048]{2,0,1:T(4,128)}), f32[4,8,2048]{2,0,1:T(4,128)S(1)}, u32[]{:S(2)}, u32[]{:S(2)}) async-start(f32[4,8,2048]{2,0,1:T(4,128)} %copy.13), calls=%async_computation.1 | async-start | bytes 524288 | tf_op jit(solution)/shard_map/all_to_all | solution.py:155
  42.6 0.0 collective-permute-done.3
  42.6 0.0 collective-permute-done.2
  42.6 1.3 %broadcast_select_fusion = (bf16[32,1,1024]{2,1,0:T(2,128)(2,1)S(1)}, bf16[32,1,1024]{2,1,0:T(2,128)(2,1)S(1)}) fusion(bf16[32,1,1024]{2,1,0:T(2,128)(2,1)} %collective-permute-done.3, pred[]{:T(512)S(6)} %lt.31, bf16[32,16,1024]{2,1,0:T(8,128)(2,1)S(1)} %copy-done, bf16[32,1,1024]{2,1,0:T(2,128)(2,1)} %collective-permute-done.2, pred[]{:T(512)S(6)} %gt.21), kind=kLoop, calls=%fused_computation.11 | loop fusion | flops 65536 | bytes 393218 | tf_op jit(solution)/shard_map/jit(_where)/select_n | solution.py:133
  43.9 4.3 %fusion.3.smooth_ref = f32[32,16,1024]{2,1,0:T(8,128)} fusion(bf16[32,16,1024]{2,1,0:T(8,128)(2,1)S(1)} %copy-done, bf16[31,16,1024]{2,1,0:T(8,128)(2,1)} %get-tuple-element.11, bf16[1,16,1024]{2,1,0:T(8,128)(2,1)S(1)} %get-tuple-element.13, bf16[1,16,1024]{2,1,0:T(8,128)(2,1)S(1)} %get-tuple-element.12, bf16[31,16,1024]{2,1,0:T(8,128)(2,1)} %get-tuple-element.10, ...), kind=kLoop, calls=%fused_computation.7 | loop fusion | flops 13107200 | bytes 7340032 | tf_op jit(solution)/shard_map/mul | solution.py:139
  48.2 3.9 %all-to-all-done.1 = f32[4,8,2048]{2,0,1:T(4,128)S(1)} async-done(((f32[4,8,2048]{2,0,1:T(4,128)}), f32[4,8,2048]{2,0,1:T(4,128)S(1)}, u32[]{:S(2)}, u32[]{:S(2)}) %all-to-all-start.1) | async-done | bytes 262176 | tf_op jit(solution)/shard_map/all_to_all | solution.py:155
  52.1 0.2 copy.14
  52.3 0.7 %reshape.91.ans_ref = f32[4,16,1024]{2,1,0:T(8,128)} reshape(f32[4,8,2048]{2,1,0:T(8,128)S(1)} %copy.14) | data formatting | bytes 524288 | tf_op jit(solution)/shard_map/reshape | solution.py:156
  53.0 12.0 %shard_map.60 = (f32[32,16,1024]{2,1,0:T(8,128)}, f32[3,32,16,1024]{3,2,1,0:T(8,128)}) custom-call(bf16[32,16,1024]{2,1,0:T(8,128)(2,1)} %d_ref.3, bf16[3,32,16,1024]{3,2,1,0:T(8,128)(2,1)} %c_ref.3, f32[4,16,1024]{2,1,0:T(8,128)} %shard_map.59.part_ref, f32[4,16,1024]{2,1,0:T(8,128)} %reshape.91.ans_ref, ...), custom_call_target="tpu_custom_call", output_to_operand_aliasing={{0}: (4, {})} | custom-call | tf_op jit(solution)/shard_map/pallas_call | solution.py:89
  (7 shorter events, 0.2 us)
Async XLA Ops:
  1.4 32.3 %collective-permute-start.1 = (bf16[1,16,1024]{2,1,0:T(8,128)(2,1)S(1)}, bf16[1,16,1024]{2,1,0:T(8,128)(2,1)S(1)}, u32[]{:S(2)}, u32[]{:S(2)}) collective-permute-start(bf16[1,16,1024]{2,1,0:T(8,128)(2,1)S(1)} %get-tuple-element.14), channel_id=1, source_target_pairs={{4,0},{8,4},{12,8},{16,12},{20,16},{24,20},{28,24},{5,1},{9,5},{13... | collective-permute-start | bytes 98312 | tf_op jit(solution)/shard_map/ppermute | solution.py:127
  2.7 21.2 %copy-start = (bf16[32,16,1024]{2,1,0:T(8,128)(2,1)S(1)}, bf16[32,16,1024]{2,1,0:T(8,128)(2,1)}, u32[]{:S(2)}) copy-start(bf16[32,16,1024]{2,1,0:T(8,128)(2,1)} %d_ref.3) | copy-start | bytes 3145732
  2.7 31.0 %collective-permute-start = (bf16[1,16,1024]{2,1,0:T(8,128)(2,1)S(1)}, bf16[1,16,1024]{2,1,0:T(8,128)(2,1)S(1)}, u32[]{:S(2)}, u32[]{:S(2)}) collective-permute-start(bf16[1,16,1024]{2,1,0:T(8,128)(2,1)S(1)} %get-tuple-element.15), channel_id=1, source_target_pairs={{0,4},{4,8},{8,12},{12,16},{16,20},{20,24},{24,28},{1,5},{5,9},{9,... | collective-permute-start | bytes 98312 | tf_op jit(solution)/shard_map/ppermute | solution.py:126
  17.6 16.1 %all-to-all-start = ((f32[4,8,2048]{2,0,1:T(4,128)}), f32[4,8,2048]{2,0,1:T(4,128)S(1)}, u32[]{:S(2)}, u32[]{:S(2)}) async-start(f32[4,8,2048]{2,0,1:T(4,128)} %copy.10), calls=%async_computation | async-start | bytes 524288 | tf_op jit(solution)/shard_map/all_to_all | solution.py:151
  24.8 17.8 %collective-permute-start.3 = (bf16[32,1,1024]{2,1,0:T(2,128)(2,1)}, bf16[32,1,1024]{2,1,0:T(2,128)(2,1)}, u32[]{:S(2)}, u32[]{:S(2)}) collective-permute-start(bf16[32,1,1024]{2,1,0:T(2,128)(2,1)} %get-tuple-element.8), channel_id=1, source_target_pairs={{1,0},{2,1},{3,2},{5,4},{6,5},{7,6},{9,8},{10,9},{11,10},{13,12},{... | collective-permute-start | bytes 196616 | tf_op jit(solution)/shard_map/ppermute | solution.py:129
  26.1 16.5 %collective-permute-start.2 = (bf16[32,1,1024]{2,1,0:T(2,128)(2,1)}, bf16[32,1,1024]{2,1,0:T(2,128)(2,1)}, u32[]{:S(2)}, u32[]{:S(2)}) collective-permute-start(bf16[32,1,1024]{2,1,0:T(2,128)(2,1)} %get-tuple-element.9), channel_id=1, source_target_pairs={{0,1},{1,2},{2,3},{4,5},{5,6},{6,7},{8,9},{9,10},{10,11},{12,13},{... | collective-permute-start | bytes 196616 | tf_op jit(solution)/shard_map/ppermute | solution.py:128
  30.3 1.6 %copy-start.1 = (s32[8]{0:T(128)S(1)}, s32[8]{0:T(128)}, u32[]{:S(2)}) copy-start(s32[8]{0:T(128)} %param.7) | copy-start | bytes 100
  36.6 15.5 %all-to-all-start.1 = ((f32[4,8,2048]{2,0,1:T(4,128)}), f32[4,8,2048]{2,0,1:T(4,128)S(1)}, u32[]{:S(2)}, u32[]{:S(2)}) async-start(f32[4,8,2048]{2,0,1:T(4,128)} %copy.13), calls=%async_computation.1 | async-start | bytes 524288 | tf_op jit(solution)/shard_map/all_to_all | solution.py:155

commit v2 on v1

v2 whole, which is shorter than its diff:
```python
import functools

import jax
import jax.numpy as jnp
from jax import lax
from jax.experimental import pallas as pl
from jax.experimental.pallas import tpu as pltpu
from jax.sharding import PartitionSpec as P

optical_depth = 2.5
smooth_weight = 0.05
lanes = 128


def softplus(x):
    return jnp.maximum(x, 0.0) + jnp.log1p(jnp.exp(-jnp.abs(x)))


def chunking(rows, width, depth_count):
    tiles = width // lanes
    per_tile = max(depth_count // tiles, 1)
    return tiles, per_tile, rows // per_tile


def forward_kernel(d_ref, c_ref, out_ref, *, step):
    slices = d_ref.shape[0]
    shape = d_ref.shape[1:]
    per_tile, _, chunk_rows, _ = out_ref.shape

    def body(z, carry):
        acc, e0, e1, e2 = carry
        dt = step * softplus(d_ref[z].astype(jnp.float32))
        opacity = 1.0 - jnp.exp(-dt)
        lit = jnp.exp(-acc) * opacity
        e0 = e0 + lit * jax.nn.sigmoid(c_ref[0, z].astype(jnp.float32))
        e1 = e1 + lit * jax.nn.sigmoid(c_ref[1, z].astype(jnp.float32))
        e2 = e2 + lit * jax.nn.sigmoid(c_ref[2, z].astype(jnp.float32))
        return (acc + dt, e0, e1, e2)

    zero = jnp.zeros(shape, jnp.float32)
    acc, e0, e1, e2 = lax.fori_loop(0, slices, body, (zero, zero, zero, zero), unroll=4)
    values = (e0, e1, e2, jnp.exp(-acc))
    for g in range(per_tile):
        for c in range(4):
            out_ref[g, c] = values[c][g * chunk_rows:(g + 1) * chunk_rows]


def backward_kernel(
    d_ref, c_ref, part_ref, ans_ref, zhalo_ref, rhalo_ref, gd_ref, gc_ref, *, step, slices_total
):
    slices = d_ref.shape[0]
    shape = d_ref.shape[1:]
    per_tile = part_ref.shape[0]

    def pixel(ref, c):
        if per_tile == 1:
            return ref[0, c]
        return jnp.concatenate([ref[g, c] for g in range(per_tile)], axis=0)

    row = lax.broadcasted_iota(jnp.int32, shape, 0)
    first_row = row == 0
    last_row = row == shape[0] - 1

    def body(z, carry):
        acc, front, w0, w1, w2, d_prev, d = carry
        d_next = jnp.where(
            z + 1 < slices,
            d_ref[jnp.minimum(z + 1, slices - 1)].astype(jnp.float32),
            zhalo_ref[1],
        )
        rims = rhalo_ref[z]
        upper = jnp.where(first_row, rims[0:1], pltpu.roll(d, 1, 0))
        lower = jnp.where(last_row, rims[1:2], pltpu.roll(d, shape[0] - 1, 0))
        smooth = 2.0 * smooth_weight * ((d - d_prev) + (d - d_next) + (d - upper) + (d - lower))
        sp = softplus(d)
        dt = step * sp
        opacity = 1.0 - jnp.exp(-dt)
        acc_next = acc + dt
        through = jnp.exp(-acc_next)
        inv = 1.0 / through
        lit = front * opacity
        col = [jax.nn.sigmoid(c_ref[c, z].astype(jnp.float32)) for c in range(3)]
        w = [w0 + lit * col[0], w1 + lit * col[1], w2 + lit * col[2]]
        inner = -(pixel(part_ref, 3) * inv) * pixel(ans_ref, 3)
        for c in range(3):
            sr = pixel(ans_ref, c)
            inner = inner + sr * (col[c] - (pixel(part_ref, c) - w[c]) * inv)
            gc_ref[c, z] = slices_total * sr * lit * col[c] * (1.0 - col[c])
        gd_ref[z] = optical_depth * through * jnp.exp(d - sp) * inner + smooth
        return (acc_next, through, w[0], w[1], w[2], d, d_next)

    zero = jnp.zeros(shape, jnp.float32)
    one = jnp.ones(shape, jnp.float32)
    start = (zero, one, zero, zero, zero, zhalo_ref[0], d_ref[0].astype(jnp.float32))
    lax.fori_loop(0, slices, body, start, unroll=2)


def forward_partial(density, colour_raw, step, depth_count):
    slices, rows, width = density.shape
    tiles, per_tile, chunk_rows = chunking(rows, width, depth_count)
    return pl.pallas_call(
        functools.partial(forward_kernel, step=step),
        grid=(tiles,),
        in_specs=[
            pl.BlockSpec((slices, rows, lanes), lambda i: (0, 0, i)),
            pl.BlockSpec((3, slices, rows, lanes), lambda i: (0, 0, 0, i)),
        ],
        out_specs=pl.BlockSpec((per_tile, 4, chunk_rows, lanes), lambda i: (i, 0, 0, 0)),
        out_shape=jax.ShapeDtypeStruct((tiles * per_tile, 4, chunk_rows, lanes), jnp.float32),
    )(density, colour_raw)


def backward_grads(density, colour_raw, partial_value, answers, zhalo, rhalo, step, slices_total):
    slices, rows, width = density.shape
    per_tile, _, chunk_rows, _ = answers.shape
    per_tile = per_tile // (width // lanes)
    slab = pl.BlockSpec((slices, rows, lanes), lambda i: (0, 0, i))
    colours = pl.BlockSpec((3, slices, rows, lanes), lambda i: (0, 0, 0, i))
    pixel = pl.BlockSpec((per_tile, 4, chunk_rows, lanes), lambda i: (i, 0, 0, 0))
    return pl.pallas_call(
        functools.partial(backward_kernel, step=step, slices_total=float(slices_total)),
        grid=(width // lanes,),
        in_specs=[
            slab,
            colours,
            pixel,
            pixel,
            pl.BlockSpec((2, rows, lanes), lambda i: (0, 0, i)),
            pl.BlockSpec((slices, 2, lanes), lambda i: (0, 0, i)),
        ],
        out_specs=[slab, colours],
        out_shape=[
            jax.ShapeDtypeStruct((slices, rows, width), jnp.float32),
            jax.ShapeDtypeStruct((3, slices, rows, width), jnp.float32),
        ],
    )(density, colour_raw, partial_value, answers, zhalo, rhalo)


def composite(parts, slab_rank, target_piece):
    emitted, passing = (parts[:, :3], parts[:, 3])
    earlier = (slab_rank[None, :] < slab_rank[:, None]).astype(jnp.float32)[:, :, None, None]
    later = (slab_rank[None, :] > slab_rank[:, None]).astype(jnp.float32)[:, :, None, None, None]
    front = jnp.exp(jnp.sum(earlier * jnp.log(passing)[None], axis=1))
    weighted = front[:, None] * emitted
    behind = jnp.sum(later * weighted[None], axis=1) / (front * passing)[:, None]
    residual = jnp.sum(weighted, axis=0) - target_piece
    scaled_residual = front[:, None] * residual[None]
    scaled_behind = front * jnp.sum(residual[None] * behind, axis=1)
    return jnp.concatenate([scaled_residual, scaled_behind[:, None]], axis=1)


def halos(density_raw):
    depth_count = lax.axis_size("depth")
    rows_count = lax.axis_size("rows")
    depth_at = lax.axis_index("depth")
    rows_at = lax.axis_index("rows")
    up_d = [(i, i + 1) for i in range(depth_count - 1)]
    up_r = [(i, i + 1) for i in range(rows_count - 1)]
    first_slice = density_raw[:1]
    last_slice = density_raw[-1:]
    first_row = density_raw[:, :1]
    last_row = density_raw[:, -1:]
    prev_slice = lax.ppermute(last_slice, "depth", up_d)
    next_slice = lax.ppermute(first_slice, "depth", [(j, i) for i, j in up_d])
    prev_row = lax.ppermute(last_row, "rows", up_r)
    next_row = lax.ppermute(first_row, "rows", [(j, i) for i, j in up_r])
    prev_slice = jnp.where(depth_at > 0, prev_slice, first_slice)
    next_slice = jnp.where(depth_at < depth_count - 1, next_slice, last_slice)
    prev_row = jnp.where(rows_at > 0, prev_row, first_row)
    next_row = jnp.where(rows_at < rows_count - 1, next_row, last_row)
    zhalo = jnp.concatenate([prev_slice, next_slice], axis=0).astype(jnp.float32)
    rhalo = jnp.concatenate([prev_row, next_row], axis=1).astype(jnp.float32)
    return zhalo, rhalo


def local(density_raw, colour_raw, target, slab_rank):
    slices_dev, rows_dev, width = density_raw.shape
    depth_count = lax.axis_size("depth")
    slices_total = slices_dev * depth_count
    step = optical_depth / slices_total
    tiles, per_tile, chunk_rows = chunking(rows_dev, width, depth_count)
    zhalo, rhalo = halos(density_raw)
    partial_value = forward_partial(density_raw, colour_raw, step, depth_count)
    received = lax.all_to_all(partial_value, "depth", 0, 0, tiled=True)
    position = lax.axis_index("depth")
    target_piece = lax.dynamic_slice(
        target,
        (0, (position % per_tile) * chunk_rows, (position // per_tile) * lanes),
        (3, chunk_rows, lanes),
    )
    answers = composite(received, slab_rank, target_piece)
    returned = lax.all_to_all(answers, "depth", 0, 0, tiled=True)
    return backward_grads(
        density_raw, colour_raw, partial_value, returned, zhalo, rhalo, step, slices_total
    )


def solution(mesh):
    placed = (P("depth", "rows", None), P(None, "depth", "rows", None), P(None, "rows", None), P())
    return jax.shard_map(
        local,
        mesh=mesh,
        in_specs=placed,
        out_specs=(P("depth", "rows", None), P(None, "depth", "rows", None)),
        check_vma=False,
    )
```

time: 66.1 us -> 58.7 us (0.89)
  waiting for transfers between devices: 3.93 us -> 12.4 us
  local copies, waits for them, and re-layouts: 9.35 us -> 1.74 us
  starting transfers between devices: 24.1 us -> 19.3 us
  other arithmetic: 7.5 us -> 4.03 us
    all_to_all x2, waiting for transfers between devices: 3.92 us -> 12.4 us  [the longest x1 6.84 us: local(): returned = lax.all_to_all(answers, 'depth', 0, 0, tiled=True)]
    mul x3 -> x2, other arithmetic: 4.36 us -> 0.05 us  [the longest x1 0.04 us: composite(): scaled_residual = front[:, None] * residual[None]]
    ppermute x4, starting transfers between devices: 11.9 us -> 8.87 us  [the longest x1 4.86 us: halos(): prev_slice = lax.ppermute(last_slice, 'depth', up_d)]
    slice x5 -> x2, local copies, waits for them, and re-layouts: 3.85 us -> 0.99 us  [the longest x1 0.78 us: halos(): last_slice = density_raw[-1:]]
    reshape x3 -> x0, local copies, waits for them, and re-layouts: 2.65 us -> none  [the longest x2 1.91 us: local(): sent = partial_value.reshape(4, depth_count, chunk)]
    all_to_all x2, starting transfers between devices: 12.2 us -> 10.4 us  [the longest x1 6.96 us: local(): received = lax.all_to_all(partial_value, 'depth', 0, 0, tiled=True)]
    convert_element_type x1 -> x3, other arithmetic: 0.07 us -> 1.75 us  [the longest x1 1.01 us: halos(): rhalo = jnp.concatenate([prev_row, next_row], axis=1).astype(jnp.float32)]
    unnamed x5 -> x6, local copies, waits for them, and re-layouts: 1.78 us -> 0.71 us
  transfers between devices with their start and end apart: 6 -> 6, of which waited for: 1 -> 2; matrix products, arithmetic and copies ran while one was open for 23% -> 7% of each run, Pallas kernels for 11% -> 13%
where the time goes in v2:
time: 58.7 us; the launch traced here: 57.8 us
  Pallas kernels  19.6 us (33%)
  starting transfers between devices  19.3 us (33%)
  waiting for transfers between devices  12.4 us (21%)
  other arithmetic  4.03 us (7%)
  local copies, waits for them, and re-layouts  1.74 us (3%)
  between operations  0.76 us (1%)
    pallas_call x1, Pallas kernels, backward_grads(): pl.pallas_call(functools.partial(backward_kernel, step=step, slices_total...  12.2 us
    pallas_call x1, Pallas kernels, forward_partial(): pl.pallas_call(functools.partial(forward_kernel, step=step), grid=(tiles,...  7.38 us
    all_to_all x1, starting transfers between devices, local(): received = lax.all_to_all(partial_value, 'depth', 0, 0, tiled=True)  6.96 us
    all_to_all x1, waiting for transfers between devices, local(): returned = lax.all_to_all(answers, 'depth', 0, 0, tiled=True)  6.84 us
    all_to_all x1, waiting for transfers between devices, local(): received = lax.all_to_all(partial_value, 'depth', 0, 0, tiled=True)  5.57 us
    ppermute x1, starting transfers between devices, halos(): prev_slice = lax.ppermute(last_slice, 'depth', up_d)  4.86 us
    all_to_all x1, starting transfers between devices, local(): returned = lax.all_to_all(answers, 'depth', 0, 0, tiled=True)  3.44 us
    ppermute x1, starting transfers between devices, halos(): next_slice = lax.ppermute(first_slice, 'depth', [(j, i) for i, j in up_d])  1.42 us
  transfers between devices with their start and end apart: 6, of which 2 were waited for; matrix products, arithmetic and copies ran while one was open for 7% of the time, Pallas kernels for 13%

profile of v2, /device:TPU:0, one launch (start us, length us, event | category | flops | bytes accessed | tf_op | source)
XLA Modules:
  0.0 57.8 jit_solution(9768201647981132697)
XLA Ops:
  0.6 0.8 %fusion.3 = (bf16[1,16,1024]{2,1,0:T(8,128)(2,1)S(1)}, bf16[1,16,1024]{2,1,0:T(8,128)(2,1)S(1)}) fusion(bf16[32,16,1024]{2,1,0:T(8,128)(2,1)} %d_ref.3), kind=kLoop, calls=%fused_computation.21 | loop fusion | bytes 131072 | tf_op jit(solution)/shard_map/slice | solution.py:160
  1.4 4.9 %collective-permute-start = (bf16[1,16,1024]{2,1,0:T(8,128)(2,1)S(1)}, bf16[1,16,1024]{2,1,0:T(8,128)(2,1)S(1)}, u32[]{:S(2)}, u32[]{:S(2)}) collective-permute-start(bf16[1,16,1024]{2,1,0:T(8,128)(2,1)S(1)} %get-tuple-element.10), channel_id=1, source_target_pairs={{0,4},{4,8},{8,12},{12,16},{16,20},{20,24},{24,28},{1,5},{5,9},{9,... | collective-permute-start | bytes 98312 | tf_op jit(solution)/shard_map/ppermute | solution.py:163
  6.3 0.0 copy-start
  6.3 0.0 copy-start.2
  6.3 1.4 %collective-permute-start.1 = (bf16[1,16,1024]{2,1,0:T(8,128)(2,1)S(1)}, bf16[1,16,1024]{2,1,0:T(8,128)(2,1)S(1)}, u32[]{:S(2)}, u32[]{:S(2)}) collective-permute-start(bf16[1,16,1024]{2,1,0:T(8,128)(2,1)S(1)} %get-tuple-element.11), channel_id=1, source_target_pairs={{4,0},{8,4},{12,8},{16,12},{20,16},{24,20},{28,24},{5,1},{9,5},{13... | collective-permute-start | bytes 98312 | tf_op jit(solution)/shard_map/ppermute | solution.py:164
  7.7 7.4 %shard_map.59.part_ref = f32[8,4,16,128]{3,2,1,0:T(8,128)} custom-call(bf16[32,16,1024]{2,1,0:T(8,128)(2,1)} %d_ref.3, bf16[3,32,16,1024]{3,2,1,0:T(8,128)(2,1)} %c_ref.3), custom_call_target="tpu_custom_call" | custom-call | tf_op jit(solution)/shard_map/pallas_call | solution.py:101
  15.1 7.0 %all-to-all-start = ((f32[8,4,16,128]{3,2,1,0:T(8,128)}), f32[8,4,16,128]{3,2,1,0:T(8,128)S(1)}, u32[]{:S(2)}, u32[]{:S(2)}) async-start(f32[8,4,16,128]{3,2,1,0:T(8,128)} %shard_map.59.part_ref), calls=%async_computation | async-start | bytes 524288 | tf_op jit(solution)/shard_map/all_to_all | solution.py:184
  22.1 0.0 copy-done
  22.1 0.2 fusion.2
  22.3 1.3 %collective-permute-start.2 = (bf16[32,1,1024]{2,1,0:T(2,128)(2,1)S(1)}, bf16[32,1,1024]{2,1,0:T(2,128)(2,1)S(1)}, u32[]{:S(2)}, u32[]{:S(2)}) collective-permute-start(bf16[32,1,1024]{2,1,0:T(2,128)(2,1)S(1)} %get-tuple-element.6), channel_id=1, source_target_pairs={{0,1},{1,2},{2,3},{4,5},{5,6},{6,7},{8,9},{9,10},{10,11},{12,13},{... | collective-permute-start | bytes 196616 | tf_op jit(solution)/shard_map/ppermute | solution.py:165
  23.6 1.3 %collective-permute-start.3 = (bf16[32,1,1024]{2,1,0:T(2,128)(2,1)S(1)}, bf16[32,1,1024]{2,1,0:T(2,128)(2,1)S(1)}, u32[]{:S(2)}, u32[]{:S(2)}) collective-permute-start(bf16[32,1,1024]{2,1,0:T(2,128)(2,1)S(1)} %get-tuple-element.7), channel_id=1, source_target_pairs={{1,0},{2,1},{3,2},{5,4},{6,5},{7,6},{9,8},{10,9},{11,10},{13,12},{... | collective-permute-start | bytes 196616 | tf_op jit(solution)/shard_map/ppermute | solution.py:166
  24.9 0.0 copy-done.2
  24.9 0.1 compare_convert_fusion
  25.0 0.0 collective-permute-done
  25.0 0.0 collective-permute-done.1
  25.0 5.6 %all-to-all-done = f32[8,4,16,128]{3,2,1,0:T(8,128)S(1)} async-done(((f32[8,4,16,128]{3,2,1,0:T(8,128)}), f32[8,4,16,128]{3,2,1,0:T(8,128)S(1)}, u32[]{:S(2)}, u32[]{:S(2)}) %all-to-all-start) | async-done | bytes 262176 | tf_op jit(solution)/shard_map/all_to_all | solution.py:184
  30.6 0.1 multiply_reduce_fusion.1
  30.8 0.2 multiply_reduce_fusion
  31.0 0.8 %dynamic-slice_subtract_fusion = f32[3,16,128]{2,1,0:T(8,128)S(1)} fusion(f32[3,16,128]{2,1,0:T(8,128)S(1)} %get-tuple-element.2, f32[3,16,1024]{2,1,0:T(8,128)} %param.6, s32[]{:T(128)S(6)} %select_n.39), kind=kLoop, calls=%fused_computation.16 | loop fusion | flops 6144 | bytes 73732 | tf_op jit(solution)/shard_map/sub | solution.py:146
  31.8 0.7 %pad_maximum_fusion = f32[8,4,16,128]{3,2,1,0:T(8,128)} fusion(f32[8,1,16,128]{3,2,1,0:T(8,128)S(1)} %bitcast_multiply_fusion, f32[8,3,16,128]{3,2,1,0:T(8,128)S(1)} %get-tuple-element.12), kind=kLoop, calls=%fused_computation.2 | loop fusion | flops 65536 | bytes 524288 | tf_op jit(solution)/shard_map/concatenate | solution.py:149
  32.5 3.4 %all-to-all-start.1 = ((f32[8,4,16,128]{3,2,1,0:T(8,128)}), f32[8,4,16,128]{3,2,1,0:T(8,128)S(1)}, u32[]{:S(2)}, u32[]{:S(2)}) async-start(f32[8,4,16,128]{3,2,1,0:T(8,128)} %pad_maximum_fusion), calls=%async_computation.1 | async-start | bytes 524288 | tf_op jit(solution)/shard_map/all_to_all | solution.py:192
  36.0 0.7 %maximum_convert_fusion.1.zhalo_ref = f32[2,16,1024]{2,1,0:T(8,128)} fusion(bf16[1,16,1024]{2,1,0:T(8,128)(2,1)S(1)} %get-tuple-element.9, bf16[1,16,1024]{2,1,0:T(8,128)(2,1)S(1)} %get-tuple-element.8), kind=kLoop, calls=%fused_computation.9 | loop fusion | flops 65536 | bytes 196608 | tf_op jit(solution)/shard_map/convert_element_type | solution.py:171
  36.6 0.0 collective-permute-done.2
  36.7 0.0 collective-permute-done.3
  36.7 0.4 broadcast_select_fusion.1
  37.1 1.0 %maximum_convert_fusion.rhalo_ref = f32[32,2,1024]{2,1,0:T(2,128)} fusion(bf16[32,1,1024]{2,1,0:T(2,128)(2,1)S(1)} %get-tuple-element.5, bf16[32,1,1024]{2,1,0:T(2,128)(2,1)S(1)} %get-tuple-element.4), kind=kLoop, calls=%fused_computation.7 | loop fusion | flops 262144 | bytes 393216 | tf_op jit(solution)/shard_map/convert_element_type | solution.py:172
  38.1 6.8 %all-to-all-done.1.ans_ref = f32[8,4,16,128]{3,2,1,0:T(8,128)S(1)} async-done(((f32[8,4,16,128]{3,2,1,0:T(8,128)}), f32[8,4,16,128]{3,2,1,0:T(8,128)S(1)}, u32[]{:S(2)}, u32[]{:S(2)}) %all-to-all-start.1) | async-done | bytes 262176 | tf_op jit(solution)/shard_map/all_to_all | solution.py:192
  44.9 0.0 copy-start.1
  44.9 0.7 %copy-done.1 = f32[8,4,16,128]{3,2,1,0:T(8,128)} copy-done((f32[8,4,16,128]{3,2,1,0:T(8,128)}, f32[8,4,16,128]{3,2,1,0:T(8,128)S(1)}, u32[]{:S(2)}) %copy-start.1) | copy-done | bytes 262168
  45.6 12.2 %shard_map.60 = (f32[32,16,1024]{2,1,0:T(8,128)}, f32[3,32,16,1024]{3,2,1,0:T(8,128)}) custom-call(bf16[32,16,1024]{2,1,0:T(8,128)(2,1)} %d_ref.3, bf16[3,32,16,1024]{3,2,1,0:T(8,128)(2,1)} %c_ref.3, f32[8,4,16,128]{3,2,1,0:T(8,128)} %shard_map.59.part_ref, f32[8,4,16,128]{3,2,1,0:T(8,128)} %copy-done.1, f32[2,16,1024]{2,1,0:T(8,128)} %maximum_convert_fusion.1.zhalo_ref, ...), custom_call_target="tpu_custom_call" | custom-call | tf_op jit(solution)/shard_map/pallas_call | solution.py:120
  (7 shorter events, 0.1 us)
Async XLA Ops:
  1.4 23.6 %collective-permute-start = (bf16[1,16,1024]{2,1,0:T(8,128)(2,1)S(1)}, bf16[1,16,1024]{2,1,0:T(8,128)(2,1)S(1)}, u32[]{:S(2)}, u32[]{:S(2)}) collective-permute-start(bf16[1,16,1024]{2,1,0:T(8,128)(2,1)S(1)} %get-tuple-element.10), channel_id=1, source_target_pairs={{0,4},{4,8},{8,12},{12,16},{16,20},{20,24},{24,28},{1,5},{5,9},{9,... | collective-permute-start | bytes 98312 | tf_op jit(solution)/shard_map/ppermute | solution.py:163
  6.3 15.8 %copy-start = (bf16[32,16,1024]{2,1,0:T(8,128)(2,1)S(1)}, bf16[32,16,1024]{2,1,0:T(8,128)(2,1)}, u32[]{:S(2)}) copy-start(bf16[32,16,1024]{2,1,0:T(8,128)(2,1)} %d_ref.3) | copy-start | bytes 3145732
  6.3 18.6 %copy-start.2 = (s32[8]{0:T(128)S(1)}, s32[8]{0:T(128)}, u32[]{:S(2)}) copy-start(s32[8]{0:T(128)} %param.7) | copy-start | bytes 100
  6.3 18.7 %collective-permute-start.1 = (bf16[1,16,1024]{2,1,0:T(8,128)(2,1)S(1)}, bf16[1,16,1024]{2,1,0:T(8,128)(2,1)S(1)}, u32[]{:S(2)}, u32[]{:S(2)}) collective-permute-start(bf16[1,16,1024]{2,1,0:T(8,128)(2,1)S(1)} %get-tuple-element.11), channel_id=1, source_target_pairs={{4,0},{8,4},{12,8},{16,12},{20,16},{24,20},{28,24},{5,1},{9,5},{13... | collective-permute-start | bytes 98312 | tf_op jit(solution)/shard_map/ppermute | solution.py:164
  15.1 15.5 %all-to-all-start = ((f32[8,4,16,128]{3,2,1,0:T(8,128)}), f32[8,4,16,128]{3,2,1,0:T(8,128)S(1)}, u32[]{:S(2)}, u32[]{:S(2)}) async-start(f32[8,4,16,128]{3,2,1,0:T(8,128)} %shard_map.59.part_ref), calls=%async_computation | async-start | bytes 524288 | tf_op jit(solution)/shard_map/all_to_all | solution.py:184
  22.3 14.4 %collective-permute-start.2 = (bf16[32,1,1024]{2,1,0:T(2,128)(2,1)S(1)}, bf16[32,1,1024]{2,1,0:T(2,128)(2,1)S(1)}, u32[]{:S(2)}, u32[]{:S(2)}) collective-permute-start(bf16[32,1,1024]{2,1,0:T(2,128)(2,1)S(1)} %get-tuple-element.6), channel_id=1, source_target_pairs={{0,1},{1,2},{2,3},{4,5},{5,6},{6,7},{8,9},{9,10},{10,11},{12,13},{... | collective-permute-start | bytes 196616 | tf_op jit(solution)/shard_map/ppermute | solution.py:165
  23.6 13.1 %collective-permute-start.3 = (bf16[32,1,1024]{2,1,0:T(2,128)(2,1)S(1)}, bf16[32,1,1024]{2,1,0:T(2,128)(2,1)S(1)}, u32[]{:S(2)}, u32[]{:S(2)}) collective-permute-start(bf16[32,1,1024]{2,1,0:T(2,128)(2,1)S(1)} %get-tuple-element.7), channel_id=1, source_target_pairs={{1,0},{2,1},{3,2},{5,4},{6,5},{7,6},{9,8},{10,9},{11,10},{13,12},{... | collective-permute-start | bytes 196616 | tf_op jit(solution)/shard_map/ppermute | solution.py:166
  32.5 12.4 %all-to-all-start.1 = ((f32[8,4,16,128]{3,2,1,0:T(8,128)}), f32[8,4,16,128]{3,2,1,0:T(8,128)S(1)}, u32[]{:S(2)}, u32[]{:S(2)}) async-start(f32[8,4,16,128]{3,2,1,0:T(8,128)} %pad_maximum_fusion), calls=%async_computation.1 | async-start | bytes 524288 | tf_op jit(solution)/shard_map/all_to_all | solution.py:192
  44.9 0.7 %copy-start.1 = (f32[8,4,16,128]{3,2,1,0:T(8,128)}, f32[8,4,16,128]{3,2,1,0:T(8,128)S(1)}, u32[]{:S(2)}) copy-start(f32[8,4,16,128]{3,2,1,0:T(8,128)S(1)} %all-to-all-done.1.ans_ref) | copy-start | bytes 786436

commit v3 on v2

--- a/solution.py
+++ b/solution.py
@@ -12,8 +12,12 @@
 lanes = 128
 
 
+log2e = 1.4426950408889634
+ln2 = 0.6931471805599453
+
+
 def softplus(x):
-    return jnp.maximum(x, 0.0) + jnp.log1p(jnp.exp(-jnp.abs(x)))
+    return jnp.maximum(x, 0.0) + ln2 * jnp.log2(1.0 + jnp.exp2(jnp.abs(x) * -log2e))
 
 
 def chunking(rows, width, depth_count):
@@ -26,31 +30,33 @@
     slices = d_ref.shape[0]
     shape = d_ref.shape[1:]
     per_tile, _, chunk_rows, _ = out_ref.shape
+    scale = -step * log2e
 
     def body(z, carry):
-        acc, e0, e1, e2 = carry
-        dt = step * softplus(d_ref[z].astype(jnp.float32))
-        opacity = 1.0 - jnp.exp(-dt)
-        lit = jnp.exp(-acc) * opacity
+        n, front, e0, e1, e2 = carry
+        dtn = softplus(d_ref[z].astype(jnp.float32)) * scale
+        lit = front * (1.0 - jnp.exp2(dtn))
+        n = n + dtn
         e0 = e0 + lit * jax.nn.sigmoid(c_ref[0, z].astype(jnp.float32))
         e1 = e1 + lit * jax.nn.sigmoid(c_ref[1, z].astype(jnp.float32))
         e2 = e2 + lit * jax.nn.sigmoid(c_ref[2, z].astype(jnp.float32))
-        return (acc + dt, e0, e1, e2)
+        return (n, jnp.exp2(n), e0, e1, e2)
 
     zero = jnp.zeros(shape, jnp.float32)
-    acc, e0, e1, e2 = lax.fori_loop(0, slices, body, (zero, zero, zero, zero), unroll=4)
-    values = (e0, e1, e2, jnp.exp(-acc))
+    one = jnp.ones(shape, jnp.float32)
+    _, passing, e0, e1, e2 = lax.fori_loop(0, slices, body, (zero, one, zero, zero, zero), unroll=4)
+    values = (e0, e1, e2, passing)
     for g in range(per_tile):
         for c in range(4):
             out_ref[g, c] = values[c][g * chunk_rows:(g + 1) * chunk_rows]
 
 
-def backward_kernel(
-    d_ref, c_ref, part_ref, ans_ref, zhalo_ref, rhalo_ref, gd_ref, gc_ref, *, step, slices_total
-):
+def backward_kernel(d_ref, c_ref, ans_ref, zhalo_ref, rhalo_ref, gd_ref, gc_ref, *, step, slices_total):
     slices = d_ref.shape[0]
     shape = d_ref.shape[1:]
-    per_tile = part_ref.shape[0]
+    per_tile = ans_ref.shape[0]
+    scale = -step * log2e
+    gain = optical_depth / slices_total
 
     def pixel(ref, c):
         if per_tile == 1:
@@ -62,7 +68,7 @@
     last_row = row == shape[0] - 1
 
     def body(z, carry):
-        acc, front, w0, w1, w2, d_prev, d = carry
+        n, front, w0, w1, w2, d_prev, d = carry
         d_next = jnp.where(
             z + 1 < slices,
             d_ref[jnp.minimum(z + 1, slices - 1)].astype(jnp.float32),
@@ -72,22 +78,22 @@
         upper = jnp.where(first_row, rims[0:1], pltpu.roll(d, 1, 0))
         lower = jnp.where(last_row, rims[1:2], pltpu.roll(d, shape[0] - 1, 0))
         smooth = 2.0 * smooth_weight * ((d - d_prev) + (d - d_next) + (d - upper) + (d - lower))
-        sp = softplus(d)
-        dt = step * sp
-        opacity = 1.0 - jnp.exp(-dt)
-        acc_next = acc + dt
-        through = jnp.exp(-acc_next)
-        inv = 1.0 / through
-        lit = front * opacity
+        dtn = softplus(d) * scale
+        lit = front * (1.0 - jnp.exp2(dtn))
+        n_next = n + dtn
+        through = jnp.exp2(n_next)
+        inv = jnp.exp2(-n_next)
         col = [jax.nn.sigmoid(c_ref[c, z].astype(jnp.float32)) for c in range(3)]
-        w = [w0 + lit * col[0], w1 + lit * col[1], w2 + lit * col[2]]
-        inner = -(pixel(part_ref, 3) * inv) * pixel(ans_ref, 3)
+        lit_col = [lit * col[c] for c in range(3)]
+        w = [w0 + lit_col[0], w1 + lit_col[1], w2 + lit_col[2]]
+        res = [pixel(ans_ref, c) for c in range(3)]
+        emitted = res[0] * col[0] + res[1] * col[1] + res[2] * col[2]
+        left = res[0] * w[0] + res[1] * w[1] + res[2] * w[2]
+        inner = emitted - inv * (pixel(ans_ref, 3) - left)
         for c in range(3):
-            sr = pixel(ans_ref, c)
-            inner = inner + sr * (col[c] - (pixel(part_ref, c) - w[c]) * inv)
-            gc_ref[c, z] = slices_total * sr * lit * col[c] * (1.0 - col[c])
-        gd_ref[z] = optical_depth * through * jnp.exp(d - sp) * inner + smooth
-        return (acc_next, through, w[0], w[1], w[2], d, d_next)
+            gc_ref[c, z] = res[c] * lit_col[c] * (1.0 - col[c])
+        gd_ref[z] = gain * through * jax.nn.sigmoid(d) * inner + smooth
+        return (n_next, through, w[0], w[1], w[2], d, d_next)
 
     zero = jnp.zeros(shape, jnp.float32)
     one = jnp.ones(shape, jnp.float32)
@@ -110,7 +116,7 @@
     )(density, colour_raw)
 
 
-def backward_grads(density, colour_raw, partial_value, answers, zhalo, rhalo, step, slices_total):
+def backward_grads(density, colour_raw, answers, zhalo, rhalo, step, slices_total):
     slices, rows, width = density.shape
     per_tile, _, chunk_rows, _ = answers.shape
     per_tile = per_tile // (width // lanes)
@@ -124,7 +130,6 @@
             slab,
             colours,
             pixel,
-            pixel,
             pl.BlockSpec((2, rows, lanes), lambda i: (0, 0, i)),
             pl.BlockSpec((slices, 2, lanes), lambda i: (0, 0, i)),
         ],
@@ -133,10 +138,10 @@
             jax.ShapeDtypeStruct((slices, rows, width), jnp.float32),
             jax.ShapeDtypeStruct((3, slices, rows, width), jnp.float32),
         ],
-    )(density, colour_raw, partial_value, answers, zhalo, rhalo)
-
-
-def composite(parts, slab_rank, target_piece):
+    )(density, colour_raw, answers, zhalo, rhalo)
+
+
+def composite(parts, slab_rank, target_piece, slices_total):
     emitted, passing = (parts[:, :3], parts[:, 3])
     earlier = (slab_rank[None, :] < slab_rank[:, None]).astype(jnp.float32)[:, :, None, None]
     later = (slab_rank[None, :] > slab_rank[:, None]).astype(jnp.float32)[:, :, None, None, None]
@@ -144,9 +149,10 @@
     weighted = front[:, None] * emitted
     behind = jnp.sum(later * weighted[None], axis=1) / (front * passing)[:, None]
     residual = jnp.sum(weighted, axis=0) - target_piece
-    scaled_residual = front[:, None] * residual[None]
-    scaled_behind = front * jnp.sum(residual[None] * behind, axis=1)
-    return jnp.concatenate([scaled_residual, scaled_behind[:, None]], axis=1)
+    scaled_residual = slices_total * (front[:, None] * residual[None])
+    scaled_behind = slices_total * (front * jnp.sum(residual[None] * behind, axis=1))
+    folded = jnp.sum(scaled_residual * emitted, axis=1) + passing * scaled_behind
+    return jnp.concatenate([scaled_residual, folded[:, None]], axis=1)
 
 
 def halos(density_raw):
@@ -188,10 +194,10 @@
         (0, (position % per_tile) * chunk_rows, (position // per_tile) * lanes),
         (3, chunk_rows, lanes),
     )
-    answers = composite(received, slab_rank, target_piece)
+    answers = composite(received, slab_rank, target_piece, float(slices_total))
     returned = lax.all_to_all(answers, "depth", 0, 0, tiled=True)
     return backward_grads(
-        density_raw, colour_raw, partial_value, returned, zhalo, rhalo, step, slices_total
+        density_raw, colour_raw, returned, zhalo, rhalo, step, slices_total
     )
 
 

time: 58.7 us -> 57.2 us (0.974)
  Pallas kernels: 19.6 us -> 18.1 us
    pallas_call x1, Pallas kernels: 12.2 us -> 11 us  [backward_grads(): pl.pallas_call(functools.partial(backward_kernel, step=step, slices_total...]
  transfers between devices with their start and end apart: 6 -> 6, of which waited for: 2 -> 2; matrix products, arithmetic and copies ran while one was open for 7% -> 8% of each run, Pallas kernels for 13% -> 13%
where the time goes in v3:
time: 57.2 us; the launch traced here: 56.3 us
  starting transfers between devices  19.3 us (34%)
  Pallas kernels  18.1 us (32%)
  waiting for transfers between devices  12.5 us (22%)
  other arithmetic  4.03 us (7%)
  local copies, waits for them, and re-layouts  1.73 us (3%)
  between operations  0.76 us (1%)
    pallas_call x1, Pallas kernels, backward_grads(): pl.pallas_call(functools.partial(backward_kernel, step=step, slices_total...  11 us
    pallas_call x1, Pallas kernels, forward_partial(): pl.pallas_call(functools.partial(forward_kernel, step=step), grid=(tiles,...  7.04 us
    all_to_all x1, starting transfers between devices, local(): received = lax.all_to_all(partial_value, 'depth', 0, 0, tiled=True)  6.96 us
    all_to_all x1, waiting for transfers between devices, local(): returned = lax.all_to_all(answers, 'depth', 0, 0, tiled=True)  6.87 us
    all_to_all x1, waiting for transfers between devices, local(): received = lax.all_to_all(partial_value, 'depth', 0, 0, tiled=True)  5.57 us
    ppermute x1, starting transfers between devices, halos(): prev_slice = lax.ppermute(last_slice, 'depth', up_d)  4.86 us
    all_to_all x1, starting transfers between devices, local(): returned = lax.all_to_all(answers, 'depth', 0, 0, tiled=True)  3.44 us
    ppermute x1, starting transfers between devices, halos(): next_slice = lax.ppermute(first_slice, 'depth', [(j, i) for i, j in up_d])  1.42 us
  transfers between devices with their start and end apart: 6, of which 2 were waited for; matrix products, arithmetic and copies ran while one was open for 8% of the time, Pallas kernels for 13%

profile of v3, /device:TPU:0, one launch (start us, length us, event | category | flops | bytes accessed | tf_op | source)
XLA Modules:
  0.0 56.3 jit_solution(4006037575224258492)
XLA Ops:
  0.6 0.8 %fusion.6 = (bf16[1,16,1024]{2,1,0:T(8,128)(2,1)S(1)}, bf16[1,16,1024]{2,1,0:T(8,128)(2,1)S(1)}) fusion(bf16[32,16,1024]{2,1,0:T(8,128)(2,1)} %d_ref.3), kind=kLoop, calls=%fused_computation.25 | loop fusion | bytes 131072 | tf_op jit(solution)/shard_map/slice | solution.py:166
  1.4 4.9 %collective-permute-start = (bf16[1,16,1024]{2,1,0:T(8,128)(2,1)S(1)}, bf16[1,16,1024]{2,1,0:T(8,128)(2,1)S(1)}, u32[]{:S(2)}, u32[]{:S(2)}) collective-permute-start(bf16[1,16,1024]{2,1,0:T(8,128)(2,1)S(1)} %get-tuple-element.12), channel_id=1, source_target_pairs={{0,4},{4,8},{8,12},{12,16},{16,20},{20,24},{24,28},{1,5},{5,9},{9,... | collective-permute-start | bytes 98312 | tf_op jit(solution)/shard_map/ppermute | solution.py:169
  6.3 0.0 copy-start
  6.3 0.0 copy-start.2
  6.3 1.4 %collective-permute-start.1 = (bf16[1,16,1024]{2,1,0:T(8,128)(2,1)S(1)}, bf16[1,16,1024]{2,1,0:T(8,128)(2,1)S(1)}, u32[]{:S(2)}, u32[]{:S(2)}) collective-permute-start(bf16[1,16,1024]{2,1,0:T(8,128)(2,1)S(1)} %get-tuple-element.13), channel_id=1, source_target_pairs={{4,0},{8,4},{12,8},{16,12},{20,16},{24,20},{28,24},{5,1},{9,5},{13... | collective-permute-start | bytes 98312 | tf_op jit(solution)/shard_map/ppermute | solution.py:170
  7.7 7.0 %shard_map.59 = f32[8,4,16,128]{3,2,1,0:T(8,128)} custom-call(bf16[32,16,1024]{2,1,0:T(8,128)(2,1)} %d_ref.3, bf16[3,32,16,1024]{3,2,1,0:T(8,128)(2,1)} %c_ref.3), custom_call_target="tpu_custom_call" | custom-call | tf_op jit(solution)/shard_map/pallas_call | solution.py:107
  14.8 7.0 %all-to-all-start = ((f32[8,4,16,128]{3,2,1,0:T(8,128)}), f32[8,4,16,128]{3,2,1,0:T(8,128)S(1)}, u32[]{:S(2)}, u32[]{:S(2)}) async-start(f32[8,4,16,128]{3,2,1,0:T(8,128)} %shard_map.59), calls=%async_computation | async-start | bytes 524288 | tf_op jit(solution)/shard_map/all_to_all | solution.py:190
  21.7 0.0 copy-done
  21.7 0.2 fusion.5
  22.0 1.3 %collective-permute-start.2 = (bf16[32,1,1024]{2,1,0:T(2,128)(2,1)S(1)}, bf16[32,1,1024]{2,1,0:T(2,128)(2,1)S(1)}, u32[]{:S(2)}, u32[]{:S(2)}) collective-permute-start(bf16[32,1,1024]{2,1,0:T(2,128)(2,1)S(1)} %get-tuple-element.8), channel_id=1, source_target_pairs={{0,1},{1,2},{2,3},{4,5},{5,6},{6,7},{8,9},{9,10},{10,11},{12,13},{... | collective-permute-start | bytes 196616 | tf_op jit(solution)/shard_map/ppermute | solution.py:171
  23.3 1.3 %collective-permute-start.3 = (bf16[32,1,1024]{2,1,0:T(2,128)(2,1)S(1)}, bf16[32,1,1024]{2,1,0:T(2,128)(2,1)S(1)}, u32[]{:S(2)}, u32[]{:S(2)}) collective-permute-start(bf16[32,1,1024]{2,1,0:T(2,128)(2,1)S(1)} %get-tuple-element.9), channel_id=1, source_target_pairs={{1,0},{2,1},{3,2},{5,4},{6,5},{7,6},{9,8},{10,9},{11,10},{13,12},{... | collective-permute-start | bytes 196616 | tf_op jit(solution)/shard_map/ppermute | solution.py:172
  24.6 0.0 copy-done.2
  24.6 0.1 compare_convert_fusion
  24.6 0.0 collective-permute-done
  24.7 0.0 collective-permute-done.1
  24.7 5.6 %all-to-all-done = f32[8,4,16,128]{3,2,1,0:T(8,128)S(1)} async-done(((f32[8,4,16,128]{3,2,1,0:T(8,128)}), f32[8,4,16,128]{3,2,1,0:T(8,128)S(1)}, u32[]{:S(2)}, u32[]{:S(2)}) %all-to-all-start) | async-done | bytes 262176 | tf_op jit(solution)/shard_map/all_to_all | solution.py:190
  30.3 0.1 multiply_reduce_fusion.1
  30.5 0.2 multiply_reduce_fusion
  30.6 0.8 %dynamic-slice_subtract_fusion = f32[3,16,128]{2,1,0:T(8,128)S(1)} fusion(f32[3,16,128]{2,1,0:T(8,128)S(1)} %get-tuple-element.4, f32[3,16,1024]{2,1,0:T(8,128)} %param.6, s32[]{:T(128)S(6)} %select_n.39), kind=kLoop, calls=%fused_computation.20 | loop fusion | flops 6144 | bytes 73732 | tf_op jit(solution)/shard_map/sub | solution.py:151
  31.4 0.1 multiply_reduce_fusion.3
  31.5 0.7 %pad_maximum_fusion = f32[8,4,16,128]{3,2,1,0:T(8,128)} fusion(f32[8,1,16,128]{3,2,1,0:T(8,128)S(1)} %fusion.2, f32[8,3,16,128]{3,2,1,0:T(8,128)S(1)} %get-tuple-element.14), kind=kLoop, calls=%fused_computation.2 | loop fusion | flops 65536 | bytes 524288 | tf_op jit(solution)/shard_map/concatenate | solution.py:155
  32.2 3.4 %all-to-all-start.1 = ((f32[8,4,16,128]{3,2,1,0:T(8,128)}), f32[8,4,16,128]{3,2,1,0:T(8,128)S(1)}, u32[]{:S(2)}, u32[]{:S(2)}) async-start(f32[8,4,16,128]{3,2,1,0:T(8,128)} %pad_maximum_fusion), calls=%async_computation.1 | async-start | bytes 524288 | tf_op jit(solution)/shard_map/all_to_all | solution.py:198
  35.7 0.7 %maximum_convert_fusion.1.zhalo_ref = f32[2,16,1024]{2,1,0:T(8,128)} fusion(bf16[1,16,1024]{2,1,0:T(8,128)(2,1)S(1)} %get-tuple-element.11, bf16[1,16,1024]{2,1,0:T(8,128)(2,1)S(1)} %get-tuple-element.10), kind=kLoop, calls=%fused_computation.10 | loop fusion | flops 65536 | bytes 196608 | tf_op jit(solution)/shard_map/convert_element_type | solution.py:177
  36.3 0.0 collective-permute-done.2
  36.3 0.0 collective-permute-done.3
  36.3 0.4 broadcast_select_fusion.1
  36.7 1.0 %maximum_convert_fusion.rhalo_ref = f32[32,2,1024]{2,1,0:T(2,128)} fusion(bf16[32,1,1024]{2,1,0:T(2,128)(2,1)S(1)} %get-tuple-element.7, bf16[32,1,1024]{2,1,0:T(2,128)(2,1)S(1)} %get-tuple-element.6), kind=kLoop, calls=%fused_computation.9 | loop fusion | flops 262144 | bytes 393216 | tf_op jit(solution)/shard_map/convert_element_type | solution.py:178
  37.7 6.9 %all-to-all-done.1.ans_ref = f32[8,4,16,128]{3,2,1,0:T(8,128)S(1)} async-done(((f32[8,4,16,128]{3,2,1,0:T(8,128)}), f32[8,4,16,128]{3,2,1,0:T(8,128)S(1)}, u32[]{:S(2)}, u32[]{:S(2)}) %all-to-all-start.1) | async-done | bytes 262176 | tf_op jit(solution)/shard_map/all_to_all | solution.py:198
  44.6 0.0 copy-start.1
  44.6 0.7 %copy-done.1 = f32[8,4,16,128]{3,2,1,0:T(8,128)} copy-done((f32[8,4,16,128]{3,2,1,0:T(8,128)}, f32[8,4,16,128]{3,2,1,0:T(8,128)S(1)}, u32[]{:S(2)}) %copy-start.1) | copy-done | bytes 262168
  45.3 11.0 %shard_map.60 = (f32[32,16,1024]{2,1,0:T(8,128)}, f32[3,32,16,1024]{3,2,1,0:T(8,128)}) custom-call(bf16[32,16,1024]{2,1,0:T(8,128)(2,1)} %d_ref.3, bf16[3,32,16,1024]{3,2,1,0:T(8,128)(2,1)} %c_ref.3, f32[8,4,16,128]{3,2,1,0:T(8,128)} %copy-done.1, f32[2,16,1024]{2,1,0:T(8,128)} %maximum_convert_fusion.1.zhalo_ref, f32[32,2,1024]{2,1,0:T(2,128)} %maximum_convert_fusion.rhalo_ref), custom_call_target="tpu_custom_call" | custom-call | tf_op jit(solution)/shard_map/pallas_call | solution.py:126
  (6 shorter events, 0.1 us)
Async XLA Ops:
  1.4 23.2 %collective-permute-start = (bf16[1,16,1024]{2,1,0:T(8,128)(2,1)S(1)}, bf16[1,16,1024]{2,1,0:T(8,128)(2,1)S(1)}, u32[]{:S(2)}, u32[]{:S(2)}) collective-permute-start(bf16[1,16,1024]{2,1,0:T(8,128)(2,1)S(1)} %get-tuple-element.12), channel_id=1, source_target_pairs={{0,4},{4,8},{8,12},{12,16},{16,20},{20,24},{24,28},{1,5},{5,9},{9,... | collective-permute-start | bytes 98312 | tf_op jit(solution)/shard_map/ppermute | solution.py:169
  6.3 15.5 %copy-start = (bf16[32,16,1024]{2,1,0:T(8,128)(2,1)S(1)}, bf16[32,16,1024]{2,1,0:T(8,128)(2,1)}, u32[]{:S(2)}) copy-start(bf16[32,16,1024]{2,1,0:T(8,128)(2,1)} %d_ref.3) | copy-start | bytes 3145732
  6.3 18.3 %copy-start.2 = (s32[8]{0:T(128)S(1)}, s32[8]{0:T(128)}, u32[]{:S(2)}) copy-start(s32[8]{0:T(128)} %param.7) | copy-start | bytes 100
  6.3 18.3 %collective-permute-start.1 = (bf16[1,16,1024]{2,1,0:T(8,128)(2,1)S(1)}, bf16[1,16,1024]{2,1,0:T(8,128)(2,1)S(1)}, u32[]{:S(2)}, u32[]{:S(2)}) collective-permute-start(bf16[1,16,1024]{2,1,0:T(8,128)(2,1)S(1)} %get-tuple-element.13), channel_id=1, source_target_pairs={{4,0},{8,4},{12,8},{16,12},{20,16},{24,20},{28,24},{5,1},{9,5},{13... | collective-permute-start | bytes 98312 | tf_op jit(solution)/shard_map/ppermute | solution.py:170
  14.8 15.5 %all-to-all-start = ((f32[8,4,16,128]{3,2,1,0:T(8,128)}), f32[8,4,16,128]{3,2,1,0:T(8,128)S(1)}, u32[]{:S(2)}, u32[]{:S(2)}) async-start(f32[8,4,16,128]{3,2,1,0:T(8,128)} %shard_map.59), calls=%async_computation | async-start | bytes 524288 | tf_op jit(solution)/shard_map/all_to_all | solution.py:190
  22.0 14.4 %collective-permute-start.2 = (bf16[32,1,1024]{2,1,0:T(2,128)(2,1)S(1)}, bf16[32,1,1024]{2,1,0:T(2,128)(2,1)S(1)}, u32[]{:S(2)}, u32[]{:S(2)}) collective-permute-start(bf16[32,1,1024]{2,1,0:T(2,128)(2,1)S(1)} %get-tuple-element.8), channel_id=1, source_target_pairs={{0,1},{1,2},{2,3},{4,5},{5,6},{6,7},{8,9},{9,10},{10,11},{12,13},{... | collective-permute-start | bytes 196616 | tf_op jit(solution)/shard_map/ppermute | solution.py:171
  23.3 13.1 %collective-permute-start.3 = (bf16[32,1,1024]{2,1,0:T(2,128)(2,1)S(1)}, bf16[32,1,1024]{2,1,0:T(2,128)(2,1)S(1)}, u32[]{:S(2)}, u32[]{:S(2)}) collective-permute-start(bf16[32,1,1024]{2,1,0:T(2,128)(2,1)S(1)} %get-tuple-element.9), channel_id=1, source_target_pairs={{1,0},{2,1},{3,2},{5,4},{6,5},{7,6},{9,8},{10,9},{11,10},{13,12},{... | collective-permute-start | bytes 196616 | tf_op jit(solution)/shard_map/ppermute | solution.py:172
  32.2 12.4 %all-to-all-start.1 = ((f32[8,4,16,128]{3,2,1,0:T(8,128)}), f32[8,4,16,128]{3,2,1,0:T(8,128)S(1)}, u32[]{:S(2)}, u32[]{:S(2)}) async-start(f32[8,4,16,128]{3,2,1,0:T(8,128)} %pad_maximum_fusion), calls=%async_computation.1 | async-start | bytes 524288 | tf_op jit(solution)/shard_map/all_to_all | solution.py:198
  44.6 0.7 %copy-start.1 = (f32[8,4,16,128]{3,2,1,0:T(8,128)}, f32[8,4,16,128]{3,2,1,0:T(8,128)S(1)}, u32[]{:S(2)}) copy-start(f32[8,4,16,128]{3,2,1,0:T(8,128)S(1)} %all-to-all-done.1.ans_ref) | copy-start | bytes 786436

commit v4 on v3

--- a/solution.py
+++ b/solution.py
@@ -185,8 +185,9 @@
     slices_total = slices_dev * depth_count
     step = optical_depth / slices_total
     tiles, per_tile, chunk_rows = chunking(rows_dev, width, depth_count)
-    zhalo, rhalo = halos(density_raw)
     partial_value = forward_partial(density_raw, colour_raw, step, depth_count)
+    partial_value, after_forward = lax.optimization_barrier((partial_value, density_raw))
+    zhalo, rhalo = halos(after_forward)
     received = lax.all_to_all(partial_value, "depth", 0, 0, tiled=True)
     position = lax.axis_index("depth")
     target_piece = lax.dynamic_slice(

time: 57.2 us -> 54.5 us (0.953)
  the two profiles are of different devices: /device:TPU:0 before, /device:TPU:1 now
where the time goes in v4:
time: 54.5 us; the launch traced here: 53.7 us
  starting transfers between devices  23.8 us (44%)
  Pallas kernels  18.1 us (33%)
  waiting for transfers between devices  5.96 us (11%)
  other arithmetic  4.03 us (7%)
  local copies, waits for them, and re-layouts  0.95 us (2%)
  between operations  0.78 us (1%)
    pallas_call x1, Pallas kernels, backward_grads(): pl.pallas_call(functools.partial(backward_kernel, step=step, slices_total...  11 us
    pallas_call x1, Pallas kernels, forward_partial(): pl.pallas_call(functools.partial(forward_kernel, step=step), grid=(tiles,...  7.12 us
    all_to_all x1, starting transfers between devices, local(): received = lax.all_to_all(partial_value, 'depth', 0, 0, tiled=True)  6.38 us
    all_to_all x1, starting transfers between devices, local(): returned = lax.all_to_all(answers, 'depth', 0, 0, tiled=True)  6.34 us
    all_to_all x1, waiting for transfers between devices, local(): returned = lax.all_to_all(answers, 'depth', 0, 0, tiled=True)  5.95 us
    ppermute x1, starting transfers between devices, halos(): prev_row = lax.ppermute(last_row, 'rows', up_r)  4.52 us
    ppermute x1, starting transfers between devices, halos(): prev_slice = lax.ppermute(last_slice, 'depth', up_d)  3.36 us
    ppermute x1, starting transfers between devices, halos(): next_row = lax.ppermute(first_row, 'rows', [(j, i) for i, j in up_r])  1.92 us
  transfers between devices with their start and end apart: 6, of which 1 were waited for; matrix products, arithmetic and copies ran while one was open for 8% of the time, Pallas kernels for 0%

profile of v4, /device:TPU:1, one launch (start us, length us, event | category | flops | bytes accessed | tf_op | source)
XLA Modules:
  0.0 53.7 jit_solution(4339067424557872108)
XLA Ops:
  0.6 0.0 copy-start
  0.6 0.0 copy-start.2
  0.7 7.1 %shard_map.59 = f32[8,4,16,128]{3,2,1,0:T(8,128)} custom-call(bf16[32,16,1024]{2,1,0:T(8,128)(2,1)} %d_ref.3, bf16[3,32,16,1024]{3,2,1,0:T(8,128)(2,1)} %c_ref.3), custom_call_target="tpu_custom_call" | custom-call | tf_op jit(solution)/shard_map/pallas_call | solution.py:107
  7.8 6.4 %all-to-all-start = ((f32[8,4,16,128]{3,2,1,0:T(8,128)}), f32[8,4,16,128]{3,2,1,0:T(8,128)S(1)}, u32[]{:S(2)}, u32[]{:S(2)}) async-start(f32[8,4,16,128]{3,2,1,0:T(8,128)} %shard_map.59), calls=%async_computation | async-start | bytes 524288 | tf_op jit(solution)/shard_map/all_to_all | solution.py:191
  14.2 0.0 copy-done
  14.2 3.4 %collective-permute-start = (bf16[1,16,1024]{2,1,0:T(8,128)(2,1)S(1)}, bf16[1,16,1024]{2,1,0:T(8,128)(2,1)S(1)}, u32[]{:S(2)}, u32[]{:S(2)}) collective-permute-start(bf16[1,16,1024]{2,1,0:T(8,128)(2,1)S(1)} %get-tuple-element.16), channel_id=1, source_target_pairs={{0,4},{4,8},{8,12},{12,16},{16,20},{20,24},{24,28},{1,5},{5,9},{9,... | collective-permute-start | bytes 98312 | tf_op jit(solution)/shard_map/ppermute | solution.py:169
  17.5 1.3 %collective-permute-start.1 = (bf16[1,16,1024]{2,1,0:T(8,128)(2,1)S(1)}, bf16[1,16,1024]{2,1,0:T(8,128)(2,1)S(1)}, u32[]{:S(2)}, u32[]{:S(2)}) collective-permute-start(bf16[1,16,1024]{2,1,0:T(8,128)(2,1)S(1)} %get-tuple-element.17), channel_id=1, source_target_pairs={{4,0},{8,4},{12,8},{16,12},{20,16},{24,20},{28,24},{5,1},{9,5},{13... | collective-permute-start | bytes 98312 | tf_op jit(solution)/shard_map/ppermute | solution.py:170
  18.8 0.2 fusion.5
  19.1 4.5 %collective-permute-start.2 = (bf16[32,1,1024]{2,1,0:T(2,128)(2,1)S(1)}, bf16[32,1,1024]{2,1,0:T(2,128)(2,1)S(1)}, u32[]{:S(2)}, u32[]{:S(2)}) collective-permute-start(bf16[32,1,1024]{2,1,0:T(2,128)(2,1)S(1)} %get-tuple-element.12), channel_id=1, source_target_pairs={{0,1},{1,2},{2,3},{4,5},{5,6},{6,7},{8,9},{9,10},{10,11},{12,13},{... | collective-permute-start | bytes 196616 | tf_op jit(solution)/shard_map/ppermute | solution.py:171
  23.6 1.9 %collective-permute-start.3 = (bf16[32,1,1024]{2,1,0:T(2,128)(2,1)S(1)}, bf16[32,1,1024]{2,1,0:T(2,128)(2,1)S(1)}, u32[]{:S(2)}, u32[]{:S(2)}) collective-permute-start(bf16[32,1,1024]{2,1,0:T(2,128)(2,1)S(1)} %get-tuple-element.13), channel_id=1, source_target_pairs={{1,0},{2,1},{3,2},{5,4},{6,5},{7,6},{9,8},{10,9},{11,10},{13,12},{... | collective-permute-start | bytes 196616 | tf_op jit(solution)/shard_map/ppermute | solution.py:172
  25.5 0.0 copy-done.2
  25.5 0.1 compare_convert_fusion
  25.6 0.0 collective-permute-done
  25.6 0.0 collective-permute-done.1
  25.6 0.0 all-to-all-done
  25.7 0.1 multiply_reduce_fusion.1
  25.9 0.2 multiply_reduce_fusion
  26.0 0.8 %dynamic-slice_subtract_fusion = f32[3,16,128]{2,1,0:T(8,128)S(1)} fusion(f32[3,16,128]{2,1,0:T(8,128)S(1)} %get-tuple-element.8, f32[3,16,1024]{2,1,0:T(8,128)} %param.6, s32[]{:T(128)S(6)} %select_n.39), kind=kLoop, calls=%fused_computation.20 | loop fusion | flops 6144 | bytes 73732 | tf_op jit(solution)/shard_map/sub | solution.py:151
  26.8 0.1 multiply_reduce_fusion.3
  26.9 0.7 %pad_maximum_fusion = f32[8,4,16,128]{3,2,1,0:T(8,128)} fusion(f32[8,1,16,128]{3,2,1,0:T(8,128)S(1)} %fusion.2, f32[8,3,16,128]{3,2,1,0:T(8,128)S(1)} %get-tuple-element.18), kind=kLoop, calls=%fused_computation.2 | loop fusion | flops 65536 | bytes 524288 | tf_op jit(solution)/shard_map/concatenate | solution.py:155
  27.6 6.3 %all-to-all-start.1 = ((f32[8,4,16,128]{3,2,1,0:T(8,128)}), f32[8,4,16,128]{3,2,1,0:T(8,128)S(1)}, u32[]{:S(2)}, u32[]{:S(2)}) async-start(f32[8,4,16,128]{3,2,1,0:T(8,128)} %pad_maximum_fusion), calls=%async_computation.1 | async-start | bytes 524288 | tf_op jit(solution)/shard_map/all_to_all | solution.py:199
  34.0 0.7 %maximum_convert_fusion.1.zhalo_ref = f32[2,16,1024]{2,1,0:T(8,128)} fusion(bf16[1,16,1024]{2,1,0:T(8,128)(2,1)S(1)} %get-tuple-element.15, bf16[1,16,1024]{2,1,0:T(8,128)(2,1)S(1)} %get-tuple-element.14), kind=kLoop, calls=%fused_computation.10 | loop fusion | flops 65536 | bytes 196608 | tf_op jit(solution)/shard_map/convert_element_type | solution.py:177
  34.6 0.0 collective-permute-done.2
  34.6 0.0 collective-permute-done.3
  34.6 0.4 broadcast_select_fusion.1
  35.0 1.0 %maximum_convert_fusion.rhalo_ref = f32[32,2,1024]{2,1,0:T(2,128)} fusion(bf16[32,1,1024]{2,1,0:T(2,128)(2,1)S(1)} %get-tuple-element.11, bf16[32,1,1024]{2,1,0:T(2,128)(2,1)S(1)} %get-tuple-element.10), kind=kLoop, calls=%fused_computation.9 | loop fusion | flops 262144 | bytes 393216 | tf_op jit(solution)/shard_map/convert_element_type | solution.py:178
  36.0 6.0 %all-to-all-done.1.ans_ref = f32[8,4,16,128]{3,2,1,0:T(8,128)S(1)} async-done(((f32[8,4,16,128]{3,2,1,0:T(8,128)}), f32[8,4,16,128]{3,2,1,0:T(8,128)S(1)}, u32[]{:S(2)}, u32[]{:S(2)}) %all-to-all-start.1) | async-done | bytes 262176 | tf_op jit(solution)/shard_map/all_to_all | solution.py:199
  42.0 0.0 copy-start.1
  42.0 0.7 %copy-done.1 = f32[8,4,16,128]{3,2,1,0:T(8,128)} copy-done((f32[8,4,16,128]{3,2,1,0:T(8,128)}, f32[8,4,16,128]{3,2,1,0:T(8,128)S(1)}, u32[]{:S(2)}) %copy-start.1) | copy-done | bytes 262168
  42.7 11.0 %shard_map.60 = (f32[32,16,1024]{2,1,0:T(8,128)}, f32[3,32,16,1024]{3,2,1,0:T(8,128)}) custom-call(bf16[32,16,1024]{2,1,0:T(8,128)(2,1)} %d_ref.3, bf16[3,32,16,1024]{3,2,1,0:T(8,128)(2,1)} %c_ref.3, f32[8,4,16,128]{3,2,1,0:T(8,128)} %copy-done.1, f32[2,16,1024]{2,1,0:T(8,128)} %maximum_convert_fusion.1.zhalo_ref, f32[32,2,1024]{2,1,0:T(2,128)} %maximum_convert_fusion.rhalo_ref), custom_call_target="tpu_custom_call" | custom-call | tf_op jit(solution)/shard_map/pallas_call | solution.py:126
  (7 shorter events, 0.1 us)
Async XLA Ops:
  0.6 13.5 %copy-start = (bf16[32,16,1024]{2,1,0:T(8,128)(2,1)S(1)}, bf16[32,16,1024]{2,1,0:T(8,128)(2,1)}, u32[]{:S(2)}) copy-start(bf16[32,16,1024]{2,1,0:T(8,128)(2,1)} %d_ref.3) | copy-start | bytes 3145732
  0.6 24.9 %copy-start.2 = (s32[8]{0:T(128)S(1)}, s32[8]{0:T(128)}, u32[]{:S(2)}) copy-start(s32[8]{0:T(128)} %param.7) | copy-start | bytes 100
  7.8 17.8 %all-to-all-start = ((f32[8,4,16,128]{3,2,1,0:T(8,128)}), f32[8,4,16,128]{3,2,1,0:T(8,128)S(1)}, u32[]{:S(2)}, u32[]{:S(2)}) async-start(f32[8,4,16,128]{3,2,1,0:T(8,128)} %shard_map.59), calls=%async_computation | async-start | bytes 524288 | tf_op jit(solution)/shard_map/all_to_all | solution.py:191
  14.2 11.4 %collective-permute-start = (bf16[1,16,1024]{2,1,0:T(8,128)(2,1)S(1)}, bf16[1,16,1024]{2,1,0:T(8,128)(2,1)S(1)}, u32[]{:S(2)}, u32[]{:S(2)}) collective-permute-start(bf16[1,16,1024]{2,1,0:T(8,128)(2,1)S(1)} %get-tuple-element.16), channel_id=1, source_target_pairs={{0,4},{4,8},{8,12},{12,16},{16,20},{20,24},{24,28},{1,5},{5,9},{9,... | collective-permute-start | bytes 98312 | tf_op jit(solution)/shard_map/ppermute | solution.py:169
  17.5 8.1 %collective-permute-start.1 = (bf16[1,16,1024]{2,1,0:T(8,128)(2,1)S(1)}, bf16[1,16,1024]{2,1,0:T(8,128)(2,1)S(1)}, u32[]{:S(2)}, u32[]{:S(2)}) collective-permute-start(bf16[1,16,1024]{2,1,0:T(8,128)(2,1)S(1)} %get-tuple-element.17), channel_id=1, source_target_pairs={{4,0},{8,4},{12,8},{16,12},{20,16},{24,20},{28,24},{5,1},{9,5},{13... | collective-permute-start | bytes 98312 | tf_op jit(solution)/shard_map/ppermute | solution.py:170
  19.1 15.6 %collective-permute-start.2 = (bf16[32,1,1024]{2,1,0:T(2,128)(2,1)S(1)}, bf16[32,1,1024]{2,1,0:T(2,128)(2,1)S(1)}, u32[]{:S(2)}, u32[]{:S(2)}) collective-permute-start(bf16[32,1,1024]{2,1,0:T(2,128)(2,1)S(1)} %get-tuple-element.12), channel_id=1, source_target_pairs={{0,1},{1,2},{2,3},{4,5},{5,6},{6,7},{8,9},{9,10},{10,11},{12,13},{... | collective-permute-start | bytes 196616 | tf_op jit(solution)/shard_map/ppermute | solution.py:171
  23.6 11.0 %collective-permute-start.3 = (bf16[32,1,1024]{2,1,0:T(2,128)(2,1)S(1)}, bf16[32,1,1024]{2,1,0:T(2,128)(2,1)S(1)}, u32[]{:S(2)}, u32[]{:S(2)}) collective-permute-start(bf16[32,1,1024]{2,1,0:T(2,128)(2,1)S(1)} %get-tuple-element.13), channel_id=1, source_target_pairs={{1,0},{2,1},{3,2},{5,4},{6,5},{7,6},{9,8},{10,9},{11,10},{13,12},{... | collective-permute-start | bytes 196616 | tf_op jit(solution)/shard_map/ppermute | solution.py:172
  27.6 14.3 %all-to-all-start.1 = ((f32[8,4,16,128]{3,2,1,0:T(8,128)}), f32[8,4,16,128]{3,2,1,0:T(8,128)S(1)}, u32[]{:S(2)}, u32[]{:S(2)}) async-start(f32[8,4,16,128]{3,2,1,0:T(8,128)} %pad_maximum_fusion), calls=%async_computation.1 | async-start | bytes 524288 | tf_op jit(solution)/shard_map/all_to_all | solution.py:199
  42.0 0.7 %copy-start.1 = (f32[8,4,16,128]{3,2,1,0:T(8,128)}, f32[8,4,16,128]{3,2,1,0:T(8,128)S(1)}, u32[]{:S(2)}) copy-start(f32[8,4,16,128]{3,2,1,0:T(8,128)S(1)} %all-to-all-done.1.ans_ref) | copy-start | bytes 786436

commit v5 on v4

--- a/solution.py
+++ b/solution.py
@@ -179,6 +179,20 @@
     return zhalo, rhalo
 
 
+def exchange(x, axis):
+    count = lax.axis_size(axis)
+    me = lax.axis_index(axis)
+    result = lax.dynamic_update_index_in_dim(
+        jnp.zeros_like(x), lax.dynamic_index_in_dim(x, me, 0, keepdims=True), me, 0
+    )
+    for shift in range(1, count):
+        perm = [(i, (i + shift) % count) for i in range(count)]
+        send = lax.dynamic_index_in_dim(x, (me + shift) % count, 0, keepdims=True)
+        got = lax.ppermute(send, axis, perm)
+        result = lax.dynamic_update_index_in_dim(result, got, (me + count - shift) % count, 0)
+    return result
+
+
 def local(density_raw, colour_raw, target, slab_rank):
     slices_dev, rows_dev, width = density_raw.shape
     depth_count = lax.axis_size("depth")
@@ -188,7 +202,7 @@
     partial_value = forward_partial(density_raw, colour_raw, step, depth_count)
     partial_value, after_forward = lax.optimization_barrier((partial_value, density_raw))
     zhalo, rhalo = halos(after_forward)
-    received = lax.all_to_all(partial_value, "depth", 0, 0, tiled=True)
+    received = exchange(partial_value, "depth")
     position = lax.axis_index("depth")
     target_piece = lax.dynamic_slice(
         target,
@@ -196,7 +210,7 @@
         (3, chunk_rows, lanes),
     )
     answers = composite(received, slab_rank, target_piece, float(slices_total))
-    returned = lax.all_to_all(answers, "depth", 0, 0, tiled=True)
+    returned = exchange(answers, "depth")
     return backward_grads(
         density_raw, colour_raw, returned, zhalo, rhalo, step, slices_total
     )

time: 54.5 us -> 81.7 us (1.50)
  the two profiles are of different devices: /device:TPU:1 before, /device:TPU:10 now
where the time goes in v5:
time: 81.7 us; the launch traced here: 81 us
  starting transfers between devices  31.3 us (38%)
  waiting for transfers between devices  25.2 us (31%)
  Pallas kernels  18.1 us (22%)
  other arithmetic  3.38 us (4%)
  local copies, waits for them, and re-layouts  1.99 us (2%)
  between operations  1.03 us (1%)
    ppermute x14, waiting for transfers between devices, exchange(): got = lax.ppermute(send, axis, perm)  25.1 us
    ppermute x14, starting transfers between devices, exchange(): got = lax.ppermute(send, axis, perm)  19 us
    pallas_call x1, Pallas kernels, backward_grads(): pl.pallas_call(functools.partial(backward_kernel, step=step, slices_total...  11 us
    pallas_call x1, Pallas kernels, forward_partial(): pl.pallas_call(functools.partial(forward_kernel, step=step), grid=(tiles,...  7.12 us
    ppermute x1, starting transfers between devices, halos(): next_row = lax.ppermute(first_row, 'rows', [(j, i) for i, j in up_r])  3.64 us
    ppermute x1, starting transfers between devices, halos(): prev_slice = lax.ppermute(last_slice, 'depth', up_d)  3.43 us
    ppermute x1, starting transfers between devices, halos(): next_slice = lax.ppermute(first_slice, 'depth', [(j, i) for i, j in up_d])  3.31 us
    ppermute x1, starting transfers between devices, halos(): prev_row = lax.ppermute(last_row, 'rows', up_r)  1.91 us
  transfers between devices with their start and end apart: 18, of which 7 were waited for; matrix products, arithmetic and copies ran while one was open for 6% of the time, Pallas kernels for 0%

profile of v5, /device:TPU:10, one launch (start us, length us, event | category | flops | bytes accessed | tf_op | source)
XLA Modules:
  0.0 81.0 jit_solution(10968939338238603198)
XLA Ops:
  0.6 0.0 copy-start
  0.7 7.1 %shard_map.59 = f32[8,4,16,128]{3,2,1,0:T(8,128)} custom-call(bf16[32,16,1024]{2,1,0:T(8,128)(2,1)} %d_ref.3, bf16[3,32,16,1024]{3,2,1,0:T(8,128)(2,1)} %c_ref.3), custom_call_target="tpu_custom_call" | custom-call | tf_op jit(solution)/shard_map/pallas_call | solution.py:107
  7.8 3.4 %collective-permute-start.14 = (bf16[1,16,1024]{2,1,0:T(8,128)(2,1)S(1)}, bf16[1,16,1024]{2,1,0:T(8,128)(2,1)S(1)}, u32[]{:S(2)}, u32[]{:S(2)}) collective-permute-start(bf16[1,16,1024]{2,1,0:T(8,128)(2,1)S(1)} %get-tuple-element.16), channel_id=1, source_target_pairs={{0,4},{4,8},{8,12},{12,16},{16,20},{20,24},{24,28},{1,5},{5,9},{9,... | collective-permute-start | bytes 98312 | tf_op jit(solution)/shard_map/ppermute | solution.py:169
  11.2 3.3 %collective-permute-start.15 = (bf16[1,16,1024]{2,1,0:T(8,128)(2,1)S(1)}, bf16[1,16,1024]{2,1,0:T(8,128)(2,1)S(1)}, u32[]{:S(2)}, u32[]{:S(2)}) collective-permute-start(bf16[1,16,1024]{2,1,0:T(8,128)(2,1)S(1)} %get-tuple-element.17), channel_id=1, source_target_pairs={{4,0},{8,4},{12,8},{16,12},{20,16},{24,20},{28,24},{5,1},{9,5},{13... | collective-permute-start | bytes 98312 | tf_op jit(solution)/shard_map/ppermute | solution.py:170
  14.7 0.9 %constant_dynamic-slice_fusion = (f32[1,4,16,128]{3,2,1,0:T(8,128)S(1)}, f32[1,4,16,128]{3,2,1,0:T(8,128)S(1)}, f32[1,4,16,128]{3,2,1,0:T(8,128)S(1)}, f32[1,4,1...) fusion(f32[8,4,16,128]{3,2,1,0:T(8,128)} %shard_map.59, ...), kind=kLoop, calls=%fused_computation.54 | loop fusion | bytes 524320 | tf_op jit(solution)/shard_map/jit(dynamic_index_in_dim)/dynamic_slice | solution.py:190
  15.6 0.6 collective-permute-start.6
  16.2 3.6 %collective-permute-start.5 = (f32[1,4,16,128]{3,2,1,0:T(8,128)S(1)}, f32[1,4,16,128]{3,2,1,0:T(8,128)S(1)}, u32[]{:S(2)}, u32[]{:S(2)}) collective-permute-start(f32[1,4,16,128]{3,2,1,0:T(8,128)S(1)} %get-tuple-element.27), channel_id=1, source_target_pairs={{0,24},{4,28},{8,0},{12,4},{16,8},{20,12},{24,16},{28,20},{1,25},{... | collective-permute-start | bytes 98312 | tf_op jit(solution)/shard_map/ppermute | solution.py:191
  19.8 0.0 collective-permute-start
  19.8 0.2 fusion.14
  20.0 0.1 compare_convert_fusion
  20.1 4.5 %collective-permute-done = f32[1,4,16,128]{3,2,1,0:T(8,128)S(1)} collective-permute-done((f32[1,4,16,128]{3,2,1,0:T(8,128)S(1)}, f32[1,4,16,128]{3,2,1,0:T(8,128)S(1)}, u32[]{:S(2)}, u32[]{:S(2)}) %collective-permute-start) | collective-permute-done | bytes 32800 | tf_op jit(solution)/shard_map/ppermute | solution.py:191
  24.6 0.0 collective-permute-start.1
  24.6 4.1 %collective-permute-done.1 = f32[1,4,16,128]{3,2,1,0:T(8,128)S(1)} collective-permute-done((f32[1,4,16,128]{3,2,1,0:T(8,128)S(1)}, f32[1,4,16,128]{3,2,1,0:T(8,128)S(1)}, u32[]{:S(2)}, u32[]{:S(2)}) %collective-permute-start.1) | collective-permute-done | bytes 32800 | tf_op jit(solution)/shard_map/ppermute | solution.py:191
  28.7 0.0 collective-permute-start.2
  28.7 5.8 %collective-permute-done.2 = f32[1,4,16,128]{3,2,1,0:T(8,128)S(1)} collective-permute-done((f32[1,4,16,128]{3,2,1,0:T(8,128)S(1)}, f32[1,4,16,128]{3,2,1,0:T(8,128)S(1)}, u32[]{:S(2)}, u32[]{:S(2)}) %collective-permute-start.2) | collective-permute-done | bytes 32800 | tf_op jit(solution)/shard_map/ppermute | solution.py:191
  34.5 2.0 %collective-permute-start.3 = (f32[1,4,16,128]{3,2,1,0:T(8,128)S(1)}, f32[1,4,16,128]{3,2,1,0:T(8,128)S(1)}, u32[]{:S(2)}, u32[]{:S(2)}) collective-permute-start(f32[1,4,16,128]{3,2,1,0:T(8,128)S(1)} %get-tuple-element.29), channel_id=1, source_target_pairs={{0,16},{4,20},{8,24},{12,28},{16,0},{20,4},{24,8},{28,12},{1,17},{... | collective-permute-start | bytes 98312 | tf_op jit(solution)/shard_map/ppermute | solution.py:191
  36.5 2.9 %collective-permute-done.3 = f32[1,4,16,128]{3,2,1,0:T(8,128)S(1)} collective-permute-done((f32[1,4,16,128]{3,2,1,0:T(8,128)S(1)}, f32[1,4,16,128]{3,2,1,0:T(8,128)S(1)}, u32[]{:S(2)}, u32[]{:S(2)}) %collective-permute-start.3) | collective-permute-done | bytes 32800 | tf_op jit(solution)/shard_map/ppermute | solution.py:191
  39.4 0.8 collective-permute-start.4
  40.2 4.0 %collective-permute-done.4 = f32[1,4,16,128]{3,2,1,0:T(8,128)S(1)} collective-permute-done((f32[1,4,16,128]{3,2,1,0:T(8,128)S(1)}, f32[1,4,16,128]{3,2,1,0:T(8,128)S(1)}, u32[]{:S(2)}, u32[]{:S(2)}) %collective-permute-start.4) | collective-permute-done | bytes 32800 | tf_op jit(solution)/shard_map/ppermute | solution.py:191
  44.2 1.9 %collective-permute-start.16 = (bf16[32,1,1024]{2,1,0:T(2,128)(2,1)S(1)}, bf16[32,1,1024]{2,1,0:T(2,128)(2,1)S(1)}, u32[]{:S(2)}, u32[]{:S(2)}) collective-permute-start(bf16[32,1,1024]{2,1,0:T(2,128)(2,1)S(1)} %get-tuple-element.12), channel_id=1, source_target_pairs={{0,1},{1,2},{2,3},{4,5},{5,6},{6,7},{8,9},{9,10},{10,11},{12,13},{... | collective-permute-start | bytes 196616 | tf_op jit(solution)/shard_map/ppermute | solution.py:171
  46.1 0.0 collective-permute-done.5
  46.2 3.6 %collective-permute-start.17 = (bf16[32,1,1024]{2,1,0:T(2,128)(2,1)S(1)}, bf16[32,1,1024]{2,1,0:T(2,128)(2,1)S(1)}, u32[]{:S(2)}, u32[]{:S(2)}) collective-permute-start(bf16[32,1,1024]{2,1,0:T(2,128)(2,1)S(1)} %get-tuple-element.13), channel_id=1, source_target_pairs={{1,0},{2,1},{3,2},{5,4},{6,5},{7,6},{9,8},{10,9},{11,10},{13,12},{... | collective-permute-start | bytes 196616 | tf_op jit(solution)/shard_map/ppermute | solution.py:172
  49.8 0.0 collective-permute-done.6
  49.9 0.1 multiply_reduce_fusion.1
  50.1 0.2 multiply_reduce_fusion
  50.3 0.8 dynamic-slice_subtract_fusion
  51.0 0.1 multiply_reduce_fusion.3
  51.2 3.8 %collective-permute-start.13 = (f32[1,4,16,128]{3,2,1,0:T(8,128)S(1)}, f32[1,4,16,128]{3,2,1,0:T(8,128)S(1)}, u32[]{:S(2)}, u32[]{:S(2)}) collective-permute-start(f32[1,4,16,128]{3,2,1,0:T(8,128)S(1)} %get-tuple-element.18), channel_id=1, source_target_pairs={{0,28},{4,0},{8,4},{12,8},{16,12},{20,16},{24,20},{28,24},{1,29},{... | collective-permute-start | bytes 98312 | tf_op jit(solution)/shard_map/ppermute | solution.py:191
  54.9 0.0 collective-permute-done.14
  54.9 0.0 collective-permute-start.7
  54.9 0.0 collective-permute-done.15
  54.9 0.5 collective-permute-start.8
  55.5 0.7 maximum_convert_fusion.1.zhalo_ref
  56.2 0.0 collective-permute-done.16
  56.2 3.4 %collective-permute-start.9 = (f32[1,4,16,128]{3,2,1,0:T(8,128)S(1)}, f32[1,4,16,128]{3,2,1,0:T(8,128)S(1)}, u32[]{:S(2)}, u32[]{:S(2)}) collective-permute-start(f32[1,4,16,128]{3,2,1,0:T(8,128)S(1)} %get-tuple-element.21), channel_id=1, source_target_pairs={{0,12},{4,16},{8,20},{12,24},{16,28},{20,0},{24,4},{28,8},{1,13},{... | collective-permute-start | bytes 98312 | tf_op jit(solution)/shard_map/ppermute | solution.py:191
  59.6 1.5 %collective-permute-start.10 = (f32[1,4,16,128]{3,2,1,0:T(8,128)S(1)}, f32[1,4,16,128]{3,2,1,0:T(8,128)S(1)}, u32[]{:S(2)}, u32[]{:S(2)}) collective-permute-start(f32[1,4,16,128]{3,2,1,0:T(8,128)S(1)} %get-tuple-element.22), channel_id=1, source_target_pairs={{0,16},{4,20},{8,24},{12,28},{16,0},{20,4},{24,8},{28,12},{1,17},{... | collective-permute-start | bytes 98312 | tf_op jit(solution)/shard_map/ppermute | solution.py:191
  61.0 0.4 broadcast_select_fusion.1
  61.4 1.0 %maximum_convert_fusion.rhalo_ref = f32[32,2,1024]{2,1,0:T(2,128)} fusion(bf16[32,1,1024]{2,1,0:T(2,128)(2,1)S(1)} %get-tuple-element.11, bf16[32,1,1024]{2,1,0:T(2,128)(2,1)S(1)} %get-tuple-element.10), kind=kLoop, calls=%fused_computation.24 | loop fusion | flops 262144 | bytes 393216 | tf_op jit(solution)/shard_map/convert_element_type | solution.py:178
  62.4 0.0 collective-permute-done.7
  62.4 2.9 %collective-permute-start.11 = (f32[1,4,16,128]{3,2,1,0:T(8,128)S(1)}, f32[1,4,16,128]{3,2,1,0:T(8,128)S(1)}, u32[]{:S(2)}, u32[]{:S(2)}) collective-permute-start(f32[1,4,16,128]{3,2,1,0:T(8,128)S(1)} %get-tuple-element.23), channel_id=1, source_target_pairs={{0,20},{4,24},{8,28},{12,0},{16,4},{20,8},{24,12},{28,16},{1,21},{... | collective-permute-start | bytes 98312 | tf_op jit(solution)/shard_map/ppermute | solution.py:191
  65.3 0.0 collective-permute-done.8
  65.3 0.1 collective-permute-start.12
  65.4 0.0 collective-permute-done.10
  65.4 1.8 %collective-permute-done.11 = f32[1,4,16,128]{3,2,1,0:T(8,128)S(1)} collective-permute-done((f32[1,4,16,128]{3,2,1,0:T(8,128)S(1)}, f32[1,4,16,128]{3,2,1,0:T(8,128)S(1)}, u32[]{:S(2)}, u32[]{:S(2)}) %collective-permute-start.11) | collective-permute-done | bytes 32800 | tf_op jit(solution)/shard_map/ppermute | solution.py:191
  67.3 2.0 %collective-permute-done.12 = f32[1,4,16,128]{3,2,1,0:T(8,128)S(1)} collective-permute-done((f32[1,4,16,128]{3,2,1,0:T(8,128)S(1)}, f32[1,4,16,128]{3,2,1,0:T(8,128)S(1)}, u32[]{:S(2)}, u32[]{:S(2)}) %collective-permute-start.12) | collective-permute-done | bytes 32800 | tf_op jit(solution)/shard_map/ppermute | solution.py:191
  69.3 0.0 collective-permute-done.13
  69.3 0.7 copy-done.1
  70.0 11.0 %shard_map.60 = (f32[32,16,1024]{2,1,0:T(8,128)}, f32[3,32,16,1024]{3,2,1,0:T(8,128)}) custom-call(bf16[32,16,1024]{2,1,0:T(8,128)(2,1)} %d_ref.3, bf16[3,32,16,1024]{3,2,1,0:T(8,128)(2,1)} %c_ref.3, f32[8,4,16,128]{3,2,1,0:T(8,128)} %copy-done.1, f32[2,16,1024]{2,1,0:T(8,128)} %maximum_convert_fusion.1.zhalo_ref, f32[32,2,1024]{2,1,0:T(2,128)} %maximum_convert_fusion.rhalo_ref), custom_call_target="tpu_custom_call" | custom-call | tf_op jit(solution)/shard_map/pallas_call | solution.py:126
  (31 shorter events, 0.3 us)
Async XLA Ops:
  0.6 7.1 %copy-start = (bf16[32,16,1024]{2,1,0:T(8,128)(2,1)S(1)}, bf16[32,16,1024]{2,1,0:T(8,128)(2,1)}, u32[]{:S(2)}) copy-start(bf16[32,16,1024]{2,1,0:T(8,128)(2,1)} %d_ref.3) | copy-start | bytes 3145732
  0.6 19.3 %copy-start.2 = (s32[8]{0:T(128)S(1)}, s32[8]{0:T(128)}, u32[]{:S(2)}) copy-start(s32[8]{0:T(128)} %param.7) | copy-start | bytes 100
  7.8 47.1 %collective-permute-start.14 = (bf16[1,16,1024]{2,1,0:T(8,128)(2,1)S(1)}, bf16[1,16,1024]{2,1,0:T(8,128)(2,1)S(1)}, u32[]{:S(2)}, u32[]{:S(2)}) collective-permute-start(bf16[1,16,1024]{2,1,0:T(8,128)(2,1)S(1)} %get-tuple-element.16), channel_id=1, source_target_pairs={{0,4},{4,8},{8,12},{12,16},{16,20},{20,24},{24,28},{1,5},{5,9},{9,... | collective-permute-start | bytes 98312 | tf_op jit(solution)/shard_map/ppermute | solution.py:169
  11.2 43.7 %collective-permute-start.15 = (bf16[1,16,1024]{2,1,0:T(8,128)(2,1)S(1)}, bf16[1,16,1024]{2,1,0:T(8,128)(2,1)S(1)}, u32[]{:S(2)}, u32[]{:S(2)}) collective-permute-start(bf16[1,16,1024]{2,1,0:T(8,128)(2,1)S(1)} %get-tuple-element.17), channel_id=1, source_target_pairs={{4,0},{8,4},{12,8},{16,12},{20,16},{24,20},{28,24},{5,1},{9,5},{13... | collective-permute-start | bytes 98312 | tf_op jit(solution)/shard_map/ppermute | solution.py:170
  15.6 34.2 %collective-permute-start.6 = (f32[1,4,16,128]{3,2,1,0:T(8,128)S(1)}, f32[1,4,16,128]{3,2,1,0:T(8,128)S(1)}, u32[]{:S(2)}, u32[]{:S(2)}) collective-permute-start(f32[1,4,16,128]{3,2,1,0:T(8,128)S(1)} %get-tuple-element.26), channel_id=1, source_target_pairs={{0,28},{4,0},{8,4},{12,8},{16,12},{20,16},{24,20},{28,24},{1,29},{... | collective-permute-start | bytes 98312 | tf_op jit(solution)/shard_map/ppermute | solution.py:191
  16.2 30.0 %collective-permute-start.5 = (f32[1,4,16,128]{3,2,1,0:T(8,128)S(1)}, f32[1,4,16,128]{3,2,1,0:T(8,128)S(1)}, u32[]{:S(2)}, u32[]{:S(2)}) collective-permute-start(f32[1,4,16,128]{3,2,1,0:T(8,128)S(1)} %get-tuple-element.27), channel_id=1, source_target_pairs={{0,24},{4,28},{8,0},{12,4},{16,8},{20,12},{24,16},{28,20},{1,25},{... | collective-permute-start | bytes 98312 | tf_op jit(solution)/shard_map/ppermute | solution.py:191
  19.8 4.8 %collective-permute-start = (f32[1,4,16,128]{3,2,1,0:T(8,128)S(1)}, f32[1,4,16,128]{3,2,1,0:T(8,128)S(1)}, u32[]{:S(2)}, u32[]{:S(2)}) collective-permute-start(f32[1,4,16,128]{3,2,1,0:T(8,128)S(1)} %get-tuple-element.32), channel_id=1, source_target_pairs={{0,4},{4,8},{8,12},{12,16},{16,20},{20,24},{24,28},{28,0},{1,5},{5... | collective-permute-start | bytes 98312 | tf_op jit(solution)/shard_map/ppermute | solution.py:191
  24.6 4.1 %collective-permute-start.1 = (f32[1,4,16,128]{3,2,1,0:T(8,128)S(1)}, f32[1,4,16,128]{3,2,1,0:T(8,128)S(1)}, u32[]{:S(2)}, u32[]{:S(2)}) collective-permute-start(f32[1,4,16,128]{3,2,1,0:T(8,128)S(1)} %get-tuple-element.31), channel_id=1, source_target_pairs={{0,8},{4,12},{8,16},{12,20},{16,24},{20,28},{24,0},{28,4},{1,9},{5... | collective-permute-start | bytes 98312 | tf_op jit(solution)/shard_map/ppermute | solution.py:191
  28.7 5.8 %collective-permute-start.2 = (f32[1,4,16,128]{3,2,1,0:T(8,128)S(1)}, f32[1,4,16,128]{3,2,1,0:T(8,128)S(1)}, u32[]{:S(2)}, u32[]{:S(2)}) collective-permute-start(f32[1,4,16,128]{3,2,1,0:T(8,128)S(1)} %get-tuple-element.30), channel_id=1, source_target_pairs={{0,12},{4,16},{8,20},{12,24},{16,28},{20,0},{24,4},{28,8},{1,13},{... | collective-permute-start | bytes 98312 | tf_op jit(solution)/shard_map/ppermute | solution.py:191
  34.5 4.9 %collective-permute-start.3 = (f32[1,4,16,128]{3,2,1,0:T(8,128)S(1)}, f32[1,4,16,128]{3,2,1,0:T(8,128)S(1)}, u32[]{:S(2)}, u32[]{:S(2)}) collective-permute-start(f32[1,4,16,128]{3,2,1,0:T(8,128)S(1)} %get-tuple-element.29), channel_id=1, source_target_pairs={{0,16},{4,20},{8,24},{12,28},{16,0},{20,4},{24,8},{28,12},{1,17},{... | collective-permute-start | bytes 98312 | tf_op jit(solution)/shard_map/ppermute | solution.py:191
  39.4 4.8 %collective-permute-start.4 = (f32[1,4,16,128]{3,2,1,0:T(8,128)S(1)}, f32[1,4,16,128]{3,2,1,0:T(8,128)S(1)}, u32[]{:S(2)}, u32[]{:S(2)}) collective-permute-start(f32[1,4,16,128]{3,2,1,0:T(8,128)S(1)} %get-tuple-element.28), channel_id=1, source_target_pairs={{0,20},{4,24},{8,28},{12,0},{16,4},{20,8},{24,12},{28,16},{1,21},{... | collective-permute-start | bytes 98312 | tf_op jit(solution)/shard_map/ppermute | solution.py:191
  44.2 12.0 %collective-permute-start.16 = (bf16[32,1,1024]{2,1,0:T(2,128)(2,1)S(1)}, bf16[32,1,1024]{2,1,0:T(2,128)(2,1)S(1)}, u32[]{:S(2)}, u32[]{:S(2)}) collective-permute-start(bf16[32,1,1024]{2,1,0:T(2,128)(2,1)S(1)} %get-tuple-element.12), channel_id=1, source_target_pairs={{0,1},{1,2},{2,3},{4,5},{5,6},{6,7},{8,9},{9,10},{10,11},{12,13},{... | collective-permute-start | bytes 196616 | tf_op jit(solution)/shard_map/ppermute | solution.py:171
  46.2 13.4 %collective-permute-start.17 = (bf16[32,1,1024]{2,1,0:T(2,128)(2,1)S(1)}, bf16[32,1,1024]{2,1,0:T(2,128)(2,1)S(1)}, u32[]{:S(2)}, u32[]{:S(2)}) collective-permute-start(bf16[32,1,1024]{2,1,0:T(2,128)(2,1)S(1)} %get-tuple-element.13), channel_id=1, source_target_pairs={{1,0},{2,1},{3,2},{5,4},{6,5},{7,6},{9,8},{10,9},{11,10},{13,12},{... | collective-permute-start | bytes 196616 | tf_op jit(solution)/shard_map/ppermute | solution.py:172
  51.2 18.1 %collective-permute-start.13 = (f32[1,4,16,128]{3,2,1,0:T(8,128)S(1)}, f32[1,4,16,128]{3,2,1,0:T(8,128)S(1)}, u32[]{:S(2)}, u32[]{:S(2)}) collective-permute-start(f32[1,4,16,128]{3,2,1,0:T(8,128)S(1)} %get-tuple-element.18), channel_id=1, source_target_pairs={{0,28},{4,0},{8,4},{12,8},{16,12},{20,16},{24,20},{28,24},{1,29},{... | collective-permute-start | bytes 98312 | tf_op jit(solution)/shard_map/ppermute | solution.py:191
  54.9 7.5 %collective-permute-start.7 = (f32[1,4,16,128]{3,2,1,0:T(8,128)S(1)}, f32[1,4,16,128]{3,2,1,0:T(8,128)S(1)}, u32[]{:S(2)}, u32[]{:S(2)}) collective-permute-start(f32[1,4,16,128]{3,2,1,0:T(8,128)S(1)} %get-tuple-element.19), channel_id=1, source_target_pairs={{0,4},{4,8},{8,12},{12,16},{16,20},{20,24},{24,28},{28,0},{1,5},{5... | collective-permute-start | bytes 98312 | tf_op jit(solution)/shard_map/ppermute | solution.py:191
  54.9 10.4 %collective-permute-start.8 = (f32[1,4,16,128]{3,2,1,0:T(8,128)S(1)}, f32[1,4,16,128]{3,2,1,0:T(8,128)S(1)}, u32[]{:S(2)}, u32[]{:S(2)}) collective-permute-start(f32[1,4,16,128]{3,2,1,0:T(8,128)S(1)} %get-tuple-element.20), channel_id=1, source_target_pairs={{0,8},{4,12},{8,16},{12,20},{16,24},{20,28},{24,0},{28,4},{1,9},{5... | collective-permute-start | bytes 98312 | tf_op jit(solution)/shard_map/ppermute | solution.py:191
  56.2 9.2 %collective-permute-start.9 = (f32[1,4,16,128]{3,2,1,0:T(8,128)S(1)}, f32[1,4,16,128]{3,2,1,0:T(8,128)S(1)}, u32[]{:S(2)}, u32[]{:S(2)}) collective-permute-start(f32[1,4,16,128]{3,2,1,0:T(8,128)S(1)} %get-tuple-element.21), channel_id=1, source_target_pairs={{0,12},{4,16},{8,20},{12,24},{16,28},{20,0},{24,4},{28,8},{1,13},{... | collective-permute-start | bytes 98312 | tf_op jit(solution)/shard_map/ppermute | solution.py:191
  59.6 5.8 %collective-permute-start.10 = (f32[1,4,16,128]{3,2,1,0:T(8,128)S(1)}, f32[1,4,16,128]{3,2,1,0:T(8,128)S(1)}, u32[]{:S(2)}, u32[]{:S(2)}) collective-permute-start(f32[1,4,16,128]{3,2,1,0:T(8,128)S(1)} %get-tuple-element.22), channel_id=1, source_target_pairs={{0,16},{4,20},{8,24},{12,28},{16,0},{20,4},{24,8},{28,12},{1,17},{... | collective-permute-start | bytes 98312 | tf_op jit(solution)/shard_map/ppermute | solution.py:191
  62.4 4.8 %collective-permute-start.11 = (f32[1,4,16,128]{3,2,1,0:T(8,128)S(1)}, f32[1,4,16,128]{3,2,1,0:T(8,128)S(1)}, u32[]{:S(2)}, u32[]{:S(2)}) collective-permute-start(f32[1,4,16,128]{3,2,1,0:T(8,128)S(1)} %get-tuple-element.23), channel_id=1, source_target_pairs={{0,20},{4,24},{8,28},{12,0},{16,4},{20,8},{24,12},{28,16},{1,21},{... | collective-permute-start | bytes 98312 | tf_op jit(solution)/shard_map/ppermute | solution.py:191
  65.3 4.0 %collective-permute-start.12 = (f32[1,4,16,128]{3,2,1,0:T(8,128)S(1)}, f32[1,4,16,128]{3,2,1,0:T(8,128)S(1)}, u32[]{:S(2)}, u32[]{:S(2)}) collective-permute-start(f32[1,4,16,128]{3,2,1,0:T(8,128)S(1)} %get-tuple-element.24), channel_id=1, source_target_pairs={{0,24},{4,28},{8,0},{12,4},{16,8},{20,12},{24,16},{28,20},{1,25},{... | collective-permute-start | bytes 98312 | tf_op jit(solution)/shard_map/ppermute | solution.py:191
  69.3 0.7 copy-start.1

commit v6 on v4

--- a/solution.py
+++ b/solution.py
@@ -35,17 +35,18 @@
     def body(z, carry):
         n, front, e0, e1, e2 = carry
         dtn = softplus(d_ref[z].astype(jnp.float32)) * scale
-        lit = front * (1.0 - jnp.exp2(dtn))
+        kept = jnp.exp2(dtn)
+        lit = front * (1.0 - kept)
         n = n + dtn
         e0 = e0 + lit * jax.nn.sigmoid(c_ref[0, z].astype(jnp.float32))
         e1 = e1 + lit * jax.nn.sigmoid(c_ref[1, z].astype(jnp.float32))
         e2 = e2 + lit * jax.nn.sigmoid(c_ref[2, z].astype(jnp.float32))
-        return (n, jnp.exp2(n), e0, e1, e2)
+        return (n, front * kept, e0, e1, e2)
 
     zero = jnp.zeros(shape, jnp.float32)
     one = jnp.ones(shape, jnp.float32)
-    _, passing, e0, e1, e2 = lax.fori_loop(0, slices, body, (zero, one, zero, zero, zero), unroll=4)
-    values = (e0, e1, e2, passing)
+    n, _, e0, e1, e2 = lax.fori_loop(0, slices, body, (zero, one, zero, zero, zero), unroll=4)
+    values = (e0, e1, e2, jnp.exp2(n))
     for g in range(per_tile):
         for c in range(4):
             out_ref[g, c] = values[c][g * chunk_rows:(g + 1) * chunk_rows]
@@ -54,14 +55,16 @@
 def backward_kernel(d_ref, c_ref, ans_ref, zhalo_ref, rhalo_ref, gd_ref, gc_ref, *, step, slices_total):
     slices = d_ref.shape[0]
     shape = d_ref.shape[1:]
-    per_tile = ans_ref.shape[0]
+    per_tile = ans_ref.shape[0] // pl.num_programs(0)
     scale = -step * log2e
     gain = optical_depth / slices_total
 
+    base = pl.program_id(0) * per_tile
+
     def pixel(ref, c):
         if per_tile == 1:
-            return ref[0, c]
-        return jnp.concatenate([ref[g, c] for g in range(per_tile)], axis=0)
+            return ref[base, c]
+        return jnp.concatenate([ref[base + g, c] for g in range(per_tile)], axis=0)
 
     row = lax.broadcasted_iota(jnp.int32, shape, 0)
     first_row = row == 0
@@ -129,7 +132,7 @@
         in_specs=[
             slab,
             colours,
-            pixel,
+            pl.BlockSpec(memory_space=pltpu.VMEM),
             pl.BlockSpec((2, rows, lanes), lambda i: (0, 0, i)),
             pl.BlockSpec((slices, 2, lanes), lambda i: (0, 0, i)),
         ],

time: 54.5 us -> 54.7 us (level)
  no operation moved by 1% of the time
where the time goes in v6:
time: 54.7 us; the launch traced here: 53.9 us
  starting transfers between devices  23.8 us (44%)
  Pallas kernels  18.4 us (34%)
  waiting for transfers between devices  5.96 us (11%)
  other arithmetic  4.03 us (7%)
  local copies, waits for them, and re-layouts  0.95 us (2%)
  between operations  0.78 us (1%)
    pallas_call x1, Pallas kernels, backward_grads(): pl.pallas_call(functools.partial(backward_kernel, step=step, slices_total...  11.3 us
    pallas_call x1, Pallas kernels, forward_partial(): pl.pallas_call(functools.partial(forward_kernel, step=step), grid=(tiles,...  7.1 us
    all_to_all x1, starting transfers between devices, local(): received = lax.all_to_all(partial_value, 'depth', 0, 0, tiled=True)  6.38 us
    all_to_all x1, starting transfers between devices, local(): returned = lax.all_to_all(answers, 'depth', 0, 0, tiled=True)  6.34 us
    all_to_all x1, waiting for transfers between devices, local(): returned = lax.all_to_all(answers, 'depth', 0, 0, tiled=True)  5.95 us
    ppermute x1, starting transfers between devices, halos(): prev_row = lax.ppermute(last_row, 'rows', up_r)  4.52 us
    ppermute x1, starting transfers between devices, halos(): prev_slice = lax.ppermute(last_slice, 'depth', up_d)  3.36 us
    ppermute x1, starting transfers between devices, halos(): next_row = lax.ppermute(first_row, 'rows', [(j, i) for i, j in up_r])  1.92 us
  transfers between devices with their start and end apart: 6, of which 1 were waited for; matrix products, arithmetic and copies ran while one was open for 8% of the time, Pallas kernels for 0%

profile of v6, /device:TPU:1, one launch (start us, length us, event | category | flops | bytes accessed | tf_op | source)
XLA Modules:
  0.0 53.9 jit_solution(18248046431136934647)
XLA Ops:
  0.6 0.0 copy-start
  0.6 0.0 copy-start.2
  0.7 7.1 %shard_map.59 = f32[8,4,16,128]{3,2,1,0:T(8,128)} custom-call(bf16[32,16,1024]{2,1,0:T(8,128)(2,1)} %d_ref.3, bf16[3,32,16,1024]{3,2,1,0:T(8,128)(2,1)} %c_ref.3), custom_call_target="tpu_custom_call" | custom-call | tf_op jit(solution)/shard_map/pallas_call | solution.py:110
  7.7 6.4 %all-to-all-start = ((f32[8,4,16,128]{3,2,1,0:T(8,128)}), f32[8,4,16,128]{3,2,1,0:T(8,128)S(1)}, u32[]{:S(2)}, u32[]{:S(2)}) async-start(f32[8,4,16,128]{3,2,1,0:T(8,128)} %shard_map.59), calls=%async_computation | async-start | bytes 524288 | tf_op jit(solution)/shard_map/all_to_all | solution.py:194
  14.1 0.0 copy-done
  14.2 3.4 %collective-permute-start = (bf16[1,16,1024]{2,1,0:T(8,128)(2,1)S(1)}, bf16[1,16,1024]{2,1,0:T(8,128)(2,1)S(1)}, u32[]{:S(2)}, u32[]{:S(2)}) collective-permute-start(bf16[1,16,1024]{2,1,0:T(8,128)(2,1)S(1)} %get-tuple-element.16), channel_id=1, source_target_pairs={{0,4},{4,8},{8,12},{12,16},{16,20},{20,24},{24,28},{1,5},{5,9},{9,... | collective-permute-start | bytes 98312 | tf_op jit(solution)/shard_map/ppermute | solution.py:172
  17.5 1.3 %collective-permute-start.1 = (bf16[1,16,1024]{2,1,0:T(8,128)(2,1)S(1)}, bf16[1,16,1024]{2,1,0:T(8,128)(2,1)S(1)}, u32[]{:S(2)}, u32[]{:S(2)}) collective-permute-start(bf16[1,16,1024]{2,1,0:T(8,128)(2,1)S(1)} %get-tuple-element.17), channel_id=1, source_target_pairs={{4,0},{8,4},{12,8},{16,12},{20,16},{24,20},{28,24},{5,1},{9,5},{13... | collective-permute-start | bytes 98312 | tf_op jit(solution)/shard_map/ppermute | solution.py:173
  18.8 0.2 fusion.5
  19.0 4.5 %collective-permute-start.2 = (bf16[32,1,1024]{2,1,0:T(2,128)(2,1)S(1)}, bf16[32,1,1024]{2,1,0:T(2,128)(2,1)S(1)}, u32[]{:S(2)}, u32[]{:S(2)}) collective-permute-start(bf16[32,1,1024]{2,1,0:T(2,128)(2,1)S(1)} %get-tuple-element.12), channel_id=1, source_target_pairs={{0,1},{1,2},{2,3},{4,5},{5,6},{6,7},{8,9},{9,10},{10,11},{12,13},{... | collective-permute-start | bytes 196616 | tf_op jit(solution)/shard_map/ppermute | solution.py:174
  23.6 1.9 %collective-permute-start.3 = (bf16[32,1,1024]{2,1,0:T(2,128)(2,1)S(1)}, bf16[32,1,1024]{2,1,0:T(2,128)(2,1)S(1)}, u32[]{:S(2)}, u32[]{:S(2)}) collective-permute-start(bf16[32,1,1024]{2,1,0:T(2,128)(2,1)S(1)} %get-tuple-element.13), channel_id=1, source_target_pairs={{1,0},{2,1},{3,2},{5,4},{6,5},{7,6},{9,8},{10,9},{11,10},{13,12},{... | collective-permute-start | bytes 196616 | tf_op jit(solution)/shard_map/ppermute | solution.py:175
  25.5 0.0 copy-done.2
  25.5 0.1 compare_convert_fusion
  25.6 0.0 collective-permute-done
  25.6 0.0 collective-permute-done.1
  25.6 0.0 all-to-all-done
  25.6 0.1 multiply_reduce_fusion.1
  25.8 0.2 multiply_reduce_fusion
  26.0 0.8 %dynamic-slice_subtract_fusion = f32[3,16,128]{2,1,0:T(8,128)S(1)} fusion(f32[3,16,128]{2,1,0:T(8,128)S(1)} %get-tuple-element.8, f32[3,16,1024]{2,1,0:T(8,128)} %param.6, s32[]{:T(128)S(6)} %select_n.39), kind=kLoop, calls=%fused_computation.20 | loop fusion | flops 6144 | bytes 73732 | tf_op jit(solution)/shard_map/sub | solution.py:154
  26.8 0.1 multiply_reduce_fusion.3
  26.9 0.7 %pad_maximum_fusion = f32[8,4,16,128]{3,2,1,0:T(8,128)} fusion(f32[8,1,16,128]{3,2,1,0:T(8,128)S(1)} %fusion.2, f32[8,3,16,128]{3,2,1,0:T(8,128)S(1)} %get-tuple-element.18), kind=kLoop, calls=%fused_computation.2 | loop fusion | flops 65536 | bytes 524288 | tf_op jit(solution)/shard_map/concatenate | solution.py:158
  27.6 6.3 %all-to-all-start.1 = ((f32[8,4,16,128]{3,2,1,0:T(8,128)}), f32[8,4,16,128]{3,2,1,0:T(8,128)S(1)}, u32[]{:S(2)}, u32[]{:S(2)}) async-start(f32[8,4,16,128]{3,2,1,0:T(8,128)} %pad_maximum_fusion), calls=%async_computation.1 | async-start | bytes 524288 | tf_op jit(solution)/shard_map/all_to_all | solution.py:202
  33.9 0.7 %maximum_convert_fusion.1.zhalo_ref = f32[2,16,1024]{2,1,0:T(8,128)} fusion(bf16[1,16,1024]{2,1,0:T(8,128)(2,1)S(1)} %get-tuple-element.15, bf16[1,16,1024]{2,1,0:T(8,128)(2,1)S(1)} %get-tuple-element.14), kind=kLoop, calls=%fused_computation.10 | loop fusion | flops 65536 | bytes 196608 | tf_op jit(solution)/shard_map/convert_element_type | solution.py:180
  34.6 0.0 collective-permute-done.2
  34.6 0.0 collective-permute-done.3
  34.6 0.4 broadcast_select_fusion.1
  35.0 1.0 %maximum_convert_fusion.rhalo_ref = f32[32,2,1024]{2,1,0:T(2,128)} fusion(bf16[32,1,1024]{2,1,0:T(2,128)(2,1)S(1)} %get-tuple-element.11, bf16[32,1,1024]{2,1,0:T(2,128)(2,1)S(1)} %get-tuple-element.10), kind=kLoop, calls=%fused_computation.9 | loop fusion | flops 262144 | bytes 393216 | tf_op jit(solution)/shard_map/convert_element_type | solution.py:181
  36.0 6.0 %all-to-all-done.1.ans_ref = f32[8,4,16,128]{3,2,1,0:T(8,128)S(1)} async-done(((f32[8,4,16,128]{3,2,1,0:T(8,128)}), f32[8,4,16,128]{3,2,1,0:T(8,128)S(1)}, u32[]{:S(2)}, u32[]{:S(2)}) %all-to-all-start.1) | async-done | bytes 262176 | tf_op jit(solution)/shard_map/all_to_all | solution.py:202
  41.9 0.0 copy-start.1
  41.9 0.7 %copy-done.1 = f32[8,4,16,128]{3,2,1,0:T(8,128)} copy-done((f32[8,4,16,128]{3,2,1,0:T(8,128)}, f32[8,4,16,128]{3,2,1,0:T(8,128)S(1)}, u32[]{:S(2)}) %copy-start.1) | copy-done | bytes 262168
  42.6 11.3 %shard_map.60 = (f32[32,16,1024]{2,1,0:T(8,128)}, f32[3,32,16,1024]{3,2,1,0:T(8,128)}) custom-call(bf16[32,16,1024]{2,1,0:T(8,128)(2,1)} %d_ref.3, bf16[3,32,16,1024]{3,2,1,0:T(8,128)(2,1)} %c_ref.3, f32[8,4,16,128]{3,2,1,0:T(8,128)} %copy-done.1, f32[2,16,1024]{2,1,0:T(8,128)} %maximum_convert_fusion.1.zhalo_ref, f32[32,2,1024]{2,1,0:T(2,128)} %maximum_convert_fusion.rhalo_ref), custom_call_target="tpu_custom_call" | custom-call | tf_op jit(solution)/shard_map/pallas_call | solution.py:129
  (7 shorter events, 0.1 us)
Async XLA Ops:
  0.6 13.5 %copy-start = (bf16[32,16,1024]{2,1,0:T(8,128)(2,1)S(1)}, bf16[32,16,1024]{2,1,0:T(8,128)(2,1)}, u32[]{:S(2)}) copy-start(bf16[32,16,1024]{2,1,0:T(8,128)(2,1)} %d_ref.3) | copy-start | bytes 3145732
  0.6 24.9 %copy-start.2 = (s32[8]{0:T(128)S(1)}, s32[8]{0:T(128)}, u32[]{:S(2)}) copy-start(s32[8]{0:T(128)} %param.7) | copy-start | bytes 100
  7.7 17.8 %all-to-all-start = ((f32[8,4,16,128]{3,2,1,0:T(8,128)}), f32[8,4,16,128]{3,2,1,0:T(8,128)S(1)}, u32[]{:S(2)}, u32[]{:S(2)}) async-start(f32[8,4,16,128]{3,2,1,0:T(8,128)} %shard_map.59), calls=%async_computation | async-start | bytes 524288 | tf_op jit(solution)/shard_map/all_to_all | solution.py:194
  14.2 11.4 %collective-permute-start = (bf16[1,16,1024]{2,1,0:T(8,128)(2,1)S(1)}, bf16[1,16,1024]{2,1,0:T(8,128)(2,1)S(1)}, u32[]{:S(2)}, u32[]{:S(2)}) collective-permute-start(bf16[1,16,1024]{2,1,0:T(8,128)(2,1)S(1)} %get-tuple-element.16), channel_id=1, source_target_pairs={{0,4},{4,8},{8,12},{12,16},{16,20},{20,24},{24,28},{1,5},{5,9},{9,... | collective-permute-start | bytes 98312 | tf_op jit(solution)/shard_map/ppermute | solution.py:172
  17.5 8.1 %collective-permute-start.1 = (bf16[1,16,1024]{2,1,0:T(8,128)(2,1)S(1)}, bf16[1,16,1024]{2,1,0:T(8,128)(2,1)S(1)}, u32[]{:S(2)}, u32[]{:S(2)}) collective-permute-start(bf16[1,16,1024]{2,1,0:T(8,128)(2,1)S(1)} %get-tuple-element.17), channel_id=1, source_target_pairs={{4,0},{8,4},{12,8},{16,12},{20,16},{24,20},{28,24},{5,1},{9,5},{13... | collective-permute-start | bytes 98312 | tf_op jit(solution)/shard_map/ppermute | solution.py:173
  19.0 15.6 %collective-permute-start.2 = (bf16[32,1,1024]{2,1,0:T(2,128)(2,1)S(1)}, bf16[32,1,1024]{2,1,0:T(2,128)(2,1)S(1)}, u32[]{:S(2)}, u32[]{:S(2)}) collective-permute-start(bf16[32,1,1024]{2,1,0:T(2,128)(2,1)S(1)} %get-tuple-element.12), channel_id=1, source_target_pairs={{0,1},{1,2},{2,3},{4,5},{5,6},{6,7},{8,9},{9,10},{10,11},{12,13},{... | collective-permute-start | bytes 196616 | tf_op jit(solution)/shard_map/ppermute | solution.py:174
  23.6 11.0 %collective-permute-start.3 = (bf16[32,1,1024]{2,1,0:T(2,128)(2,1)S(1)}, bf16[32,1,1024]{2,1,0:T(2,128)(2,1)S(1)}, u32[]{:S(2)}, u32[]{:S(2)}) collective-permute-start(bf16[32,1,1024]{2,1,0:T(2,128)(2,1)S(1)} %get-tuple-element.13), channel_id=1, source_target_pairs={{1,0},{2,1},{3,2},{5,4},{6,5},{7,6},{9,8},{10,9},{11,10},{13,12},{... | collective-permute-start | bytes 196616 | tf_op jit(solution)/shard_map/ppermute | solution.py:175
  27.6 14.3 %all-to-all-start.1 = ((f32[8,4,16,128]{3,2,1,0:T(8,128)}), f32[8,4,16,128]{3,2,1,0:T(8,128)S(1)}, u32[]{:S(2)}, u32[]{:S(2)}) async-start(f32[8,4,16,128]{3,2,1,0:T(8,128)} %pad_maximum_fusion), calls=%async_computation.1 | async-start | bytes 524288 | tf_op jit(solution)/shard_map/all_to_all | solution.py:202
  41.9 0.7 %copy-start.1 = (f32[8,4,16,128]{3,2,1,0:T(8,128)}, f32[8,4,16,128]{3,2,1,0:T(8,128)S(1)}, u32[]{:S(2)}) copy-start(f32[8,4,16,128]{3,2,1,0:T(8,128)S(1)} %all-to-all-done.1.ans_ref) | copy-start | bytes 786436

commit v7 on v6

--- a/solution.py
+++ b/solution.py
@@ -10,6 +10,8 @@
 optical_depth = 2.5
 smooth_weight = 0.05
 lanes = 128
+forward_subs = 4
+backward_subs = 2
 
 
 log2e = 1.4426950408889634
@@ -27,114 +29,127 @@
 
 
 def forward_kernel(d_ref, c_ref, out_ref, *, step):
-    slices = d_ref.shape[0]
-    shape = d_ref.shape[1:]
-    per_tile, _, chunk_rows, _ = out_ref.shape
+    slices, rows, block = d_ref.shape
+    shape = (rows, lanes)
+    subs = block // lanes
+    per_tile = out_ref.shape[0] // subs
+    chunk_rows = out_ref.shape[2]
     scale = -step * log2e
 
-    def body(z, carry):
-        n, front, e0, e1, e2 = carry
-        dtn = softplus(d_ref[z].astype(jnp.float32)) * scale
-        kept = jnp.exp2(dtn)
-        lit = front * (1.0 - kept)
-        n = n + dtn
-        e0 = e0 + lit * jax.nn.sigmoid(c_ref[0, z].astype(jnp.float32))
-        e1 = e1 + lit * jax.nn.sigmoid(c_ref[1, z].astype(jnp.float32))
-        e2 = e2 + lit * jax.nn.sigmoid(c_ref[2, z].astype(jnp.float32))
-        return (n, front * kept, e0, e1, e2)
-
-    zero = jnp.zeros(shape, jnp.float32)
-    one = jnp.ones(shape, jnp.float32)
-    n, _, e0, e1, e2 = lax.fori_loop(0, slices, body, (zero, one, zero, zero, zero), unroll=4)
-    values = (e0, e1, e2, jnp.exp2(n))
-    for g in range(per_tile):
-        for c in range(4):
-            out_ref[g, c] = values[c][g * chunk_rows:(g + 1) * chunk_rows]
+    for j in range(subs):
+        cols = pl.ds(j * lanes, lanes)
+
+        def body(z, carry):
+            n, front, e0, e1, e2 = carry
+            dtn = softplus(d_ref[z, :, cols].astype(jnp.float32)) * scale
+            kept = jnp.exp2(dtn)
+            lit = front * (1.0 - kept)
+            n = n + dtn
+            e0 = e0 + lit * jax.nn.sigmoid(c_ref[0, z, :, cols].astype(jnp.float32))
+            e1 = e1 + lit * jax.nn.sigmoid(c_ref[1, z, :, cols].astype(jnp.float32))
+            e2 = e2 + lit * jax.nn.sigmoid(c_ref[2, z, :, cols].astype(jnp.float32))
+            return (n, front * kept, e0, e1, e2)
+
+        zero = jnp.zeros(shape, jnp.float32)
+        one = jnp.ones(shape, jnp.float32)
+        n, _, e0, e1, e2 = lax.fori_loop(0, slices, body, (zero, one, zero, zero, zero), unroll=4)
+        values = (e0, e1, e2, jnp.exp2(n))
+        for g in range(per_tile):
+            for c in range(4):
+                out_ref[j * per_tile + g, c] = values[c][g * chunk_rows:(g + 1) * chunk_rows]
 
 
 def backward_kernel(d_ref, c_ref, ans_ref, zhalo_ref, rhalo_ref, gd_ref, gc_ref, *, step, slices_total):
-    slices = d_ref.shape[0]
-    shape = d_ref.shape[1:]
-    per_tile = ans_ref.shape[0] // pl.num_programs(0)
+    slices, rows, block = d_ref.shape
+    shape = (rows, lanes)
+    subs = block // lanes
+    per_tile = ans_ref.shape[0] // (pl.num_programs(0) * subs)
     scale = -step * log2e
     gain = optical_depth / slices_total
-
-    base = pl.program_id(0) * per_tile
-
-    def pixel(ref, c):
-        if per_tile == 1:
-            return ref[base, c]
-        return jnp.concatenate([ref[base + g, c] for g in range(per_tile)], axis=0)
-
     row = lax.broadcasted_iota(jnp.int32, shape, 0)
     first_row = row == 0
     last_row = row == shape[0] - 1
 
-    def body(z, carry):
-        n, front, w0, w1, w2, d_prev, d = carry
-        d_next = jnp.where(
-            z + 1 < slices,
-            d_ref[jnp.minimum(z + 1, slices - 1)].astype(jnp.float32),
-            zhalo_ref[1],
+    for j in range(subs):
+        cols = pl.ds(j * lanes, lanes)
+        base = (pl.program_id(0) * subs + j) * per_tile
+
+        def pixel(c):
+            if per_tile == 1:
+                return ans_ref[base, c]
+            return jnp.concatenate([ans_ref[base + g, c] for g in range(per_tile)], axis=0)
+
+        def body(z, carry):
+            n, front, w0, w1, w2, d_prev, d = carry
+            d_next = jnp.where(
+                z + 1 < slices,
+                d_ref[jnp.minimum(z + 1, slices - 1), :, cols].astype(jnp.float32),
+                zhalo_ref[1, :, cols],
+            )
+            rims = rhalo_ref[z, :, cols]
+            upper = jnp.where(first_row, rims[0:1], pltpu.roll(d, 1, 0))
+            lower = jnp.where(last_row, rims[1:2], pltpu.roll(d, shape[0] - 1, 0))
+            smooth = 2.0 * smooth_weight * ((d - d_prev) + (d - d_next) + (d - upper) + (d - lower))
+            dtn = softplus(d) * scale
+            lit = front * (1.0 - jnp.exp2(dtn))
+            n_next = n + dtn
+            through = jnp.exp2(n_next)
+            inv = jnp.exp2(-n_next)
+            col = [jax.nn.sigmoid(c_ref[c, z, :, cols].astype(jnp.float32)) for c in range(3)]
+            lit_col = [lit * col[c] for c in range(3)]
+            w = [w0 + lit_col[0], w1 + lit_col[1], w2 + lit_col[2]]
+            res = [pixel(c) for c in range(3)]
+            emitted = res[0] * col[0] + res[1] * col[1] + res[2] * col[2]
+            left = res[0] * w[0] + res[1] * w[1] + res[2] * w[2]
+            inner = emitted - inv * (pixel(3) - left)
+            for c in range(3):
+                gc_ref[c, z, :, cols] = res[c] * lit_col[c] * (1.0 - col[c])
+            gd_ref[z, :, cols] = gain * through * jax.nn.sigmoid(d) * inner + smooth
+            return (n_next, through, w[0], w[1], w[2], d, d_next)
+
+        zero = jnp.zeros(shape, jnp.float32)
+        one = jnp.ones(shape, jnp.float32)
+        start = (
+            zero, one, zero, zero, zero,
+            zhalo_ref[0, :, cols],
+            d_ref[0, :, cols].astype(jnp.float32),
         )
-        rims = rhalo_ref[z]
-        upper = jnp.where(first_row, rims[0:1], pltpu.roll(d, 1, 0))
-        lower = jnp.where(last_row, rims[1:2], pltpu.roll(d, shape[0] - 1, 0))
-        smooth = 2.0 * smooth_weight * ((d - d_prev) + (d - d_next) + (d - upper) + (d - lower))
-        dtn = softplus(d) * scale
-        lit = front * (1.0 - jnp.exp2(dtn))
-        n_next = n + dtn
-        through = jnp.exp2(n_next)
-        inv = jnp.exp2(-n_next)
-        col = [jax.nn.sigmoid(c_ref[c, z].astype(jnp.float32)) for c in range(3)]
-        lit_col = [lit * col[c] for c in range(3)]
-        w = [w0 + lit_col[0], w1 + lit_col[1], w2 + lit_col[2]]
-        res = [pixel(ans_ref, c) for c in range(3)]
-        emitted = res[0] * col[0] + res[1] * col[1] + res[2] * col[2]
-        left = res[0] * w[0] + res[1] * w[1] + res[2] * w[2]
-        inner = emitted - inv * (pixel(ans_ref, 3) - left)
-        for c in range(3):
-            gc_ref[c, z] = res[c] * lit_col[c] * (1.0 - col[c])
-        gd_ref[z] = gain * through * jax.nn.sigmoid(d) * inner + smooth
-        return (n_next, through, w[0], w[1], w[2], d, d_next)
-
-    zero = jnp.zeros(shape, jnp.float32)
-    one = jnp.ones(shape, jnp.float32)
-    start = (zero, one, zero, zero, zero, zhalo_ref[0], d_ref[0].astype(jnp.float32))
-    lax.fori_loop(0, slices, body, start, unroll=2)
+        lax.fori_loop(0, slices, body, start, unroll=2)
 
 
 def forward_partial(density, colour_raw, step, depth_count):
     slices, rows, width = density.shape
     tiles, per_tile, chunk_rows = chunking(rows, width, depth_count)
+    block = lanes * forward_subs if tiles % forward_subs == 0 else lanes
     return pl.pallas_call(
         functools.partial(forward_kernel, step=step),
-        grid=(tiles,),
+        grid=(width // block,),
         in_specs=[
-            pl.BlockSpec((slices, rows, lanes), lambda i: (0, 0, i)),
-            pl.BlockSpec((3, slices, rows, lanes), lambda i: (0, 0, 0, i)),
+            pl.BlockSpec((slices, rows, block), lambda i: (0, 0, i)),
+            pl.BlockSpec((3, slices, rows, block), lambda i: (0, 0, 0, i)),
         ],
-        out_specs=pl.BlockSpec((per_tile, 4, chunk_rows, lanes), lambda i: (i, 0, 0, 0)),
+        out_specs=pl.BlockSpec(
+            (per_tile * (block // lanes), 4, chunk_rows, lanes), lambda i: (i, 0, 0, 0)
+        ),
         out_shape=jax.ShapeDtypeStruct((tiles * per_tile, 4, chunk_rows, lanes), jnp.float32),
     )(density, colour_raw)
 
 
 def backward_grads(density, colour_raw, answers, zhalo, rhalo, step, slices_total):
     slices, rows, width = density.shape
-    per_tile, _, chunk_rows, _ = answers.shape
-    per_tile = per_tile // (width // lanes)
-    slab = pl.BlockSpec((slices, rows, lanes), lambda i: (0, 0, i))
-    colours = pl.BlockSpec((3, slices, rows, lanes), lambda i: (0, 0, 0, i))
-    pixel = pl.BlockSpec((per_tile, 4, chunk_rows, lanes), lambda i: (i, 0, 0, 0))
+    tiles = width // lanes
+    block = lanes * backward_subs if tiles % backward_subs == 0 else lanes
+    slab = pl.BlockSpec((slices, rows, block), lambda i: (0, 0, i))
+    colours = pl.BlockSpec((3, slices, rows, block), lambda i: (0, 0, 0, i))
     return pl.pallas_call(
         functools.partial(backward_kernel, step=step, slices_total=float(slices_total)),
-        grid=(width // lanes,),
+        grid=(width // block,),
         in_specs=[
             slab,
             colours,
             pl.BlockSpec(memory_space=pltpu.VMEM),
-            pl.BlockSpec((2, rows, lanes), lambda i: (0, 0, i)),
-            pl.BlockSpec((slices, 2, lanes), lambda i: (0, 0, i)),
+            pl.BlockSpec((2, rows, block), lambda i: (0, 0, i)),
+            pl.BlockSpec((slices, 2, block), lambda i: (0, 0, i)),
         ],
         out_specs=[slab, colours],
         out_shape=[

time: 54.7 us -> 51.5 us (0.941)
  Pallas kernels: 18.4 us -> 15.4 us
    pallas_call x1, Pallas kernels: 7.1 us -> 5.19 us  [forward_partial(): pl.pallas_call(functools.partial(forward_kernel, step=step), grid=(width...]
    pallas_call x1, Pallas kernels: 11.3 us -> 10.2 us  [backward_grads(): pl.pallas_call(functools.partial(backward_kernel, step=step, slices_total...]
where the time goes in v7:
time: 51.5 us; the launch traced here: 51 us
  starting transfers between devices  23.8 us (46%)
  Pallas kernels  15.4 us (30%)
  waiting for transfers between devices  5.96 us (12%)
  other arithmetic  4.03 us (8%)
  local copies, waits for them, and re-layouts  0.95 us (2%)
  between operations  0.78 us (2%)
    pallas_call x1, Pallas kernels, backward_grads(): pl.pallas_call(functools.partial(backward_kernel, step=step, slices_total...  10.2 us
    all_to_all x1, starting transfers between devices, local(): received = lax.all_to_all(partial_value, 'depth', 0, 0, tiled=True)  6.38 us
    all_to_all x1, starting transfers between devices, local(): returned = lax.all_to_all(answers, 'depth', 0, 0, tiled=True)  6.34 us
    all_to_all x1, waiting for transfers between devices, local(): returned = lax.all_to_all(answers, 'depth', 0, 0, tiled=True)  5.95 us
    pallas_call x1, Pallas kernels, forward_partial(): pl.pallas_call(functools.partial(forward_kernel, step=step), grid=(width...  5.19 us
    ppermute x1, starting transfers between devices, halos(): prev_row = lax.ppermute(last_row, 'rows', up_r)  4.52 us
    ppermute x1, starting transfers between devices, halos(): prev_slice = lax.ppermute(last_slice, 'depth', up_d)  3.36 us
    ppermute x1, starting transfers between devices, halos(): next_row = lax.ppermute(first_row, 'rows', [(j, i) for i, j in up_r])  1.92 us
  transfers between devices with their start and end apart: 6, of which 1 were waited for; matrix products, arithmetic and copies ran while one was open for 8% of the time, Pallas kernels for 0%

profile of v7, /device:TPU:1, one launch (start us, length us, event | category | flops | bytes accessed | tf_op | source)
XLA Modules:
  0.0 51.0 jit_solution(3891561132711156547)
XLA Ops:
  0.6 0.0 copy-start
  0.6 0.0 copy-start.2
  0.7 5.2 %shard_map.59 = f32[8,4,16,128]{3,2,1,0:T(8,128)} custom-call(bf16[32,16,1024]{2,1,0:T(8,128)(2,1)} %d_ref.3, bf16[3,32,16,1024]{3,2,1,0:T(8,128)(2,1)} %c_ref.3), custom_call_target="tpu_custom_call" | custom-call | tf_op jit(solution)/shard_map/pallas_call | solution.py:124
  5.8 6.4 %all-to-all-start = ((f32[8,4,16,128]{3,2,1,0:T(8,128)}), f32[8,4,16,128]{3,2,1,0:T(8,128)S(1)}, u32[]{:S(2)}, u32[]{:S(2)}) async-start(f32[8,4,16,128]{3,2,1,0:T(8,128)} %shard_map.59), calls=%async_computation | async-start | bytes 524288 | tf_op jit(solution)/shard_map/all_to_all | solution.py:209
  12.2 0.0 copy-done
  12.2 3.4 %collective-permute-start = (bf16[1,16,1024]{2,1,0:T(8,128)(2,1)S(1)}, bf16[1,16,1024]{2,1,0:T(8,128)(2,1)S(1)}, u32[]{:S(2)}, u32[]{:S(2)}) collective-permute-start(bf16[1,16,1024]{2,1,0:T(8,128)(2,1)S(1)} %get-tuple-element.16), channel_id=1, source_target_pairs={{0,4},{4,8},{8,12},{12,16},{16,20},{20,24},{24,28},{1,5},{5,9},{9,... | collective-permute-start | bytes 98312 | tf_op jit(solution)/shard_map/ppermute | solution.py:187
  15.6 1.3 %collective-permute-start.1 = (bf16[1,16,1024]{2,1,0:T(8,128)(2,1)S(1)}, bf16[1,16,1024]{2,1,0:T(8,128)(2,1)S(1)}, u32[]{:S(2)}, u32[]{:S(2)}) collective-permute-start(bf16[1,16,1024]{2,1,0:T(8,128)(2,1)S(1)} %get-tuple-element.17), channel_id=1, source_target_pairs={{4,0},{8,4},{12,8},{16,12},{20,16},{24,20},{28,24},{5,1},{9,5},{13... | collective-permute-start | bytes 98312 | tf_op jit(solution)/shard_map/ppermute | solution.py:188
  16.9 0.2 fusion.5
  17.1 4.5 %collective-permute-start.2 = (bf16[32,1,1024]{2,1,0:T(2,128)(2,1)S(1)}, bf16[32,1,1024]{2,1,0:T(2,128)(2,1)S(1)}, u32[]{:S(2)}, u32[]{:S(2)}) collective-permute-start(bf16[32,1,1024]{2,1,0:T(2,128)(2,1)S(1)} %get-tuple-element.12), channel_id=1, source_target_pairs={{0,1},{1,2},{2,3},{4,5},{5,6},{6,7},{8,9},{9,10},{10,11},{12,13},{... | collective-permute-start | bytes 196616 | tf_op jit(solution)/shard_map/ppermute | solution.py:189
  21.7 1.9 %collective-permute-start.3 = (bf16[32,1,1024]{2,1,0:T(2,128)(2,1)S(1)}, bf16[32,1,1024]{2,1,0:T(2,128)(2,1)S(1)}, u32[]{:S(2)}, u32[]{:S(2)}) collective-permute-start(bf16[32,1,1024]{2,1,0:T(2,128)(2,1)S(1)} %get-tuple-element.13), channel_id=1, source_target_pairs={{1,0},{2,1},{3,2},{5,4},{6,5},{7,6},{9,8},{10,9},{11,10},{13,12},{... | collective-permute-start | bytes 196616 | tf_op jit(solution)/shard_map/ppermute | solution.py:190
  23.6 0.0 copy-done.2
  23.6 0.1 compare_convert_fusion
  23.7 0.0 collective-permute-done
  23.7 0.0 collective-permute-done.1
  23.7 0.0 all-to-all-done
  23.7 0.1 multiply_reduce_fusion.1
  23.9 0.2 multiply_reduce_fusion
  24.1 0.8 %dynamic-slice_subtract_fusion = f32[3,16,128]{2,1,0:T(8,128)S(1)} fusion(f32[3,16,128]{2,1,0:T(8,128)S(1)} %get-tuple-element.8, f32[3,16,1024]{2,1,0:T(8,128)} %param.6, s32[]{:T(128)S(6)} %select_n.39), kind=kLoop, calls=%fused_computation.20 | loop fusion | flops 6144 | bytes 73732 | tf_op jit(solution)/shard_map/sub | solution.py:169
  24.9 0.1 multiply_reduce_fusion.3
  25.0 0.7 %pad_maximum_fusion = f32[8,4,16,128]{3,2,1,0:T(8,128)} fusion(f32[8,1,16,128]{3,2,1,0:T(8,128)S(1)} %fusion.2, f32[8,3,16,128]{3,2,1,0:T(8,128)S(1)} %get-tuple-element.18), kind=kLoop, calls=%fused_computation.2 | loop fusion | flops 65536 | bytes 524288 | tf_op jit(solution)/shard_map/concatenate | solution.py:173
  25.7 6.3 %all-to-all-start.1 = ((f32[8,4,16,128]{3,2,1,0:T(8,128)}), f32[8,4,16,128]{3,2,1,0:T(8,128)S(1)}, u32[]{:S(2)}, u32[]{:S(2)}) async-start(f32[8,4,16,128]{3,2,1,0:T(8,128)} %pad_maximum_fusion), calls=%async_computation.1 | async-start | bytes 524288 | tf_op jit(solution)/shard_map/all_to_all | solution.py:217
  32.0 0.7 %maximum_convert_fusion.1.zhalo_ref = f32[2,16,1024]{2,1,0:T(8,128)} fusion(bf16[1,16,1024]{2,1,0:T(8,128)(2,1)S(1)} %get-tuple-element.15, bf16[1,16,1024]{2,1,0:T(8,128)(2,1)S(1)} %get-tuple-element.14), kind=kLoop, calls=%fused_computation.10 | loop fusion | flops 65536 | bytes 196608 | tf_op jit(solution)/shard_map/convert_element_type | solution.py:195
  32.7 0.0 collective-permute-done.2
  32.7 0.0 collective-permute-done.3
  32.7 0.4 broadcast_select_fusion.1
  33.1 1.0 %maximum_convert_fusion.rhalo_ref = f32[32,2,1024]{2,1,0:T(2,128)} fusion(bf16[32,1,1024]{2,1,0:T(2,128)(2,1)S(1)} %get-tuple-element.11, bf16[32,1,1024]{2,1,0:T(2,128)(2,1)S(1)} %get-tuple-element.10), kind=kLoop, calls=%fused_computation.9 | loop fusion | flops 262144 | bytes 393216 | tf_op jit(solution)/shard_map/convert_element_type | solution.py:196
  34.1 6.0 %all-to-all-done.1.ans_ref = f32[8,4,16,128]{3,2,1,0:T(8,128)S(1)} async-done(((f32[8,4,16,128]{3,2,1,0:T(8,128)}), f32[8,4,16,128]{3,2,1,0:T(8,128)S(1)}, u32[]{:S(2)}, u32[]{:S(2)}) %all-to-all-start.1) | async-done | bytes 262176 | tf_op jit(solution)/shard_map/all_to_all | solution.py:217
  40.0 0.0 copy-start.1
  40.0 0.7 %copy-done.1 = f32[8,4,16,128]{3,2,1,0:T(8,128)} copy-done((f32[8,4,16,128]{3,2,1,0:T(8,128)}, f32[8,4,16,128]{3,2,1,0:T(8,128)S(1)}, u32[]{:S(2)}) %copy-start.1) | copy-done | bytes 262168
  40.7 10.2 %shard_map.60 = (f32[32,16,1024]{2,1,0:T(8,128)}, f32[3,32,16,1024]{3,2,1,0:T(8,128)}) custom-call(bf16[32,16,1024]{2,1,0:T(8,128)(2,1)} %d_ref.3, bf16[3,32,16,1024]{3,2,1,0:T(8,128)(2,1)} %c_ref.3, f32[8,4,16,128]{3,2,1,0:T(8,128)} %copy-done.1, f32[2,16,1024]{2,1,0:T(8,128)} %maximum_convert_fusion.1.zhalo_ref, f32[32,2,1024]{2,1,0:T(2,128)} %maximum_convert_fusion.rhalo_ref), custom_call_target="tpu_custom_call" | custom-call | tf_op jit(solution)/shard_map/pallas_call | solution.py:144
  (7 shorter events, 0.1 us)
Async XLA Ops:
  0.6 11.6 %copy-start = (bf16[32,16,1024]{2,1,0:T(8,128)(2,1)S(1)}, bf16[32,16,1024]{2,1,0:T(8,128)(2,1)}, u32[]{:S(2)}) copy-start(bf16[32,16,1024]{2,1,0:T(8,128)(2,1)} %d_ref.3) | copy-start | bytes 3145732
  0.6 22.9 %copy-start.2 = (s32[8]{0:T(128)S(1)}, s32[8]{0:T(128)}, u32[]{:S(2)}) copy-start(s32[8]{0:T(128)} %param.7) | copy-start | bytes 100
  5.8 17.8 %all-to-all-start = ((f32[8,4,16,128]{3,2,1,0:T(8,128)}), f32[8,4,16,128]{3,2,1,0:T(8,128)S(1)}, u32[]{:S(2)}, u32[]{:S(2)}) async-start(f32[8,4,16,128]{3,2,1,0:T(8,128)} %shard_map.59), calls=%async_computation | async-start | bytes 524288 | tf_op jit(solution)/shard_map/all_to_all | solution.py:209
  12.2 11.4 %collective-permute-start = (bf16[1,16,1024]{2,1,0:T(8,128)(2,1)S(1)}, bf16[1,16,1024]{2,1,0:T(8,128)(2,1)S(1)}, u32[]{:S(2)}, u32[]{:S(2)}) collective-permute-start(bf16[1,16,1024]{2,1,0:T(8,128)(2,1)S(1)} %get-tuple-element.16), channel_id=1, source_target_pairs={{0,4},{4,8},{8,12},{12,16},{16,20},{20,24},{24,28},{1,5},{5,9},{9,... | collective-permute-start | bytes 98312 | tf_op jit(solution)/shard_map/ppermute | solution.py:187
  15.6 8.1 %collective-permute-start.1 = (bf16[1,16,1024]{2,1,0:T(8,128)(2,1)S(1)}, bf16[1,16,1024]{2,1,0:T(8,128)(2,1)S(1)}, u32[]{:S(2)}, u32[]{:S(2)}) collective-permute-start(bf16[1,16,1024]{2,1,0:T(8,128)(2,1)S(1)} %get-tuple-element.17), channel_id=1, source_target_pairs={{4,0},{8,4},{12,8},{16,12},{20,16},{24,20},{28,24},{5,1},{9,5},{13... | collective-permute-start | bytes 98312 | tf_op jit(solution)/shard_map/ppermute | solution.py:188
  17.1 15.6 %collective-permute-start.2 = (bf16[32,1,1024]{2,1,0:T(2,128)(2,1)S(1)}, bf16[32,1,1024]{2,1,0:T(2,128)(2,1)S(1)}, u32[]{:S(2)}, u32[]{:S(2)}) collective-permute-start(bf16[32,1,1024]{2,1,0:T(2,128)(2,1)S(1)} %get-tuple-element.12), channel_id=1, source_target_pairs={{0,1},{1,2},{2,3},{4,5},{5,6},{6,7},{8,9},{9,10},{10,11},{12,13},{... | collective-permute-start | bytes 196616 | tf_op jit(solution)/shard_map/ppermute | solution.py:189
  21.7 11.0 %collective-permute-start.3 = (bf16[32,1,1024]{2,1,0:T(2,128)(2,1)S(1)}, bf16[32,1,1024]{2,1,0:T(2,128)(2,1)S(1)}, u32[]{:S(2)}, u32[]{:S(2)}) collective-permute-start(bf16[32,1,1024]{2,1,0:T(2,128)(2,1)S(1)} %get-tuple-element.13), channel_id=1, source_target_pairs={{1,0},{2,1},{3,2},{5,4},{6,5},{7,6},{9,8},{10,9},{11,10},{13,12},{... | collective-permute-start | bytes 196616 | tf_op jit(solution)/shard_map/ppermute | solution.py:190
  25.7 14.3 %all-to-all-start.1 = ((f32[8,4,16,128]{3,2,1,0:T(8,128)}), f32[8,4,16,128]{3,2,1,0:T(8,128)S(1)}, u32[]{:S(2)}, u32[]{:S(2)}) async-start(f32[8,4,16,128]{3,2,1,0:T(8,128)} %pad_maximum_fusion), calls=%async_computation.1 | async-start | bytes 524288 | tf_op jit(solution)/shard_map/all_to_all | solution.py:217
  40.0 0.7 %copy-start.1 = (f32[8,4,16,128]{3,2,1,0:T(8,128)}, f32[8,4,16,128]{3,2,1,0:T(8,128)S(1)}, u32[]{:S(2)}) copy-start(f32[8,4,16,128]{3,2,1,0:T(8,128)S(1)} %all-to-all-done.1.ans_ref) | copy-start | bytes 786436

commit v8 on v7

--- a/solution.py
+++ b/solution.py
@@ -197,6 +197,19 @@
     return zhalo, rhalo
 
 
+def exchange(x, axis):
+    count = lax.axis_size(axis)
+    if count % 2 or count == 2:
+        return lax.all_to_all(x, axis, 0, 0, tiled=True)
+    outer = count // 2
+    pairs = [[2 * k, 2 * k + 1] for k in range(outer)]
+    strides = [[b + 2 * k for k in range(outer)] for b in range(2)]
+    x = x.reshape((outer, 2) + x.shape[1:])
+    x = lax.all_to_all(x, axis, 1, 1, axis_index_groups=pairs, tiled=True)
+    x = lax.all_to_all(x, axis, 0, 0, axis_index_groups=strides, tiled=True)
+    return x.reshape((count,) + x.shape[2:])
+
+
 def local(density_raw, colour_raw, target, slab_rank):
     slices_dev, rows_dev, width = density_raw.shape
     depth_count = lax.axis_size("depth")
@@ -206,7 +219,7 @@
     partial_value = forward_partial(density_raw, colour_raw, step, depth_count)
     partial_value, after_forward = lax.optimization_barrier((partial_value, density_raw))
     zhalo, rhalo = halos(after_forward)
-    received = lax.all_to_all(partial_value, "depth", 0, 0, tiled=True)
+    received = exchange(partial_value, "depth")
     position = lax.axis_index("depth")
     target_piece = lax.dynamic_slice(
         target,
@@ -214,7 +227,7 @@
         (3, chunk_rows, lanes),
     )
     answers = composite(received, slab_rank, target_piece, float(slices_total))
-    returned = lax.all_to_all(answers, "depth", 0, 0, tiled=True)
+    returned = exchange(answers, "depth")
     return backward_grads(
         density_raw, colour_raw, returned, zhalo, rhalo, step, slices_total
     )

time: 51.5 us -> 66.5 us (1.29)
  the two profiles are of different devices: /device:TPU:1 before, /device:TPU:0 now
where the time goes in v8:
time: 66.5 us; the launch traced here: 65.9 us
  starting transfers between devices  25.5 us (38%)
  waiting for transfers between devices  16 us (24%)
  Pallas kernels  15.4 us (23%)
  local copies, waits for them, and re-layouts  4.09 us (6%)
  other arithmetic  4.06 us (6%)
  between operations  0.8 us (1%)
    all_to_all x2, waiting for transfers between devices, exchange(): x = lax.all_to_all(x, axis, 0, 0, axis_index_groups=strides, tiled=True)  10.4 us
    pallas_call x1, Pallas kernels, backward_grads(): pl.pallas_call(functools.partial(backward_kernel, step=step, slices_total...  10.2 us
    all_to_all x2, starting transfers between devices, exchange(): x = lax.all_to_all(x, axis, 0, 0, axis_index_groups=strides, tiled=True)  9.86 us
    all_to_all x2, starting transfers between devices, exchange(): x = lax.all_to_all(x, axis, 1, 1, axis_index_groups=pairs, tiled=True)  7.68 us
    all_to_all x2, waiting for transfers between devices, exchange(): x = lax.all_to_all(x, axis, 1, 1, axis_index_groups=pairs, tiled=True)  5.57 us
    pallas_call x1, Pallas kernels, forward_partial(): pl.pallas_call(functools.partial(forward_kernel, step=step), grid=(width...  5.19 us
    ppermute x1, starting transfers between devices, halos(): prev_slice = lax.ppermute(last_slice, 'depth', up_d)  4.1 us
    reshape x1, local copies, waits for them, and re-layouts, exchange(): x = x.reshape((outer, 2) + x.shape[1:])  1.68 us
  transfers between devices with their start and end apart: 8, of which 4 were waited for; matrix products, arithmetic and copies ran while one was open for 9% of the time, Pallas kernels for 0%

profile of v8, /device:TPU:0, one launch (start us, length us, event | category | flops | bytes accessed | tf_op | source)
XLA Modules:
  0.0 65.9 jit_solution(4585019373797627003)
XLA Ops:
  0.6 0.0 copy-start
  0.6 5.2 %shard_map.59 = f32[8,4,16,128]{3,2,1,0:T(8,128)} custom-call(bf16[32,16,1024]{2,1,0:T(8,128)(2,1)} %d_ref.3, bf16[3,32,16,1024]{3,2,1,0:T(8,128)(2,1)} %c_ref.3), custom_call_target="tpu_custom_call" | custom-call | tf_op jit(solution)/shard_map/pallas_call | solution.py:124
  5.8 0.0 copy-start.2
  5.8 1.7 %copy.20 = f32[4,2,4,16,128]{4,3,2,0,1:T(8,128)} copy(f32[4,2,4,16,128]{4,3,2,1,0:T(8,128)} %bitcast.38) | data formatting | bytes 524288 | tf_op jit(solution)/shard_map/reshape | solution.py:207
  7.5 4.2 %all-to-all-start = ((f32[4,2,4,16,128]{4,3,2,0,1:T(8,128)}), f32[4,2,4,16,128]{4,3,2,0,1:T(8,128)S(1)}, u32[]{:S(2)}, u32[]{:S(2)}) async-start(f32[4,2,4,16,128]{4,3,2,0,1:T(8,128)} %copy.20), calls=%async_computation | async-start | bytes 524288 | tf_op jit(solution)/shard_map/all_to_all | solution.py:208
  11.8 0.0 copy-done
  11.8 4.1 %collective-permute-start = (bf16[1,16,1024]{2,1,0:T(8,128)(2,1)S(1)}, bf16[1,16,1024]{2,1,0:T(8,128)(2,1)S(1)}, u32[]{:S(2)}, u32[]{:S(2)}) collective-permute-start(bf16[1,16,1024]{2,1,0:T(8,128)(2,1)S(1)} %get-tuple-element.16), channel_id=1, source_target_pairs={{0,4},{4,8},{8,12},{12,16},{16,20},{20,24},{24,28},{1,5},{5,9},{9,... | collective-permute-start | bytes 98312 | tf_op jit(solution)/shard_map/ppermute | solution.py:187
  15.9 1.3 %collective-permute-start.1 = (bf16[1,16,1024]{2,1,0:T(8,128)(2,1)S(1)}, bf16[1,16,1024]{2,1,0:T(8,128)(2,1)S(1)}, u32[]{:S(2)}, u32[]{:S(2)}) collective-permute-start(bf16[1,16,1024]{2,1,0:T(8,128)(2,1)S(1)} %get-tuple-element.17), channel_id=1, source_target_pairs={{4,0},{8,4},{12,8},{16,12},{20,16},{24,20},{28,24},{5,1},{9,5},{13... | collective-permute-start | bytes 98312 | tf_op jit(solution)/shard_map/ppermute | solution.py:188
  17.2 0.5 all-to-all-done
  17.6 0.7 %copy.21 = f32[4,2,4,16,128]{4,3,2,1,0:T(8,128)} copy(f32[4,2,4,16,128]{4,3,2,0,1:T(8,128)S(1)} %all-to-all-done) | data formatting | bytes 524288 | tf_op jit(solution)/shard_map/all_to_all | solution.py:208
  18.4 6.5 %all-to-all-start.1 = ((f32[4,2,4,16,128]{4,3,2,1,0:T(8,128)}), f32[4,2,4,16,128]{4,3,2,1,0:T(8,128)S(1)}, u32[]{:S(2)}, u32[]{:S(2)}) async-start(f32[4,2,4,16,128]{4,3,2,1,0:T(8,128)} %copy.21), calls=%async_computation.1 | async-start | bytes 524288 | tf_op jit(solution)/shard_map/all_to_all | solution.py:209
  24.8 0.2 fusion.5
  25.0 1.3 %collective-permute-start.2 = (bf16[32,1,1024]{2,1,0:T(2,128)(2,1)S(1)}, bf16[32,1,1024]{2,1,0:T(2,128)(2,1)S(1)}, u32[]{:S(2)}, u32[]{:S(2)}) collective-permute-start(bf16[32,1,1024]{2,1,0:T(2,128)(2,1)S(1)} %get-tuple-element.12), channel_id=1, source_target_pairs={{0,1},{1,2},{2,3},{4,5},{5,6},{6,7},{8,9},{9,10},{10,11},{12,13},{... | collective-permute-start | bytes 196616 | tf_op jit(solution)/shard_map/ppermute | solution.py:189
  26.3 1.3 %collective-permute-start.3 = (bf16[32,1,1024]{2,1,0:T(2,128)(2,1)S(1)}, bf16[32,1,1024]{2,1,0:T(2,128)(2,1)S(1)}, u32[]{:S(2)}, u32[]{:S(2)}) collective-permute-start(bf16[32,1,1024]{2,1,0:T(2,128)(2,1)S(1)} %get-tuple-element.13), channel_id=1, source_target_pairs={{1,0},{2,1},{3,2},{5,4},{6,5},{7,6},{9,8},{10,9},{11,10},{13,12},{... | collective-permute-start | bytes 196616 | tf_op jit(solution)/shard_map/ppermute | solution.py:190
  27.6 0.0 copy-done.2
  27.7 0.1 compare_convert_fusion
  27.7 5.4 %all-to-all-done.1 = f32[4,2,4,16,128]{4,3,2,1,0:T(8,128)S(1)} async-done(((f32[4,2,4,16,128]{4,3,2,1,0:T(8,128)}), f32[4,2,4,16,128]{4,3,2,1,0:T(8,128)S(1)}, u32[]{:S(2)}, u32[]{:S(2)}) %all-to-all-start.1) | async-done | bytes 262176 | tf_op jit(solution)/shard_map/all_to_all | solution.py:209
  33.1 0.1 multiply_reduce_fusion.1
  33.4 0.2 multiply_reduce_fusion
  33.5 0.8 %dynamic-slice_subtract_fusion = f32[3,16,128]{2,1,0:T(8,128)S(1)} fusion(f32[3,16,128]{2,1,0:T(8,128)S(1)} %get-tuple-element.8, f32[3,16,1024]{2,1,0:T(8,128)} %param.6, s32[]{:T(128)S(6)} %select_n.39), kind=kLoop, calls=%fused_computation.21 | loop fusion | flops 6144 | bytes 73732 | tf_op jit(solution)/shard_map/sub | solution.py:169
  34.3 0.1 multiply_reduce_fusion.3
  34.4 0.7 %pad_maximum_fusion = f32[4,2,4,16,128]{4,3,2,0,1:T(8,128)} fusion(f32[4,2,3,16,128]{4,3,2,0,1:T(8,128)S(1)} %multiply_multiply_fusion, f32[4,2,1,16,128]{4,3,1,0,2:T(8,128)S(1)} %bitcast.40), kind=kLoop, calls=%fused_computation.2 | loop fusion | flops 65536 | bytes 524288 | tf_op jit(solution)/shard_map/concatenate | solution.py:173
  35.1 3.4 %all-to-all-start.2 = ((f32[4,2,4,16,128]{4,3,2,0,1:T(8,128)}), f32[4,2,4,16,128]{4,3,2,0,1:T(8,128)S(1)}, u32[]{:S(2)}, u32[]{:S(2)}) async-start(f32[4,2,4,16,128]{4,3,2,0,1:T(8,128)} %pad_maximum_fusion), calls=%async_computation.2 | async-start | bytes 524288 | tf_op jit(solution)/shard_map/all_to_all | solution.py:208
  38.6 0.0 collective-permute-done
  38.6 0.0 collective-permute-done.1
  38.6 5.1 %all-to-all-done.2 = f32[4,2,4,16,128]{4,3,2,0,1:T(8,128)S(1)} async-done(((f32[4,2,4,16,128]{4,3,2,0,1:T(8,128)}), f32[4,2,4,16,128]{4,3,2,0,1:T(8,128)S(1)}, u32[]{:S(2)}, u32[]{:S(2)}) %all-to-all-start.2) | async-done | bytes 262176 | tf_op jit(solution)/shard_map/all_to_all | solution.py:208
  43.7 0.7 %copy.25 = f32[4,2,4,16,128]{4,3,2,1,0:T(8,128)} copy(f32[4,2,4,16,128]{4,3,2,0,1:T(8,128)S(1)} %all-to-all-done.2) | data formatting | bytes 524288 | tf_op jit(solution)/shard_map/all_to_all | solution.py:208
  44.5 3.4 %all-to-all-start.3 = ((f32[4,2,4,16,128]{4,3,2,1,0:T(8,128)}), f32[4,2,4,16,128]{4,3,2,1,0:T(8,128)S(1)}, u32[]{:S(2)}, u32[]{:S(2)}) async-start(f32[4,2,4,16,128]{4,3,2,1,0:T(8,128)} %copy.25), calls=%async_computation.3 | async-start | bytes 524288 | tf_op jit(solution)/shard_map/all_to_all | solution.py:209
  47.9 0.6 maximum_convert_fusion.1.zhalo_ref
  48.5 0.0 collective-permute-done.2
  48.5 0.0 collective-permute-done.3
  48.5 0.4 broadcast_select_fusion.1
  48.9 1.0 %maximum_convert_fusion.rhalo_ref = f32[32,2,1024]{2,1,0:T(2,128)} fusion(bf16[32,1,1024]{2,1,0:T(2,128)(2,1)S(1)} %get-tuple-element.11, bf16[32,1,1024]{2,1,0:T(2,128)(2,1)S(1)} %get-tuple-element.10), kind=kLoop, calls=%fused_computation.9 | loop fusion | flops 262144 | bytes 393216 | tf_op jit(solution)/shard_map/convert_element_type | solution.py:196
  49.9 5.0 %all-to-all-done.3 = f32[4,2,4,16,128]{4,3,2,1,0:T(8,128)S(1)} async-done(((f32[4,2,4,16,128]{4,3,2,1,0:T(8,128)}), f32[4,2,4,16,128]{4,3,2,1,0:T(8,128)S(1)}, u32[]{:S(2)}, u32[]{:S(2)}) %all-to-all-start.3) | async-done | bytes 262176 | tf_op jit(solution)/shard_map/all_to_all | solution.py:209
  54.9 0.0 copy-start.1
  54.9 0.7 %copy-done.1 = f32[4,2,4,16,128]{4,3,2,1,0:T(8,128)} copy-done((f32[4,2,4,16,128]{4,3,2,1,0:T(8,128)}, f32[4,2,4,16,128]{4,3,2,1,0:T(8,128)S(1)}, u32[]{:S(2)}) %copy-start.1) | copy-done | bytes 262168
  55.6 10.2 %shard_map.60 = (f32[32,16,1024]{2,1,0:T(8,128)}, f32[3,32,16,1024]{3,2,1,0:T(8,128)}) custom-call(bf16[32,16,1024]{2,1,0:T(8,128)(2,1)} %d_ref.3, bf16[3,32,16,1024]{3,2,1,0:T(8,128)(2,1)} %c_ref.3, f32[8,4,16,128]{3,2,1,0:T(8,128)} %bitcast.37, f32[2,16,1024]{2,1,0:T(8,128)} %maximum_convert_fusion.1.zhalo_ref, f32[32,2,1024]{2,1,0:T(2,128)} %maximum_convert_fusion.rhalo_ref), custom_call_target="tpu_custom_call" | custom-call | tf_op jit(solution)/shard_map/pallas_call | solution.py:144
  (8 shorter events, 0.1 us)
Async XLA Ops:
  0.6 11.1 %copy-start = (bf16[32,16,1024]{2,1,0:T(8,128)(2,1)S(1)}, bf16[32,16,1024]{2,1,0:T(8,128)(2,1)}, u32[]{:S(2)}) copy-start(bf16[32,16,1024]{2,1,0:T(8,128)(2,1)} %d_ref.3) | copy-start | bytes 3145732
  5.8 21.8 %copy-start.2 = (s32[8]{0:T(128)S(1)}, s32[8]{0:T(128)}, u32[]{:S(2)}) copy-start(s32[8]{0:T(128)} %param.7) | copy-start | bytes 100
  7.5 10.1 %all-to-all-start = ((f32[4,2,4,16,128]{4,3,2,0,1:T(8,128)}), f32[4,2,4,16,128]{4,3,2,0,1:T(8,128)S(1)}, u32[]{:S(2)}, u32[]{:S(2)}) async-start(f32[4,2,4,16,128]{4,3,2,0,1:T(8,128)} %copy.20), calls=%async_computation | async-start | bytes 524288 | tf_op jit(solution)/shard_map/all_to_all | solution.py:208
  11.8 26.8 %collective-permute-start = (bf16[1,16,1024]{2,1,0:T(8,128)(2,1)S(1)}, bf16[1,16,1024]{2,1,0:T(8,128)(2,1)S(1)}, u32[]{:S(2)}, u32[]{:S(2)}) collective-permute-start(bf16[1,16,1024]{2,1,0:T(8,128)(2,1)S(1)} %get-tuple-element.16), channel_id=1, source_target_pairs={{0,4},{4,8},{8,12},{12,16},{16,20},{20,24},{24,28},{1,5},{5,9},{9,... | collective-permute-start | bytes 98312 | tf_op jit(solution)/shard_map/ppermute | solution.py:187
  15.9 22.7 %collective-permute-start.1 = (bf16[1,16,1024]{2,1,0:T(8,128)(2,1)S(1)}, bf16[1,16,1024]{2,1,0:T(8,128)(2,1)S(1)}, u32[]{:S(2)}, u32[]{:S(2)}) collective-permute-start(bf16[1,16,1024]{2,1,0:T(8,128)(2,1)S(1)} %get-tuple-element.17), channel_id=1, source_target_pairs={{4,0},{8,4},{12,8},{16,12},{20,16},{24,20},{28,24},{5,1},{9,5},{13... | collective-permute-start | bytes 98312 | tf_op jit(solution)/shard_map/ppermute | solution.py:188
  18.4 14.8 %all-to-all-start.1 = ((f32[4,2,4,16,128]{4,3,2,1,0:T(8,128)}), f32[4,2,4,16,128]{4,3,2,1,0:T(8,128)S(1)}, u32[]{:S(2)}, u32[]{:S(2)}) async-start(f32[4,2,4,16,128]{4,3,2,1,0:T(8,128)} %copy.21), calls=%async_computation.1 | async-start | bytes 524288 | tf_op jit(solution)/shard_map/all_to_all | solution.py:209
  25.0 23.5 %collective-permute-start.2 = (bf16[32,1,1024]{2,1,0:T(2,128)(2,1)S(1)}, bf16[32,1,1024]{2,1,0:T(2,128)(2,1)S(1)}, u32[]{:S(2)}, u32[]{:S(2)}) collective-permute-start(bf16[32,1,1024]{2,1,0:T(2,128)(2,1)S(1)} %get-tuple-element.12), channel_id=1, source_target_pairs={{0,1},{1,2},{2,3},{4,5},{5,6},{6,7},{8,9},{9,10},{10,11},{12,13},{... | collective-permute-start | bytes 196616 | tf_op jit(solution)/shard_map/ppermute | solution.py:189
  26.3 22.2 %collective-permute-start.3 = (bf16[32,1,1024]{2,1,0:T(2,128)(2,1)S(1)}, bf16[32,1,1024]{2,1,0:T(2,128)(2,1)S(1)}, u32[]{:S(2)}, u32[]{:S(2)}) collective-permute-start(bf16[32,1,1024]{2,1,0:T(2,128)(2,1)S(1)} %get-tuple-element.13), channel_id=1, source_target_pairs={{1,0},{2,1},{3,2},{5,4},{6,5},{7,6},{9,8},{10,9},{11,10},{13,12},{... | collective-permute-start | bytes 196616 | tf_op jit(solution)/shard_map/ppermute | solution.py:190
  35.1 8.6 %all-to-all-start.2 = ((f32[4,2,4,16,128]{4,3,2,0,1:T(8,128)}), f32[4,2,4,16,128]{4,3,2,0,1:T(8,128)S(1)}, u32[]{:S(2)}, u32[]{:S(2)}) async-start(f32[4,2,4,16,128]{4,3,2,0,1:T(8,128)} %pad_maximum_fusion), calls=%async_computation.2 | async-start | bytes 524288 | tf_op jit(solution)/shard_map/all_to_all | solution.py:208
  44.5 10.4 %all-to-all-start.3 = ((f32[4,2,4,16,128]{4,3,2,1,0:T(8,128)}), f32[4,2,4,16,128]{4,3,2,1,0:T(8,128)S(1)}, u32[]{:S(2)}, u32[]{:S(2)}) async-start(f32[4,2,4,16,128]{4,3,2,1,0:T(8,128)} %copy.25), calls=%async_computation.3 | async-start | bytes 524288 | tf_op jit(solution)/shard_map/all_to_all | solution.py:209
  54.9 0.7 %copy-start.1 = (f32[4,2,4,16,128]{4,3,2,1,0:T(8,128)}, f32[4,2,4,16,128]{4,3,2,1,0:T(8,128)S(1)}, u32[]{:S(2)}) copy-start(f32[4,2,4,16,128]{4,3,2,1,0:T(8,128)S(1)} %all-to-all-done.3) | copy-start | bytes 786436

commit v9 on v7

--- a/solution.py
+++ b/solution.py
@@ -59,28 +59,18 @@
                 out_ref[j * per_tile + g, c] = values[c][g * chunk_rows:(g + 1) * chunk_rows]
 
 
-def backward_kernel(d_ref, c_ref, ans_ref, zhalo_ref, rhalo_ref, gd_ref, gc_ref, *, step, slices_total):
+def smooth_kernel(d_ref, zhalo_ref, rhalo_ref, out_ref):
     slices, rows, block = d_ref.shape
     shape = (rows, lanes)
-    subs = block // lanes
-    per_tile = ans_ref.shape[0] // (pl.num_programs(0) * subs)
-    scale = -step * log2e
-    gain = optical_depth / slices_total
     row = lax.broadcasted_iota(jnp.int32, shape, 0)
     first_row = row == 0
     last_row = row == shape[0] - 1
 
-    for j in range(subs):
+    for j in range(block // lanes):
         cols = pl.ds(j * lanes, lanes)
-        base = (pl.program_id(0) * subs + j) * per_tile
-
-        def pixel(c):
-            if per_tile == 1:
-                return ans_ref[base, c]
-            return jnp.concatenate([ans_ref[base + g, c] for g in range(per_tile)], axis=0)
 
         def body(z, carry):
-            n, front, w0, w1, w2, d_prev, d = carry
+            d_prev, d = carry
             d_next = jnp.where(
                 z + 1 < slices,
                 d_ref[jnp.minimum(z + 1, slices - 1), :, cols].astype(jnp.float32),
@@ -89,7 +79,35 @@
             rims = rhalo_ref[z, :, cols]
             upper = jnp.where(first_row, rims[0:1], pltpu.roll(d, 1, 0))
             lower = jnp.where(last_row, rims[1:2], pltpu.roll(d, shape[0] - 1, 0))
-            smooth = 2.0 * smooth_weight * ((d - d_prev) + (d - d_next) + (d - upper) + (d - lower))
+            out_ref[z, :, cols] = 2.0 * smooth_weight * (
+                (d - d_prev) + (d - d_next) + (d - upper) + (d - lower)
+            )
+            return (d, d_next)
+
+        start = (zhalo_ref[0, :, cols], d_ref[0, :, cols].astype(jnp.float32))
+        lax.fori_loop(0, slices, body, start, unroll=2)
+
+
+def backward_kernel(d_ref, c_ref, ans_ref, smooth_ref, gd_ref, gc_ref, *, step, slices_total):
+    slices, rows, block = d_ref.shape
+    shape = (rows, lanes)
+    subs = block // lanes
+    per_tile = ans_ref.shape[0] // (pl.num_programs(0) * subs)
+    scale = -step * log2e
+    gain = optical_depth / slices_total
+
+    for j in range(subs):
+        cols = pl.ds(j * lanes, lanes)
+        base = (pl.program_id(0) * subs + j) * per_tile
+
+        def pixel(c):
+            if per_tile == 1:
+                return ans_ref[base, c]
+            return jnp.concatenate([ans_ref[base + g, c] for g in range(per_tile)], axis=0)
+
+        def body(z, carry):
+            n, front, w0, w1, w2 = carry
+            d = d_ref[z, :, cols].astype(jnp.float32)
             dtn = softplus(d) * scale
             lit = front * (1.0 - jnp.exp2(dtn))
             n_next = n + dtn
@@ -104,17 +122,12 @@
             inner = emitted - inv * (pixel(3) - left)
             for c in range(3):
                 gc_ref[c, z, :, cols] = res[c] * lit_col[c] * (1.0 - col[c])
-            gd_ref[z, :, cols] = gain * through * jax.nn.sigmoid(d) * inner + smooth
-            return (n_next, through, w[0], w[1], w[2], d, d_next)
+            gd_ref[z, :, cols] = gain * through * jax.nn.sigmoid(d) * inner + smooth_ref[z, :, cols]
+            return (n_next, through, w[0], w[1], w[2])
 
         zero = jnp.zeros(shape, jnp.float32)
         one = jnp.ones(shape, jnp.float32)
-        start = (
-            zero, one, zero, zero, zero,
-            zhalo_ref[0, :, cols],
-            d_ref[0, :, cols].astype(jnp.float32),
-        )
-        lax.fori_loop(0, slices, body, start, unroll=2)
+        lax.fori_loop(0, slices, body, (zero, one, zero, zero, zero), unroll=2)
 
 
 def forward_partial(density, colour_raw, step, depth_count):
@@ -135,7 +148,25 @@
     )(density, colour_raw)
 
 
-def backward_grads(density, colour_raw, answers, zhalo, rhalo, step, slices_total):
+def smooth_term(density, zhalo, rhalo):
+    slices, rows, width = density.shape
+    tiles = width // lanes
+    block = lanes * forward_subs if tiles % forward_subs == 0 else lanes
+    slab = pl.BlockSpec((slices, rows, block), lambda i: (0, 0, i))
+    return pl.pallas_call(
+        smooth_kernel,
+        grid=(width // block,),
+        in_specs=[
+            slab,
+            pl.BlockSpec((2, rows, block), lambda i: (0, 0, i)),
+            pl.BlockSpec((slices, 2, block), lambda i: (0, 0, i)),
+        ],
+        out_specs=slab,
+        out_shape=jax.ShapeDtypeStruct((slices, rows, width), jnp.float32),
+    )(density, zhalo, rhalo)
+
+
+def backward_grads(density, colour_raw, answers, smooth, step, slices_total):
     slices, rows, width = density.shape
     tiles = width // lanes
     block = lanes * backward_subs if tiles % backward_subs == 0 else lanes
@@ -144,19 +175,14 @@
     return pl.pallas_call(
         functools.partial(backward_kernel, step=step, slices_total=float(slices_total)),
         grid=(width // block,),
-        in_specs=[
-            slab,
-            colours,
-            pl.BlockSpec(memory_space=pltpu.VMEM),
-            pl.BlockSpec((2, rows, block), lambda i: (0, 0, i)),
-            pl.BlockSpec((slices, 2, block), lambda i: (0, 0, i)),
-        ],
+        in_specs=[slab, colours, pl.BlockSpec(memory_space=pltpu.VMEM), slab],
         out_specs=[slab, colours],
         out_shape=[
             jax.ShapeDtypeStruct((slices, rows, width), jnp.float32),
             jax.ShapeDtypeStruct((3, slices, rows, width), jnp.float32),
         ],
-    )(density, colour_raw, answers, zhalo, rhalo)
+        input_output_aliases={3: 0},
+    )(density, colour_raw, answers, smooth)
 
 
 def composite(parts, slab_rank, target_piece, slices_total):
@@ -215,9 +241,8 @@
     )
     answers = composite(received, slab_rank, target_piece, float(slices_total))
     returned = lax.all_to_all(answers, "depth", 0, 0, tiled=True)
-    return backward_grads(
-        density_raw, colour_raw, returned, zhalo, rhalo, step, slices_total
-    )
+    smooth = smooth_term(density_raw, zhalo, rhalo)
+    return backward_grads(density_raw, colour_raw, returned, smooth, step, slices_total)
 
 
 def solution(mesh):

time: 51.5 us -> 51.2 us (level)
  waiting for transfers between devices: 5.96 us -> 1.92 us
  Pallas kernels: 15.4 us -> 19.1 us
    all_to_all x1, waiting for transfers between devices: 5.95 us -> 1.91 us  [local(): returned = lax.all_to_all(answers, 'depth', 0, 0, tiled=True)]
    pallas_call x0 -> x1, Pallas kernels: none -> 4.03 us  [smooth_term(): pl.pallas_call(smooth_kernel, grid=(width // block,), in_specs=[slab, pl....]
  transfers between devices with their start and end apart: 6 -> 6, of which waited for: 1 -> 1; matrix products, arithmetic and copies ran while one was open for 8% -> 8% of each run, Pallas kernels for 0% -> 8%
where the time goes in v9:
time: 51.2 us; the launch traced here: 50.6 us
  starting transfers between devices  23.8 us (46%)
  Pallas kernels  19.1 us (37%)
  other arithmetic  4.04 us (8%)
  waiting for transfers between devices  1.92 us (4%)
  local copies, waits for them, and re-layouts  0.95 us (2%)
  between operations  0.78 us (2%)
    pallas_call x1, Pallas kernels, backward_grads(): pl.pallas_call(functools.partial(backward_kernel, step=step, slices_total...  9.89 us
    all_to_all x1, starting transfers between devices, local(): received = lax.all_to_all(partial_value, 'depth', 0, 0, tiled=True)  6.38 us
    all_to_all x1, starting transfers between devices, local(): returned = lax.all_to_all(answers, 'depth', 0, 0, tiled=True)  6.34 us
    pallas_call x1, Pallas kernels, forward_partial(): pl.pallas_call(functools.partial(forward_kernel, step=step), grid=(width...  5.19 us
    ppermute x1, starting transfers between devices, halos(): prev_row = lax.ppermute(last_row, 'rows', up_r)  4.52 us
    pallas_call x1, Pallas kernels, smooth_term(): pl.pallas_call(smooth_kernel, grid=(width // block,), in_specs=[slab, pl....  4.03 us
    ppermute x1, starting transfers between devices, halos(): prev_slice = lax.ppermute(last_slice, 'depth', up_d)  3.36 us
    ppermute x1, starting transfers between devices, halos(): next_row = lax.ppermute(first_row, 'rows', [(j, i) for i, j in up_r])  1.92 us
  transfers between devices with their start and end apart: 6, of which 1 were waited for; matrix products, arithmetic and copies ran while one was open for 8% of the time, Pallas kernels for 8%

profile of v9, /device:TPU:1, one launch (start us, length us, event | category | flops | bytes accessed | tf_op | source)
XLA Modules:
  0.0 50.6 jit_solution(17429994556439930716)
XLA Ops:
  0.6 0.0 copy-start
  0.6 0.0 copy-start.2
  0.7 5.2 %shard_map.59 = f32[8,4,16,128]{3,2,1,0:T(8,128)} custom-call(bf16[32,16,1024]{2,1,0:T(8,128)(2,1)} %d_ref.5, bf16[3,32,16,1024]{3,2,1,0:T(8,128)(2,1)} %c_ref.3), custom_call_target="tpu_custom_call" | custom-call | tf_op jit(solution)/shard_map/pallas_call | solution.py:137
  5.8 6.4 %all-to-all-start = ((f32[8,4,16,128]{3,2,1,0:T(8,128)}), f32[8,4,16,128]{3,2,1,0:T(8,128)S(1)}, u32[]{:S(2)}, u32[]{:S(2)}) async-start(f32[8,4,16,128]{3,2,1,0:T(8,128)} %shard_map.59), calls=%async_computation | async-start | bytes 524288 | tf_op jit(solution)/shard_map/all_to_all | solution.py:235
  12.2 0.0 copy-done
  12.2 3.4 %collective-permute-start = (bf16[1,16,1024]{2,1,0:T(8,128)(2,1)S(1)}, bf16[1,16,1024]{2,1,0:T(8,128)(2,1)S(1)}, u32[]{:S(2)}, u32[]{:S(2)}) collective-permute-start(bf16[1,16,1024]{2,1,0:T(8,128)(2,1)S(1)} %get-tuple-element.16), channel_id=1, source_target_pairs={{0,4},{4,8},{8,12},{12,16},{16,20},{20,24},{24,28},{1,5},{5,9},{9,... | collective-permute-start | bytes 98312 | tf_op jit(solution)/shard_map/ppermute | solution.py:213
  15.6 1.3 %collective-permute-start.1 = (bf16[1,16,1024]{2,1,0:T(8,128)(2,1)S(1)}, bf16[1,16,1024]{2,1,0:T(8,128)(2,1)S(1)}, u32[]{:S(2)}, u32[]{:S(2)}) collective-permute-start(bf16[1,16,1024]{2,1,0:T(8,128)(2,1)S(1)} %get-tuple-element.17), channel_id=1, source_target_pairs={{4,0},{8,4},{12,8},{16,12},{20,16},{24,20},{28,24},{5,1},{9,5},{13... | collective-permute-start | bytes 98312 | tf_op jit(solution)/shard_map/ppermute | solution.py:214
  16.9 0.2 fusion.5
  17.1 4.5 %collective-permute-start.2 = (bf16[32,1,1024]{2,1,0:T(2,128)(2,1)S(1)}, bf16[32,1,1024]{2,1,0:T(2,128)(2,1)S(1)}, u32[]{:S(2)}, u32[]{:S(2)}) collective-permute-start(bf16[32,1,1024]{2,1,0:T(2,128)(2,1)S(1)} %get-tuple-element.12), channel_id=1, source_target_pairs={{0,1},{1,2},{2,3},{4,5},{5,6},{6,7},{8,9},{9,10},{10,11},{12,13},{... | collective-permute-start | bytes 196616 | tf_op jit(solution)/shard_map/ppermute | solution.py:215
  21.7 1.9 %collective-permute-start.3 = (bf16[32,1,1024]{2,1,0:T(2,128)(2,1)S(1)}, bf16[32,1,1024]{2,1,0:T(2,128)(2,1)S(1)}, u32[]{:S(2)}, u32[]{:S(2)}) collective-permute-start(bf16[32,1,1024]{2,1,0:T(2,128)(2,1)S(1)} %get-tuple-element.13), channel_id=1, source_target_pairs={{1,0},{2,1},{3,2},{5,4},{6,5},{7,6},{9,8},{10,9},{11,10},{13,12},{... | collective-permute-start | bytes 196616 | tf_op jit(solution)/shard_map/ppermute | solution.py:216
  23.6 0.0 copy-done.2
  23.6 0.1 compare_convert_fusion
  23.7 0.0 collective-permute-done
  23.7 0.0 collective-permute-done.1
  23.7 0.0 all-to-all-done
  23.7 0.1 multiply_reduce_fusion.1
  23.9 0.2 multiply_reduce_fusion
  24.1 0.8 %dynamic-slice_subtract_fusion = f32[3,16,128]{2,1,0:T(8,128)S(1)} fusion(f32[3,16,128]{2,1,0:T(8,128)S(1)} %get-tuple-element.8, f32[3,16,1024]{2,1,0:T(8,128)} %param.6, s32[]{:T(128)S(6)} %select_n.39), kind=kLoop, calls=%fused_computation.20 | loop fusion | flops 6144 | bytes 73732 | tf_op jit(solution)/shard_map/sub | solution.py:195
  24.9 0.1 multiply_reduce_fusion.3
  25.0 0.7 %pad_maximum_fusion = f32[8,4,16,128]{3,2,1,0:T(8,128)} fusion(f32[8,1,16,128]{3,2,1,0:T(8,128)S(1)} %fusion.2, f32[8,3,16,128]{3,2,1,0:T(8,128)S(1)} %get-tuple-element.18), kind=kLoop, calls=%fused_computation.2 | loop fusion | flops 65536 | bytes 524288 | tf_op jit(solution)/shard_map/concatenate | solution.py:199
  25.7 6.3 %all-to-all-start.1 = ((f32[8,4,16,128]{3,2,1,0:T(8,128)}), f32[8,4,16,128]{3,2,1,0:T(8,128)S(1)}, u32[]{:S(2)}, u32[]{:S(2)}) async-start(f32[8,4,16,128]{3,2,1,0:T(8,128)} %pad_maximum_fusion), calls=%async_computation.1 | async-start | bytes 524288 | tf_op jit(solution)/shard_map/all_to_all | solution.py:243
  32.0 0.7 %maximum_convert_fusion.1.zhalo_ref = f32[2,16,1024]{2,1,0:T(8,128)} fusion(bf16[1,16,1024]{2,1,0:T(8,128)(2,1)S(1)} %get-tuple-element.15, bf16[1,16,1024]{2,1,0:T(8,128)(2,1)S(1)} %get-tuple-element.14), kind=kLoop, calls=%fused_computation.10 | loop fusion | flops 65536 | bytes 196608 | tf_op jit(solution)/shard_map/convert_element_type | solution.py:221
  32.7 0.0 collective-permute-done.2
  32.7 0.0 collective-permute-done.3
  32.7 0.4 broadcast_select_fusion.1
  33.1 1.0 %maximum_convert_fusion.rhalo_ref = f32[32,2,1024]{2,1,0:T(2,128)} fusion(bf16[32,1,1024]{2,1,0:T(2,128)(2,1)S(1)} %get-tuple-element.11, bf16[32,1,1024]{2,1,0:T(2,128)(2,1)S(1)} %get-tuple-element.10), kind=kLoop, calls=%fused_computation.9 | loop fusion | flops 262144 | bytes 393216 | tf_op jit(solution)/shard_map/convert_element_type | solution.py:222
  34.1 4.0 %shard_map.60.smooth_ref = f32[32,16,1024]{2,1,0:T(8,128)} custom-call(bf16[32,16,1024]{2,1,0:T(8,128)(2,1)} %d_ref.5, f32[2,16,1024]{2,1,0:T(8,128)} %maximum_convert_fusion.1.zhalo_ref, f32[32,2,1024]{2,1,0:T(2,128)} %maximum_convert_fusion.rhalo_ref), custom_call_target="tpu_custom_call" | custom-call | tf_op jit(solution)/shard_map/pallas_call | solution.py:156
  38.1 1.9 %all-to-all-done.1.ans_ref = f32[8,4,16,128]{3,2,1,0:T(8,128)S(1)} async-done(((f32[8,4,16,128]{3,2,1,0:T(8,128)}), f32[8,4,16,128]{3,2,1,0:T(8,128)S(1)}, u32[]{:S(2)}, u32[]{:S(2)}) %all-to-all-start.1) | async-done | bytes 262176 | tf_op jit(solution)/shard_map/all_to_all | solution.py:243
  40.0 0.0 copy-start.1
  40.0 0.7 %copy-done.1 = f32[8,4,16,128]{3,2,1,0:T(8,128)} copy-done((f32[8,4,16,128]{3,2,1,0:T(8,128)}, f32[8,4,16,128]{3,2,1,0:T(8,128)S(1)}, u32[]{:S(2)}) %copy-start.1) | copy-done | bytes 262168
  40.7 9.9 %shard_map.61 = (f32[32,16,1024]{2,1,0:T(8,128)}, f32[3,32,16,1024]{3,2,1,0:T(8,128)}) custom-call(bf16[32,16,1024]{2,1,0:T(8,128)(2,1)} %d_ref.5, bf16[3,32,16,1024]{3,2,1,0:T(8,128)(2,1)} %c_ref.3, f32[8,4,16,128]{3,2,1,0:T(8,128)} %copy-done.1, f32[32,16,1024]{2,1,0:T(8,128)} %shard_map.60.smooth_ref), custom_call_target="tpu_custom_call", output_to_operand_aliasing={{0}: (3, {})} | custom-call | tf_op jit(solution)/shard_map/pallas_call | solution.py:175
  (7 shorter events, 0.1 us)
Async XLA Ops:
  0.6 11.6 %copy-start = (bf16[32,16,1024]{2,1,0:T(8,128)(2,1)S(1)}, bf16[32,16,1024]{2,1,0:T(8,128)(2,1)}, u32[]{:S(2)}) copy-start(bf16[32,16,1024]{2,1,0:T(8,128)(2,1)} %d_ref.5) | copy-start | bytes 3145732
  0.6 22.9 %copy-start.2 = (s32[8]{0:T(128)S(1)}, s32[8]{0:T(128)}, u32[]{:S(2)}) copy-start(s32[8]{0:T(128)} %param.7) | copy-start | bytes 100
  5.8 17.8 %all-to-all-start = ((f32[8,4,16,128]{3,2,1,0:T(8,128)}), f32[8,4,16,128]{3,2,1,0:T(8,128)S(1)}, u32[]{:S(2)}, u32[]{:S(2)}) async-start(f32[8,4,16,128]{3,2,1,0:T(8,128)} %shard_map.59), calls=%async_computation | async-start | bytes 524288 | tf_op jit(solution)/shard_map/all_to_all | solution.py:235
  12.2 11.4 %collective-permute-start = (bf16[1,16,1024]{2,1,0:T(8,128)(2,1)S(1)}, bf16[1,16,1024]{2,1,0:T(8,128)(2,1)S(1)}, u32[]{:S(2)}, u32[]{:S(2)}) collective-permute-start(bf16[1,16,1024]{2,1,0:T(8,128)(2,1)S(1)} %get-tuple-element.16), channel_id=1, source_target_pairs={{0,4},{4,8},{8,12},{12,16},{16,20},{20,24},{24,28},{1,5},{5,9},{9,... | collective-permute-start | bytes 98312 | tf_op jit(solution)/shard_map/ppermute | solution.py:213
  15.6 8.1 %collective-permute-start.1 = (bf16[1,16,1024]{2,1,0:T(8,128)(2,1)S(1)}, bf16[1,16,1024]{2,1,0:T(8,128)(2,1)S(1)}, u32[]{:S(2)}, u32[]{:S(2)}) collective-permute-start(bf16[1,16,1024]{2,1,0:T(8,128)(2,1)S(1)} %get-tuple-element.17), channel_id=1, source_target_pairs={{4,0},{8,4},{12,8},{16,12},{20,16},{24,20},{28,24},{5,1},{9,5},{13... | collective-permute-start | bytes 98312 | tf_op jit(solution)/shard_map/ppermute | solution.py:214
  17.1 15.6 %collective-permute-start.2 = (bf16[32,1,1024]{2,1,0:T(2,128)(2,1)S(1)}, bf16[32,1,1024]{2,1,0:T(2,128)(2,1)S(1)}, u32[]{:S(2)}, u32[]{:S(2)}) collective-permute-start(bf16[32,1,1024]{2,1,0:T(2,128)(2,1)S(1)} %get-tuple-element.12), channel_id=1, source_target_pairs={{0,1},{1,2},{2,3},{4,5},{5,6},{6,7},{8,9},{9,10},{10,11},{12,13},{... | collective-permute-start | bytes 196616 | tf_op jit(solution)/shard_map/ppermute | solution.py:215
  21.7 11.0 %collective-permute-start.3 = (bf16[32,1,1024]{2,1,0:T(2,128)(2,1)S(1)}, bf16[32,1,1024]{2,1,0:T(2,128)(2,1)S(1)}, u32[]{:S(2)}, u32[]{:S(2)}) collective-permute-start(bf16[32,1,1024]{2,1,0:T(2,128)(2,1)S(1)} %get-tuple-element.13), channel_id=1, source_target_pairs={{1,0},{2,1},{3,2},{5,4},{6,5},{7,6},{9,8},{10,9},{11,10},{13,12},{... | collective-permute-start | bytes 196616 | tf_op jit(solution)/shard_map/ppermute | solution.py:216
  25.7 14.3 %all-to-all-start.1 = ((f32[8,4,16,128]{3,2,1,0:T(8,128)}), f32[8,4,16,128]{3,2,1,0:T(8,128)S(1)}, u32[]{:S(2)}, u32[]{:S(2)}) async-start(f32[8,4,16,128]{3,2,1,0:T(8,128)} %pad_maximum_fusion), calls=%async_computation.1 | async-start | bytes 524288 | tf_op jit(solution)/shard_map/all_to_all | solution.py:243
  40.0 0.7 %copy-start.1 = (f32[8,4,16,128]{3,2,1,0:T(8,128)}, f32[8,4,16,128]{3,2,1,0:T(8,128)S(1)}, u32[]{:S(2)}) copy-start(f32[8,4,16,128]{3,2,1,0:T(8,128)S(1)} %all-to-all-done.1.ans_ref) | copy-start | bytes 786436

commit v10 on v9

--- a/solution.py
+++ b/solution.py
@@ -59,33 +59,43 @@
                 out_ref[j * per_tile + g, c] = values[c][g * chunk_rows:(g + 1) * chunk_rows]
 
 
-def smooth_kernel(d_ref, zhalo_ref, rhalo_ref, out_ref):
+def smooth_kernel(flags_ref, d_ref, zprev_ref, znext_ref, rprev_ref, rnext_ref, out_ref):
     slices, rows, block = d_ref.shape
     shape = (rows, lanes)
     row = lax.broadcasted_iota(jnp.int32, shape, 0)
     first_row = row == 0
     last_row = row == shape[0] - 1
+    has_prev_slice = flags_ref[0] > 0
+    has_next_slice = flags_ref[1] > 0
+    has_prev_row = flags_ref[2] > 0
+    has_next_row = flags_ref[3] > 0
 
     for j in range(block // lanes):
         cols = pl.ds(j * lanes, lanes)
+        d_first = d_ref[0, :, cols].astype(jnp.float32)
+        d_last = d_ref[slices - 1, :, cols].astype(jnp.float32)
+        prev_slice = jnp.where(has_prev_slice, zprev_ref[0, :, cols].astype(jnp.float32), d_first)
+        next_slice = jnp.where(has_next_slice, znext_ref[0, :, cols].astype(jnp.float32), d_last)
 
         def body(z, carry):
             d_prev, d = carry
             d_next = jnp.where(
                 z + 1 < slices,
                 d_ref[jnp.minimum(z + 1, slices - 1), :, cols].astype(jnp.float32),
-                zhalo_ref[1, :, cols],
+                next_slice,
             )
-            rims = rhalo_ref[z, :, cols]
-            upper = jnp.where(first_row, rims[0:1], pltpu.roll(d, 1, 0))
-            lower = jnp.where(last_row, rims[1:2], pltpu.roll(d, shape[0] - 1, 0))
+            top = jnp.where(has_prev_row, rprev_ref[z, :, cols].astype(jnp.float32), d[0:1])
+            bottom = jnp.where(
+                has_next_row, rnext_ref[z, :, cols].astype(jnp.float32), d[rows - 1:rows]
+            )
+            upper = jnp.where(first_row, top, pltpu.roll(d, 1, 0))
+            lower = jnp.where(last_row, bottom, pltpu.roll(d, shape[0] - 1, 0))
             out_ref[z, :, cols] = 2.0 * smooth_weight * (
                 (d - d_prev) + (d - d_next) + (d - upper) + (d - lower)
             )
             return (d, d_next)
 
-        start = (zhalo_ref[0, :, cols], d_ref[0, :, cols].astype(jnp.float32))
-        lax.fori_loop(0, slices, body, start, unroll=2)
+        lax.fori_loop(0, slices, body, (prev_slice, d_first), unroll=2)
 
 
 def backward_kernel(d_ref, c_ref, ans_ref, smooth_ref, gd_ref, gc_ref, *, step, slices_total):
@@ -148,22 +158,20 @@
     )(density, colour_raw)
 
 
-def smooth_term(density, zhalo, rhalo):
+def smooth_term(density, flags, zprev, znext, rprev, rnext):
     slices, rows, width = density.shape
     tiles = width // lanes
     block = lanes * forward_subs if tiles % forward_subs == 0 else lanes
     slab = pl.BlockSpec((slices, rows, block), lambda i: (0, 0, i))
+    face = pl.BlockSpec((1, rows, block), lambda i: (0, 0, i))
+    rim = pl.BlockSpec((slices, 1, block), lambda i: (0, 0, i))
     return pl.pallas_call(
         smooth_kernel,
         grid=(width // block,),
-        in_specs=[
-            slab,
-            pl.BlockSpec((2, rows, block), lambda i: (0, 0, i)),
-            pl.BlockSpec((slices, 2, block), lambda i: (0, 0, i)),
-        ],
+        in_specs=[pl.BlockSpec(memory_space=pltpu.SMEM), slab, face, face, rim, rim],
         out_specs=slab,
         out_shape=jax.ShapeDtypeStruct((slices, rows, width), jnp.float32),
-    )(density, zhalo, rhalo)
+    )(flags, density, zprev, znext, rprev, rnext)
 
 
 def backward_grads(density, colour_raw, answers, smooth, step, slices_total):
@@ -199,28 +207,33 @@
     return jnp.concatenate([scaled_residual, folded[:, None]], axis=1)
 
 
-def halos(density_raw):
+def depth_halos(density_raw):
     depth_count = lax.axis_size("depth")
+    up = [(i, i + 1) for i in range(depth_count - 1)]
+    prev_slice = lax.ppermute(density_raw[-1:], "depth", up)
+    next_slice = lax.ppermute(density_raw[:1], "depth", [(j, i) for i, j in up])
+    return prev_slice, next_slice
+
+
+def row_halos(density_raw):
     rows_count = lax.axis_size("rows")
+    up = [(i, i + 1) for i in range(rows_count - 1)]
+    prev_row = lax.ppermute(density_raw[:, -1:], "rows", up)
+    next_row = lax.ppermute(density_raw[:, :1], "rows", [(j, i) for i, j in up])
+    return prev_row, next_row
+
+
+def edge_flags():
     depth_at = lax.axis_index("depth")
     rows_at = lax.axis_index("rows")
-    up_d = [(i, i + 1) for i in range(depth_count - 1)]
-    up_r = [(i, i + 1) for i in range(rows_count - 1)]
-    first_slice = density_raw[:1]
-    last_slice = density_raw[-1:]
-    first_row = density_raw[:, :1]
-    last_row = density_raw[:, -1:]
-    prev_slice = lax.ppermute(last_slice, "depth", up_d)
-    next_slice = lax.ppermute(first_slice, "depth", [(j, i) for i, j in up_d])
-    prev_row = lax.ppermute(last_row, "rows", up_r)
-    next_row = lax.ppermute(first_row, "rows", [(j, i) for i, j in up_r])
-    prev_slice = jnp.where(depth_at > 0, prev_slice, first_slice)
-    next_slice = jnp.where(depth_at < depth_count - 1, next_slice, last_slice)
-    prev_row = jnp.where(rows_at > 0, prev_row, first_row)
-    next_row = jnp.where(rows_at < rows_count - 1, next_row, last_row)
-    zhalo = jnp.concatenate([prev_slice, next_slice], axis=0).astype(jnp.float32)
-    rhalo = jnp.concatenate([prev_row, next_row], axis=1).astype(jnp.float32)
-    return zhalo, rhalo
+    return jnp.stack(
+        [
+            depth_at > 0,
+            depth_at < lax.axis_size("depth") - 1,
+            rows_at > 0,
+            rows_at < lax.axis_size("rows") - 1,
+        ]
+    ).astype(jnp.int32)
 
 
 def local(density_raw, colour_raw, target, slab_rank):
@@ -231,8 +244,9 @@
     tiles, per_tile, chunk_rows = chunking(rows_dev, width, depth_count)
     partial_value = forward_partial(density_raw, colour_raw, step, depth_count)
     partial_value, after_forward = lax.optimization_barrier((partial_value, density_raw))
-    zhalo, rhalo = halos(after_forward)
+    zprev, znext = depth_halos(after_forward)
     received = lax.all_to_all(partial_value, "depth", 0, 0, tiled=True)
+    received, zprev, znext = lax.optimization_barrier((received, zprev, znext))
     position = lax.axis_index("depth")
     target_piece = lax.dynamic_slice(
         target,
@@ -240,8 +254,10 @@
         (3, chunk_rows, lanes),
     )
     answers = composite(received, slab_rank, target_piece, float(slices_total))
+    answers, after_composite = lax.optimization_barrier((answers, density_raw))
+    rprev, rnext = row_halos(after_composite)
     returned = lax.all_to_all(answers, "depth", 0, 0, tiled=True)
-    smooth = smooth_term(density_raw, zhalo, rhalo)
+    smooth = smooth_term(density_raw, edge_flags(), zprev, znext, rprev, rnext)
     return backward_grads(density_raw, colour_raw, returned, smooth, step, slices_total)
 
 

time: 51.2 us -> 56.3 us (1.100)
  local copies, waits for them, and re-layouts: 0.95 us -> 3.58 us
  starting transfers between devices: 23.8 us -> 26.1 us
  other arithmetic: 4.04 us -> 2.58 us
  waiting for transfers between devices: 1.92 us -> 2.52 us
  Pallas kernels: 19.1 us -> 19.7 us
    ppermute x4, waiting for transfers between devices: 0.01 us -> 2.24 us  [the longest x1 0.92 us: row_halos(): prev_row = lax.ppermute(density_raw[:, -1:], 'rows', up)]
    ppermute x4, starting transfers between devices: 11.1 us -> 13.1 us  [the longest x1 4.85 us: row_halos(): next_row = lax.ppermute(density_raw[:, :1], 'rows', [(j, i) for i, j in up])]
    slice x2, local copies, waits for them, and re-layouts: 0.22 us -> 2.19 us  [the longest x1 1.41 us: row_halos(): next_row = lax.ppermute(density_raw[:, :1], 'rows', [(j, i) for i, j in up])]
    all_to_all x1, waiting for transfers between devices: 1.91 us -> 0.01 us  [local(): returned = lax.all_to_all(answers, 'depth', 0, 0, tiled=True)]
    convert_element_type x2 -> x1, other arithmetic: 1.66 us -> 0.61 us  [edge_flags(): return jnp.stack([depth_at > 0, depth_at < lax.axis_size('depth') - 1, ro...]
    unnamed x6 -> x12, local copies, waits for them, and re-layouts: 0.7 us -> 1.36 us
    pallas_call x1, Pallas kernels: 4.03 us -> 4.66 us  [smooth_term(): pl.pallas_call(smooth_kernel, grid=(width // block,), in_specs=[pl.BlockS...]
  transfers between devices with their start and end apart: 6 -> 6, of which waited for: 1 -> 4; matrix products, arithmetic and copies ran while one was open for 8% -> 5% of each run, Pallas kernels for 8% -> 8%
where the time goes in v10:
time: 56.3 us; the launch traced here: 55.2 us
  starting transfers between devices  26.1 us (46%)
  Pallas kernels  19.7 us (35%)
  local copies, waits for them, and re-layouts  3.58 us (6%)
  other arithmetic  2.58 us (5%)
  waiting for transfers between devices  2.52 us (4%)
  between operations  0.76 us (1%)
    pallas_call x1, Pallas kernels, backward_grads(): pl.pallas_call(functools.partial(backward_kernel, step=step, slices_total...  9.89 us
    all_to_all x1, starting transfers between devices, local(): returned = lax.all_to_all(answers, 'depth', 0, 0, tiled=True)  6.6 us
    all_to_all x1, starting transfers between devices, local(): received = lax.all_to_all(partial_value, 'depth', 0, 0, tiled=True)  6.38 us
    pallas_call x1, Pallas kernels, forward_partial(): pl.pallas_call(functools.partial(forward_kernel, step=step), grid=(width...  5.12 us
    ppermute x1, starting transfers between devices, row_halos(): next_row = lax.ppermute(density_raw[:, :1], 'rows', [(j, i) for i, j in up])  4.85 us
    pallas_call x1, Pallas kernels, smooth_term(): pl.pallas_call(smooth_kernel, grid=(width // block,), in_specs=[pl.BlockS...  4.66 us
    ppermute x1, starting transfers between devices, depth_halos(): prev_slice = lax.ppermute(density_raw[-1:], 'depth', up)  4 us
    ppermute x1, starting transfers between devices, row_halos(): prev_row = lax.ppermute(density_raw[:, -1:], 'rows', up)  3.02 us
  transfers between devices with their start and end apart: 6, of which 4 were waited for; matrix products, arithmetic and copies ran while one was open for 5% of the time, Pallas kernels for 8%

profile of v10, /device:TPU:1, one launch (start us, length us, event | category | flops | bytes accessed | tf_op | source)
XLA Modules:
  0.0 55.2 jit_solution(4573398046389110620)
XLA Ops:
  0.6 0.0 copy-start.5
  0.6 5.1 %shard_map.59 = f32[8,4,16,128]{3,2,1,0:T(8,128)} custom-call(bf16[32,16,1024]{2,1,0:T(8,128)(2,1)} %d_ref.5, bf16[3,32,16,1024]{3,2,1,0:T(8,128)(2,1)} %c_ref.3), custom_call_target="tpu_custom_call" | custom-call | tf_op jit(solution)/shard_map/pallas_call | solution.py:147
  5.8 6.4 %all-to-all-start = ((f32[8,4,16,128]{3,2,1,0:T(8,128)}), f32[8,4,16,128]{3,2,1,0:T(8,128)S(1)}, u32[]{:S(2)}, u32[]{:S(2)}) async-start(f32[8,4,16,128]{3,2,1,0:T(8,128)} %shard_map.59), calls=%async_computation | async-start | bytes 524288 | tf_op jit(solution)/shard_map/all_to_all | solution.py:248
  12.1 0.8 %fusion.6 = (bf16[1,16,1024]{2,1,0:T(8,128)(2,1)S(1)}, bf16[1,16,1024]{2,1,0:T(8,128)(2,1)S(1)}) fusion(bf16[32,16,1024]{2,1,0:T(8,128)(2,1)} %d_ref.5), kind=kLoop, calls=%fused_computation.20 | loop fusion | bytes 131072 | tf_op jit(solution)/shard_map/slice | solution.py:214
  12.9 1.3 %collective-permute-start.1 = (bf16[1,16,1024]{2,1,0:T(8,128)(2,1)S(1)}, bf16[1,16,1024]{2,1,0:T(8,128)(2,1)S(1)}, u32[]{:S(2)}, u32[]{:S(2)}) collective-permute-start(bf16[1,16,1024]{2,1,0:T(8,128)(2,1)S(1)} %get-tuple-element.22), channel_id=1, source_target_pairs={{4,0},{8,4},{12,8},{16,12},{20,16},{24,20},{28,24},{5,1},{9,5},{13... | collective-permute-start | bytes 98312 | tf_op jit(solution)/shard_map/ppermute | solution.py:214
  14.2 4.0 %collective-permute-start = (bf16[1,16,1024]{2,1,0:T(8,128)(2,1)S(1)}, bf16[1,16,1024]{2,1,0:T(8,128)(2,1)S(1)}, u32[]{:S(2)}, u32[]{:S(2)}) collective-permute-start(bf16[1,16,1024]{2,1,0:T(8,128)(2,1)S(1)} %get-tuple-element.23), channel_id=1, source_target_pairs={{0,4},{4,8},{8,12},{12,16},{16,20},{20,24},{24,28},{1,5},{5,9},{9,... | collective-permute-start | bytes 98312 | tf_op jit(solution)/shard_map/ppermute | solution.py:213
  18.2 0.0 copy-done.5
  18.2 0.1 compare_convert_fusion
  18.3 0.0 collective-permute-done.1.znext_ref
  18.3 0.0 copy-start.3
  18.3 0.9 %collective-permute-done.zprev_ref = bf16[1,16,1024]{2,1,0:T(8,128)(2,1)S(1)} collective-permute-done((bf16[1,16,1024]{2,1,0:T(8,128)(2,1)S(1)}, bf16[1,16,1024]{2,1,0:T(8,128)(2,1)S(1)}, u32[]{:S(2)}, u32[]{:S(2)}) %collective-permute-start) | collective-permute-done | bytes 32800 | tf_op jit(solution)/shard_map/ppermute | solution.py:213
  19.2 0.0 copy-start.4
  19.2 0.3 all-to-all-done
  19.5 0.1 multiply_reduce_fusion.1
  19.8 0.2 multiply_reduce_fusion
  19.9 0.8 %dynamic-slice_subtract_fusion = f32[3,16,128]{2,1,0:T(8,128)S(1)} fusion(f32[3,16,128]{2,1,0:T(8,128)S(1)} %get-tuple-element.18, f32[3,16,1024]{2,1,0:T(8,128)} %param.6, s32[]{:T(128)S(6)} %select_n.11), kind=kLoop, calls=%fused_computation.14 | loop fusion | flops 6144 | bytes 73732 | tf_op jit(solution)/shard_map/sub | solution.py:203
  20.7 0.1 multiply_reduce_fusion.3
  20.8 0.7 %pad_maximum_fusion = f32[8,4,16,128]{3,2,1,0:T(8,128)} fusion(f32[8,1,16,128]{3,2,1,0:T(8,128)S(1)} %fusion.2, f32[8,3,16,128]{3,2,1,0:T(8,128)S(1)} %get-tuple-element.24), kind=kLoop, calls=%fused_computation.2 | loop fusion | flops 65536 | bytes 524288 | tf_op jit(solution)/shard_map/concatenate | solution.py:207
  21.5 6.6 %all-to-all-start.1 = ((f32[8,4,16,128]{3,2,1,0:T(8,128)}), f32[8,4,16,128]{3,2,1,0:T(8,128)S(1)}, u32[]{:S(2)}, u32[]{:S(2)}) async-start(f32[8,4,16,128]{3,2,1,0:T(8,128)} %pad_maximum_fusion), calls=%async_computation.1 | async-start | bytes 524288 | tf_op jit(solution)/shard_map/all_to_all | solution.py:259
  28.1 1.4 %fusion.5 = (bf16[32,1,1024]{2,1,0:T(2,128)(2,1)S(1)}, bf16[32,1,1024]{2,1,0:T(2,128)(2,1)S(1)}) fusion(bf16[32,16,1024]{2,1,0:T(8,128)(2,1)} %d_ref.5), kind=kLoop, calls=%fused_computation.19 | loop fusion | bytes 262144 | tf_op jit(solution)/shard_map/slice | solution.py:222
  29.5 0.0 copy-done.3
  29.5 0.0 copy-done.4
  29.5 4.9 %collective-permute-start.3 = (bf16[32,1,1024]{2,1,0:T(2,128)(2,1)S(1)}, bf16[32,1,1024]{2,1,0:T(2,128)(2,1)S(1)}, u32[]{:S(2)}, u32[]{:S(2)}) collective-permute-start(bf16[32,1,1024]{2,1,0:T(2,128)(2,1)S(1)} %get-tuple-element.20), channel_id=1, source_target_pairs={{1,0},{2,1},{3,2},{5,4},{6,5},{7,6},{9,8},{10,9},{11,10},{13,12},{... | collective-permute-start | bytes 196616 | tf_op jit(solution)/shard_map/ppermute | solution.py:222
  34.4 3.0 %collective-permute-start.2 = (bf16[32,1,1024]{2,1,0:T(2,128)(2,1)S(1)}, bf16[32,1,1024]{2,1,0:T(2,128)(2,1)S(1)}, u32[]{:S(2)}, u32[]{:S(2)}) collective-permute-start(bf16[32,1,1024]{2,1,0:T(2,128)(2,1)S(1)} %get-tuple-element.21), channel_id=1, source_target_pairs={{0,1},{1,2},{2,3},{4,5},{5,6},{6,7},{8,9},{9,10},{10,11},{12,13},{... | collective-permute-start | bytes 196616 | tf_op jit(solution)/shard_map/ppermute | solution.py:221
  37.4 0.6 %add_convert_fusion.flags_ref = s32[4]{0:T(128)} fusion(pred[1]{0:T(512)(128)(4,1)} %bitcast.8, pred[1]{0:T(512)(128)(4,1)} %bitcast.7, pred[1]{0:T(512)(128)(4,1)} %bitcast.6, pred[1]{0:T(512)(128)(4,1)} %bitcast.5), kind=kLoop, calls=%fused_computation.17 | loop fusion | flops 16 | bytes 20 | tf_op jit(solution)/shard_map/convert_element_type | solution.py:236
  38.0 0.4 collective-permute-done.3.rnext_ref
  38.4 0.0 copy-start.1
  38.4 0.9 %collective-permute-done.2.rprev_ref = bf16[32,1,1024]{2,1,0:T(2,128)(2,1)S(1)} collective-permute-done((bf16[32,1,1024]{2,1,0:T(2,128)(2,1)S(1)}, bf16[32,1,1024]{2,1,0:T(2,128)(2,1)S(1)}, u32[]{:S(2)}, u32[]{:S(2)}) %collective-permute-start.2) | collective-permute-done | bytes 65568 | tf_op jit(solution)/shard_map/ppermute | solution.py:221
  39.3 0.0 copy-done.1
  39.3 0.0 copy-start.2
  39.3 0.7 %copy-done.2 = bf16[32,1,1024]{2,1,0:T(2,128)(2,1)} copy-done((bf16[32,1,1024]{2,1,0:T(2,128)(2,1)}, bf16[32,1,1024]{2,1,0:T(2,128)(2,1)S(1)}, u32[]{:S(2)}) %copy-start.2) | copy-done | bytes 65560
  40.0 4.7 %shard_map.60.smooth_ref = f32[32,16,1024]{2,1,0:T(8,128)} custom-call(s32[4]{0:T(128)} %add_convert_fusion.flags_ref, bf16[32,16,1024]{2,1,0:T(8,128)(2,1)} %d_ref.5, bf16[1,16,1024]{2,1,0:T(8,128)(2,1)} %copy-done.4, bf16[1,16,1024]{2,1,0:T(8,128)(2,1)} %copy-done.3, bf16[32,1,1024]{2,1,0:T(2,128)(2,1)} %copy-done.2, bf16[32,1,1024]{2,1,0:T(2,128)(2,1)} %copy-done.1), custom_call_target="tpu_custom_call" | custom-call | tf_op jit(solution)/shard_map/pallas_call | solution.py:168
  44.7 0.0 all-to-all-done.1.ans_ref
  44.7 0.0 copy-start
  44.7 0.7 %copy-done = f32[8,4,16,128]{3,2,1,0:T(8,128)} copy-done((f32[8,4,16,128]{3,2,1,0:T(8,128)}, f32[8,4,16,128]{3,2,1,0:T(8,128)S(1)}, u32[]{:S(2)}) %copy-start) | copy-done | bytes 262168
  45.4 9.9 %shard_map.61 = (f32[32,16,1024]{2,1,0:T(8,128)}, f32[3,32,16,1024]{3,2,1,0:T(8,128)}) custom-call(bf16[32,16,1024]{2,1,0:T(8,128)(2,1)} %d_ref.5, bf16[3,32,16,1024]{3,2,1,0:T(8,128)(2,1)} %c_ref.3, f32[8,4,16,128]{3,2,1,0:T(8,128)} %copy-done, f32[32,16,1024]{2,1,0:T(8,128)} %shard_map.60.smooth_ref), custom_call_target="tpu_custom_call", output_to_operand_aliasing={{0}: (3, {})} | custom-call | tf_op jit(solution)/shard_map/pallas_call | solution.py:183
  (5 shorter events, 0.1 us)
Async XLA Ops:
  0.6 17.6 %copy-start.5 = (s32[8]{0:T(128)S(1)}, s32[8]{0:T(128)}, u32[]{:S(2)}) copy-start(s32[8]{0:T(128)} %param.7) | copy-start | bytes 100
  5.8 13.7 %all-to-all-start = ((f32[8,4,16,128]{3,2,1,0:T(8,128)}), f32[8,4,16,128]{3,2,1,0:T(8,128)S(1)}, u32[]{:S(2)}, u32[]{:S(2)}) async-start(f32[8,4,16,128]{3,2,1,0:T(8,128)} %shard_map.59), calls=%async_computation | async-start | bytes 524288 | tf_op jit(solution)/shard_map/all_to_all | solution.py:248
  12.9 5.4 %collective-permute-start.1 = (bf16[1,16,1024]{2,1,0:T(8,128)(2,1)S(1)}, bf16[1,16,1024]{2,1,0:T(8,128)(2,1)S(1)}, u32[]{:S(2)}, u32[]{:S(2)}) collective-permute-start(bf16[1,16,1024]{2,1,0:T(8,128)(2,1)S(1)} %get-tuple-element.22), channel_id=1, source_target_pairs={{4,0},{8,4},{12,8},{16,12},{20,16},{24,20},{28,24},{5,1},{9,5},{13... | collective-permute-start | bytes 98312 | tf_op jit(solution)/shard_map/ppermute | solution.py:214
  14.2 5.0 %collective-permute-start = (bf16[1,16,1024]{2,1,0:T(8,128)(2,1)S(1)}, bf16[1,16,1024]{2,1,0:T(8,128)(2,1)S(1)}, u32[]{:S(2)}, u32[]{:S(2)}) collective-permute-start(bf16[1,16,1024]{2,1,0:T(8,128)(2,1)S(1)} %get-tuple-element.23), channel_id=1, source_target_pairs={{0,4},{4,8},{8,12},{12,16},{16,20},{20,24},{24,28},{1,5},{5,9},{9,... | collective-permute-start | bytes 98312 | tf_op jit(solution)/shard_map/ppermute | solution.py:213
  18.3 11.2 %copy-start.3 = (bf16[1,16,1024]{2,1,0:T(8,128)(2,1)}, bf16[1,16,1024]{2,1,0:T(8,128)(2,1)S(1)}, u32[]{:S(2)}) copy-start(bf16[1,16,1024]{2,1,0:T(8,128)(2,1)S(1)} %collective-permute-done.1.znext_ref) | copy-start | bytes 98308
  19.2 10.3 %copy-start.4 = (bf16[1,16,1024]{2,1,0:T(8,128)(2,1)}, bf16[1,16,1024]{2,1,0:T(8,128)(2,1)S(1)}, u32[]{:S(2)}) copy-start(bf16[1,16,1024]{2,1,0:T(8,128)(2,1)S(1)} %collective-permute-done.zprev_ref) | copy-start | bytes 98308
  21.5 23.2 %all-to-all-start.1 = ((f32[8,4,16,128]{3,2,1,0:T(8,128)}), f32[8,4,16,128]{3,2,1,0:T(8,128)S(1)}, u32[]{:S(2)}, u32[]{:S(2)}) async-start(f32[8,4,16,128]{3,2,1,0:T(8,128)} %pad_maximum_fusion), calls=%async_computation.1 | async-start | bytes 524288 | tf_op jit(solution)/shard_map/all_to_all | solution.py:259
  29.5 8.9 %collective-permute-start.3 = (bf16[32,1,1024]{2,1,0:T(2,128)(2,1)S(1)}, bf16[32,1,1024]{2,1,0:T(2,128)(2,1)S(1)}, u32[]{:S(2)}, u32[]{:S(2)}) collective-permute-start(bf16[32,1,1024]{2,1,0:T(2,128)(2,1)S(1)} %get-tuple-element.20), channel_id=1, source_target_pairs={{1,0},{2,1},{3,2},{5,4},{6,5},{7,6},{9,8},{10,9},{11,10},{13,12},{... | collective-permute-start | bytes 196616 | tf_op jit(solution)/shard_map/ppermute | solution.py:222
  34.4 5.0 %collective-permute-start.2 = (bf16[32,1,1024]{2,1,0:T(2,128)(2,1)S(1)}, bf16[32,1,1024]{2,1,0:T(2,128)(2,1)S(1)}, u32[]{:S(2)}, u32[]{:S(2)}) collective-permute-start(bf16[32,1,1024]{2,1,0:T(2,128)(2,1)S(1)} %get-tuple-element.21), channel_id=1, source_target_pairs={{0,1},{1,2},{2,3},{4,5},{5,6},{6,7},{8,9},{9,10},{10,11},{12,13},{... | collective-permute-start | bytes 196616 | tf_op jit(solution)/shard_map/ppermute | solution.py:221
  38.4 0.9 %copy-start.1 = (bf16[32,1,1024]{2,1,0:T(2,128)(2,1)}, bf16[32,1,1024]{2,1,0:T(2,128)(2,1)S(1)}, u32[]{:S(2)}) copy-start(bf16[32,1,1024]{2,1,0:T(2,128)(2,1)S(1)} %collective-permute-done.3.rnext_ref) | copy-start | bytes 196612
  39.3 0.7 %copy-start.2 = (bf16[32,1,1024]{2,1,0:T(2,128)(2,1)}, bf16[32,1,1024]{2,1,0:T(2,128)(2,1)S(1)}, u32[]{:S(2)}) copy-start(bf16[32,1,1024]{2,1,0:T(2,128)(2,1)S(1)} %collective-permute-done.2.rprev_ref) | copy-start | bytes 196612
  44.7 0.7 %copy-start = (f32[8,4,16,128]{3,2,1,0:T(8,128)}, f32[8,4,16,128]{3,2,1,0:T(8,128)S(1)}, u32[]{:S(2)}) copy-start(f32[8,4,16,128]{3,2,1,0:T(8,128)S(1)} %all-to-all-done.1.ans_ref) | copy-start | bytes 786436

commit v11 on v9

--- a/solution.py
+++ b/solution.py
@@ -12,6 +12,8 @@
 lanes = 128
 forward_subs = 4
 backward_subs = 2
+forward_unroll = 32
+backward_unroll = 8
 
 
 log2e = 1.4426950408889634
@@ -52,7 +54,7 @@
 
         zero = jnp.zeros(shape, jnp.float32)
         one = jnp.ones(shape, jnp.float32)
-        n, _, e0, e1, e2 = lax.fori_loop(0, slices, body, (zero, one, zero, zero, zero), unroll=4)
+        n, _, e0, e1, e2 = lax.fori_loop(0, slices, body, (zero, one, zero, zero, zero), unroll=forward_unroll)
         values = (e0, e1, e2, jnp.exp2(n))
         for g in range(per_tile):
             for c in range(4):
@@ -127,7 +129,7 @@
 
         zero = jnp.zeros(shape, jnp.float32)
         one = jnp.ones(shape, jnp.float32)
-        lax.fori_loop(0, slices, body, (zero, one, zero, zero, zero), unroll=2)
+        lax.fori_loop(0, slices, body, (zero, one, zero, zero, zero), unroll=backward_unroll)
 
 
 def forward_partial(density, colour_raw, step, depth_count):

time: 51.2 us -> 49.5 us (0.967)
  Pallas kernels: 19.1 us -> 17.4 us
    pallas_call x1, Pallas kernels: 9.89 us -> 8.93 us  [backward_grads(): pl.pallas_call(functools.partial(backward_kernel, step=step, slices_total...]
    pallas_call x1, Pallas kernels: 5.19 us -> 4.43 us  [forward_partial(): pl.pallas_call(functools.partial(forward_kernel, step=step), grid=(width...]
  transfers between devices with their start and end apart: 6 -> 6, of which waited for: 1 -> 1; matrix products, arithmetic and copies ran while one was open for 8% -> 9% of each run, Pallas kernels for 8% -> 8%
where the time goes in v11:
time: 49.5 us; the launch traced here: 48.9 us
  starting transfers between devices  23.8 us (48%)
  Pallas kernels  17.4 us (35%)
  other arithmetic  4.04 us (8%)
  waiting for transfers between devices  1.92 us (4%)
  local copies, waits for them, and re-layouts  0.95 us (2%)
  between operations  0.78 us (2%)
    pallas_call x1, Pallas kernels, backward_grads(): pl.pallas_call(functools.partial(backward_kernel, step=step, slices_total...  8.93 us
    all_to_all x1, starting transfers between devices, local(): received = lax.all_to_all(partial_value, 'depth', 0, 0, tiled=True)  6.38 us
    all_to_all x1, starting transfers between devices, local(): returned = lax.all_to_all(answers, 'depth', 0, 0, tiled=True)  6.34 us
    ppermute x1, starting transfers between devices, halos(): prev_row = lax.ppermute(last_row, 'rows', up_r)  4.52 us
    pallas_call x1, Pallas kernels, forward_partial(): pl.pallas_call(functools.partial(forward_kernel, step=step), grid=(width...  4.43 us
    pallas_call x1, Pallas kernels, smooth_term(): pl.pallas_call(smooth_kernel, grid=(width // block,), in_specs=[slab, pl....  4.03 us
    ppermute x1, starting transfers between devices, halos(): prev_slice = lax.ppermute(last_slice, 'depth', up_d)  3.36 us
    ppermute x1, starting transfers between devices, halos(): next_row = lax.ppermute(first_row, 'rows', [(j, i) for i, j in up_r])  1.92 us
  transfers between devices with their start and end apart: 6, of which 1 were waited for; matrix products, arithmetic and copies ran while one was open for 9% of the time, Pallas kernels for 8%

profile of v11, /device:TPU:1, one launch (start us, length us, event | category | flops | bytes accessed | tf_op | source)
XLA Modules:
  0.0 48.9 jit_solution(11141681623070079528)
XLA Ops:
  0.6 0.0 copy-start
  0.6 0.0 copy-start.2
  0.7 4.4 %shard_map.59 = f32[8,4,16,128]{3,2,1,0:T(8,128)} custom-call(bf16[32,16,1024]{2,1,0:T(8,128)(2,1)} %d_ref.5, bf16[3,32,16,1024]{3,2,1,0:T(8,128)(2,1)} %c_ref.3), custom_call_target="tpu_custom_call" | custom-call | tf_op jit(solution)/shard_map/pallas_call | solution.py:139
  5.1 6.4 %all-to-all-start = ((f32[8,4,16,128]{3,2,1,0:T(8,128)}), f32[8,4,16,128]{3,2,1,0:T(8,128)S(1)}, u32[]{:S(2)}, u32[]{:S(2)}) async-start(f32[8,4,16,128]{3,2,1,0:T(8,128)} %shard_map.59), calls=%async_computation | async-start | bytes 524288 | tf_op jit(solution)/shard_map/all_to_all | solution.py:237
  11.5 0.0 copy-done
  11.5 3.4 %collective-permute-start = (bf16[1,16,1024]{2,1,0:T(8,128)(2,1)S(1)}, bf16[1,16,1024]{2,1,0:T(8,128)(2,1)S(1)}, u32[]{:S(2)}, u32[]{:S(2)}) collective-permute-start(bf16[1,16,1024]{2,1,0:T(8,128)(2,1)S(1)} %get-tuple-element.16), channel_id=1, source_target_pairs={{0,4},{4,8},{8,12},{12,16},{16,20},{20,24},{24,28},{1,5},{5,9},{9,... | collective-permute-start | bytes 98312 | tf_op jit(solution)/shard_map/ppermute | solution.py:215
  14.8 1.3 %collective-permute-start.1 = (bf16[1,16,1024]{2,1,0:T(8,128)(2,1)S(1)}, bf16[1,16,1024]{2,1,0:T(8,128)(2,1)S(1)}, u32[]{:S(2)}, u32[]{:S(2)}) collective-permute-start(bf16[1,16,1024]{2,1,0:T(8,128)(2,1)S(1)} %get-tuple-element.17), channel_id=1, source_target_pairs={{4,0},{8,4},{12,8},{16,12},{20,16},{24,20},{28,24},{5,1},{9,5},{13... | collective-permute-start | bytes 98312 | tf_op jit(solution)/shard_map/ppermute | solution.py:216
  16.1 0.2 fusion.5
  16.4 4.5 %collective-permute-start.2 = (bf16[32,1,1024]{2,1,0:T(2,128)(2,1)S(1)}, bf16[32,1,1024]{2,1,0:T(2,128)(2,1)S(1)}, u32[]{:S(2)}, u32[]{:S(2)}) collective-permute-start(bf16[32,1,1024]{2,1,0:T(2,128)(2,1)S(1)} %get-tuple-element.12), channel_id=1, source_target_pairs={{0,1},{1,2},{2,3},{4,5},{5,6},{6,7},{8,9},{9,10},{10,11},{12,13},{... | collective-permute-start | bytes 196616 | tf_op jit(solution)/shard_map/ppermute | solution.py:217
  20.9 1.9 %collective-permute-start.3 = (bf16[32,1,1024]{2,1,0:T(2,128)(2,1)S(1)}, bf16[32,1,1024]{2,1,0:T(2,128)(2,1)S(1)}, u32[]{:S(2)}, u32[]{:S(2)}) collective-permute-start(bf16[32,1,1024]{2,1,0:T(2,128)(2,1)S(1)} %get-tuple-element.13), channel_id=1, source_target_pairs={{1,0},{2,1},{3,2},{5,4},{6,5},{7,6},{9,8},{10,9},{11,10},{13,12},{... | collective-permute-start | bytes 196616 | tf_op jit(solution)/shard_map/ppermute | solution.py:218
  22.8 0.0 copy-done.2
  22.8 0.1 compare_convert_fusion
  22.9 0.0 collective-permute-done
  22.9 0.0 collective-permute-done.1
  22.9 0.0 all-to-all-done
  23.0 0.1 multiply_reduce_fusion.1
  23.2 0.2 multiply_reduce_fusion
  23.3 0.8 %dynamic-slice_subtract_fusion = f32[3,16,128]{2,1,0:T(8,128)S(1)} fusion(f32[3,16,128]{2,1,0:T(8,128)S(1)} %get-tuple-element.8, f32[3,16,1024]{2,1,0:T(8,128)} %param.6, s32[]{:T(128)S(6)} %select_n.39), kind=kLoop, calls=%fused_computation.20 | loop fusion | flops 6144 | bytes 73732 | tf_op jit(solution)/shard_map/sub | solution.py:197
  24.1 0.1 multiply_reduce_fusion.3
  24.2 0.7 %pad_maximum_fusion = f32[8,4,16,128]{3,2,1,0:T(8,128)} fusion(f32[8,1,16,128]{3,2,1,0:T(8,128)S(1)} %fusion.2, f32[8,3,16,128]{3,2,1,0:T(8,128)S(1)} %get-tuple-element.18), kind=kLoop, calls=%fused_computation.2 | loop fusion | flops 65536 | bytes 524288 | tf_op jit(solution)/shard_map/concatenate | solution.py:201
  24.9 6.3 %all-to-all-start.1 = ((f32[8,4,16,128]{3,2,1,0:T(8,128)}), f32[8,4,16,128]{3,2,1,0:T(8,128)S(1)}, u32[]{:S(2)}, u32[]{:S(2)}) async-start(f32[8,4,16,128]{3,2,1,0:T(8,128)} %pad_maximum_fusion), calls=%async_computation.1 | async-start | bytes 524288 | tf_op jit(solution)/shard_map/all_to_all | solution.py:245
  31.3 0.7 %maximum_convert_fusion.1.zhalo_ref = f32[2,16,1024]{2,1,0:T(8,128)} fusion(bf16[1,16,1024]{2,1,0:T(8,128)(2,1)S(1)} %get-tuple-element.15, bf16[1,16,1024]{2,1,0:T(8,128)(2,1)S(1)} %get-tuple-element.14), kind=kLoop, calls=%fused_computation.10 | loop fusion | flops 65536 | bytes 196608 | tf_op jit(solution)/shard_map/convert_element_type | solution.py:223
  31.9 0.0 collective-permute-done.2
  31.9 0.0 collective-permute-done.3
  31.9 0.4 broadcast_select_fusion.1
  32.3 1.0 %maximum_convert_fusion.rhalo_ref = f32[32,2,1024]{2,1,0:T(2,128)} fusion(bf16[32,1,1024]{2,1,0:T(2,128)(2,1)S(1)} %get-tuple-element.11, bf16[32,1,1024]{2,1,0:T(2,128)(2,1)S(1)} %get-tuple-element.10), kind=kLoop, calls=%fused_computation.9 | loop fusion | flops 262144 | bytes 393216 | tf_op jit(solution)/shard_map/convert_element_type | solution.py:224
  33.3 4.0 %shard_map.60.smooth_ref = f32[32,16,1024]{2,1,0:T(8,128)} custom-call(bf16[32,16,1024]{2,1,0:T(8,128)(2,1)} %d_ref.5, f32[2,16,1024]{2,1,0:T(8,128)} %maximum_convert_fusion.1.zhalo_ref, f32[32,2,1024]{2,1,0:T(2,128)} %maximum_convert_fusion.rhalo_ref), custom_call_target="tpu_custom_call" | custom-call | tf_op jit(solution)/shard_map/pallas_call | solution.py:158
  37.4 1.9 %all-to-all-done.1.ans_ref = f32[8,4,16,128]{3,2,1,0:T(8,128)S(1)} async-done(((f32[8,4,16,128]{3,2,1,0:T(8,128)}), f32[8,4,16,128]{3,2,1,0:T(8,128)S(1)}, u32[]{:S(2)}, u32[]{:S(2)}) %all-to-all-start.1) | async-done | bytes 262176 | tf_op jit(solution)/shard_map/all_to_all | solution.py:245
  39.3 0.0 copy-start.1
  39.3 0.7 %copy-done.1 = f32[8,4,16,128]{3,2,1,0:T(8,128)} copy-done((f32[8,4,16,128]{3,2,1,0:T(8,128)}, f32[8,4,16,128]{3,2,1,0:T(8,128)S(1)}, u32[]{:S(2)}) %copy-start.1) | copy-done | bytes 262168
  40.0 8.9 %shard_map.61 = (f32[32,16,1024]{2,1,0:T(8,128)}, f32[3,32,16,1024]{3,2,1,0:T(8,128)}) custom-call(bf16[32,16,1024]{2,1,0:T(8,128)(2,1)} %d_ref.5, bf16[3,32,16,1024]{3,2,1,0:T(8,128)(2,1)} %c_ref.3, f32[8,4,16,128]{3,2,1,0:T(8,128)} %copy-done.1, f32[32,16,1024]{2,1,0:T(8,128)} %shard_map.60.smooth_ref), custom_call_target="tpu_custom_call", output_to_operand_aliasing={{0}: (3, {})} | custom-call | tf_op jit(solution)/shard_map/pallas_call | solution.py:177
  (7 shorter events, 0.1 us)
Async XLA Ops:
  0.6 10.8 %copy-start = (bf16[32,16,1024]{2,1,0:T(8,128)(2,1)S(1)}, bf16[32,16,1024]{2,1,0:T(8,128)(2,1)}, u32[]{:S(2)}) copy-start(bf16[32,16,1024]{2,1,0:T(8,128)(2,1)} %d_ref.5) | copy-start | bytes 3145732
  0.6 22.2 %copy-start.2 = (s32[8]{0:T(128)S(1)}, s32[8]{0:T(128)}, u32[]{:S(2)}) copy-start(s32[8]{0:T(128)} %param.7) | copy-start | bytes 100
  5.1 17.8 %all-to-all-start = ((f32[8,4,16,128]{3,2,1,0:T(8,128)}), f32[8,4,16,128]{3,2,1,0:T(8,128)S(1)}, u32[]{:S(2)}, u32[]{:S(2)}) async-start(f32[8,4,16,128]{3,2,1,0:T(8,128)} %shard_map.59), calls=%async_computation | async-start | bytes 524288 | tf_op jit(solution)/shard_map/all_to_all | solution.py:237
  11.5 11.4 %collective-permute-start = (bf16[1,16,1024]{2,1,0:T(8,128)(2,1)S(1)}, bf16[1,16,1024]{2,1,0:T(8,128)(2,1)S(1)}, u32[]{:S(2)}, u32[]{:S(2)}) collective-permute-start(bf16[1,16,1024]{2,1,0:T(8,128)(2,1)S(1)} %get-tuple-element.16), channel_id=1, source_target_pairs={{0,4},{4,8},{8,12},{12,16},{16,20},{20,24},{24,28},{1,5},{5,9},{9,... | collective-permute-start | bytes 98312 | tf_op jit(solution)/shard_map/ppermute | solution.py:215
  14.8 8.1 %collective-permute-start.1 = (bf16[1,16,1024]{2,1,0:T(8,128)(2,1)S(1)}, bf16[1,16,1024]{2,1,0:T(8,128)(2,1)S(1)}, u32[]{:S(2)}, u32[]{:S(2)}) collective-permute-start(bf16[1,16,1024]{2,1,0:T(8,128)(2,1)S(1)} %get-tuple-element.17), channel_id=1, source_target_pairs={{4,0},{8,4},{12,8},{16,12},{20,16},{24,20},{28,24},{5,1},{9,5},{13... | collective-permute-start | bytes 98312 | tf_op jit(solution)/shard_map/ppermute | solution.py:216
  16.4 15.6 %collective-permute-start.2 = (bf16[32,1,1024]{2,1,0:T(2,128)(2,1)S(1)}, bf16[32,1,1024]{2,1,0:T(2,128)(2,1)S(1)}, u32[]{:S(2)}, u32[]{:S(2)}) collective-permute-start(bf16[32,1,1024]{2,1,0:T(2,128)(2,1)S(1)} %get-tuple-element.12), channel_id=1, source_target_pairs={{0,1},{1,2},{2,3},{4,5},{5,6},{6,7},{8,9},{9,10},{10,11},{12,13},{... | collective-permute-start | bytes 196616 | tf_op jit(solution)/shard_map/ppermute | solution.py:217
  20.9 11.0 %collective-permute-start.3 = (bf16[32,1,1024]{2,1,0:T(2,128)(2,1)S(1)}, bf16[32,1,1024]{2,1,0:T(2,128)(2,1)S(1)}, u32[]{:S(2)}, u32[]{:S(2)}) collective-permute-start(bf16[32,1,1024]{2,1,0:T(2,128)(2,1)S(1)} %get-tuple-element.13), channel_id=1, source_target_pairs={{1,0},{2,1},{3,2},{5,4},{6,5},{7,6},{9,8},{10,9},{11,10},{13,12},{... | collective-permute-start | bytes 196616 | tf_op jit(solution)/shard_map/ppermute | solution.py:218
  24.9 14.3 %all-to-all-start.1 = ((f32[8,4,16,128]{3,2,1,0:T(8,128)}), f32[8,4,16,128]{3,2,1,0:T(8,128)S(1)}, u32[]{:S(2)}, u32[]{:S(2)}) async-start(f32[8,4,16,128]{3,2,1,0:T(8,128)} %pad_maximum_fusion), calls=%async_computation.1 | async-start | bytes 524288 | tf_op jit(solution)/shard_map/all_to_all | solution.py:245
  39.3 0.7 %copy-start.1 = (f32[8,4,16,128]{3,2,1,0:T(8,128)}, f32[8,4,16,128]{3,2,1,0:T(8,128)S(1)}, u32[]{:S(2)}) copy-start(f32[8,4,16,128]{3,2,1,0:T(8,128)S(1)} %all-to-all-done.1.ans_ref) | copy-start | bytes 786436

commit v12 on v11

--- a/solution.py
+++ b/solution.py
@@ -187,18 +187,56 @@
     )(density, colour_raw, answers, smooth)
 
 
+def composite_kernel(rank_ref, parts_ref, target_ref, out_ref, front_ref, *, scale):
+    count = parts_ref.shape[0]
+    shape = parts_ref.shape[2:]
+    zero = jnp.zeros(shape, jnp.float32)
+
+    def forward(s, total):
+        acc = zero
+        for j in range(count):
+            acc = acc + jnp.where(rank_ref[j] < rank_ref[s], jnp.log2(parts_ref[j, 3]), 0.0)
+        front = jnp.exp2(acc)
+        front_ref[s] = front
+        return tuple(total[c] + front * parts_ref[s, c] for c in range(3))
+
+    total = lax.fori_loop(0, count, forward, (zero, zero, zero))
+    residual = [total[c] - target_ref[c] for c in range(3)]
+
+    def backward(s, carry):
+        behind = [zero, zero, zero]
+        for j in range(count):
+            later = rank_ref[j] > rank_ref[s]
+            for c in range(3):
+                behind[c] = behind[c] + jnp.where(later, front_ref[j] * parts_ref[j, c], 0.0)
+        front = front_ref[s]
+        passing = parts_ref[s, 3]
+        through = front * passing
+        mixed = residual[0] * (behind[0] / through)
+        mixed = mixed + residual[1] * (behind[1] / through)
+        mixed = mixed + residual[2] * (behind[2] / through)
+        scaled_behind = scale * (front * mixed)
+        folded = passing * scaled_behind
+        for c in range(3):
+            scaled = scale * (front * residual[c])
+            out_ref[s, c] = scaled
+            folded = folded + scaled * parts_ref[s, c]
+        out_ref[s, 3] = folded
+        return carry
+
+    lax.fori_loop(0, count, backward, 0)
+
+
 def composite(parts, slab_rank, target_piece, slices_total):
-    emitted, passing = (parts[:, :3], parts[:, 3])
-    earlier = (slab_rank[None, :] < slab_rank[:, None]).astype(jnp.float32)[:, :, None, None]
-    later = (slab_rank[None, :] > slab_rank[:, None]).astype(jnp.float32)[:, :, None, None, None]
-    front = jnp.exp(jnp.sum(earlier * jnp.log(passing)[None], axis=1))
-    weighted = front[:, None] * emitted
-    behind = jnp.sum(later * weighted[None], axis=1) / (front * passing)[:, None]
-    residual = jnp.sum(weighted, axis=0) - target_piece
-    scaled_residual = slices_total * (front[:, None] * residual[None])
-    scaled_behind = slices_total * (front * jnp.sum(residual[None] * behind, axis=1))
-    folded = jnp.sum(scaled_residual * emitted, axis=1) + passing * scaled_behind
-    return jnp.concatenate([scaled_residual, folded[:, None]], axis=1)
+    count = parts.shape[0]
+    vmem = pl.BlockSpec(memory_space=pltpu.VMEM)
+    return pl.pallas_call(
+        functools.partial(composite_kernel, scale=slices_total),
+        in_specs=[pl.BlockSpec(memory_space=pltpu.SMEM), vmem, vmem],
+        out_specs=vmem,
+        out_shape=jax.ShapeDtypeStruct(parts.shape, jnp.float32),
+        scratch_shapes=[pltpu.VMEM((count,) + parts.shape[2:], jnp.float32)],
+    )(slab_rank, parts, target_piece)
 
 
 def halos(density_raw):

time: 49.5 us -> 50.5 us (1.020)
  Pallas kernels: 17.4 us -> 19.6 us
  other arithmetic: 4.04 us -> 2.07 us
  local copies, waits for them, and re-layouts: 0.95 us -> 2.24 us
    pallas_call x0 -> x1, Pallas kernels: none -> 2.21 us  [composite(): pl.pallas_call(functools.partial(composite_kernel, scale=slices_total), i...]
    sub x1 -> x0, other arithmetic: 0.75 us -> none  [composite(): residual = jnp.sum(weighted, axis=0) - target_piece]
    concatenate x1 -> x0, other arithmetic: 0.73 us -> none  [composite(): return jnp.concatenate([scaled_residual, folded[:, None]], axis=1)]
    unnamed x6 -> x8, local copies, waits for them, and re-layouts: 0.7 us -> 1.41 us
    dynamic_slice x0 -> x1, local copies, waits for them, and re-layouts: none -> 0.61 us  [local(): lax.dynamic_slice(target, (0, position % per_tile * chunk_rows, position...]
  transfers between devices with their start and end apart: 6 -> 6, of which waited for: 1 -> 1; matrix products, arithmetic and copies ran while one was open for 9% -> 6% of each run, Pallas kernels for 8% -> 12%
where the time goes in v12:
time: 50.5 us; the launch traced here: 50 us
  starting transfers between devices  23.8 us (47%)
  Pallas kernels  19.6 us (39%)
  local copies, waits for them, and re-layouts  2.24 us (4%)
  other arithmetic  2.07 us (4%)
  waiting for transfers between devices  1.5 us (3%)
  between operations  0.74 us (1%)
    pallas_call x1, Pallas kernels, backward_grads(): pl.pallas_call(functools.partial(backward_kernel, step=step, slices_total...  8.93 us
    all_to_all x1, starting transfers between devices, local(): received = lax.all_to_all(partial_value, 'depth', 0, 0, tiled=True)  6.38 us
    all_to_all x1, starting transfers between devices, local(): returned = lax.all_to_all(answers, 'depth', 0, 0, tiled=True)  6.34 us
    ppermute x1, starting transfers between devices, halos(): prev_row = lax.ppermute(last_row, 'rows', up_r)  4.52 us
    pallas_call x1, Pallas kernels, forward_partial(): pl.pallas_call(functools.partial(forward_kernel, step=step), grid=(width...  4.44 us
    pallas_call x1, Pallas kernels, smooth_term(): pl.pallas_call(smooth_kernel, grid=(width // block,), in_specs=[slab, pl....  4.03 us
    ppermute x1, starting transfers between devices, halos(): prev_slice = lax.ppermute(last_slice, 'depth', up_d)  3.36 us
    pallas_call x1, Pallas kernels, composite(): pl.pallas_call(functools.partial(composite_kernel, scale=slices_total), i...  2.21 us
  transfers between devices with their start and end apart: 6, of which 1 were waited for; matrix products, arithmetic and copies ran while one was open for 6% of the time, Pallas kernels for 12%

profile of v12, /device:TPU:1, one launch (start us, length us, event | category | flops | bytes accessed | tf_op | source)
XLA Modules:
  0.0 50.0 jit_solution(18033350638267154220)
XLA Ops:
  0.6 0.0 copy-start
  0.6 0.0 copy-start.1
  0.7 4.4 %shard_map.59 = f32[8,4,16,128]{3,2,1,0:T(8,128)} custom-call(bf16[32,16,1024]{2,1,0:T(8,128)(2,1)} %d_ref.5, bf16[3,32,16,1024]{3,2,1,0:T(8,128)(2,1)} %c_ref.3), custom_call_target="tpu_custom_call" | custom-call | tf_op jit(solution)/shard_map/pallas_call | solution.py:139
  5.1 6.4 %all-to-all-start = ((f32[8,4,16,128]{3,2,1,0:T(8,128)}), f32[8,4,16,128]{3,2,1,0:T(8,128)S(1)}, u32[]{:S(2)}, u32[]{:S(2)}) async-start(f32[8,4,16,128]{3,2,1,0:T(8,128)} %shard_map.59), calls=%async_computation | async-start | bytes 524288 | tf_op jit(solution)/shard_map/all_to_all | solution.py:275
  11.5 0.0 copy-done.1
  11.5 3.4 %collective-permute-start = (bf16[1,16,1024]{2,1,0:T(8,128)(2,1)S(1)}, bf16[1,16,1024]{2,1,0:T(8,128)(2,1)S(1)}, u32[]{:S(2)}, u32[]{:S(2)}) collective-permute-start(bf16[1,16,1024]{2,1,0:T(8,128)(2,1)S(1)} %get-tuple-element.12), channel_id=1, source_target_pairs={{0,4},{4,8},{8,12},{12,16},{16,20},{20,24},{24,28},{1,5},{5,9},{9,... | collective-permute-start | bytes 98312 | tf_op jit(solution)/shard_map/ppermute | solution.py:253
  14.9 1.3 %collective-permute-start.1 = (bf16[1,16,1024]{2,1,0:T(8,128)(2,1)S(1)}, bf16[1,16,1024]{2,1,0:T(8,128)(2,1)S(1)}, u32[]{:S(2)}, u32[]{:S(2)}) collective-permute-start(bf16[1,16,1024]{2,1,0:T(8,128)(2,1)S(1)} %get-tuple-element.13), channel_id=1, source_target_pairs={{4,0},{8,4},{12,8},{16,12},{20,16},{24,20},{28,24},{5,1},{9,5},{13... | collective-permute-start | bytes 98312 | tf_op jit(solution)/shard_map/ppermute | solution.py:254
  16.2 0.2 fusion
  16.4 4.5 %collective-permute-start.2 = (bf16[32,1,1024]{2,1,0:T(2,128)(2,1)S(1)}, bf16[32,1,1024]{2,1,0:T(2,128)(2,1)S(1)}, u32[]{:S(2)}, u32[]{:S(2)}) collective-permute-start(bf16[32,1,1024]{2,1,0:T(2,128)(2,1)S(1)} %get-tuple-element.8), channel_id=1, source_target_pairs={{0,1},{1,2},{2,3},{4,5},{5,6},{6,7},{8,9},{9,10},{10,11},{12,13},{... | collective-permute-start | bytes 196616 | tf_op jit(solution)/shard_map/ppermute | solution.py:255
  20.9 1.9 %collective-permute-start.3 = (bf16[32,1,1024]{2,1,0:T(2,128)(2,1)S(1)}, bf16[32,1,1024]{2,1,0:T(2,128)(2,1)S(1)}, u32[]{:S(2)}, u32[]{:S(2)}) collective-permute-start(bf16[32,1,1024]{2,1,0:T(2,128)(2,1)S(1)} %get-tuple-element.9), channel_id=1, source_target_pairs={{1,0},{2,1},{3,2},{5,4},{6,5},{7,6},{9,8},{10,9},{11,10},{13,12},{... | collective-permute-start | bytes 196616 | tf_op jit(solution)/shard_map/ppermute | solution.py:256
  22.8 0.0 copy-done
  22.9 0.6 %constant_dynamic-slice_fusion.target_ref = f32[3,16,128]{2,1,0:T(8,128)} fusion(f32[3,16,1024]{2,1,0:T(8,128)S(1)} %copy-done, s32[]{:T(128)S(6)} %select_n.39), kind=kLoop, calls=%fused_computation.6 | loop fusion | bytes 49156 | tf_op jit(solution)/shard_map/dynamic_slice | solution.py:277
  23.5 0.0 collective-permute-done
  23.5 0.0 collective-permute-done.1
  23.5 0.0 all-to-all-done.parts_ref
  23.5 0.0 copy-start.3
  23.5 0.7 %copy-done.3 = f32[8,4,16,128]{3,2,1,0:T(8,128)} copy-done((f32[8,4,16,128]{3,2,1,0:T(8,128)}, f32[8,4,16,128]{3,2,1,0:T(8,128)S(1)}, u32[]{:S(2)}) %copy-start.3) | copy-done | bytes 262168
  24.2 2.2 %shard_map.60 = f32[8,4,16,128]{3,2,1,0:T(8,128)} custom-call(s32[8]{0:T(128)} %rank_ref.1, f32[8,4,16,128]{3,2,1,0:T(8,128)} %copy-done.3, f32[3,16,128]{2,1,0:T(8,128)} %constant_dynamic-slice_fusion.target_ref), custom_call_target="tpu_custom_call" | custom-call | tf_op jit(solution)/shard_map/pallas_call | solution.py:233
  26.4 6.3 %all-to-all-start.1 = ((f32[8,4,16,128]{3,2,1,0:T(8,128)}), f32[8,4,16,128]{3,2,1,0:T(8,128)S(1)}, u32[]{:S(2)}, u32[]{:S(2)}) async-start(f32[8,4,16,128]{3,2,1,0:T(8,128)} %shard_map.60), calls=%async_computation.1 | async-start | bytes 524288 | tf_op jit(solution)/shard_map/all_to_all | solution.py:283
  32.8 0.7 %maximum_convert_fusion.1.zhalo_ref = f32[2,16,1024]{2,1,0:T(8,128)} fusion(bf16[1,16,1024]{2,1,0:T(8,128)(2,1)S(1)} %get-tuple-element.11, bf16[1,16,1024]{2,1,0:T(8,128)(2,1)S(1)} %get-tuple-element.10), kind=kLoop, calls=%fused_computation.3 | loop fusion | flops 65536 | bytes 196608 | tf_op jit(solution)/shard_map/convert_element_type | solution.py:261
  33.4 0.0 collective-permute-done.2
  33.4 0.0 collective-permute-done.3
  33.4 0.4 broadcast_select_fusion.1
  33.8 1.0 %maximum_convert_fusion.rhalo_ref = f32[32,2,1024]{2,1,0:T(2,128)} fusion(bf16[32,1,1024]{2,1,0:T(2,128)(2,1)S(1)} %get-tuple-element.7, bf16[32,1,1024]{2,1,0:T(2,128)(2,1)S(1)} %get-tuple-element.6), kind=kLoop, calls=%fused_computation.2 | loop fusion | flops 262144 | bytes 393216 | tf_op jit(solution)/shard_map/convert_element_type | solution.py:262
  34.8 4.0 %shard_map.61.smooth_ref = f32[32,16,1024]{2,1,0:T(8,128)} custom-call(bf16[32,16,1024]{2,1,0:T(8,128)(2,1)} %d_ref.5, f32[2,16,1024]{2,1,0:T(8,128)} %maximum_convert_fusion.1.zhalo_ref, f32[32,2,1024]{2,1,0:T(2,128)} %maximum_convert_fusion.rhalo_ref), custom_call_target="tpu_custom_call" | custom-call | tf_op jit(solution)/shard_map/pallas_call | solution.py:158
  38.9 1.5 %all-to-all-done.1.ans_ref = f32[8,4,16,128]{3,2,1,0:T(8,128)S(1)} async-done(((f32[8,4,16,128]{3,2,1,0:T(8,128)}), f32[8,4,16,128]{3,2,1,0:T(8,128)S(1)}, u32[]{:S(2)}, u32[]{:S(2)}) %all-to-all-start.1) | async-done | bytes 262176 | tf_op jit(solution)/shard_map/all_to_all | solution.py:283
  40.3 0.0 copy-start.2
  40.3 0.7 %copy-done.2 = f32[8,4,16,128]{3,2,1,0:T(8,128)} copy-done((f32[8,4,16,128]{3,2,1,0:T(8,128)}, f32[8,4,16,128]{3,2,1,0:T(8,128)S(1)}, u32[]{:S(2)}) %copy-start.2) | copy-done | bytes 262168
  41.0 8.9 %shard_map.62 = (f32[32,16,1024]{2,1,0:T(8,128)}, f32[3,32,16,1024]{3,2,1,0:T(8,128)}) custom-call(bf16[32,16,1024]{2,1,0:T(8,128)(2,1)} %d_ref.5, bf16[3,32,16,1024]{3,2,1,0:T(8,128)(2,1)} %c_ref.3, f32[8,4,16,128]{3,2,1,0:T(8,128)} %copy-done.2, f32[32,16,1024]{2,1,0:T(8,128)} %shard_map.61.smooth_ref), custom_call_target="tpu_custom_call", output_to_operand_aliasing={{0}: (3, {})} | custom-call | tf_op jit(solution)/shard_map/pallas_call | solution.py:177
  (2 shorter events, 0.0 us)
Async XLA Ops:
  0.6 22.2 %copy-start = (f32[3,16,1024]{2,1,0:T(8,128)S(1)}, f32[3,16,1024]{2,1,0:T(8,128)}, u32[]{:S(2)}) copy-start(f32[3,16,1024]{2,1,0:T(8,128)} %param.6) | copy-start | bytes 589828
  0.6 10.8 %copy-start.1 = (bf16[32,16,1024]{2,1,0:T(8,128)(2,1)S(1)}, bf16[32,16,1024]{2,1,0:T(8,128)(2,1)}, u32[]{:S(2)}) copy-start(bf16[32,16,1024]{2,1,0:T(8,128)(2,1)} %d_ref.5) | copy-start | bytes 3145732
  5.1 18.4 %all-to-all-start = ((f32[8,4,16,128]{3,2,1,0:T(8,128)}), f32[8,4,16,128]{3,2,1,0:T(8,128)S(1)}, u32[]{:S(2)}, u32[]{:S(2)}) async-start(f32[8,4,16,128]{3,2,1,0:T(8,128)} %shard_map.59), calls=%async_computation | async-start | bytes 524288 | tf_op jit(solution)/shard_map/all_to_all | solution.py:275
  11.5 12.0 %collective-permute-start = (bf16[1,16,1024]{2,1,0:T(8,128)(2,1)S(1)}, bf16[1,16,1024]{2,1,0:T(8,128)(2,1)S(1)}, u32[]{:S(2)}, u32[]{:S(2)}) collective-permute-start(bf16[1,16,1024]{2,1,0:T(8,128)(2,1)S(1)} %get-tuple-element.12), channel_id=1, source_target_pairs={{0,4},{4,8},{8,12},{12,16},{16,20},{20,24},{24,28},{1,5},{5,9},{9,... | collective-permute-start | bytes 98312 | tf_op jit(solution)/shard_map/ppermute | solution.py:253
  14.9 8.6 %collective-permute-start.1 = (bf16[1,16,1024]{2,1,0:T(8,128)(2,1)S(1)}, bf16[1,16,1024]{2,1,0:T(8,128)(2,1)S(1)}, u32[]{:S(2)}, u32[]{:S(2)}) collective-permute-start(bf16[1,16,1024]{2,1,0:T(8,128)(2,1)S(1)} %get-tuple-element.13), channel_id=1, source_target_pairs={{4,0},{8,4},{12,8},{16,12},{20,16},{24,20},{28,24},{5,1},{9,5},{13... | collective-permute-start | bytes 98312 | tf_op jit(solution)/shard_map/ppermute | solution.py:254
  16.4 17.0 %collective-permute-start.2 = (bf16[32,1,1024]{2,1,0:T(2,128)(2,1)S(1)}, bf16[32,1,1024]{2,1,0:T(2,128)(2,1)S(1)}, u32[]{:S(2)}, u32[]{:S(2)}) collective-permute-start(bf16[32,1,1024]{2,1,0:T(2,128)(2,1)S(1)} %get-tuple-element.8), channel_id=1, source_target_pairs={{0,1},{1,2},{2,3},{4,5},{5,6},{6,7},{8,9},{9,10},{10,11},{12,13},{... | collective-permute-start | bytes 196616 | tf_op jit(solution)/shard_map/ppermute | solution.py:255
  20.9 12.5 %collective-permute-start.3 = (bf16[32,1,1024]{2,1,0:T(2,128)(2,1)S(1)}, bf16[32,1,1024]{2,1,0:T(2,128)(2,1)S(1)}, u32[]{:S(2)}, u32[]{:S(2)}) collective-permute-start(bf16[32,1,1024]{2,1,0:T(2,128)(2,1)S(1)} %get-tuple-element.9), channel_id=1, source_target_pairs={{1,0},{2,1},{3,2},{5,4},{6,5},{7,6},{9,8},{10,9},{11,10},{13,12},{... | collective-permute-start | bytes 196616 | tf_op jit(solution)/shard_map/ppermute | solution.py:256
  23.5 0.7 %copy-start.3 = (f32[8,4,16,128]{3,2,1,0:T(8,128)}, f32[8,4,16,128]{3,2,1,0:T(8,128)S(1)}, u32[]{:S(2)}) copy-start(f32[8,4,16,128]{3,2,1,0:T(8,128)S(1)} %all-to-all-done.parts_ref) | copy-start | bytes 786436
  26.4 13.9 %all-to-all-start.1 = ((f32[8,4,16,128]{3,2,1,0:T(8,128)}), f32[8,4,16,128]{3,2,1,0:T(8,128)S(1)}, u32[]{:S(2)}, u32[]{:S(2)}) async-start(f32[8,4,16,128]{3,2,1,0:T(8,128)} %shard_map.60), calls=%async_computation.1 | async-start | bytes 524288 | tf_op jit(solution)/shard_map/all_to_all | solution.py:283
  40.3 0.7 %copy-start.2 = (f32[8,4,16,128]{3,2,1,0:T(8,128)}, f32[8,4,16,128]{3,2,1,0:T(8,128)S(1)}, u32[]{:S(2)}) copy-start(f32[8,4,16,128]{3,2,1,0:T(8,128)S(1)} %all-to-all-done.1.ans_ref) | copy-start | bytes 786436

commit v13 on v11

--- a/solution.py
+++ b/solution.py
@@ -201,28 +201,30 @@
     return jnp.concatenate([scaled_residual, folded[:, None]], axis=1)
 
 
-def halos(density_raw):
+def depth_halos(density_raw):
     depth_count = lax.axis_size("depth")
-    rows_count = lax.axis_size("rows")
     depth_at = lax.axis_index("depth")
-    rows_at = lax.axis_index("rows")
-    up_d = [(i, i + 1) for i in range(depth_count - 1)]
-    up_r = [(i, i + 1) for i in range(rows_count - 1)]
+    up = [(i, i + 1) for i in range(depth_count - 1)]
     first_slice = density_raw[:1]
     last_slice = density_raw[-1:]
+    prev_slice = lax.ppermute(last_slice, "depth", up)
+    next_slice = lax.ppermute(first_slice, "depth", [(j, i) for i, j in up])
+    prev_slice = jnp.where(depth_at > 0, prev_slice, first_slice)
+    next_slice = jnp.where(depth_at < depth_count - 1, next_slice, last_slice)
+    return jnp.concatenate([prev_slice, next_slice], axis=0).astype(jnp.float32)
+
+
+def row_halos(density_raw):
+    rows_count = lax.axis_size("rows")
+    rows_at = lax.axis_index("rows")
+    up = [(i, i + 1) for i in range(rows_count - 1)]
     first_row = density_raw[:, :1]
     last_row = density_raw[:, -1:]
-    prev_slice = lax.ppermute(last_slice, "depth", up_d)
-    next_slice = lax.ppermute(first_slice, "depth", [(j, i) for i, j in up_d])
-    prev_row = lax.ppermute(last_row, "rows", up_r)
-    next_row = lax.ppermute(first_row, "rows", [(j, i) for i, j in up_r])
-    prev_slice = jnp.where(depth_at > 0, prev_slice, first_slice)
-    next_slice = jnp.where(depth_at < depth_count - 1, next_slice, last_slice)
+    prev_row = lax.ppermute(last_row, "rows", up)
+    next_row = lax.ppermute(first_row, "rows", [(j, i) for i, j in up])
     prev_row = jnp.where(rows_at > 0, prev_row, first_row)
     next_row = jnp.where(rows_at < rows_count - 1, next_row, last_row)
-    zhalo = jnp.concatenate([prev_slice, next_slice], axis=0).astype(jnp.float32)
-    rhalo = jnp.concatenate([prev_row, next_row], axis=1).astype(jnp.float32)
-    return zhalo, rhalo
+    return jnp.concatenate([prev_row, next_row], axis=1).astype(jnp.float32)
 
 
 def local(density_raw, colour_raw, target, slab_rank):
@@ -233,7 +235,7 @@
     tiles, per_tile, chunk_rows = chunking(rows_dev, width, depth_count)
     partial_value = forward_partial(density_raw, colour_raw, step, depth_count)
     partial_value, after_forward = lax.optimization_barrier((partial_value, density_raw))
-    zhalo, rhalo = halos(after_forward)
+    zhalo = depth_halos(after_forward)
     received = lax.all_to_all(partial_value, "depth", 0, 0, tiled=True)
     position = lax.axis_index("depth")
     target_piece = lax.dynamic_slice(
@@ -242,6 +244,8 @@
         (3, chunk_rows, lanes),
     )
     answers = composite(received, slab_rank, target_piece, float(slices_total))
+    answers, after_composite = lax.optimization_barrier((answers, density_raw))
+    rhalo = row_halos(after_composite)
     returned = lax.all_to_all(answers, "depth", 0, 0, tiled=True)
     smooth = smooth_term(density_raw, zhalo, rhalo)
     return backward_grads(density_raw, colour_raw, returned, smooth, step, slices_total)

time: 49.5 us -> 54.7 us (1.11)
  waiting for transfers between devices: 1.92 us -> 7.32 us
    ppermute x4, waiting for transfers between devices: 0.01 us -> 7.31 us  [the longest x1 3.69 us: row_halos(): next_row = lax.ppermute(first_row, 'rows', [(j, i) for i, j in up])]
    all_to_all x1, waiting for transfers between devices: 1.91 us -> 0.01 us  [local(): returned = lax.all_to_all(answers, 'depth', 0, 0, tiled=True)]
    all_to_all x1, starting transfers between devices: 6.34 us -> 4.82 us  [local(): returned = lax.all_to_all(answers, 'depth', 0, 0, tiled=True)]
    ppermute x4, starting transfers between devices: 11.1 us -> 12.5 us  [the longest x1 5.95 us: row_halos(): prev_row = lax.ppermute(last_row, 'rows', up)]
  transfers between devices with their start and end apart: 6 -> 6, of which waited for: 1 -> 2; matrix products, arithmetic and copies ran while one was open for 9% -> 4% of each run, Pallas kernels for 8% -> 7%
where the time goes in v13:
time: 54.7 us; the launch traced here: 54.2 us
  starting transfers between devices  23.7 us (43%)
  Pallas kernels  17.4 us (32%)
  waiting for transfers between devices  7.32 us (13%)
  other arithmetic  4.04 us (7%)
  local copies, waits for them, and re-layouts  0.95 us (2%)
  between operations  0.77 us (1%)
    pallas_call x1, Pallas kernels, backward_grads(): pl.pallas_call(functools.partial(backward_kernel, step=step, slices_total...  8.93 us
    all_to_all x1, starting transfers between devices, local(): received = lax.all_to_all(partial_value, 'depth', 0, 0, tiled=True)  6.38 us
    ppermute x1, starting transfers between devices, row_halos(): prev_row = lax.ppermute(last_row, 'rows', up)  5.95 us
    all_to_all x1, starting transfers between devices, local(): returned = lax.all_to_all(answers, 'depth', 0, 0, tiled=True)  4.82 us
    pallas_call x1, Pallas kernels, forward_partial(): pl.pallas_call(functools.partial(forward_kernel, step=step), grid=(width...  4.43 us
    pallas_call x1, Pallas kernels, smooth_term(): pl.pallas_call(smooth_kernel, grid=(width // block,), in_specs=[slab, pl....  4.03 us
    ppermute x1, waiting for transfers between devices, row_halos(): next_row = lax.ppermute(first_row, 'rows', [(j, i) for i, j in up])  3.69 us
    ppermute x1, waiting for transfers between devices, depth_halos(): next_slice = lax.ppermute(first_slice, 'depth', [(j, i) for i, j in up])  3.62 us
  transfers between devices with their start and end apart: 6, of which 2 were waited for; matrix products, arithmetic and copies ran while one was open for 4% of the time, Pallas kernels for 7%

profile of v13, /device:TPU:1, one launch (start us, length us, event | category | flops | bytes accessed | tf_op | source)
XLA Modules:
  0.0 54.2 jit_solution(5094968080859961345)
XLA Ops:
  0.6 0.0 copy-start
  0.6 0.0 copy-start.2
  0.7 4.4 %shard_map.59 = f32[8,4,16,128]{3,2,1,0:T(8,128)} custom-call(bf16[32,16,1024]{2,1,0:T(8,128)(2,1)} %d_ref.5, bf16[3,32,16,1024]{3,2,1,0:T(8,128)(2,1)} %c_ref.3), custom_call_target="tpu_custom_call" | custom-call | tf_op jit(solution)/shard_map/pallas_call | solution.py:139
  5.1 6.4 %all-to-all-start = ((f32[8,4,16,128]{3,2,1,0:T(8,128)}), f32[8,4,16,128]{3,2,1,0:T(8,128)S(1)}, u32[]{:S(2)}, u32[]{:S(2)}) async-start(f32[8,4,16,128]{3,2,1,0:T(8,128)} %shard_map.59), calls=%async_computation | async-start | bytes 524288 | tf_op jit(solution)/shard_map/all_to_all | solution.py:239
  11.5 0.0 copy-done
  11.5 3.4 %collective-permute-start = (bf16[1,16,1024]{2,1,0:T(8,128)(2,1)S(1)}, bf16[1,16,1024]{2,1,0:T(8,128)(2,1)S(1)}, u32[]{:S(2)}, u32[]{:S(2)}) collective-permute-start(bf16[1,16,1024]{2,1,0:T(8,128)(2,1)S(1)} %get-tuple-element.20), channel_id=1, source_target_pairs={{0,4},{4,8},{8,12},{12,16},{16,20},{20,24},{24,28},{1,5},{5,9},{9,... | collective-permute-start | bytes 98312 | tf_op jit(solution)/shard_map/ppermute | solution.py:210
  14.8 1.3 %collective-permute-start.1 = (bf16[1,16,1024]{2,1,0:T(8,128)(2,1)S(1)}, bf16[1,16,1024]{2,1,0:T(8,128)(2,1)S(1)}, u32[]{:S(2)}, u32[]{:S(2)}) collective-permute-start(bf16[1,16,1024]{2,1,0:T(8,128)(2,1)S(1)} %get-tuple-element.21), channel_id=1, source_target_pairs={{4,0},{8,4},{12,8},{16,12},{20,16},{24,20},{28,24},{5,1},{9,5},{13... | collective-permute-start | bytes 98312 | tf_op jit(solution)/shard_map/ppermute | solution.py:211
  16.1 0.0 copy-done.2
  16.2 0.1 compare_convert_fusion
  16.2 0.0 collective-permute-done
  16.2 3.6 %collective-permute-done.1 = bf16[1,16,1024]{2,1,0:T(8,128)(2,1)S(1)} collective-permute-done((bf16[1,16,1024]{2,1,0:T(8,128)(2,1)S(1)}, bf16[1,16,1024]{2,1,0:T(8,128)(2,1)S(1)}, u32[]{:S(2)}, u32[]{:S(2)}) %collective-permute-start.1) | collective-permute-done | bytes 32800 | tf_op jit(solution)/shard_map/ppermute | solution.py:211
  19.9 0.0 all-to-all-done
  19.9 0.1 multiply_reduce_fusion.1
  20.1 0.2 multiply_reduce_fusion
  20.3 0.8 %dynamic-slice_subtract_fusion = f32[3,16,128]{2,1,0:T(8,128)S(1)} fusion(f32[3,16,128]{2,1,0:T(8,128)S(1)} %get-tuple-element.12, f32[3,16,1024]{2,1,0:T(8,128)} %param.6, s32[]{:T(128)S(6)} %select_n.39), kind=kLoop, calls=%fused_computation.20 | loop fusion | flops 6144 | bytes 73732 | tf_op jit(solution)/shard_map/sub | solution.py:197
  21.0 0.1 multiply_reduce_fusion.3
  21.1 0.7 %pad_maximum_fusion = f32[8,4,16,128]{3,2,1,0:T(8,128)} fusion(f32[8,1,16,128]{3,2,1,0:T(8,128)S(1)} %fusion.2, f32[8,3,16,128]{3,2,1,0:T(8,128)S(1)} %get-tuple-element.22), kind=kLoop, calls=%fused_computation.2 | loop fusion | flops 65536 | bytes 524288 | tf_op jit(solution)/shard_map/concatenate | solution.py:201
  21.9 4.8 %all-to-all-start.1 = ((f32[8,4,16,128]{3,2,1,0:T(8,128)}), f32[8,4,16,128]{3,2,1,0:T(8,128)S(1)}, u32[]{:S(2)}, u32[]{:S(2)}) async-start(f32[8,4,16,128]{3,2,1,0:T(8,128)} %pad_maximum_fusion), calls=%async_computation.1 | async-start | bytes 524288 | tf_op jit(solution)/shard_map/all_to_all | solution.py:249
  26.7 0.2 fusion.5
  26.9 5.9 %collective-permute-start.2 = (bf16[32,1,1024]{2,1,0:T(2,128)(2,1)S(1)}, bf16[32,1,1024]{2,1,0:T(2,128)(2,1)S(1)}, u32[]{:S(2)}, u32[]{:S(2)}) collective-permute-start(bf16[32,1,1024]{2,1,0:T(2,128)(2,1)S(1)} %get-tuple-element.16), channel_id=1, source_target_pairs={{0,1},{1,2},{2,3},{4,5},{5,6},{6,7},{8,9},{9,10},{10,11},{12,13},{... | collective-permute-start | bytes 196616 | tf_op jit(solution)/shard_map/ppermute | solution.py:223
  32.9 1.9 %collective-permute-start.3 = (bf16[32,1,1024]{2,1,0:T(2,128)(2,1)S(1)}, bf16[32,1,1024]{2,1,0:T(2,128)(2,1)S(1)}, u32[]{:S(2)}, u32[]{:S(2)}) collective-permute-start(bf16[32,1,1024]{2,1,0:T(2,128)(2,1)S(1)} %get-tuple-element.17), channel_id=1, source_target_pairs={{1,0},{2,1},{3,2},{5,4},{6,5},{7,6},{9,8},{10,9},{11,10},{13,12},{... | collective-permute-start | bytes 196616 | tf_op jit(solution)/shard_map/ppermute | solution.py:224
  34.8 0.7 %maximum_convert_fusion.1.zhalo_ref = f32[2,16,1024]{2,1,0:T(8,128)} fusion(bf16[1,16,1024]{2,1,0:T(8,128)(2,1)S(1)} %get-tuple-element.19, bf16[1,16,1024]{2,1,0:T(8,128)(2,1)S(1)} %get-tuple-element.18), kind=kLoop, calls=%fused_computation.10 | loop fusion | flops 65536 | bytes 196608 | tf_op jit(solution)/shard_map/convert_element_type | solution.py:214
  35.4 0.0 collective-permute-done.2
  35.5 3.7 %collective-permute-done.3 = bf16[32,1,1024]{2,1,0:T(2,128)(2,1)S(1)} collective-permute-done((bf16[32,1,1024]{2,1,0:T(2,128)(2,1)S(1)}, bf16[32,1,1024]{2,1,0:T(2,128)(2,1)S(1)}, u32[]{:S(2)}, u32[]{:S(2)}) %collective-permute-start.3) | collective-permute-done | bytes 65568 | tf_op jit(solution)/shard_map/ppermute | solution.py:224
  39.1 0.4 broadcast_select_fusion.1
  39.5 1.0 %maximum_convert_fusion.rhalo_ref = f32[32,2,1024]{2,1,0:T(2,128)} fusion(bf16[32,1,1024]{2,1,0:T(2,128)(2,1)S(1)} %get-tuple-element.15, bf16[32,1,1024]{2,1,0:T(2,128)(2,1)S(1)} %get-tuple-element.14), kind=kLoop, calls=%fused_computation.9 | loop fusion | flops 262144 | bytes 393216 | tf_op jit(solution)/shard_map/convert_element_type | solution.py:227
  40.5 4.0 %shard_map.60.smooth_ref = f32[32,16,1024]{2,1,0:T(8,128)} custom-call(bf16[32,16,1024]{2,1,0:T(8,128)(2,1)} %d_ref.5, f32[2,16,1024]{2,1,0:T(8,128)} %maximum_convert_fusion.1.zhalo_ref, f32[32,2,1024]{2,1,0:T(2,128)} %maximum_convert_fusion.rhalo_ref), custom_call_target="tpu_custom_call" | custom-call | tf_op jit(solution)/shard_map/pallas_call | solution.py:158
  44.6 0.0 all-to-all-done.1.ans_ref
  44.6 0.0 copy-start.1
  44.6 0.7 %copy-done.1 = f32[8,4,16,128]{3,2,1,0:T(8,128)} copy-done((f32[8,4,16,128]{3,2,1,0:T(8,128)}, f32[8,4,16,128]{3,2,1,0:T(8,128)S(1)}, u32[]{:S(2)}) %copy-start.1) | copy-done | bytes 262168
  45.3 8.9 %shard_map.61 = (f32[32,16,1024]{2,1,0:T(8,128)}, f32[3,32,16,1024]{3,2,1,0:T(8,128)}) custom-call(bf16[32,16,1024]{2,1,0:T(8,128)(2,1)} %d_ref.5, bf16[3,32,16,1024]{3,2,1,0:T(8,128)(2,1)} %c_ref.3, f32[8,4,16,128]{3,2,1,0:T(8,128)} %copy-done.1, f32[32,16,1024]{2,1,0:T(8,128)} %shard_map.60.smooth_ref), custom_call_target="tpu_custom_call", output_to_operand_aliasing={{0}: (3, {})} | custom-call | tf_op jit(solution)/shard_map/pallas_call | solution.py:177
  (7 shorter events, 0.1 us)
Async XLA Ops:
  0.6 10.8 %copy-start = (bf16[32,16,1024]{2,1,0:T(8,128)(2,1)S(1)}, bf16[32,16,1024]{2,1,0:T(8,128)(2,1)}, u32[]{:S(2)}) copy-start(bf16[32,16,1024]{2,1,0:T(8,128)(2,1)} %d_ref.5) | copy-start | bytes 3145732
  0.6 15.5 %copy-start.2 = (s32[8]{0:T(128)S(1)}, s32[8]{0:T(128)}, u32[]{:S(2)}) copy-start(s32[8]{0:T(128)} %param.7) | copy-start | bytes 100
  5.1 14.8 %all-to-all-start = ((f32[8,4,16,128]{3,2,1,0:T(8,128)}), f32[8,4,16,128]{3,2,1,0:T(8,128)S(1)}, u32[]{:S(2)}, u32[]{:S(2)}) async-start(f32[8,4,16,128]{3,2,1,0:T(8,128)} %shard_map.59), calls=%async_computation | async-start | bytes 524288 | tf_op jit(solution)/shard_map/all_to_all | solution.py:239
  11.5 4.8 %collective-permute-start = (bf16[1,16,1024]{2,1,0:T(8,128)(2,1)S(1)}, bf16[1,16,1024]{2,1,0:T(8,128)(2,1)S(1)}, u32[]{:S(2)}, u32[]{:S(2)}) collective-permute-start(bf16[1,16,1024]{2,1,0:T(8,128)(2,1)S(1)} %get-tuple-element.20), channel_id=1, source_target_pairs={{0,4},{4,8},{8,12},{12,16},{16,20},{20,24},{24,28},{1,5},{5,9},{9,... | collective-permute-start | bytes 98312 | tf_op jit(solution)/shard_map/ppermute | solution.py:210
  14.8 5.0 %collective-permute-start.1 = (bf16[1,16,1024]{2,1,0:T(8,128)(2,1)S(1)}, bf16[1,16,1024]{2,1,0:T(8,128)(2,1)S(1)}, u32[]{:S(2)}, u32[]{:S(2)}) collective-permute-start(bf16[1,16,1024]{2,1,0:T(8,128)(2,1)S(1)} %get-tuple-element.21), channel_id=1, source_target_pairs={{4,0},{8,4},{12,8},{16,12},{20,16},{24,20},{28,24},{5,1},{9,5},{13... | collective-permute-start | bytes 98312 | tf_op jit(solution)/shard_map/ppermute | solution.py:211
  21.9 22.7 %all-to-all-start.1 = ((f32[8,4,16,128]{3,2,1,0:T(8,128)}), f32[8,4,16,128]{3,2,1,0:T(8,128)S(1)}, u32[]{:S(2)}, u32[]{:S(2)}) async-start(f32[8,4,16,128]{3,2,1,0:T(8,128)} %pad_maximum_fusion), calls=%async_computation.1 | async-start | bytes 524288 | tf_op jit(solution)/shard_map/all_to_all | solution.py:249
  26.9 8.6 %collective-permute-start.2 = (bf16[32,1,1024]{2,1,0:T(2,128)(2,1)S(1)}, bf16[32,1,1024]{2,1,0:T(2,128)(2,1)S(1)}, u32[]{:S(2)}, u32[]{:S(2)}) collective-permute-start(bf16[32,1,1024]{2,1,0:T(2,128)(2,1)S(1)} %get-tuple-element.16), channel_id=1, source_target_pairs={{0,1},{1,2},{2,3},{4,5},{5,6},{6,7},{8,9},{9,10},{10,11},{12,13},{... | collective-permute-start | bytes 196616 | tf_op jit(solution)/shard_map/ppermute | solution.py:223
  32.9 6.3 %collective-permute-start.3 = (bf16[32,1,1024]{2,1,0:T(2,128)(2,1)S(1)}, bf16[32,1,1024]{2,1,0:T(2,128)(2,1)S(1)}, u32[]{:S(2)}, u32[]{:S(2)}) collective-permute-start(bf16[32,1,1024]{2,1,0:T(2,128)(2,1)S(1)} %get-tuple-element.17), channel_id=1, source_target_pairs={{1,0},{2,1},{3,2},{5,4},{6,5},{7,6},{9,8},{10,9},{11,10},{13,12},{... | collective-permute-start | bytes 196616 | tf_op jit(solution)/shard_map/ppermute | solution.py:224
  44.6 0.7 %copy-start.1 = (f32[8,4,16,128]{3,2,1,0:T(8,128)}, f32[8,4,16,128]{3,2,1,0:T(8,128)S(1)}, u32[]{:S(2)}) copy-start(f32[8,4,16,128]{3,2,1,0:T(8,128)S(1)} %all-to-all-done.1.ans_ref) | copy-start | bytes 786436

commit v14 on v11

--- a/solution.py
+++ b/solution.py
@@ -184,7 +184,7 @@
             jax.ShapeDtypeStruct((3, slices, rows, width), jnp.float32),
         ],
         input_output_aliases={3: 0},
-    )(density, colour_raw, answers, smooth)
+    )(density, colour_raw, pltpu.with_memory_space_constraint(answers, pltpu.VMEM), smooth)
 
 
 def composite(parts, slab_rank, target_piece, slices_total):

time: 49.5 us -> 48.4 us (0.978)
  local copies, waits for them, and re-layouts: 0.95 us -> 0.26 us
    unnamed x6 -> x4, local copies, waits for them, and re-layouts: 0.7 us -> 0.01 us
where the time goes in v14:
time: 48.4 us; the launch traced here: 47.9 us
  starting transfers between devices  23.8 us (49%)
  Pallas kernels  17.1 us (35%)
  other arithmetic  4.05 us (8%)
  waiting for transfers between devices  1.91 us (4%)
  between operations  0.78 us (2%)
    pallas_call x1, Pallas kernels, backward_grads(): pl.pallas_call(functools.partial(backward_kernel, step=step, slices_total...  8.61 us
    all_to_all x1, starting transfers between devices, local(): received = lax.all_to_all(partial_value, 'depth', 0, 0, tiled=True)  6.38 us
    all_to_all x1, starting transfers between devices, local(): returned = lax.all_to_all(answers, 'depth', 0, 0, tiled=True)  6.34 us
    ppermute x1, starting transfers between devices, halos(): prev_row = lax.ppermute(last_row, 'rows', up_r)  4.52 us
    pallas_call x1, Pallas kernels, forward_partial(): pl.pallas_call(functools.partial(forward_kernel, step=step), grid=(width...  4.43 us
    pallas_call x1, Pallas kernels, smooth_term(): pl.pallas_call(smooth_kernel, grid=(width // block,), in_specs=[slab, pl....  4.03 us
    ppermute x1, starting transfers between devices, halos(): prev_slice = lax.ppermute(last_slice, 'depth', up_d)  3.36 us
    ppermute x1, starting transfers between devices, halos(): next_row = lax.ppermute(first_row, 'rows', [(j, i) for i, j in up_r])  1.92 us
  transfers between devices with their start and end apart: 6, of which 1 were waited for; matrix products, arithmetic and copies ran while one was open for 9% of the time, Pallas kernels for 8%

profile of v14, /device:TPU:1, one launch (start us, length us, event | category | flops | bytes accessed | tf_op | source)
XLA Modules:
  0.0 47.9 jit_solution(2654984712732153460)
XLA Ops:
  0.6 0.0 copy-start
  0.6 0.0 copy-start.1
  0.7 4.4 %shard_map.59 = f32[8,4,16,128]{3,2,1,0:T(8,128)} custom-call(bf16[32,16,1024]{2,1,0:T(8,128)(2,1)} %d_ref.5, bf16[3,32,16,1024]{3,2,1,0:T(8,128)(2,1)} %c_ref.3), custom_call_target="tpu_custom_call" | custom-call | tf_op jit(solution)/shard_map/pallas_call | solution.py:139
  5.1 6.4 %all-to-all-start = ((f32[8,4,16,128]{3,2,1,0:T(8,128)}), f32[8,4,16,128]{3,2,1,0:T(8,128)S(1)}, u32[]{:S(2)}, u32[]{:S(2)}) async-start(f32[8,4,16,128]{3,2,1,0:T(8,128)} %shard_map.59), calls=%async_computation | async-start | bytes 524288 | tf_op jit(solution)/shard_map/all_to_all | solution.py:237
  11.5 0.0 copy-done
  11.5 3.4 %collective-permute-start = (bf16[1,16,1024]{2,1,0:T(8,128)(2,1)S(1)}, bf16[1,16,1024]{2,1,0:T(8,128)(2,1)S(1)}, u32[]{:S(2)}, u32[]{:S(2)}) collective-permute-start(bf16[1,16,1024]{2,1,0:T(8,128)(2,1)S(1)} %get-tuple-element.16), channel_id=1, source_target_pairs={{0,4},{4,8},{8,12},{12,16},{16,20},{20,24},{24,28},{1,5},{5,9},{9,... | collective-permute-start | bytes 98312 | tf_op jit(solution)/shard_map/ppermute | solution.py:215
  14.8 1.3 %collective-permute-start.1 = (bf16[1,16,1024]{2,1,0:T(8,128)(2,1)S(1)}, bf16[1,16,1024]{2,1,0:T(8,128)(2,1)S(1)}, u32[]{:S(2)}, u32[]{:S(2)}) collective-permute-start(bf16[1,16,1024]{2,1,0:T(8,128)(2,1)S(1)} %get-tuple-element.17), channel_id=1, source_target_pairs={{4,0},{8,4},{12,8},{16,12},{20,16},{24,20},{28,24},{5,1},{9,5},{13... | collective-permute-start | bytes 98312 | tf_op jit(solution)/shard_map/ppermute | solution.py:216
  16.1 0.2 fusion.5
  16.4 4.5 %collective-permute-start.2 = (bf16[32,1,1024]{2,1,0:T(2,128)(2,1)S(1)}, bf16[32,1,1024]{2,1,0:T(2,128)(2,1)S(1)}, u32[]{:S(2)}, u32[]{:S(2)}) collective-permute-start(bf16[32,1,1024]{2,1,0:T(2,128)(2,1)S(1)} %get-tuple-element.12), channel_id=1, source_target_pairs={{0,1},{1,2},{2,3},{4,5},{5,6},{6,7},{8,9},{9,10},{10,11},{12,13},{... | collective-permute-start | bytes 196616 | tf_op jit(solution)/shard_map/ppermute | solution.py:217
  20.9 1.9 %collective-permute-start.3 = (bf16[32,1,1024]{2,1,0:T(2,128)(2,1)S(1)}, bf16[32,1,1024]{2,1,0:T(2,128)(2,1)S(1)}, u32[]{:S(2)}, u32[]{:S(2)}) collective-permute-start(bf16[32,1,1024]{2,1,0:T(2,128)(2,1)S(1)} %get-tuple-element.13), channel_id=1, source_target_pairs={{1,0},{2,1},{3,2},{5,4},{6,5},{7,6},{9,8},{10,9},{11,10},{13,12},{... | collective-permute-start | bytes 196616 | tf_op jit(solution)/shard_map/ppermute | solution.py:218
  22.8 0.0 copy-done.1
  22.8 0.1 compare_convert_fusion
  22.9 0.0 collective-permute-done
  22.9 0.0 collective-permute-done.1
  22.9 0.0 all-to-all-done
  23.0 0.1 multiply_reduce_fusion.1
  23.2 0.2 multiply_reduce_fusion
  23.3 0.8 %dynamic-slice_subtract_fusion = f32[3,16,128]{2,1,0:T(8,128)S(1)} fusion(f32[3,16,128]{2,1,0:T(8,128)S(1)} %get-tuple-element.8, f32[3,16,1024]{2,1,0:T(8,128)} %param.6, s32[]{:T(128)S(6)} %select_n.39), kind=kLoop, calls=%fused_computation.20 | loop fusion | flops 6144 | bytes 73732 | tf_op jit(solution)/shard_map/sub | solution.py:197
  24.1 0.1 multiply_reduce_fusion.3
  24.2 0.7 %pad_maximum_fusion = f32[8,4,16,128]{3,2,1,0:T(8,128)} fusion(f32[8,1,16,128]{3,2,1,0:T(8,128)S(1)} %fusion.2, f32[8,3,16,128]{3,2,1,0:T(8,128)S(1)} %get-tuple-element.18), kind=kLoop, calls=%fused_computation.2 | loop fusion | flops 65536 | bytes 524288 | tf_op jit(solution)/shard_map/concatenate | solution.py:201
  24.9 6.3 %all-to-all-start.1 = ((f32[8,4,16,128]{3,2,1,0:T(8,128)}), f32[8,4,16,128]{3,2,1,0:T(8,128)S(1)}, u32[]{:S(2)}, u32[]{:S(2)}) async-start(f32[8,4,16,128]{3,2,1,0:T(8,128)} %pad_maximum_fusion), calls=%async_computation.1 | async-start | bytes 524288 | tf_op jit(solution)/shard_map/all_to_all | solution.py:245
  31.3 0.7 %maximum_convert_fusion.1.zhalo_ref = f32[2,16,1024]{2,1,0:T(8,128)} fusion(bf16[1,16,1024]{2,1,0:T(8,128)(2,1)S(1)} %get-tuple-element.15, bf16[1,16,1024]{2,1,0:T(8,128)(2,1)S(1)} %get-tuple-element.14), kind=kLoop, calls=%fused_computation.10 | loop fusion | flops 65536 | bytes 196608 | tf_op jit(solution)/shard_map/convert_element_type | solution.py:223
  31.9 0.0 collective-permute-done.2
  32.0 0.0 collective-permute-done.3
  32.0 0.4 broadcast_select_fusion.1
  32.4 1.0 %maximum_convert_fusion.rhalo_ref = f32[32,2,1024]{2,1,0:T(2,128)} fusion(bf16[32,1,1024]{2,1,0:T(2,128)(2,1)S(1)} %get-tuple-element.11, bf16[32,1,1024]{2,1,0:T(2,128)(2,1)S(1)} %get-tuple-element.10), kind=kLoop, calls=%fused_computation.9 | loop fusion | flops 262144 | bytes 393216 | tf_op jit(solution)/shard_map/convert_element_type | solution.py:224
  33.3 4.0 %shard_map.60.smooth_ref = f32[32,16,1024]{2,1,0:T(8,128)} custom-call(bf16[32,16,1024]{2,1,0:T(8,128)(2,1)} %d_ref.5, f32[2,16,1024]{2,1,0:T(8,128)} %maximum_convert_fusion.1.zhalo_ref, f32[32,2,1024]{2,1,0:T(2,128)} %maximum_convert_fusion.rhalo_ref), custom_call_target="tpu_custom_call" | custom-call | tf_op jit(solution)/shard_map/pallas_call | solution.py:158
  37.4 1.9 %all-to-all-done.1.ans_ref = f32[8,4,16,128]{3,2,1,0:T(8,128)S(1)} async-done(((f32[8,4,16,128]{3,2,1,0:T(8,128)}), f32[8,4,16,128]{3,2,1,0:T(8,128)S(1)}, u32[]{:S(2)}, u32[]{:S(2)}) %all-to-all-start.1) | async-done | bytes 262176 | tf_op jit(solution)/shard_map/all_to_all | solution.py:245
  39.3 8.6 %shard_map.61 = (f32[32,16,1024]{2,1,0:T(8,128)}, f32[3,32,16,1024]{3,2,1,0:T(8,128)}) custom-call(bf16[32,16,1024]{2,1,0:T(8,128)(2,1)} %d_ref.5, bf16[3,32,16,1024]{3,2,1,0:T(8,128)(2,1)} %c_ref.3, f32[8,4,16,128]{3,2,1,0:T(8,128)S(1)} %all-to-all-done.1.ans_ref, f32[32,16,1024]{2,1,0:T(8,128)} %shard_map.60.smooth_ref), custom_call_target="tpu_custom_call", output_to_operand_aliasing={{0}: (3, {})} | custom-call | tf_op jit(solution)/shard_map/pallas_call | solution.py:177
  (7 shorter events, 0.1 us)
Async XLA Ops:
  0.6 10.8 %copy-start = (bf16[32,16,1024]{2,1,0:T(8,128)(2,1)S(1)}, bf16[32,16,1024]{2,1,0:T(8,128)(2,1)}, u32[]{:S(2)}) copy-start(bf16[32,16,1024]{2,1,0:T(8,128)(2,1)} %d_ref.5) | copy-start | bytes 3145732
  0.6 22.2 %copy-start.1 = (s32[8]{0:T(128)S(1)}, s32[8]{0:T(128)}, u32[]{:S(2)}) copy-start(s32[8]{0:T(128)} %param.7) | copy-start | bytes 100
  5.1 17.8 %all-to-all-start = ((f32[8,4,16,128]{3,2,1,0:T(8,128)}), f32[8,4,16,128]{3,2,1,0:T(8,128)S(1)}, u32[]{:S(2)}, u32[]{:S(2)}) async-start(f32[8,4,16,128]{3,2,1,0:T(8,128)} %shard_map.59), calls=%async_computation | async-start | bytes 524288 | tf_op jit(solution)/shard_map/all_to_all | solution.py:237
  11.5 11.4 %collective-permute-start = (bf16[1,16,1024]{2,1,0:T(8,128)(2,1)S(1)}, bf16[1,16,1024]{2,1,0:T(8,128)(2,1)S(1)}, u32[]{:S(2)}, u32[]{:S(2)}) collective-permute-start(bf16[1,16,1024]{2,1,0:T(8,128)(2,1)S(1)} %get-tuple-element.16), channel_id=1, source_target_pairs={{0,4},{4,8},{8,12},{12,16},{16,20},{20,24},{24,28},{1,5},{5,9},{9,... | collective-permute-start | bytes 98312 | tf_op jit(solution)/shard_map/ppermute | solution.py:215
  14.8 8.1 %collective-permute-start.1 = (bf16[1,16,1024]{2,1,0:T(8,128)(2,1)S(1)}, bf16[1,16,1024]{2,1,0:T(8,128)(2,1)S(1)}, u32[]{:S(2)}, u32[]{:S(2)}) collective-permute-start(bf16[1,16,1024]{2,1,0:T(8,128)(2,1)S(1)} %get-tuple-element.17), channel_id=1, source_target_pairs={{4,0},{8,4},{12,8},{16,12},{20,16},{24,20},{28,24},{5,1},{9,5},{13... | collective-permute-start | bytes 98312 | tf_op jit(solution)/shard_map/ppermute | solution.py:216
  16.4 15.6 %collective-permute-start.2 = (bf16[32,1,1024]{2,1,0:T(2,128)(2,1)S(1)}, bf16[32,1,1024]{2,1,0:T(2,128)(2,1)S(1)}, u32[]{:S(2)}, u32[]{:S(2)}) collective-permute-start(bf16[32,1,1024]{2,1,0:T(2,128)(2,1)S(1)} %get-tuple-element.12), channel_id=1, source_target_pairs={{0,1},{1,2},{2,3},{4,5},{5,6},{6,7},{8,9},{9,10},{10,11},{12,13},{... | collective-permute-start | bytes 196616 | tf_op jit(solution)/shard_map/ppermute | solution.py:217
  20.9 11.1 %collective-permute-start.3 = (bf16[32,1,1024]{2,1,0:T(2,128)(2,1)S(1)}, bf16[32,1,1024]{2,1,0:T(2,128)(2,1)S(1)}, u32[]{:S(2)}, u32[]{:S(2)}) collective-permute-start(bf16[32,1,1024]{2,1,0:T(2,128)(2,1)S(1)} %get-tuple-element.13), channel_id=1, source_target_pairs={{1,0},{2,1},{3,2},{5,4},{6,5},{7,6},{9,8},{10,9},{11,10},{13,12},{... | collective-permute-start | bytes 196616 | tf_op jit(solution)/shard_map/ppermute | solution.py:218
  24.9 14.3 %all-to-all-start.1 = ((f32[8,4,16,128]{3,2,1,0:T(8,128)}), f32[8,4,16,128]{3,2,1,0:T(8,128)S(1)}, u32[]{:S(2)}, u32[]{:S(2)}) async-start(f32[8,4,16,128]{3,2,1,0:T(8,128)} %pad_maximum_fusion), calls=%async_computation.1 | async-start | bytes 524288 | tf_op jit(solution)/shard_map/all_to_all | solution.py:245

commit v15 on v14

--- a/solution.py
+++ b/solution.py
@@ -70,6 +70,7 @@
 
     for j in range(block // lanes):
         cols = pl.ds(j * lanes, lanes)
+        place = pl.ds(pl.multiple_of((pl.program_id(0) * (block // lanes) + j) * lanes, lanes), lanes)
 
         def body(z, carry):
             d_prev, d = carry
@@ -81,7 +82,7 @@
             rims = rhalo_ref[z, :, cols]
             upper = jnp.where(first_row, rims[0:1], pltpu.roll(d, 1, 0))
             lower = jnp.where(last_row, rims[1:2], pltpu.roll(d, shape[0] - 1, 0))
-            out_ref[z, :, cols] = 2.0 * smooth_weight * (
+            out_ref[z, :, place] = 2.0 * smooth_weight * (
                 (d - d_prev) + (d - d_next) + (d - upper) + (d - lower)
             )
             return (d, d_next)
@@ -101,6 +102,7 @@
     for j in range(subs):
         cols = pl.ds(j * lanes, lanes)
         base = (pl.program_id(0) * subs + j) * per_tile
+        place = pl.ds(pl.multiple_of((pl.program_id(0) * subs + j) * lanes, lanes), lanes)
 
         def pixel(c):
             if per_tile == 1:
@@ -124,7 +126,7 @@
             inner = emitted - inv * (pixel(3) - left)
             for c in range(3):
                 gc_ref[c, z, :, cols] = res[c] * lit_col[c] * (1.0 - col[c])
-            gd_ref[z, :, cols] = gain * through * jax.nn.sigmoid(d) * inner + smooth_ref[z, :, cols]
+            gd_ref[z, :, cols] = gain * through * jax.nn.sigmoid(d) * inner + smooth_ref[z, :, place]
             return (n_next, through, w[0], w[1], w[2])
 
         zero = jnp.zeros(shape, jnp.float32)
@@ -163,7 +165,7 @@
             pl.BlockSpec((2, rows, block), lambda i: (0, 0, i)),
             pl.BlockSpec((slices, 2, block), lambda i: (0, 0, i)),
         ],
-        out_specs=slab,
+        out_specs=pl.BlockSpec(memory_space=pltpu.VMEM),
         out_shape=jax.ShapeDtypeStruct((slices, rows, width), jnp.float32),
     )(density, zhalo, rhalo)
 
@@ -177,14 +179,23 @@
     return pl.pallas_call(
         functools.partial(backward_kernel, step=step, slices_total=float(slices_total)),
         grid=(width // block,),
-        in_specs=[slab, colours, pl.BlockSpec(memory_space=pltpu.VMEM), slab],
+        in_specs=[
+            slab,
+            colours,
+            pl.BlockSpec(memory_space=pltpu.VMEM),
+            pl.BlockSpec(memory_space=pltpu.VMEM),
+        ],
         out_specs=[slab, colours],
         out_shape=[
             jax.ShapeDtypeStruct((slices, rows, width), jnp.float32),
             jax.ShapeDtypeStruct((3, slices, rows, width), jnp.float32),
         ],
-        input_output_aliases={3: 0},
-    )(density, colour_raw, pltpu.with_memory_space_constraint(answers, pltpu.VMEM), smooth)
+    )(
+        density,
+        colour_raw,
+        pltpu.with_memory_space_constraint(answers, pltpu.VMEM),
+        pltpu.with_memory_space_constraint(smooth, pltpu.VMEM),
+    )
 
 
 def composite(parts, slab_rank, target_piece, slices_total):

time: 48.4 us -> 49.7 us (1.027)
  local copies, waits for them, and re-layouts: 0.26 us -> 1.85 us
    unnamed x4 -> x6, local copies, waits for them, and re-layouts: 0.01 us -> 1.6 us
  transfers between devices with their start and end apart: 6 -> 6, of which waited for: 1 -> 1; matrix products, arithmetic and copies ran while one was open for 9% -> 9% of each run, Pallas kernels for 8% -> 9%
where the time goes in v15:
time: 49.7 us; the launch traced here: 49.1 us
  starting transfers between devices  23.8 us (48%)
  Pallas kernels  17.1 us (34%)
  other arithmetic  4.04 us (8%)
  local copies, waits for them, and re-layouts  1.85 us (4%)
  waiting for transfers between devices  1.48 us (3%)
  between operations  0.78 us (2%)
    pallas_call x1, Pallas kernels, backward_grads(): pl.pallas_call(functools.partial(backward_kernel, step=step, slices_total...  8.22 us
    all_to_all x1, starting transfers between devices, local(): received = lax.all_to_all(partial_value, 'depth', 0, 0, tiled=True)  6.38 us
    all_to_all x1, starting transfers between devices, local(): returned = lax.all_to_all(answers, 'depth', 0, 0, tiled=True)  6.34 us
    ppermute x1, starting transfers between devices, halos(): prev_row = lax.ppermute(last_row, 'rows', up_r)  4.52 us
    pallas_call x1, Pallas kernels, smooth_term(): pl.pallas_call(smooth_kernel, grid=(width // block,), in_specs=[slab, pl....  4.47 us
    pallas_call x1, Pallas kernels, forward_partial(): pl.pallas_call(functools.partial(forward_kernel, step=step), grid=(width...  4.43 us
    ppermute x1, starting transfers between devices, halos(): prev_slice = lax.ppermute(last_slice, 'depth', up_d)  3.36 us
    ppermute x1, starting transfers between devices, halos(): next_row = lax.ppermute(first_row, 'rows', [(j, i) for i, j in up_r])  1.92 us
  transfers between devices with their start and end apart: 6, of which 1 were waited for; matrix products, arithmetic and copies ran while one was open for 9% of the time, Pallas kernels for 9%

profile of v15, /device:TPU:1, one launch (start us, length us, event | category | flops | bytes accessed | tf_op | source)
XLA Modules:
  0.0 49.1 jit_solution(1759966027281137557)
XLA Ops:
  0.6 0.0 copy-start.1
  0.6 0.0 copy-start.2
  0.7 4.4 %shard_map.59 = f32[8,4,16,128]{3,2,1,0:T(8,128)} custom-call(bf16[32,16,1024]{2,1,0:T(8,128)(2,1)} %d_ref.5, bf16[3,32,16,1024]{3,2,1,0:T(8,128)(2,1)} %c_ref.3), custom_call_target="tpu_custom_call" | custom-call | tf_op jit(solution)/shard_map/pallas_call | solution.py:141
  5.1 6.4 %all-to-all-start = ((f32[8,4,16,128]{3,2,1,0:T(8,128)}), f32[8,4,16,128]{3,2,1,0:T(8,128)S(1)}, u32[]{:S(2)}, u32[]{:S(2)}) async-start(f32[8,4,16,128]{3,2,1,0:T(8,128)} %shard_map.59), calls=%async_computation | async-start | bytes 524288 | tf_op jit(solution)/shard_map/all_to_all | solution.py:248
  11.5 0.0 copy-done.1
  11.5 3.4 %collective-permute-start = (bf16[1,16,1024]{2,1,0:T(8,128)(2,1)S(1)}, bf16[1,16,1024]{2,1,0:T(8,128)(2,1)S(1)}, u32[]{:S(2)}, u32[]{:S(2)}) collective-permute-start(bf16[1,16,1024]{2,1,0:T(8,128)(2,1)S(1)} %get-tuple-element.16), channel_id=1, source_target_pairs={{0,4},{4,8},{8,12},{12,16},{16,20},{20,24},{24,28},{1,5},{5,9},{9,... | collective-permute-start | bytes 98312 | tf_op jit(solution)/shard_map/ppermute | solution.py:226
  14.8 1.3 %collective-permute-start.1 = (bf16[1,16,1024]{2,1,0:T(8,128)(2,1)S(1)}, bf16[1,16,1024]{2,1,0:T(8,128)(2,1)S(1)}, u32[]{:S(2)}, u32[]{:S(2)}) collective-permute-start(bf16[1,16,1024]{2,1,0:T(8,128)(2,1)S(1)} %get-tuple-element.17), channel_id=1, source_target_pairs={{4,0},{8,4},{12,8},{16,12},{20,16},{24,20},{28,24},{5,1},{9,5},{13... | collective-permute-start | bytes 98312 | tf_op jit(solution)/shard_map/ppermute | solution.py:227
  16.1 0.2 fusion.5
  16.4 4.5 %collective-permute-start.2 = (bf16[32,1,1024]{2,1,0:T(2,128)(2,1)S(1)}, bf16[32,1,1024]{2,1,0:T(2,128)(2,1)S(1)}, u32[]{:S(2)}, u32[]{:S(2)}) collective-permute-start(bf16[32,1,1024]{2,1,0:T(2,128)(2,1)S(1)} %get-tuple-element.12), channel_id=1, source_target_pairs={{0,1},{1,2},{2,3},{4,5},{5,6},{6,7},{8,9},{9,10},{10,11},{12,13},{... | collective-permute-start | bytes 196616 | tf_op jit(solution)/shard_map/ppermute | solution.py:228
  20.9 1.9 %collective-permute-start.3 = (bf16[32,1,1024]{2,1,0:T(2,128)(2,1)S(1)}, bf16[32,1,1024]{2,1,0:T(2,128)(2,1)S(1)}, u32[]{:S(2)}, u32[]{:S(2)}) collective-permute-start(bf16[32,1,1024]{2,1,0:T(2,128)(2,1)S(1)} %get-tuple-element.13), channel_id=1, source_target_pairs={{1,0},{2,1},{3,2},{5,4},{6,5},{7,6},{9,8},{10,9},{11,10},{13,12},{... | collective-permute-start | bytes 196616 | tf_op jit(solution)/shard_map/ppermute | solution.py:229
  22.8 0.0 copy-done.2
  22.8 0.1 compare_convert_fusion
  22.9 0.0 collective-permute-done
  22.9 0.0 collective-permute-done.1
  22.9 0.0 all-to-all-done
  23.0 0.1 multiply_reduce_fusion.1
  23.2 0.2 multiply_reduce_fusion
  23.3 0.8 %dynamic-slice_subtract_fusion = f32[3,16,128]{2,1,0:T(8,128)S(1)} fusion(f32[3,16,128]{2,1,0:T(8,128)S(1)} %get-tuple-element.8, f32[3,16,1024]{2,1,0:T(8,128)} %param.6, s32[]{:T(128)S(6)} %select_n.39), kind=kLoop, calls=%fused_computation.20 | loop fusion | flops 6144 | bytes 73732 | tf_op jit(solution)/shard_map/sub | solution.py:208
  24.1 0.1 multiply_reduce_fusion.3
  24.2 0.7 %pad_maximum_fusion = f32[8,4,16,128]{3,2,1,0:T(8,128)} fusion(f32[8,1,16,128]{3,2,1,0:T(8,128)S(1)} %fusion.2, f32[8,3,16,128]{3,2,1,0:T(8,128)S(1)} %get-tuple-element.18), kind=kLoop, calls=%fused_computation.2 | loop fusion | flops 65536 | bytes 524288 | tf_op jit(solution)/shard_map/concatenate | solution.py:212
  24.9 6.3 %all-to-all-start.1 = ((f32[8,4,16,128]{3,2,1,0:T(8,128)}), f32[8,4,16,128]{3,2,1,0:T(8,128)S(1)}, u32[]{:S(2)}, u32[]{:S(2)}) async-start(f32[8,4,16,128]{3,2,1,0:T(8,128)} %pad_maximum_fusion), calls=%async_computation.1 | async-start | bytes 524288 | tf_op jit(solution)/shard_map/all_to_all | solution.py:256
  31.3 0.7 %maximum_convert_fusion.1.zhalo_ref = f32[2,16,1024]{2,1,0:T(8,128)} fusion(bf16[1,16,1024]{2,1,0:T(8,128)(2,1)S(1)} %get-tuple-element.15, bf16[1,16,1024]{2,1,0:T(8,128)(2,1)S(1)} %get-tuple-element.14), kind=kLoop, calls=%fused_computation.10 | loop fusion | flops 65536 | bytes 196608 | tf_op jit(solution)/shard_map/convert_element_type | solution.py:234
  31.9 0.0 collective-permute-done.2
  31.9 0.0 collective-permute-done.3
  31.9 0.4 broadcast_select_fusion.1
  32.3 1.0 %maximum_convert_fusion.rhalo_ref = f32[32,2,1024]{2,1,0:T(2,128)} fusion(bf16[32,1,1024]{2,1,0:T(2,128)(2,1)S(1)} %get-tuple-element.11, bf16[32,1,1024]{2,1,0:T(2,128)(2,1)S(1)} %get-tuple-element.10), kind=kLoop, calls=%fused_computation.9 | loop fusion | flops 262144 | bytes 393216 | tf_op jit(solution)/shard_map/convert_element_type | solution.py:235
  33.3 4.5 %shard_map.60.smooth_ref = f32[32,16,1024]{2,1,0:T(8,128)} custom-call(bf16[32,16,1024]{2,1,0:T(8,128)(2,1)} %d_ref.5, f32[2,16,1024]{2,1,0:T(8,128)} %maximum_convert_fusion.1.zhalo_ref, f32[32,2,1024]{2,1,0:T(2,128)} %maximum_convert_fusion.rhalo_ref), custom_call_target="tpu_custom_call" | custom-call | tf_op jit(solution)/shard_map/pallas_call | solution.py:160
  37.8 1.5 %all-to-all-done.1.ans_ref = f32[8,4,16,128]{3,2,1,0:T(8,128)S(1)} async-done(((f32[8,4,16,128]{3,2,1,0:T(8,128)}), f32[8,4,16,128]{3,2,1,0:T(8,128)S(1)}, u32[]{:S(2)}, u32[]{:S(2)}) %all-to-all-start.1) | async-done | bytes 262176 | tf_op jit(solution)/shard_map/all_to_all | solution.py:256
  39.3 0.0 copy-start
  39.3 1.6 %copy-done = f32[32,16,1024]{2,1,0:T(8,128)S(1)} copy-done((f32[32,16,1024]{2,1,0:T(8,128)S(1)}, f32[32,16,1024]{2,1,0:T(8,128)}, u32[]{:S(2)}) %copy-start) | copy-done | bytes 2097176
  40.9 8.2 %shard_map.61 = (f32[32,16,1024]{2,1,0:T(8,128)}, f32[3,32,16,1024]{3,2,1,0:T(8,128)}) custom-call(bf16[32,16,1024]{2,1,0:T(8,128)(2,1)} %d_ref.5, bf16[3,32,16,1024]{3,2,1,0:T(8,128)(2,1)} %c_ref.3, f32[8,4,16,128]{3,2,1,0:T(8,128)S(1)} %all-to-all-done.1.ans_ref, f32[32,16,1024]{2,1,0:T(8,128)S(1)} %copy-done), custom_call_target="tpu_custom_call" | custom-call | tf_op jit(solution)/shard_map/pallas_call | solution.py:179
  (7 shorter events, 0.1 us)
Async XLA Ops:
  0.6 10.8 %copy-start.1 = (bf16[32,16,1024]{2,1,0:T(8,128)(2,1)S(1)}, bf16[32,16,1024]{2,1,0:T(8,128)(2,1)}, u32[]{:S(2)}) copy-start(bf16[32,16,1024]{2,1,0:T(8,128)(2,1)} %d_ref.5) | copy-start | bytes 3145732
  0.6 22.2 %copy-start.2 = (s32[8]{0:T(128)S(1)}, s32[8]{0:T(128)}, u32[]{:S(2)}) copy-start(s32[8]{0:T(128)} %param.7) | copy-start | bytes 100
  5.1 17.8 %all-to-all-start = ((f32[8,4,16,128]{3,2,1,0:T(8,128)}), f32[8,4,16,128]{3,2,1,0:T(8,128)S(1)}, u32[]{:S(2)}, u32[]{:S(2)}) async-start(f32[8,4,16,128]{3,2,1,0:T(8,128)} %shard_map.59), calls=%async_computation | async-start | bytes 524288 | tf_op jit(solution)/shard_map/all_to_all | solution.py:248
  11.5 11.4 %collective-permute-start = (bf16[1,16,1024]{2,1,0:T(8,128)(2,1)S(1)}, bf16[1,16,1024]{2,1,0:T(8,128)(2,1)S(1)}, u32[]{:S(2)}, u32[]{:S(2)}) collective-permute-start(bf16[1,16,1024]{2,1,0:T(8,128)(2,1)S(1)} %get-tuple-element.16), channel_id=1, source_target_pairs={{0,4},{4,8},{8,12},{12,16},{16,20},{20,24},{24,28},{1,5},{5,9},{9,... | collective-permute-start | bytes 98312 | tf_op jit(solution)/shard_map/ppermute | solution.py:226
  14.8 8.1 %collective-permute-start.1 = (bf16[1,16,1024]{2,1,0:T(8,128)(2,1)S(1)}, bf16[1,16,1024]{2,1,0:T(8,128)(2,1)S(1)}, u32[]{:S(2)}, u32[]{:S(2)}) collective-permute-start(bf16[1,16,1024]{2,1,0:T(8,128)(2,1)S(1)} %get-tuple-element.17), channel_id=1, source_target_pairs={{4,0},{8,4},{12,8},{16,12},{20,16},{24,20},{28,24},{5,1},{9,5},{13... | collective-permute-start | bytes 98312 | tf_op jit(solution)/shard_map/ppermute | solution.py:227
  16.4 15.6 %collective-permute-start.2 = (bf16[32,1,1024]{2,1,0:T(2,128)(2,1)S(1)}, bf16[32,1,1024]{2,1,0:T(2,128)(2,1)S(1)}, u32[]{:S(2)}, u32[]{:S(2)}) collective-permute-start(bf16[32,1,1024]{2,1,0:T(2,128)(2,1)S(1)} %get-tuple-element.12), channel_id=1, source_target_pairs={{0,1},{1,2},{2,3},{4,5},{5,6},{6,7},{8,9},{9,10},{10,11},{12,13},{... | collective-permute-start | bytes 196616 | tf_op jit(solution)/shard_map/ppermute | solution.py:228
  20.9 11.0 %collective-permute-start.3 = (bf16[32,1,1024]{2,1,0:T(2,128)(2,1)S(1)}, bf16[32,1,1024]{2,1,0:T(2,128)(2,1)S(1)}, u32[]{:S(2)}, u32[]{:S(2)}) collective-permute-start(bf16[32,1,1024]{2,1,0:T(2,128)(2,1)S(1)} %get-tuple-element.13), channel_id=1, source_target_pairs={{1,0},{2,1},{3,2},{5,4},{6,5},{7,6},{9,8},{10,9},{11,10},{13,12},{... | collective-permute-start | bytes 196616 | tf_op jit(solution)/shard_map/ppermute | solution.py:229
  24.9 14.3 %all-to-all-start.1 = ((f32[8,4,16,128]{3,2,1,0:T(8,128)}), f32[8,4,16,128]{3,2,1,0:T(8,128)S(1)}, u32[]{:S(2)}, u32[]{:S(2)}) async-start(f32[8,4,16,128]{3,2,1,0:T(8,128)} %pad_maximum_fusion), calls=%async_computation.1 | async-start | bytes 524288 | tf_op jit(solution)/shard_map/all_to_all | solution.py:256
  39.3 1.6 %copy-start = (f32[32,16,1024]{2,1,0:T(8,128)S(1)}, f32[32,16,1024]{2,1,0:T(8,128)}, u32[]{:S(2)}) copy-start(f32[32,16,1024]{2,1,0:T(8,128)} %shard_map.60.smooth_ref) | copy-start | bytes 6291460

commit v16 on v14

--- a/solution.py
+++ b/solution.py
@@ -91,7 +91,7 @@
 
 
 def backward_kernel(d_ref, c_ref, ans_ref, smooth_ref, gd_ref, gc_ref, *, step, slices_total):
-    slices, rows, block = d_ref.shape
+    slices, rows, block = gd_ref.shape
     shape = (rows, lanes)
     subs = block // lanes
     per_tile = ans_ref.shape[0] // (pl.num_programs(0) * subs)
@@ -101,6 +101,7 @@
     for j in range(subs):
         cols = pl.ds(j * lanes, lanes)
         base = (pl.program_id(0) * subs + j) * per_tile
+        place = pl.ds(pl.multiple_of((pl.program_id(0) * subs + j) * lanes, lanes), lanes)
 
         def pixel(c):
             if per_tile == 1:
@@ -109,7 +110,7 @@
 
         def body(z, carry):
             n, front, w0, w1, w2 = carry
-            d = d_ref[z, :, cols].astype(jnp.float32)
+            d = d_ref[z, :, place].astype(jnp.float32)
             dtn = softplus(d) * scale
             lit = front * (1.0 - jnp.exp2(dtn))
             n_next = n + dtn
@@ -177,14 +178,24 @@
     return pl.pallas_call(
         functools.partial(backward_kernel, step=step, slices_total=float(slices_total)),
         grid=(width // block,),
-        in_specs=[slab, colours, pl.BlockSpec(memory_space=pltpu.VMEM), slab],
+        in_specs=[
+            pl.BlockSpec(memory_space=pltpu.VMEM),
+            colours,
+            pl.BlockSpec(memory_space=pltpu.VMEM),
+            slab,
+        ],
         out_specs=[slab, colours],
         out_shape=[
             jax.ShapeDtypeStruct((slices, rows, width), jnp.float32),
             jax.ShapeDtypeStruct((3, slices, rows, width), jnp.float32),
         ],
         input_output_aliases={3: 0},
-    )(density, colour_raw, pltpu.with_memory_space_constraint(answers, pltpu.VMEM), smooth)
+    )(
+        pltpu.with_memory_space_constraint(density, pltpu.VMEM),
+        colour_raw,
+        pltpu.with_memory_space_constraint(answers, pltpu.VMEM),
+        smooth,
+    )
 
 
 def composite(parts, slab_rank, target_piece, slices_total):

time: 48.4 us -> 48.3 us (level)
  no operation moved by 1% of the time
where the time goes in v16:
time: 48.3 us; the launch traced here: 47.7 us
  starting transfers between devices  23.8 us (49%)
  Pallas kernels  16.9 us (35%)
  other arithmetic  4.04 us (8%)
  waiting for transfers between devices  1.91 us (4%)
  between operations  0.79 us (2%)
    pallas_call x1, Pallas kernels, backward_grads(): pl.pallas_call(functools.partial(backward_kernel, step=step, slices_total...  8.44 us
    all_to_all x1, starting transfers between devices, local(): received = lax.all_to_all(partial_value, 'depth', 0, 0, tiled=True)  6.38 us
    all_to_all x1, starting transfers between devices, local(): returned = lax.all_to_all(answers, 'depth', 0, 0, tiled=True)  6.34 us
    ppermute x1, starting transfers between devices, halos(): prev_row = lax.ppermute(last_row, 'rows', up_r)  4.52 us
    pallas_call x1, Pallas kernels, forward_partial(): pl.pallas_call(functools.partial(forward_kernel, step=step), grid=(width...  4.43 us
    pallas_call x1, Pallas kernels, smooth_term(): pl.pallas_call(smooth_kernel, grid=(width // block,), in_specs=[slab, pl....  4.03 us
    ppermute x1, starting transfers between devices, halos(): prev_slice = lax.ppermute(last_slice, 'depth', up_d)  3.36 us
    ppermute x1, starting transfers between devices, halos(): next_row = lax.ppermute(first_row, 'rows', [(j, i) for i, j in up_r])  1.92 us
  transfers between devices with their start and end apart: 6, of which 1 were waited for; matrix products, arithmetic and copies ran while one was open for 9% of the time, Pallas kernels for 8%

profile of v16, /device:TPU:1, one launch (start us, length us, event | category | flops | bytes accessed | tf_op | source)
XLA Modules:
  0.0 47.7 jit_solution(12213240005564476211)
XLA Ops:
  0.6 0.0 copy-start
  0.6 0.0 copy-start.2
  0.7 4.4 %shard_map.59 = f32[8,4,16,128]{3,2,1,0:T(8,128)} custom-call(bf16[32,16,1024]{2,1,0:T(8,128)(2,1)} %d_ref.5, bf16[3,32,16,1024]{3,2,1,0:T(8,128)(2,1)} %c_ref.3), custom_call_target="tpu_custom_call" | custom-call | tf_op jit(solution)/shard_map/pallas_call | solution.py:140
  5.1 6.4 %all-to-all-start = ((f32[8,4,16,128]{3,2,1,0:T(8,128)}), f32[8,4,16,128]{3,2,1,0:T(8,128)S(1)}, u32[]{:S(2)}, u32[]{:S(2)}) async-start(f32[8,4,16,128]{3,2,1,0:T(8,128)} %shard_map.59), calls=%async_computation | async-start | bytes 524288 | tf_op jit(solution)/shard_map/all_to_all | solution.py:248
  11.5 0.0 copy-done
  11.5 3.4 %collective-permute-start = (bf16[1,16,1024]{2,1,0:T(8,128)(2,1)S(1)}, bf16[1,16,1024]{2,1,0:T(8,128)(2,1)S(1)}, u32[]{:S(2)}, u32[]{:S(2)}) collective-permute-start(bf16[1,16,1024]{2,1,0:T(8,128)(2,1)S(1)} %get-tuple-element.16), channel_id=1, source_target_pairs={{0,4},{4,8},{8,12},{12,16},{16,20},{20,24},{24,28},{1,5},{5,9},{9,... | collective-permute-start | bytes 98312 | tf_op jit(solution)/shard_map/ppermute | solution.py:226
  14.8 1.3 %collective-permute-start.1 = (bf16[1,16,1024]{2,1,0:T(8,128)(2,1)S(1)}, bf16[1,16,1024]{2,1,0:T(8,128)(2,1)S(1)}, u32[]{:S(2)}, u32[]{:S(2)}) collective-permute-start(bf16[1,16,1024]{2,1,0:T(8,128)(2,1)S(1)} %get-tuple-element.17), channel_id=1, source_target_pairs={{4,0},{8,4},{12,8},{16,12},{20,16},{24,20},{28,24},{5,1},{9,5},{13... | collective-permute-start | bytes 98312 | tf_op jit(solution)/shard_map/ppermute | solution.py:227
  16.1 0.2 fusion.5
  16.4 4.5 %collective-permute-start.2 = (bf16[32,1,1024]{2,1,0:T(2,128)(2,1)S(1)}, bf16[32,1,1024]{2,1,0:T(2,128)(2,1)S(1)}, u32[]{:S(2)}, u32[]{:S(2)}) collective-permute-start(bf16[32,1,1024]{2,1,0:T(2,128)(2,1)S(1)} %get-tuple-element.12), channel_id=1, source_target_pairs={{0,1},{1,2},{2,3},{4,5},{5,6},{6,7},{8,9},{9,10},{10,11},{12,13},{... | collective-permute-start | bytes 196616 | tf_op jit(solution)/shard_map/ppermute | solution.py:228
  20.9 1.9 %collective-permute-start.3 = (bf16[32,1,1024]{2,1,0:T(2,128)(2,1)S(1)}, bf16[32,1,1024]{2,1,0:T(2,128)(2,1)S(1)}, u32[]{:S(2)}, u32[]{:S(2)}) collective-permute-start(bf16[32,1,1024]{2,1,0:T(2,128)(2,1)S(1)} %get-tuple-element.13), channel_id=1, source_target_pairs={{1,0},{2,1},{3,2},{5,4},{6,5},{7,6},{9,8},{10,9},{11,10},{13,12},{... | collective-permute-start | bytes 196616 | tf_op jit(solution)/shard_map/ppermute | solution.py:229
  22.8 0.0 copy-done.2
  22.8 0.1 compare_convert_fusion
  22.9 0.0 collective-permute-done
  22.9 0.0 collective-permute-done.1
  22.9 0.0 all-to-all-done
  23.0 0.1 multiply_reduce_fusion.1
  23.2 0.2 multiply_reduce_fusion
  23.3 0.8 %dynamic-slice_subtract_fusion = f32[3,16,128]{2,1,0:T(8,128)S(1)} fusion(f32[3,16,128]{2,1,0:T(8,128)S(1)} %get-tuple-element.8, f32[3,16,1024]{2,1,0:T(8,128)} %param.6, s32[]{:T(128)S(6)} %select_n.39), kind=kLoop, calls=%fused_computation.20 | loop fusion | flops 6144 | bytes 73732 | tf_op jit(solution)/shard_map/sub | solution.py:208
  24.1 0.1 multiply_reduce_fusion.3
  24.2 0.7 %pad_maximum_fusion = f32[8,4,16,128]{3,2,1,0:T(8,128)} fusion(f32[8,1,16,128]{3,2,1,0:T(8,128)S(1)} %fusion.2, f32[8,3,16,128]{3,2,1,0:T(8,128)S(1)} %get-tuple-element.18), kind=kLoop, calls=%fused_computation.2 | loop fusion | flops 65536 | bytes 524288 | tf_op jit(solution)/shard_map/concatenate | solution.py:212
  24.9 6.3 %all-to-all-start.1 = ((f32[8,4,16,128]{3,2,1,0:T(8,128)}), f32[8,4,16,128]{3,2,1,0:T(8,128)S(1)}, u32[]{:S(2)}, u32[]{:S(2)}) async-start(f32[8,4,16,128]{3,2,1,0:T(8,128)} %pad_maximum_fusion), calls=%async_computation.1 | async-start | bytes 524288 | tf_op jit(solution)/shard_map/all_to_all | solution.py:256
  31.3 0.7 %maximum_convert_fusion.1.zhalo_ref = f32[2,16,1024]{2,1,0:T(8,128)} fusion(bf16[1,16,1024]{2,1,0:T(8,128)(2,1)S(1)} %get-tuple-element.15, bf16[1,16,1024]{2,1,0:T(8,128)(2,1)S(1)} %get-tuple-element.14), kind=kLoop, calls=%fused_computation.10 | loop fusion | flops 65536 | bytes 196608 | tf_op jit(solution)/shard_map/convert_element_type | solution.py:234
  31.9 0.0 collective-permute-done.2
  31.9 0.0 collective-permute-done.3
  31.9 0.4 broadcast_select_fusion.1
  32.3 0.0 copy-start.1
  32.3 1.0 %maximum_convert_fusion.rhalo_ref = f32[32,2,1024]{2,1,0:T(2,128)} fusion(bf16[32,1,1024]{2,1,0:T(2,128)(2,1)S(1)} %get-tuple-element.11, bf16[32,1,1024]{2,1,0:T(2,128)(2,1)S(1)} %get-tuple-element.10), kind=kLoop, calls=%fused_computation.9 | loop fusion | flops 262144 | bytes 393216 | tf_op jit(solution)/shard_map/convert_element_type | solution.py:235
  33.3 4.0 %shard_map.60.smooth_ref = f32[32,16,1024]{2,1,0:T(8,128)} custom-call(bf16[32,16,1024]{2,1,0:T(8,128)(2,1)} %d_ref.5, f32[2,16,1024]{2,1,0:T(8,128)} %maximum_convert_fusion.1.zhalo_ref, f32[32,2,1024]{2,1,0:T(2,128)} %maximum_convert_fusion.rhalo_ref), custom_call_target="tpu_custom_call" | custom-call | tf_op jit(solution)/shard_map/pallas_call | solution.py:159
  37.4 1.9 %all-to-all-done.1.ans_ref = f32[8,4,16,128]{3,2,1,0:T(8,128)S(1)} async-done(((f32[8,4,16,128]{3,2,1,0:T(8,128)}), f32[8,4,16,128]{3,2,1,0:T(8,128)S(1)}, u32[]{:S(2)}, u32[]{:S(2)}) %all-to-all-start.1) | async-done | bytes 262176 | tf_op jit(solution)/shard_map/all_to_all | solution.py:256
  39.3 0.0 copy-done.1
  39.3 8.4 %shard_map.61 = (f32[32,16,1024]{2,1,0:T(8,128)}, f32[3,32,16,1024]{3,2,1,0:T(8,128)}) custom-call(bf16[32,16,1024]{2,1,0:T(8,128)(2,1)S(1)} %copy-done.1, bf16[3,32,16,1024]{3,2,1,0:T(8,128)(2,1)} %c_ref.3, f32[8,4,16,128]{3,2,1,0:T(8,128)S(1)} %all-to-all-done.1.ans_ref, f32[32,16,1024]{2,1,0:T(8,128)} %shard_map.60.smooth_ref), custom_call_target="tpu_custom_call", output_to_operand_aliasing={{0}: (3, {})} | custom-call | tf_op jit(solution)/shard_map/pallas_call | solution.py:178
  (7 shorter events, 0.1 us)
Async XLA Ops:
  0.6 10.8 %copy-start = (bf16[32,16,1024]{2,1,0:T(8,128)(2,1)S(1)}, bf16[32,16,1024]{2,1,0:T(8,128)(2,1)}, u32[]{:S(2)}) copy-start(bf16[32,16,1024]{2,1,0:T(8,128)(2,1)} %d_ref.5) | copy-start | bytes 3145732
  0.6 22.2 %copy-start.2 = (s32[8]{0:T(128)S(1)}, s32[8]{0:T(128)}, u32[]{:S(2)}) copy-start(s32[8]{0:T(128)} %param.7) | copy-start | bytes 100
  5.1 17.8 %all-to-all-start = ((f32[8,4,16,128]{3,2,1,0:T(8,128)}), f32[8,4,16,128]{3,2,1,0:T(8,128)S(1)}, u32[]{:S(2)}, u32[]{:S(2)}) async-start(f32[8,4,16,128]{3,2,1,0:T(8,128)} %shard_map.59), calls=%async_computation | async-start | bytes 524288 | tf_op jit(solution)/shard_map/all_to_all | solution.py:248
  11.5 11.4 %collective-permute-start = (bf16[1,16,1024]{2,1,0:T(8,128)(2,1)S(1)}, bf16[1,16,1024]{2,1,0:T(8,128)(2,1)S(1)}, u32[]{:S(2)}, u32[]{:S(2)}) collective-permute-start(bf16[1,16,1024]{2,1,0:T(8,128)(2,1)S(1)} %get-tuple-element.16), channel_id=1, source_target_pairs={{0,4},{4,8},{8,12},{12,16},{16,20},{20,24},{24,28},{1,5},{5,9},{9,... | collective-permute-start | bytes 98312 | tf_op jit(solution)/shard_map/ppermute | solution.py:226
  14.8 8.1 %collective-permute-start.1 = (bf16[1,16,1024]{2,1,0:T(8,128)(2,1)S(1)}, bf16[1,16,1024]{2,1,0:T(8,128)(2,1)S(1)}, u32[]{:S(2)}, u32[]{:S(2)}) collective-permute-start(bf16[1,16,1024]{2,1,0:T(8,128)(2,1)S(1)} %get-tuple-element.17), channel_id=1, source_target_pairs={{4,0},{8,4},{12,8},{16,12},{20,16},{24,20},{28,24},{5,1},{9,5},{13... | collective-permute-start | bytes 98312 | tf_op jit(solution)/shard_map/ppermute | solution.py:227
  16.4 15.6 %collective-permute-start.2 = (bf16[32,1,1024]{2,1,0:T(2,128)(2,1)S(1)}, bf16[32,1,1024]{2,1,0:T(2,128)(2,1)S(1)}, u32[]{:S(2)}, u32[]{:S(2)}) collective-permute-start(bf16[32,1,1024]{2,1,0:T(2,128)(2,1)S(1)} %get-tuple-element.12), channel_id=1, source_target_pairs={{0,1},{1,2},{2,3},{4,5},{5,6},{6,7},{8,9},{9,10},{10,11},{12,13},{... | collective-permute-start | bytes 196616 | tf_op jit(solution)/shard_map/ppermute | solution.py:228
  20.9 11.0 %collective-permute-start.3 = (bf16[32,1,1024]{2,1,0:T(2,128)(2,1)S(1)}, bf16[32,1,1024]{2,1,0:T(2,128)(2,1)S(1)}, u32[]{:S(2)}, u32[]{:S(2)}) collective-permute-start(bf16[32,1,1024]{2,1,0:T(2,128)(2,1)S(1)} %get-tuple-element.13), channel_id=1, source_target_pairs={{1,0},{2,1},{3,2},{5,4},{6,5},{7,6},{9,8},{10,9},{11,10},{13,12},{... | collective-permute-start | bytes 196616 | tf_op jit(solution)/shard_map/ppermute | solution.py:229
  24.9 14.3 %all-to-all-start.1 = ((f32[8,4,16,128]{3,2,1,0:T(8,128)}), f32[8,4,16,128]{3,2,1,0:T(8,128)S(1)}, u32[]{:S(2)}, u32[]{:S(2)}) async-start(f32[8,4,16,128]{3,2,1,0:T(8,128)} %pad_maximum_fusion), calls=%async_computation.1 | async-start | bytes 524288 | tf_op jit(solution)/shard_map/all_to_all | solution.py:256
  32.3 6.9 %copy-start.1 = (bf16[32,16,1024]{2,1,0:T(8,128)(2,1)S(1)}, bf16[32,16,1024]{2,1,0:T(8,128)(2,1)}, u32[]{:S(2)}) copy-start(bf16[32,16,1024]{2,1,0:T(8,128)(2,1)} %d_ref.5) | copy-start | bytes 3145732

commit v17 on v16

--- a/solution.py
+++ b/solution.py
@@ -90,7 +90,9 @@
         lax.fori_loop(0, slices, body, start, unroll=2)
 
 
-def backward_kernel(d_ref, c_ref, ans_ref, smooth_ref, gd_ref, gc_ref, *, step, slices_total):
+def backward_kernel(
+    d_ref, c0_ref, c1_ref, c2_ref, ans_ref, smooth_ref, gd_ref, gc_ref, *, step, slices_total
+):
     slices, rows, block = gd_ref.shape
     shape = (rows, lanes)
     subs = block // lanes
@@ -116,7 +118,8 @@
             n_next = n + dtn
             through = jnp.exp2(n_next)
             inv = jnp.exp2(-n_next)
-            col = [jax.nn.sigmoid(c_ref[c, z, :, cols].astype(jnp.float32)) for c in range(3)]
+            raw = (c0_ref[z, :, place], c1_ref[z, :, cols], c2_ref[z, :, cols])
+            col = [jax.nn.sigmoid(raw[c].astype(jnp.float32)) for c in range(3)]
             lit_col = [lit * col[c] for c in range(3)]
             w = [w0 + lit_col[0], w1 + lit_col[1], w2 + lit_col[2]]
             res = [pixel(c) for c in range(3)]
@@ -180,7 +183,9 @@
         grid=(width // block,),
         in_specs=[
             pl.BlockSpec(memory_space=pltpu.VMEM),
-            colours,
+            pl.BlockSpec(memory_space=pltpu.VMEM),
+            pl.BlockSpec((None, slices, rows, block), lambda i: (1, 0, 0, i)),
+            pl.BlockSpec((None, slices, rows, block), lambda i: (2, 0, 0, i)),
             pl.BlockSpec(memory_space=pltpu.VMEM),
             slab,
         ],
@@ -189,9 +194,11 @@
             jax.ShapeDtypeStruct((slices, rows, width), jnp.float32),
             jax.ShapeDtypeStruct((3, slices, rows, width), jnp.float32),
         ],
-        input_output_aliases={3: 0},
+        input_output_aliases={5: 0},
     )(
         pltpu.with_memory_space_constraint(density, pltpu.VMEM),
+        pltpu.with_memory_space_constraint(colour_raw[0], pltpu.VMEM),
+        colour_raw,
         colour_raw,
         pltpu.with_memory_space_constraint(answers, pltpu.VMEM),
         smooth,

time: 48.3 us -> 49.2 us (1.019)
  local copies, waits for them, and re-layouts: 0.27 us -> 1.59 us
    squeeze x0 -> x1, local copies, waits for them, and re-layouts: none -> 1.33 us  [backward_grads(): colour_raw[0]]
  transfers between devices with their start and end apart: 6 -> 6, of which waited for: 1 -> 1; matrix products, arithmetic and copies ran while one was open for 9% -> 12% of each run, Pallas kernels for 8% -> 8%
where the time goes in v17:
time: 49.2 us; the launch traced here: 48.6 us
  starting transfers between devices  23.9 us (49%)
  Pallas kernels  16.7 us (34%)
  other arithmetic  4.04 us (8%)
  local copies, waits for them, and re-layouts  1.59 us (3%)
  waiting for transfers between devices  1.5 us (3%)
  between operations  0.79 us (2%)
    pallas_call x1, Pallas kernels, backward_grads(): pl.pallas_call(functools.partial(backward_kernel, step=step, slices_total...  8.24 us
    all_to_all x1, starting transfers between devices, local(): received = lax.all_to_all(partial_value, 'depth', 0, 0, tiled=True)  6.51 us
    all_to_all x1, starting transfers between devices, local(): returned = lax.all_to_all(answers, 'depth', 0, 0, tiled=True)  6.34 us
    ppermute x1, starting transfers between devices, halos(): prev_row = lax.ppermute(last_row, 'rows', up_r)  4.52 us
    pallas_call x1, Pallas kernels, forward_partial(): pl.pallas_call(functools.partial(forward_kernel, step=step), grid=(width...  4.43 us
    pallas_call x1, Pallas kernels, smooth_term(): pl.pallas_call(smooth_kernel, grid=(width // block,), in_specs=[slab, pl....  4.03 us
    ppermute x1, starting transfers between devices, halos(): prev_slice = lax.ppermute(last_slice, 'depth', up_d)  3.36 us
    ppermute x1, starting transfers between devices, halos(): next_row = lax.ppermute(first_row, 'rows', [(j, i) for i, j in up_r])  1.92 us
  transfers between devices with their start and end apart: 6, of which 1 were waited for; matrix products, arithmetic and copies ran while one was open for 12% of the time, Pallas kernels for 8%

profile of v17, /device:TPU:1, one launch (start us, length us, event | category | flops | bytes accessed | tf_op | source)
XLA Modules:
  0.0 48.6 jit_solution(5982952491414135916)
XLA Ops:
  0.6 0.0 copy-start
  0.6 4.4 %shard_map.59 = f32[8,4,16,128]{3,2,1,0:T(8,128)} custom-call(bf16[32,16,1024]{2,1,0:T(8,128)(2,1)} %d_ref.5, bf16[3,32,16,1024]{3,2,1,0:T(8,128)(2,1)} %c2_ref.1), custom_call_target="tpu_custom_call" | custom-call | tf_op jit(solution)/shard_map/pallas_call | solution.py:143
  5.1 0.0 copy-start.2
  5.1 6.5 %all-to-all-start = ((f32[8,4,16,128]{3,2,1,0:T(8,128)}), f32[8,4,16,128]{3,2,1,0:T(8,128)S(1)}, u32[]{:S(2)}, u32[]{:S(2)}) async-start(f32[8,4,16,128]{3,2,1,0:T(8,128)} %shard_map.59), calls=%async_computation | async-start | bytes 524288 | tf_op jit(solution)/shard_map/all_to_all | solution.py:255
  11.6 0.0 copy-done
  11.6 3.4 %collective-permute-start = (bf16[1,16,1024]{2,1,0:T(8,128)(2,1)S(1)}, bf16[1,16,1024]{2,1,0:T(8,128)(2,1)S(1)}, u32[]{:S(2)}, u32[]{:S(2)}) collective-permute-start(bf16[1,16,1024]{2,1,0:T(8,128)(2,1)S(1)} %get-tuple-element.16), channel_id=1, source_target_pairs={{0,4},{4,8},{8,12},{12,16},{16,20},{20,24},{24,28},{1,5},{5,9},{9,... | collective-permute-start | bytes 98312 | tf_op jit(solution)/shard_map/ppermute | solution.py:233
  15.0 1.3 %collective-permute-start.1 = (bf16[1,16,1024]{2,1,0:T(8,128)(2,1)S(1)}, bf16[1,16,1024]{2,1,0:T(8,128)(2,1)S(1)}, u32[]{:S(2)}, u32[]{:S(2)}) collective-permute-start(bf16[1,16,1024]{2,1,0:T(8,128)(2,1)S(1)} %get-tuple-element.17), channel_id=1, source_target_pairs={{4,0},{8,4},{12,8},{16,12},{20,16},{24,20},{28,24},{5,1},{9,5},{13... | collective-permute-start | bytes 98312 | tf_op jit(solution)/shard_map/ppermute | solution.py:234
  16.3 0.2 fusion.5
  16.5 4.5 %collective-permute-start.2 = (bf16[32,1,1024]{2,1,0:T(2,128)(2,1)S(1)}, bf16[32,1,1024]{2,1,0:T(2,128)(2,1)S(1)}, u32[]{:S(2)}, u32[]{:S(2)}) collective-permute-start(bf16[32,1,1024]{2,1,0:T(2,128)(2,1)S(1)} %get-tuple-element.12), channel_id=1, source_target_pairs={{0,1},{1,2},{2,3},{4,5},{5,6},{6,7},{8,9},{9,10},{10,11},{12,13},{... | collective-permute-start | bytes 196616 | tf_op jit(solution)/shard_map/ppermute | solution.py:235
  21.0 1.9 %collective-permute-start.3 = (bf16[32,1,1024]{2,1,0:T(2,128)(2,1)S(1)}, bf16[32,1,1024]{2,1,0:T(2,128)(2,1)S(1)}, u32[]{:S(2)}, u32[]{:S(2)}) collective-permute-start(bf16[32,1,1024]{2,1,0:T(2,128)(2,1)S(1)} %get-tuple-element.13), channel_id=1, source_target_pairs={{1,0},{2,1},{3,2},{5,4},{6,5},{7,6},{9,8},{10,9},{11,10},{13,12},{... | collective-permute-start | bytes 196616 | tf_op jit(solution)/shard_map/ppermute | solution.py:236
  22.9 1.3 %slice_bitcast_fusion.c0_ref = bf16[32,16,1024]{2,1,0:T(8,128)(2,1)S(1)} fusion(bf16[3,32,16,1024]{3,2,1,0:T(8,128)(2,1)} %c2_ref.1), kind=kLoop, calls=%fused_computation.1 | loop fusion | bytes 2097152 | tf_op jit(solution)/shard_map/squeeze | solution.py:200
  24.3 0.0 copy-done.2
  24.3 0.1 compare_convert_fusion
  24.4 0.0 collective-permute-done
  24.4 0.0 collective-permute-done.1
  24.4 0.0 all-to-all-done
  24.4 0.1 multiply_reduce_fusion.1
  24.6 0.2 multiply_reduce_fusion
  24.8 0.8 %dynamic-slice_subtract_fusion = f32[3,16,128]{2,1,0:T(8,128)S(1)} fusion(f32[3,16,128]{2,1,0:T(8,128)S(1)} %get-tuple-element.8, f32[3,16,1024]{2,1,0:T(8,128)} %param.6, s32[]{:T(128)S(6)} %select_n.39), kind=kLoop, calls=%fused_computation.21 | loop fusion | flops 6144 | bytes 73732 | tf_op jit(solution)/shard_map/sub | solution.py:215
  25.6 0.1 multiply_reduce_fusion.3
  25.7 0.7 %pad_maximum_fusion = f32[8,4,16,128]{3,2,1,0:T(8,128)} fusion(f32[8,1,16,128]{3,2,1,0:T(8,128)S(1)} %fusion.2, f32[8,3,16,128]{3,2,1,0:T(8,128)S(1)} %get-tuple-element.18), kind=kLoop, calls=%fused_computation.3 | loop fusion | flops 65536 | bytes 524288 | tf_op jit(solution)/shard_map/concatenate | solution.py:219
  26.4 6.3 %all-to-all-start.1 = ((f32[8,4,16,128]{3,2,1,0:T(8,128)}), f32[8,4,16,128]{3,2,1,0:T(8,128)S(1)}, u32[]{:S(2)}, u32[]{:S(2)}) async-start(f32[8,4,16,128]{3,2,1,0:T(8,128)} %pad_maximum_fusion), calls=%async_computation.1 | async-start | bytes 524288 | tf_op jit(solution)/shard_map/all_to_all | solution.py:263
  32.7 0.7 %maximum_convert_fusion.1.zhalo_ref = f32[2,16,1024]{2,1,0:T(8,128)} fusion(bf16[1,16,1024]{2,1,0:T(8,128)(2,1)S(1)} %get-tuple-element.15, bf16[1,16,1024]{2,1,0:T(8,128)(2,1)S(1)} %get-tuple-element.14), kind=kLoop, calls=%fused_computation.11 | loop fusion | flops 65536 | bytes 196608 | tf_op jit(solution)/shard_map/convert_element_type | solution.py:241
  33.4 0.0 collective-permute-done.2
  33.4 0.0 collective-permute-done.3
  33.4 0.4 broadcast_select_fusion.1
  33.8 0.0 copy-start.1
  33.8 1.0 %maximum_convert_fusion.rhalo_ref = f32[32,2,1024]{2,1,0:T(2,128)} fusion(bf16[32,1,1024]{2,1,0:T(2,128)(2,1)S(1)} %get-tuple-element.11, bf16[32,1,1024]{2,1,0:T(2,128)(2,1)S(1)} %get-tuple-element.10), kind=kLoop, calls=%fused_computation.10 | loop fusion | flops 262144 | bytes 393216 | tf_op jit(solution)/shard_map/convert_element_type | solution.py:242
  34.8 4.0 %shard_map.60.smooth_ref = f32[32,16,1024]{2,1,0:T(8,128)} custom-call(bf16[32,16,1024]{2,1,0:T(8,128)(2,1)} %d_ref.5, f32[2,16,1024]{2,1,0:T(8,128)} %maximum_convert_fusion.1.zhalo_ref, f32[32,2,1024]{2,1,0:T(2,128)} %maximum_convert_fusion.rhalo_ref), custom_call_target="tpu_custom_call" | custom-call | tf_op jit(solution)/shard_map/pallas_call | solution.py:162
  38.8 1.5 %all-to-all-done.1.ans_ref = f32[8,4,16,128]{3,2,1,0:T(8,128)S(1)} async-done(((f32[8,4,16,128]{3,2,1,0:T(8,128)}), f32[8,4,16,128]{3,2,1,0:T(8,128)S(1)}, u32[]{:S(2)}, u32[]{:S(2)}) %all-to-all-start.1) | async-done | bytes 262176 | tf_op jit(solution)/shard_map/all_to_all | solution.py:263
  40.3 0.0 copy-done.1
  40.3 8.2 %shard_map.61 = (f32[32,16,1024]{2,1,0:T(8,128)}, f32[3,32,16,1024]{3,2,1,0:T(8,128)}) custom-call(bf16[32,16,1024]{2,1,0:T(8,128)(2,1)S(1)} %copy-done.1, bf16[32,16,1024]{2,1,0:T(8,128)(2,1)S(1)} %slice_bitcast_fusion.c0_ref, bf16[3,32,16,1024]{3,2,1,0:T(8,128)(2,1)} %c2_ref.1, bf16[3,32,16,1024]{3,2,1,0:T(8,128)(2,1)} %c2_ref.1, ...), custom_call_target="tpu_custom_call", output_to_operand_aliasing={{0}: (5, {})} | custom-call | tf_op jit(solution)/shard_map/pallas_call | solution.py:181
  (7 shorter events, 0.1 us)
Async XLA Ops:
  0.6 11.0 %copy-start = (bf16[32,16,1024]{2,1,0:T(8,128)(2,1)S(1)}, bf16[32,16,1024]{2,1,0:T(8,128)(2,1)}, u32[]{:S(2)}) copy-start(bf16[32,16,1024]{2,1,0:T(8,128)(2,1)} %d_ref.5) | copy-start | bytes 3145732
  5.1 19.2 %copy-start.2 = (s32[8]{0:T(128)S(1)}, s32[8]{0:T(128)}, u32[]{:S(2)}) copy-start(s32[8]{0:T(128)} %param.7) | copy-start | bytes 100
  5.1 19.3 %all-to-all-start = ((f32[8,4,16,128]{3,2,1,0:T(8,128)}), f32[8,4,16,128]{3,2,1,0:T(8,128)S(1)}, u32[]{:S(2)}, u32[]{:S(2)}) async-start(f32[8,4,16,128]{3,2,1,0:T(8,128)} %shard_map.59), calls=%async_computation | async-start | bytes 524288 | tf_op jit(solution)/shard_map/all_to_all | solution.py:255
  11.6 12.8 %collective-permute-start = (bf16[1,16,1024]{2,1,0:T(8,128)(2,1)S(1)}, bf16[1,16,1024]{2,1,0:T(8,128)(2,1)S(1)}, u32[]{:S(2)}, u32[]{:S(2)}) collective-permute-start(bf16[1,16,1024]{2,1,0:T(8,128)(2,1)S(1)} %get-tuple-element.16), channel_id=1, source_target_pairs={{0,4},{4,8},{8,12},{12,16},{16,20},{20,24},{24,28},{1,5},{5,9},{9,... | collective-permute-start | bytes 98312 | tf_op jit(solution)/shard_map/ppermute | solution.py:233
  15.0 9.4 %collective-permute-start.1 = (bf16[1,16,1024]{2,1,0:T(8,128)(2,1)S(1)}, bf16[1,16,1024]{2,1,0:T(8,128)(2,1)S(1)}, u32[]{:S(2)}, u32[]{:S(2)}) collective-permute-start(bf16[1,16,1024]{2,1,0:T(8,128)(2,1)S(1)} %get-tuple-element.17), channel_id=1, source_target_pairs={{4,0},{8,4},{12,8},{16,12},{20,16},{24,20},{28,24},{5,1},{9,5},{13... | collective-permute-start | bytes 98312 | tf_op jit(solution)/shard_map/ppermute | solution.py:234
  16.5 16.9 %collective-permute-start.2 = (bf16[32,1,1024]{2,1,0:T(2,128)(2,1)S(1)}, bf16[32,1,1024]{2,1,0:T(2,128)(2,1)S(1)}, u32[]{:S(2)}, u32[]{:S(2)}) collective-permute-start(bf16[32,1,1024]{2,1,0:T(2,128)(2,1)S(1)} %get-tuple-element.12), channel_id=1, source_target_pairs={{0,1},{1,2},{2,3},{4,5},{5,6},{6,7},{8,9},{9,10},{10,11},{12,13},{... | collective-permute-start | bytes 196616 | tf_op jit(solution)/shard_map/ppermute | solution.py:235
  21.0 12.4 %collective-permute-start.3 = (bf16[32,1,1024]{2,1,0:T(2,128)(2,1)S(1)}, bf16[32,1,1024]{2,1,0:T(2,128)(2,1)S(1)}, u32[]{:S(2)}, u32[]{:S(2)}) collective-permute-start(bf16[32,1,1024]{2,1,0:T(2,128)(2,1)S(1)} %get-tuple-element.13), channel_id=1, source_target_pairs={{1,0},{2,1},{3,2},{5,4},{6,5},{7,6},{9,8},{10,9},{11,10},{13,12},{... | collective-permute-start | bytes 196616 | tf_op jit(solution)/shard_map/ppermute | solution.py:236
  26.4 13.9 %all-to-all-start.1 = ((f32[8,4,16,128]{3,2,1,0:T(8,128)}), f32[8,4,16,128]{3,2,1,0:T(8,128)S(1)}, u32[]{:S(2)}, u32[]{:S(2)}) async-start(f32[8,4,16,128]{3,2,1,0:T(8,128)} %pad_maximum_fusion), calls=%async_computation.1 | async-start | bytes 524288 | tf_op jit(solution)/shard_map/all_to_all | solution.py:263
  33.8 6.5 %copy-start.1 = (bf16[32,16,1024]{2,1,0:T(8,128)(2,1)S(1)}, bf16[32,16,1024]{2,1,0:T(8,128)(2,1)}, u32[]{:S(2)}) copy-start(bf16[32,16,1024]{2,1,0:T(8,128)(2,1)} %d_ref.5) | copy-start | bytes 3145732

commit v18 on v16

--- a/solution.py
+++ b/solution.py
@@ -90,13 +90,18 @@
         lax.fori_loop(0, slices, body, start, unroll=2)
 
 
-def backward_kernel(d_ref, c_ref, ans_ref, smooth_ref, gd_ref, gc_ref, *, step, slices_total):
+def backward_kernel(
+    d_ref, c_ref, ans_ref, zhalo_ref, rhalo_ref, gd_ref, gc_ref, *, step, slices_total
+):
     slices, rows, block = gd_ref.shape
     shape = (rows, lanes)
     subs = block // lanes
     per_tile = ans_ref.shape[0] // (pl.num_programs(0) * subs)
     scale = -step * log2e
     gain = optical_depth / slices_total
+    row = lax.broadcasted_iota(jnp.int32, shape, 0)
+    first_row = row == 0
+    last_row = row == shape[0] - 1
 
     for j in range(subs):
         cols = pl.ds(j * lanes, lanes)
@@ -109,8 +114,16 @@
             return jnp.concatenate([ans_ref[base + g, c] for g in range(per_tile)], axis=0)
 
         def body(z, carry):
-            n, front, w0, w1, w2 = carry
-            d = d_ref[z, :, place].astype(jnp.float32)
+            n, front, w0, w1, w2, d_prev, d = carry
+            d_next = jnp.where(
+                z + 1 < slices,
+                d_ref[jnp.minimum(z + 1, slices - 1), :, place].astype(jnp.float32),
+                zhalo_ref[1, :, cols],
+            )
+            rims = rhalo_ref[z, :, cols]
+            upper = jnp.where(first_row, rims[0:1], pltpu.roll(d, 1, 0))
+            lower = jnp.where(last_row, rims[1:2], pltpu.roll(d, shape[0] - 1, 0))
+            smooth = 2.0 * smooth_weight * ((d - d_prev) + (d - d_next) + (d - upper) + (d - lower))
             dtn = softplus(d) * scale
             lit = front * (1.0 - jnp.exp2(dtn))
             n_next = n + dtn
@@ -125,12 +138,17 @@
             inner = emitted - inv * (pixel(3) - left)
             for c in range(3):
                 gc_ref[c, z, :, cols] = res[c] * lit_col[c] * (1.0 - col[c])
-            gd_ref[z, :, cols] = gain * through * jax.nn.sigmoid(d) * inner + smooth_ref[z, :, cols]
-            return (n_next, through, w[0], w[1], w[2])
+            gd_ref[z, :, cols] = gain * through * jax.nn.sigmoid(d) * inner + smooth
+            return (n_next, through, w[0], w[1], w[2], d, d_next)
 
         zero = jnp.zeros(shape, jnp.float32)
         one = jnp.ones(shape, jnp.float32)
-        lax.fori_loop(0, slices, body, (zero, one, zero, zero, zero), unroll=backward_unroll)
+        start = (
+            zero, one, zero, zero, zero,
+            zhalo_ref[0, :, cols],
+            d_ref[0, :, place].astype(jnp.float32),
+        )
+        lax.fori_loop(0, slices, body, start, unroll=backward_unroll)
 
 
 def forward_partial(density, colour_raw, step, depth_count):
@@ -169,32 +187,34 @@
     )(density, zhalo, rhalo)
 
 
-def backward_grads(density, colour_raw, answers, smooth, step, slices_total):
+def backward_grads(density, colour_raw, answers, zhalo, rhalo, step, slices_total):
     slices, rows, width = density.shape
     tiles = width // lanes
     block = lanes * backward_subs if tiles % backward_subs == 0 else lanes
     slab = pl.BlockSpec((slices, rows, block), lambda i: (0, 0, i))
     colours = pl.BlockSpec((3, slices, rows, block), lambda i: (0, 0, 0, i))
+    vmem = pl.BlockSpec(memory_space=pltpu.VMEM)
     return pl.pallas_call(
         functools.partial(backward_kernel, step=step, slices_total=float(slices_total)),
         grid=(width // block,),
         in_specs=[
-            pl.BlockSpec(memory_space=pltpu.VMEM),
+            vmem,
             colours,
-            pl.BlockSpec(memory_space=pltpu.VMEM),
-            slab,
+            vmem,
+            pl.BlockSpec((2, rows, block), lambda i: (0, 0, i)),
+            pl.BlockSpec((slices, 2, block), lambda i: (0, 0, i)),
         ],
         out_specs=[slab, colours],
         out_shape=[
             jax.ShapeDtypeStruct((slices, rows, width), jnp.float32),
             jax.ShapeDtypeStruct((3, slices, rows, width), jnp.float32),
         ],
-        input_output_aliases={3: 0},
     )(
         pltpu.with_memory_space_constraint(density, pltpu.VMEM),
         colour_raw,
         pltpu.with_memory_space_constraint(answers, pltpu.VMEM),
-        smooth,
+        zhalo,
+        rhalo,
     )
 
 
@@ -254,8 +274,7 @@
     )
     answers = composite(received, slab_rank, target_piece, float(slices_total))
     returned = lax.all_to_all(answers, "depth", 0, 0, tiled=True)
-    smooth = smooth_term(density_raw, zhalo, rhalo)
-    return backward_grads(density_raw, colour_raw, returned, smooth, step, slices_total)
+    return backward_grads(density_raw, colour_raw, returned, zhalo, rhalo, step, slices_total)
 
 
 def solution(mesh):

time: 48.3 us -> 48.5 us (level)
  waiting for transfers between devices: 1.91 us -> 5.94 us
  Pallas kernels: 16.9 us -> 13.1 us
    pallas_call x1 -> x0, Pallas kernels: 4.03 us -> none  [smooth_term(): pl.pallas_call(smooth_kernel, grid=(width // block,), in_specs=[slab, pl....]
    all_to_all x1, waiting for transfers between devices: 1.9 us -> 5.92 us  [local(): returned = lax.all_to_all(answers, 'depth', 0, 0, tiled=True)]
  transfers between devices with their start and end apart: 6 -> 6, of which waited for: 1 -> 1; matrix products, arithmetic and copies ran while one was open for 9% -> 9% of each run, Pallas kernels for 8% -> 0%
where the time goes in v18:
time: 48.5 us; the launch traced here: 48 us
  starting transfers between devices  23.8 us (49%)
  Pallas kernels  13.1 us (27%)
  waiting for transfers between devices  5.94 us (12%)
  other arithmetic  4.05 us (8%)
  between operations  0.78 us (2%)
    pallas_call x1, Pallas kernels, backward_grads(): pl.pallas_call(functools.partial(backward_kernel, step=step, slices_total...  8.69 us
    all_to_all x1, starting transfers between devices, local(): received = lax.all_to_all(partial_value, 'depth', 0, 0, tiled=True)  6.38 us
    all_to_all x1, starting transfers between devices, local(): returned = lax.all_to_all(answers, 'depth', 0, 0, tiled=True)  6.34 us
    all_to_all x1, waiting for transfers between devices, local(): returned = lax.all_to_all(answers, 'depth', 0, 0, tiled=True)  5.92 us
    ppermute x1, starting transfers between devices, halos(): prev_row = lax.ppermute(last_row, 'rows', up_r)  4.52 us
    pallas_call x1, Pallas kernels, forward_partial(): pl.pallas_call(functools.partial(forward_kernel, step=step), grid=(width...  4.43 us
    ppermute x1, starting transfers between devices, halos(): prev_slice = lax.ppermute(last_slice, 'depth', up_d)  3.36 us
    ppermute x1, starting transfers between devices, halos(): next_row = lax.ppermute(first_row, 'rows', [(j, i) for i, j in up_r])  1.92 us
  transfers between devices with their start and end apart: 6, of which 1 were waited for; matrix products, arithmetic and copies ran while one was open for 9% of the time, Pallas kernels for 0%

profile of v18, /device:TPU:1, one launch (start us, length us, event | category | flops | bytes accessed | tf_op | source)
XLA Modules:
  0.0 48.0 jit_solution(2686589775733540375)
XLA Ops:
  0.6 0.0 copy-start
  0.6 0.0 copy-start.1
  0.6 4.4 %shard_map.59 = f32[8,4,16,128]{3,2,1,0:T(8,128)} custom-call(bf16[32,16,1024]{2,1,0:T(8,128)(2,1)} %d_ref.3, bf16[3,32,16,1024]{3,2,1,0:T(8,128)(2,1)} %c_ref.3), custom_call_target="tpu_custom_call" | custom-call | tf_op jit(solution)/shard_map/pallas_call | solution.py:158
  5.1 6.4 %all-to-all-start = ((f32[8,4,16,128]{3,2,1,0:T(8,128)}), f32[8,4,16,128]{3,2,1,0:T(8,128)S(1)}, u32[]{:S(2)}, u32[]{:S(2)}) async-start(f32[8,4,16,128]{3,2,1,0:T(8,128)} %shard_map.59), calls=%async_computation | async-start | bytes 524288 | tf_op jit(solution)/shard_map/all_to_all | solution.py:268
  11.5 0.0 copy-done
  11.5 3.4 %collective-permute-start = (bf16[1,16,1024]{2,1,0:T(8,128)(2,1)S(1)}, bf16[1,16,1024]{2,1,0:T(8,128)(2,1)S(1)}, u32[]{:S(2)}, u32[]{:S(2)}) collective-permute-start(bf16[1,16,1024]{2,1,0:T(8,128)(2,1)S(1)} %get-tuple-element.16), channel_id=1, source_target_pairs={{0,4},{4,8},{8,12},{12,16},{16,20},{20,24},{24,28},{1,5},{5,9},{9,... | collective-permute-start | bytes 98312 | tf_op jit(solution)/shard_map/ppermute | solution.py:246
  14.8 1.3 %collective-permute-start.1 = (bf16[1,16,1024]{2,1,0:T(8,128)(2,1)S(1)}, bf16[1,16,1024]{2,1,0:T(8,128)(2,1)S(1)}, u32[]{:S(2)}, u32[]{:S(2)}) collective-permute-start(bf16[1,16,1024]{2,1,0:T(8,128)(2,1)S(1)} %get-tuple-element.17), channel_id=1, source_target_pairs={{4,0},{8,4},{12,8},{16,12},{20,16},{24,20},{28,24},{5,1},{9,5},{13... | collective-permute-start | bytes 98312 | tf_op jit(solution)/shard_map/ppermute | solution.py:247
  16.1 0.2 fusion.5
  16.4 4.5 %collective-permute-start.2 = (bf16[32,1,1024]{2,1,0:T(2,128)(2,1)S(1)}, bf16[32,1,1024]{2,1,0:T(2,128)(2,1)S(1)}, u32[]{:S(2)}, u32[]{:S(2)}) collective-permute-start(bf16[32,1,1024]{2,1,0:T(2,128)(2,1)S(1)} %get-tuple-element.12), channel_id=1, source_target_pairs={{0,1},{1,2},{2,3},{4,5},{5,6},{6,7},{8,9},{9,10},{10,11},{12,13},{... | collective-permute-start | bytes 196616 | tf_op jit(solution)/shard_map/ppermute | solution.py:248
  20.9 1.9 %collective-permute-start.3 = (bf16[32,1,1024]{2,1,0:T(2,128)(2,1)S(1)}, bf16[32,1,1024]{2,1,0:T(2,128)(2,1)S(1)}, u32[]{:S(2)}, u32[]{:S(2)}) collective-permute-start(bf16[32,1,1024]{2,1,0:T(2,128)(2,1)S(1)} %get-tuple-element.13), channel_id=1, source_target_pairs={{1,0},{2,1},{3,2},{5,4},{6,5},{7,6},{9,8},{10,9},{11,10},{13,12},{... | collective-permute-start | bytes 196616 | tf_op jit(solution)/shard_map/ppermute | solution.py:249
  22.8 0.0 copy-done.1
  22.8 0.1 compare_convert_fusion
  22.9 0.0 collective-permute-done
  22.9 0.0 collective-permute-done.1
  22.9 0.0 all-to-all-done
  23.0 0.1 multiply_reduce_fusion.1
  23.2 0.2 multiply_reduce_fusion
  23.3 0.8 %dynamic-slice_subtract_fusion = f32[3,16,128]{2,1,0:T(8,128)S(1)} fusion(f32[3,16,128]{2,1,0:T(8,128)S(1)} %get-tuple-element.8, f32[3,16,1024]{2,1,0:T(8,128)} %param.6, s32[]{:T(128)S(6)} %select_n.39), kind=kLoop, calls=%fused_computation.20 | loop fusion | flops 6144 | bytes 73732 | tf_op jit(solution)/shard_map/sub | solution.py:228
  24.1 0.1 multiply_reduce_fusion.3
  24.2 0.7 %pad_maximum_fusion = f32[8,4,16,128]{3,2,1,0:T(8,128)} fusion(f32[8,1,16,128]{3,2,1,0:T(8,128)S(1)} %fusion.2, f32[8,3,16,128]{3,2,1,0:T(8,128)S(1)} %get-tuple-element.18), kind=kLoop, calls=%fused_computation.2 | loop fusion | flops 65536 | bytes 524288 | tf_op jit(solution)/shard_map/concatenate | solution.py:232
  24.9 6.3 %all-to-all-start.1 = ((f32[8,4,16,128]{3,2,1,0:T(8,128)}), f32[8,4,16,128]{3,2,1,0:T(8,128)S(1)}, u32[]{:S(2)}, u32[]{:S(2)}) async-start(f32[8,4,16,128]{3,2,1,0:T(8,128)} %pad_maximum_fusion), calls=%async_computation.1 | async-start | bytes 524288 | tf_op jit(solution)/shard_map/all_to_all | solution.py:276
  31.3 0.7 %maximum_convert_fusion.1.zhalo_ref = f32[2,16,1024]{2,1,0:T(8,128)} fusion(bf16[1,16,1024]{2,1,0:T(8,128)(2,1)S(1)} %get-tuple-element.15, bf16[1,16,1024]{2,1,0:T(8,128)(2,1)S(1)} %get-tuple-element.14), kind=kLoop, calls=%fused_computation.10 | loop fusion | flops 65536 | bytes 196608 | tf_op jit(solution)/shard_map/convert_element_type | solution.py:254
  31.9 0.0 collective-permute-done.2
  31.9 0.0 collective-permute-done.3
  32.0 0.4 broadcast_select_fusion.1
  32.4 1.0 %maximum_convert_fusion.rhalo_ref = f32[32,2,1024]{2,1,0:T(2,128)} fusion(bf16[32,1,1024]{2,1,0:T(2,128)(2,1)S(1)} %get-tuple-element.11, bf16[32,1,1024]{2,1,0:T(2,128)(2,1)S(1)} %get-tuple-element.10), kind=kLoop, calls=%fused_computation.9 | loop fusion | flops 262144 | bytes 393216 | tf_op jit(solution)/shard_map/convert_element_type | solution.py:255
  33.3 5.9 %all-to-all-done.1.ans_ref = f32[8,4,16,128]{3,2,1,0:T(8,128)S(1)} async-done(((f32[8,4,16,128]{3,2,1,0:T(8,128)}), f32[8,4,16,128]{3,2,1,0:T(8,128)S(1)}, u32[]{:S(2)}, u32[]{:S(2)}) %all-to-all-start.1) | async-done | bytes 262176 | tf_op jit(solution)/shard_map/all_to_all | solution.py:276
  39.3 8.7 %shard_map.60 = (f32[32,16,1024]{2,1,0:T(8,128)}, f32[3,32,16,1024]{3,2,1,0:T(8,128)}) custom-call(bf16[32,16,1024]{2,1,0:T(8,128)(2,1)S(1)} %copy-done, bf16[3,32,16,1024]{3,2,1,0:T(8,128)(2,1)} %c_ref.3, f32[8,4,16,128]{3,2,1,0:T(8,128)S(1)} %all-to-all-done.1.ans_ref, f32[2,16,1024]{2,1,0:T(8,128)} %maximum_convert_fusion.1.zhalo_ref, ...), custom_call_target="tpu_custom_call" | custom-call | tf_op jit(solution)/shard_map/pallas_call | solution.py:197
  (7 shorter events, 0.1 us)
Async XLA Ops:
  0.6 10.8 %copy-start = (bf16[32,16,1024]{2,1,0:T(8,128)(2,1)S(1)}, bf16[32,16,1024]{2,1,0:T(8,128)(2,1)}, u32[]{:S(2)}) copy-start(bf16[32,16,1024]{2,1,0:T(8,128)(2,1)} %d_ref.3) | copy-start | bytes 3145732
  0.6 22.2 %copy-start.1 = (s32[8]{0:T(128)S(1)}, s32[8]{0:T(128)}, u32[]{:S(2)}) copy-start(s32[8]{0:T(128)} %param.7) | copy-start | bytes 100
  5.1 17.8 %all-to-all-start = ((f32[8,4,16,128]{3,2,1,0:T(8,128)}), f32[8,4,16,128]{3,2,1,0:T(8,128)S(1)}, u32[]{:S(2)}, u32[]{:S(2)}) async-start(f32[8,4,16,128]{3,2,1,0:T(8,128)} %shard_map.59), calls=%async_computation | async-start | bytes 524288 | tf_op jit(solution)/shard_map/all_to_all | solution.py:268
  11.5 11.4 %collective-permute-start = (bf16[1,16,1024]{2,1,0:T(8,128)(2,1)S(1)}, bf16[1,16,1024]{2,1,0:T(8,128)(2,1)S(1)}, u32[]{:S(2)}, u32[]{:S(2)}) collective-permute-start(bf16[1,16,1024]{2,1,0:T(8,128)(2,1)S(1)} %get-tuple-element.16), channel_id=1, source_target_pairs={{0,4},{4,8},{8,12},{12,16},{16,20},{20,24},{24,28},{1,5},{5,9},{9,... | collective-permute-start | bytes 98312 | tf_op jit(solution)/shard_map/ppermute | solution.py:246
  14.8 8.1 %collective-permute-start.1 = (bf16[1,16,1024]{2,1,0:T(8,128)(2,1)S(1)}, bf16[1,16,1024]{2,1,0:T(8,128)(2,1)S(1)}, u32[]{:S(2)}, u32[]{:S(2)}) collective-permute-start(bf16[1,16,1024]{2,1,0:T(8,128)(2,1)S(1)} %get-tuple-element.17), channel_id=1, source_target_pairs={{4,0},{8,4},{12,8},{16,12},{20,16},{24,20},{28,24},{5,1},{9,5},{13... | collective-permute-start | bytes 98312 | tf_op jit(solution)/shard_map/ppermute | solution.py:247
  16.4 15.6 %collective-permute-start.2 = (bf16[32,1,1024]{2,1,0:T(2,128)(2,1)S(1)}, bf16[32,1,1024]{2,1,0:T(2,128)(2,1)S(1)}, u32[]{:S(2)}, u32[]{:S(2)}) collective-permute-start(bf16[32,1,1024]{2,1,0:T(2,128)(2,1)S(1)} %get-tuple-element.12), channel_id=1, source_target_pairs={{0,1},{1,2},{2,3},{4,5},{5,6},{6,7},{8,9},{9,10},{10,11},{12,13},{... | collective-permute-start | bytes 196616 | tf_op jit(solution)/shard_map/ppermute | solution.py:248
  20.9 11.1 %collective-permute-start.3 = (bf16[32,1,1024]{2,1,0:T(2,128)(2,1)S(1)}, bf16[32,1,1024]{2,1,0:T(2,128)(2,1)S(1)}, u32[]{:S(2)}, u32[]{:S(2)}) collective-permute-start(bf16[32,1,1024]{2,1,0:T(2,128)(2,1)S(1)} %get-tuple-element.13), channel_id=1, source_target_pairs={{1,0},{2,1},{3,2},{5,4},{6,5},{7,6},{9,8},{10,9},{11,10},{13,12},{... | collective-permute-start | bytes 196616 | tf_op jit(solution)/shard_map/ppermute | solution.py:249
  24.9 14.3 %all-to-all-start.1 = ((f32[8,4,16,128]{3,2,1,0:T(8,128)}), f32[8,4,16,128]{3,2,1,0:T(8,128)S(1)}, u32[]{:S(2)}, u32[]{:S(2)}) async-start(f32[8,4,16,128]{3,2,1,0:T(8,128)} %pad_maximum_fusion), calls=%async_computation.1 | async-start | bytes 524288 | tf_op jit(solution)/shard_map/all_to_all | solution.py:276

commit v19 on v16

--- a/solution.py
+++ b/solution.py
@@ -13,7 +13,7 @@
 forward_subs = 4
 backward_subs = 2
 forward_unroll = 32
-backward_unroll = 8
+backward_unroll = 16
 
 
 log2e = 1.4426950408889634

time: 48.3 us -> 48.1 us (level)
  no operation moved by 1% of the time
where the time goes in v19:
time: 48.1 us; the launch traced here: 47.5 us
  starting transfers between devices  23.8 us (49%)
  Pallas kernels  16.7 us (35%)
  other arithmetic  4.04 us (8%)
  waiting for transfers between devices  1.91 us (4%)
  between operations  0.79 us (2%)
    pallas_call x1, Pallas kernels, backward_grads(): pl.pallas_call(functools.partial(backward_kernel, step=step, slices_total...  8.23 us
    all_to_all x1, starting transfers between devices, local(): received = lax.all_to_all(partial_value, 'depth', 0, 0, tiled=True)  6.38 us
    all_to_all x1, starting transfers between devices, local(): returned = lax.all_to_all(answers, 'depth', 0, 0, tiled=True)  6.34 us
    ppermute x1, starting transfers between devices, halos(): prev_row = lax.ppermute(last_row, 'rows', up_r)  4.52 us
    pallas_call x1, Pallas kernels, forward_partial(): pl.pallas_call(functools.partial(forward_kernel, step=step), grid=(width...  4.43 us
    pallas_call x1, Pallas kernels, smooth_term(): pl.pallas_call(smooth_kernel, grid=(width // block,), in_specs=[slab, pl....  4.03 us
    ppermute x1, starting transfers between devices, halos(): prev_slice = lax.ppermute(last_slice, 'depth', up_d)  3.36 us
    ppermute x1, starting transfers between devices, halos(): next_row = lax.ppermute(first_row, 'rows', [(j, i) for i, j in up_r])  1.92 us
  transfers between devices with their start and end apart: 6, of which 1 were waited for; matrix products, arithmetic and copies ran while one was open for 9% of the time, Pallas kernels for 8%

profile of v19, /device:TPU:1, one launch (start us, length us, event | category | flops | bytes accessed | tf_op | source)
XLA Modules:
  0.0 47.5 jit_solution(4318099392204317815)
XLA Ops:
  0.6 0.0 copy-start
  0.6 0.0 copy-start.2
  0.7 4.4 %shard_map.59 = f32[8,4,16,128]{3,2,1,0:T(8,128)} custom-call(bf16[32,16,1024]{2,1,0:T(8,128)(2,1)} %d_ref.5, bf16[3,32,16,1024]{3,2,1,0:T(8,128)(2,1)} %c_ref.3), custom_call_target="tpu_custom_call" | custom-call | tf_op jit(solution)/shard_map/pallas_call | solution.py:140
  5.1 6.4 %all-to-all-start = ((f32[8,4,16,128]{3,2,1,0:T(8,128)}), f32[8,4,16,128]{3,2,1,0:T(8,128)S(1)}, u32[]{:S(2)}, u32[]{:S(2)}) async-start(f32[8,4,16,128]{3,2,1,0:T(8,128)} %shard_map.59), calls=%async_computation | async-start | bytes 524288 | tf_op jit(solution)/shard_map/all_to_all | solution.py:248
  11.5 0.0 copy-done
  11.5 3.4 %collective-permute-start = (bf16[1,16,1024]{2,1,0:T(8,128)(2,1)S(1)}, bf16[1,16,1024]{2,1,0:T(8,128)(2,1)S(1)}, u32[]{:S(2)}, u32[]{:S(2)}) collective-permute-start(bf16[1,16,1024]{2,1,0:T(8,128)(2,1)S(1)} %get-tuple-element.16), channel_id=1, source_target_pairs={{0,4},{4,8},{8,12},{12,16},{16,20},{20,24},{24,28},{1,5},{5,9},{9,... | collective-permute-start | bytes 98312 | tf_op jit(solution)/shard_map/ppermute | solution.py:226
  14.8 1.3 %collective-permute-start.1 = (bf16[1,16,1024]{2,1,0:T(8,128)(2,1)S(1)}, bf16[1,16,1024]{2,1,0:T(8,128)(2,1)S(1)}, u32[]{:S(2)}, u32[]{:S(2)}) collective-permute-start(bf16[1,16,1024]{2,1,0:T(8,128)(2,1)S(1)} %get-tuple-element.17), channel_id=1, source_target_pairs={{4,0},{8,4},{12,8},{16,12},{20,16},{24,20},{28,24},{5,1},{9,5},{13... | collective-permute-start | bytes 98312 | tf_op jit(solution)/shard_map/ppermute | solution.py:227
  16.1 0.2 fusion.5
  16.4 4.5 %collective-permute-start.2 = (bf16[32,1,1024]{2,1,0:T(2,128)(2,1)S(1)}, bf16[32,1,1024]{2,1,0:T(2,128)(2,1)S(1)}, u32[]{:S(2)}, u32[]{:S(2)}) collective-permute-start(bf16[32,1,1024]{2,1,0:T(2,128)(2,1)S(1)} %get-tuple-element.12), channel_id=1, source_target_pairs={{0,1},{1,2},{2,3},{4,5},{5,6},{6,7},{8,9},{9,10},{10,11},{12,13},{... | collective-permute-start | bytes 196616 | tf_op jit(solution)/shard_map/ppermute | solution.py:228
  20.9 1.9 %collective-permute-start.3 = (bf16[32,1,1024]{2,1,0:T(2,128)(2,1)S(1)}, bf16[32,1,1024]{2,1,0:T(2,128)(2,1)S(1)}, u32[]{:S(2)}, u32[]{:S(2)}) collective-permute-start(bf16[32,1,1024]{2,1,0:T(2,128)(2,1)S(1)} %get-tuple-element.13), channel_id=1, source_target_pairs={{1,0},{2,1},{3,2},{5,4},{6,5},{7,6},{9,8},{10,9},{11,10},{13,12},{... | collective-permute-start | bytes 196616 | tf_op jit(solution)/shard_map/ppermute | solution.py:229
  22.8 0.0 copy-done.2
  22.8 0.1 compare_convert_fusion
  22.9 0.0 collective-permute-done
  22.9 0.0 collective-permute-done.1
  22.9 0.0 all-to-all-done
  23.0 0.1 multiply_reduce_fusion.1
  23.2 0.2 multiply_reduce_fusion
  23.3 0.8 %dynamic-slice_subtract_fusion = f32[3,16,128]{2,1,0:T(8,128)S(1)} fusion(f32[3,16,128]{2,1,0:T(8,128)S(1)} %get-tuple-element.8, f32[3,16,1024]{2,1,0:T(8,128)} %param.6, s32[]{:T(128)S(6)} %select_n.39), kind=kLoop, calls=%fused_computation.20 | loop fusion | flops 6144 | bytes 73732 | tf_op jit(solution)/shard_map/sub | solution.py:208
  24.1 0.1 multiply_reduce_fusion.3
  24.2 0.7 %pad_maximum_fusion = f32[8,4,16,128]{3,2,1,0:T(8,128)} fusion(f32[8,1,16,128]{3,2,1,0:T(8,128)S(1)} %fusion.2, f32[8,3,16,128]{3,2,1,0:T(8,128)S(1)} %get-tuple-element.18), kind=kLoop, calls=%fused_computation.2 | loop fusion | flops 65536 | bytes 524288 | tf_op jit(solution)/shard_map/concatenate | solution.py:212
  24.9 6.3 %all-to-all-start.1 = ((f32[8,4,16,128]{3,2,1,0:T(8,128)}), f32[8,4,16,128]{3,2,1,0:T(8,128)S(1)}, u32[]{:S(2)}, u32[]{:S(2)}) async-start(f32[8,4,16,128]{3,2,1,0:T(8,128)} %pad_maximum_fusion), calls=%async_computation.1 | async-start | bytes 524288 | tf_op jit(solution)/shard_map/all_to_all | solution.py:256
  31.3 0.7 %maximum_convert_fusion.1.zhalo_ref = f32[2,16,1024]{2,1,0:T(8,128)} fusion(bf16[1,16,1024]{2,1,0:T(8,128)(2,1)S(1)} %get-tuple-element.15, bf16[1,16,1024]{2,1,0:T(8,128)(2,1)S(1)} %get-tuple-element.14), kind=kLoop, calls=%fused_computation.10 | loop fusion | flops 65536 | bytes 196608 | tf_op jit(solution)/shard_map/convert_element_type | solution.py:234
  31.9 0.0 collective-permute-done.2
  31.9 0.0 collective-permute-done.3
  31.9 0.4 broadcast_select_fusion.1
  32.3 0.0 copy-start.1
  32.3 1.0 %maximum_convert_fusion.rhalo_ref = f32[32,2,1024]{2,1,0:T(2,128)} fusion(bf16[32,1,1024]{2,1,0:T(2,128)(2,1)S(1)} %get-tuple-element.11, bf16[32,1,1024]{2,1,0:T(2,128)(2,1)S(1)} %get-tuple-element.10), kind=kLoop, calls=%fused_computation.9 | loop fusion | flops 262144 | bytes 393216 | tf_op jit(solution)/shard_map/convert_element_type | solution.py:235
  33.3 4.0 %shard_map.60.smooth_ref = f32[32,16,1024]{2,1,0:T(8,128)} custom-call(bf16[32,16,1024]{2,1,0:T(8,128)(2,1)} %d_ref.5, f32[2,16,1024]{2,1,0:T(8,128)} %maximum_convert_fusion.1.zhalo_ref, f32[32,2,1024]{2,1,0:T(2,128)} %maximum_convert_fusion.rhalo_ref), custom_call_target="tpu_custom_call" | custom-call | tf_op jit(solution)/shard_map/pallas_call | solution.py:159
  37.4 1.9 %all-to-all-done.1.ans_ref = f32[8,4,16,128]{3,2,1,0:T(8,128)S(1)} async-done(((f32[8,4,16,128]{3,2,1,0:T(8,128)}), f32[8,4,16,128]{3,2,1,0:T(8,128)S(1)}, u32[]{:S(2)}, u32[]{:S(2)}) %all-to-all-start.1) | async-done | bytes 262176 | tf_op jit(solution)/shard_map/all_to_all | solution.py:256
  39.3 0.0 copy-done.1
  39.3 8.2 %shard_map.61 = (f32[32,16,1024]{2,1,0:T(8,128)}, f32[3,32,16,1024]{3,2,1,0:T(8,128)}) custom-call(bf16[32,16,1024]{2,1,0:T(8,128)(2,1)S(1)} %copy-done.1, bf16[3,32,16,1024]{3,2,1,0:T(8,128)(2,1)} %c_ref.3, f32[8,4,16,128]{3,2,1,0:T(8,128)S(1)} %all-to-all-done.1.ans_ref, f32[32,16,1024]{2,1,0:T(8,128)} %shard_map.60.smooth_ref), custom_call_target="tpu_custom_call", output_to_operand_aliasing={{0}: (3, {})} | custom-call | tf_op jit(solution)/shard_map/pallas_call | solution.py:178
  (7 shorter events, 0.1 us)
Async XLA Ops:
  0.6 10.8 %copy-start = (bf16[32,16,1024]{2,1,0:T(8,128)(2,1)S(1)}, bf16[32,16,1024]{2,1,0:T(8,128)(2,1)}, u32[]{:S(2)}) copy-start(bf16[32,16,1024]{2,1,0:T(8,128)(2,1)} %d_ref.5) | copy-start | bytes 3145732
  0.6 22.2 %copy-start.2 = (s32[8]{0:T(128)S(1)}, s32[8]{0:T(128)}, u32[]{:S(2)}) copy-start(s32[8]{0:T(128)} %param.7) | copy-start | bytes 100
  5.1 17.8 %all-to-all-start = ((f32[8,4,16,128]{3,2,1,0:T(8,128)}), f32[8,4,16,128]{3,2,1,0:T(8,128)S(1)}, u32[]{:S(2)}, u32[]{:S(2)}) async-start(f32[8,4,16,128]{3,2,1,0:T(8,128)} %shard_map.59), calls=%async_computation | async-start | bytes 524288 | tf_op jit(solution)/shard_map/all_to_all | solution.py:248
  11.5 11.4 %collective-permute-start = (bf16[1,16,1024]{2,1,0:T(8,128)(2,1)S(1)}, bf16[1,16,1024]{2,1,0:T(8,128)(2,1)S(1)}, u32[]{:S(2)}, u32[]{:S(2)}) collective-permute-start(bf16[1,16,1024]{2,1,0:T(8,128)(2,1)S(1)} %get-tuple-element.16), channel_id=1, source_target_pairs={{0,4},{4,8},{8,12},{12,16},{16,20},{20,24},{24,28},{1,5},{5,9},{9,... | collective-permute-start | bytes 98312 | tf_op jit(solution)/shard_map/ppermute | solution.py:226
  14.8 8.1 %collective-permute-start.1 = (bf16[1,16,1024]{2,1,0:T(8,128)(2,1)S(1)}, bf16[1,16,1024]{2,1,0:T(8,128)(2,1)S(1)}, u32[]{:S(2)}, u32[]{:S(2)}) collective-permute-start(bf16[1,16,1024]{2,1,0:T(8,128)(2,1)S(1)} %get-tuple-element.17), channel_id=1, source_target_pairs={{4,0},{8,4},{12,8},{16,12},{20,16},{24,20},{28,24},{5,1},{9,5},{13... | collective-permute-start | bytes 98312 | tf_op jit(solution)/shard_map/ppermute | solution.py:227
  16.4 15.6 %collective-permute-start.2 = (bf16[32,1,1024]{2,1,0:T(2,128)(2,1)S(1)}, bf16[32,1,1024]{2,1,0:T(2,128)(2,1)S(1)}, u32[]{:S(2)}, u32[]{:S(2)}) collective-permute-start(bf16[32,1,1024]{2,1,0:T(2,128)(2,1)S(1)} %get-tuple-element.12), channel_id=1, source_target_pairs={{0,1},{1,2},{2,3},{4,5},{5,6},{6,7},{8,9},{9,10},{10,11},{12,13},{... | collective-permute-start | bytes 196616 | tf_op jit(solution)/shard_map/ppermute | solution.py:228
  20.9 11.0 %collective-permute-start.3 = (bf16[32,1,1024]{2,1,0:T(2,128)(2,1)S(1)}, bf16[32,1,1024]{2,1,0:T(2,128)(2,1)S(1)}, u32[]{:S(2)}, u32[]{:S(2)}) collective-permute-start(bf16[32,1,1024]{2,1,0:T(2,128)(2,1)S(1)} %get-tuple-element.13), channel_id=1, source_target_pairs={{1,0},{2,1},{3,2},{5,4},{6,5},{7,6},{9,8},{10,9},{11,10},{13,12},{... | collective-permute-start | bytes 196616 | tf_op jit(solution)/shard_map/ppermute | solution.py:229
  24.9 14.3 %all-to-all-start.1 = ((f32[8,4,16,128]{3,2,1,0:T(8,128)}), f32[8,4,16,128]{3,2,1,0:T(8,128)S(1)}, u32[]{:S(2)}, u32[]{:S(2)}) async-start(f32[8,4,16,128]{3,2,1,0:T(8,128)} %pad_maximum_fusion), calls=%async_computation.1 | async-start | bytes 524288 | tf_op jit(solution)/shard_map/all_to_all | solution.py:256
  32.3 6.9 %copy-start.1 = (bf16[32,16,1024]{2,1,0:T(8,128)(2,1)S(1)}, bf16[32,16,1024]{2,1,0:T(8,128)(2,1)}, u32[]{:S(2)}) copy-start(bf16[32,16,1024]{2,1,0:T(8,128)(2,1)} %d_ref.5) | copy-start | bytes 3145732

commit v20 on v19

--- a/solution.py
+++ b/solution.py
@@ -31,7 +31,7 @@
 
 
 def forward_kernel(d_ref, c_ref, out_ref, *, step):
-    slices, rows, block = d_ref.shape
+    slices, rows, block = c_ref.shape[1:]
     shape = (rows, lanes)
     subs = block // lanes
     per_tile = out_ref.shape[0] // subs
@@ -40,10 +40,11 @@
 
     for j in range(subs):
         cols = pl.ds(j * lanes, lanes)
+        place = pl.ds(pl.multiple_of((pl.program_id(0) * subs + j) * lanes, lanes), lanes)
 
         def body(z, carry):
             n, front, e0, e1, e2 = carry
-            dtn = softplus(d_ref[z, :, cols].astype(jnp.float32)) * scale
+            dtn = softplus(d_ref[z, :, place].astype(jnp.float32)) * scale
             kept = jnp.exp2(dtn)
             lit = front * (1.0 - kept)
             n = n + dtn
@@ -141,14 +142,14 @@
         functools.partial(forward_kernel, step=step),
         grid=(width // block,),
         in_specs=[
-            pl.BlockSpec((slices, rows, block), lambda i: (0, 0, i)),
+            pl.BlockSpec(memory_space=pltpu.VMEM),
             pl.BlockSpec((3, slices, rows, block), lambda i: (0, 0, 0, i)),
         ],
         out_specs=pl.BlockSpec(
             (per_tile * (block // lanes), 4, chunk_rows, lanes), lambda i: (i, 0, 0, 0)
         ),
         out_shape=jax.ShapeDtypeStruct((tiles * per_tile, 4, chunk_rows, lanes), jnp.float32),
-    )(density, colour_raw)
+    )(pltpu.with_memory_space_constraint(density, pltpu.VMEM), colour_raw)
 
 
 def smooth_term(density, zhalo, rhalo):

time: 48.1 us -> 49.1 us (1.021)
  local copies, waits for them, and re-layouts: 0.27 us -> 1.48 us
    unnamed x6, local copies, waits for them, and re-layouts: 0.02 us -> 1.23 us
where the time goes in v20:
time: 49.1 us; the launch traced here: 48.5 us
  starting transfers between devices  23.8 us (48%)
  Pallas kernels  16.5 us (34%)
  other arithmetic  4.04 us (8%)
  waiting for transfers between devices  1.91 us (4%)
  local copies, waits for them, and re-layouts  1.48 us (3%)
  between operations  0.77 us (2%)
    pallas_call x1, Pallas kernels, backward_grads(): pl.pallas_call(functools.partial(backward_kernel, step=step, slices_total...  8.23 us
    all_to_all x1, starting transfers between devices, local(): received = lax.all_to_all(partial_value, 'depth', 0, 0, tiled=True)  6.38 us
    all_to_all x1, starting transfers between devices, local(): returned = lax.all_to_all(answers, 'depth', 0, 0, tiled=True)  6.34 us
    ppermute x1, starting transfers between devices, halos(): prev_row = lax.ppermute(last_row, 'rows', up_r)  4.52 us
    pallas_call x1, Pallas kernels, forward_partial(): pl.pallas_call(functools.partial(forward_kernel, step=step), grid=(width...  4.2 us
    pallas_call x1, Pallas kernels, smooth_term(): pl.pallas_call(smooth_kernel, grid=(width // block,), in_specs=[slab, pl....  4.03 us
    ppermute x1, starting transfers between devices, halos(): prev_slice = lax.ppermute(last_slice, 'depth', up_d)  3.37 us
    ppermute x1, starting transfers between devices, halos(): next_row = lax.ppermute(first_row, 'rows', [(j, i) for i, j in up_r])  1.92 us
  transfers between devices with their start and end apart: 6, of which 1 were waited for; matrix products, arithmetic and copies ran while one was open for 9% of the time, Pallas kernels for 8%

profile of v20, /device:TPU:1, one launch (start us, length us, event | category | flops | bytes accessed | tf_op | source)
XLA Modules:
  0.0 48.5 jit_solution(16973485400439635941)
XLA Ops:
  0.6 0.0 copy-start
  0.6 1.2 %copy-done = bf16[32,16,1024]{2,1,0:T(8,128)(2,1)S(1)} copy-done((bf16[32,16,1024]{2,1,0:T(8,128)(2,1)S(1)}, bf16[32,16,1024]{2,1,0:T(8,128)(2,1)}, u32[]{:S(2)}) %copy-start) | copy-done | bytes 1048600
  1.9 0.0 copy-start.2
  1.9 4.2 %shard_map.59 = f32[8,4,16,128]{3,2,1,0:T(8,128)} custom-call(bf16[32,16,1024]{2,1,0:T(8,128)(2,1)S(1)} %copy-done, bf16[3,32,16,1024]{3,2,1,0:T(8,128)(2,1)} %c_ref.3), custom_call_target="tpu_custom_call" | custom-call | tf_op jit(solution)/shard_map/pallas_call | solution.py:141
  6.1 6.4 %all-to-all-start = ((f32[8,4,16,128]{3,2,1,0:T(8,128)}), f32[8,4,16,128]{3,2,1,0:T(8,128)S(1)}, u32[]{:S(2)}, u32[]{:S(2)}) async-start(f32[8,4,16,128]{3,2,1,0:T(8,128)} %shard_map.59), calls=%async_computation | async-start | bytes 524288 | tf_op jit(solution)/shard_map/all_to_all | solution.py:249
  12.5 3.4 %collective-permute-start = (bf16[1,16,1024]{2,1,0:T(8,128)(2,1)S(1)}, bf16[1,16,1024]{2,1,0:T(8,128)(2,1)S(1)}, u32[]{:S(2)}, u32[]{:S(2)}) collective-permute-start(bf16[1,16,1024]{2,1,0:T(8,128)(2,1)S(1)} %get-tuple-element.16), channel_id=1, source_target_pairs={{0,4},{4,8},{8,12},{12,16},{16,20},{20,24},{24,28},{1,5},{5,9},{9,... | collective-permute-start | bytes 98312 | tf_op jit(solution)/shard_map/ppermute | solution.py:227
  15.8 1.3 %collective-permute-start.1 = (bf16[1,16,1024]{2,1,0:T(8,128)(2,1)S(1)}, bf16[1,16,1024]{2,1,0:T(8,128)(2,1)S(1)}, u32[]{:S(2)}, u32[]{:S(2)}) collective-permute-start(bf16[1,16,1024]{2,1,0:T(8,128)(2,1)S(1)} %get-tuple-element.17), channel_id=1, source_target_pairs={{4,0},{8,4},{12,8},{16,12},{20,16},{24,20},{28,24},{5,1},{9,5},{13... | collective-permute-start | bytes 98312 | tf_op jit(solution)/shard_map/ppermute | solution.py:228
  17.1 0.2 fusion.5
  17.3 4.5 %collective-permute-start.2 = (bf16[32,1,1024]{2,1,0:T(2,128)(2,1)S(1)}, bf16[32,1,1024]{2,1,0:T(2,128)(2,1)S(1)}, u32[]{:S(2)}, u32[]{:S(2)}) collective-permute-start(bf16[32,1,1024]{2,1,0:T(2,128)(2,1)S(1)} %get-tuple-element.12), channel_id=1, source_target_pairs={{0,1},{1,2},{2,3},{4,5},{5,6},{6,7},{8,9},{9,10},{10,11},{12,13},{... | collective-permute-start | bytes 196616 | tf_op jit(solution)/shard_map/ppermute | solution.py:229
  21.9 1.9 %collective-permute-start.3 = (bf16[32,1,1024]{2,1,0:T(2,128)(2,1)S(1)}, bf16[32,1,1024]{2,1,0:T(2,128)(2,1)S(1)}, u32[]{:S(2)}, u32[]{:S(2)}) collective-permute-start(bf16[32,1,1024]{2,1,0:T(2,128)(2,1)S(1)} %get-tuple-element.13), channel_id=1, source_target_pairs={{1,0},{2,1},{3,2},{5,4},{6,5},{7,6},{9,8},{10,9},{11,10},{13,12},{... | collective-permute-start | bytes 196616 | tf_op jit(solution)/shard_map/ppermute | solution.py:230
  23.8 0.0 copy-done.2
  23.8 0.1 compare_convert_fusion
  23.9 0.0 collective-permute-done
  23.9 0.0 collective-permute-done.1
  23.9 0.0 all-to-all-done
  23.9 0.1 multiply_reduce_fusion.1
  24.1 0.2 multiply_reduce_fusion
  24.3 0.8 %dynamic-slice_subtract_fusion = f32[3,16,128]{2,1,0:T(8,128)S(1)} fusion(f32[3,16,128]{2,1,0:T(8,128)S(1)} %get-tuple-element.8, f32[3,16,1024]{2,1,0:T(8,128)} %param.6, s32[]{:T(128)S(6)} %select_n.39), kind=kLoop, calls=%fused_computation.20 | loop fusion | flops 6144 | bytes 73732 | tf_op jit(solution)/shard_map/sub | solution.py:209
  25.1 0.1 multiply_reduce_fusion.3
  25.2 0.7 %pad_maximum_fusion = f32[8,4,16,128]{3,2,1,0:T(8,128)} fusion(f32[8,1,16,128]{3,2,1,0:T(8,128)S(1)} %fusion.2, f32[8,3,16,128]{3,2,1,0:T(8,128)S(1)} %get-tuple-element.18), kind=kLoop, calls=%fused_computation.2 | loop fusion | flops 65536 | bytes 524288 | tf_op jit(solution)/shard_map/concatenate | solution.py:213
  25.9 6.3 %all-to-all-start.1 = ((f32[8,4,16,128]{3,2,1,0:T(8,128)}), f32[8,4,16,128]{3,2,1,0:T(8,128)S(1)}, u32[]{:S(2)}, u32[]{:S(2)}) async-start(f32[8,4,16,128]{3,2,1,0:T(8,128)} %pad_maximum_fusion), calls=%async_computation.1 | async-start | bytes 524288 | tf_op jit(solution)/shard_map/all_to_all | solution.py:257
  32.2 0.7 %maximum_convert_fusion.1.zhalo_ref = f32[2,16,1024]{2,1,0:T(8,128)} fusion(bf16[1,16,1024]{2,1,0:T(8,128)(2,1)S(1)} %get-tuple-element.15, bf16[1,16,1024]{2,1,0:T(8,128)(2,1)S(1)} %get-tuple-element.14), kind=kLoop, calls=%fused_computation.10 | loop fusion | flops 65536 | bytes 196608 | tf_op jit(solution)/shard_map/convert_element_type | solution.py:235
  32.9 0.0 collective-permute-done.2
  32.9 0.0 collective-permute-done.3
  32.9 0.4 broadcast_select_fusion.1
  33.3 0.0 copy-start.1
  33.3 1.0 %maximum_convert_fusion.rhalo_ref = f32[32,2,1024]{2,1,0:T(2,128)} fusion(bf16[32,1,1024]{2,1,0:T(2,128)(2,1)S(1)} %get-tuple-element.11, bf16[32,1,1024]{2,1,0:T(2,128)(2,1)S(1)} %get-tuple-element.10), kind=kLoop, calls=%fused_computation.9 | loop fusion | flops 262144 | bytes 393216 | tf_op jit(solution)/shard_map/convert_element_type | solution.py:236
  34.3 4.0 %shard_map.60.smooth_ref = f32[32,16,1024]{2,1,0:T(8,128)} custom-call(bf16[32,16,1024]{2,1,0:T(8,128)(2,1)} %d_ref.5, f32[2,16,1024]{2,1,0:T(8,128)} %maximum_convert_fusion.1.zhalo_ref, f32[32,2,1024]{2,1,0:T(2,128)} %maximum_convert_fusion.rhalo_ref), custom_call_target="tpu_custom_call" | custom-call | tf_op jit(solution)/shard_map/pallas_call | solution.py:160
  38.4 1.9 %all-to-all-done.1.ans_ref = f32[8,4,16,128]{3,2,1,0:T(8,128)S(1)} async-done(((f32[8,4,16,128]{3,2,1,0:T(8,128)}), f32[8,4,16,128]{3,2,1,0:T(8,128)S(1)}, u32[]{:S(2)}, u32[]{:S(2)}) %all-to-all-start.1) | async-done | bytes 262176 | tf_op jit(solution)/shard_map/all_to_all | solution.py:257
  40.3 0.0 copy-done.1
  40.3 8.2 %shard_map.61 = (f32[32,16,1024]{2,1,0:T(8,128)}, f32[3,32,16,1024]{3,2,1,0:T(8,128)}) custom-call(bf16[32,16,1024]{2,1,0:T(8,128)(2,1)S(1)} %copy-done.1, bf16[3,32,16,1024]{3,2,1,0:T(8,128)(2,1)} %c_ref.3, f32[8,4,16,128]{3,2,1,0:T(8,128)S(1)} %all-to-all-done.1.ans_ref, f32[32,16,1024]{2,1,0:T(8,128)} %shard_map.60.smooth_ref), custom_call_target="tpu_custom_call", output_to_operand_aliasing={{0}: (3, {})} | custom-call | tf_op jit(solution)/shard_map/pallas_call | solution.py:179
  (7 shorter events, 0.1 us)
Async XLA Ops:
  0.6 1.2 %copy-start = (bf16[32,16,1024]{2,1,0:T(8,128)(2,1)S(1)}, bf16[32,16,1024]{2,1,0:T(8,128)(2,1)}, u32[]{:S(2)}) copy-start(bf16[32,16,1024]{2,1,0:T(8,128)(2,1)} %d_ref.5) | copy-start | bytes 3145732
  1.9 21.9 %copy-start.2 = (s32[8]{0:T(128)S(1)}, s32[8]{0:T(128)}, u32[]{:S(2)}) copy-start(s32[8]{0:T(128)} %param.7) | copy-start | bytes 100
  6.1 17.8 %all-to-all-start = ((f32[8,4,16,128]{3,2,1,0:T(8,128)}), f32[8,4,16,128]{3,2,1,0:T(8,128)S(1)}, u32[]{:S(2)}, u32[]{:S(2)}) async-start(f32[8,4,16,128]{3,2,1,0:T(8,128)} %shard_map.59), calls=%async_computation | async-start | bytes 524288 | tf_op jit(solution)/shard_map/all_to_all | solution.py:249
  12.5 11.4 %collective-permute-start = (bf16[1,16,1024]{2,1,0:T(8,128)(2,1)S(1)}, bf16[1,16,1024]{2,1,0:T(8,128)(2,1)S(1)}, u32[]{:S(2)}, u32[]{:S(2)}) collective-permute-start(bf16[1,16,1024]{2,1,0:T(8,128)(2,1)S(1)} %get-tuple-element.16), channel_id=1, source_target_pairs={{0,4},{4,8},{8,12},{12,16},{16,20},{20,24},{24,28},{1,5},{5,9},{9,... | collective-permute-start | bytes 98312 | tf_op jit(solution)/shard_map/ppermute | solution.py:227
  15.8 8.1 %collective-permute-start.1 = (bf16[1,16,1024]{2,1,0:T(8,128)(2,1)S(1)}, bf16[1,16,1024]{2,1,0:T(8,128)(2,1)S(1)}, u32[]{:S(2)}, u32[]{:S(2)}) collective-permute-start(bf16[1,16,1024]{2,1,0:T(8,128)(2,1)S(1)} %get-tuple-element.17), channel_id=1, source_target_pairs={{4,0},{8,4},{12,8},{16,12},{20,16},{24,20},{28,24},{5,1},{9,5},{13... | collective-permute-start | bytes 98312 | tf_op jit(solution)/shard_map/ppermute | solution.py:228
  17.3 15.6 %collective-permute-start.2 = (bf16[32,1,1024]{2,1,0:T(2,128)(2,1)S(1)}, bf16[32,1,1024]{2,1,0:T(2,128)(2,1)S(1)}, u32[]{:S(2)}, u32[]{:S(2)}) collective-permute-start(bf16[32,1,1024]{2,1,0:T(2,128)(2,1)S(1)} %get-tuple-element.12), channel_id=1, source_target_pairs={{0,1},{1,2},{2,3},{4,5},{5,6},{6,7},{8,9},{9,10},{10,11},{12,13},{... | collective-permute-start | bytes 196616 | tf_op jit(solution)/shard_map/ppermute | solution.py:229
  21.9 11.0 %collective-permute-start.3 = (bf16[32,1,1024]{2,1,0:T(2,128)(2,1)S(1)}, bf16[32,1,1024]{2,1,0:T(2,128)(2,1)S(1)}, u32[]{:S(2)}, u32[]{:S(2)}) collective-permute-start(bf16[32,1,1024]{2,1,0:T(2,128)(2,1)S(1)} %get-tuple-element.13), channel_id=1, source_target_pairs={{1,0},{2,1},{3,2},{5,4},{6,5},{7,6},{9,8},{10,9},{11,10},{13,12},{... | collective-permute-start | bytes 196616 | tf_op jit(solution)/shard_map/ppermute | solution.py:230
  25.9 14.3 %all-to-all-start.1 = ((f32[8,4,16,128]{3,2,1,0:T(8,128)}), f32[8,4,16,128]{3,2,1,0:T(8,128)S(1)}, u32[]{:S(2)}, u32[]{:S(2)}) async-start(f32[8,4,16,128]{3,2,1,0:T(8,128)} %pad_maximum_fusion), calls=%async_computation.1 | async-start | bytes 524288 | tf_op jit(solution)/shard_map/all_to_all | solution.py:257
  33.3 6.9 %copy-start.1 = (bf16[32,16,1024]{2,1,0:T(8,128)(2,1)S(1)}, bf16[32,16,1024]{2,1,0:T(8,128)(2,1)}, u32[]{:S(2)}) copy-start(bf16[32,16,1024]{2,1,0:T(8,128)(2,1)} %d_ref.5) | copy-start | bytes 3145732
